TPU v7x, 32 devices: a whole 2x2x4 slice. The times are simulated.
32 devices in a mesh: groups: 2 (over y), ctx: 8 (over z, x), tp: 2 (over core).
Axes of the slice: x: 2, y: 2, z: 4, core: 2. Of those that a mesh axis runs over, the one named last changes fastest.
Arguments:
- x_in: bfloat16 [4096, 4, 512], P(('groups', 'ctx'), 'tp'), parts along dimension 0, may hold values from -6 to 6
- b_in: bfloat16 [4096, 4, 64], P(('groups', 'ctx'), 'tp'), parts along dimension 0, may hold values from -1.75 to 1.75
- c_in: bfloat16 [4096, 4, 64], P(('groups', 'ctx'), 'tp'), parts along dimension 0, may hold values from -1.75 to 1.75
- dt_in: float32 [4096, 4, 8], P(('groups', 'ctx'), 'tp'), parts along dimension 0, may hold values from -4 to 4
- rate: float32 [4, 8], P('tp'), may hold values from 2.4414063e-05 to 0.5
- dt_bias: float32 [4, 8], P('tp'), may hold values from -2.5 to -1
- skip: float32 [4, 8], P('tp'), may hold values from 0.5 to 1.5
- conv_x: float32 [4, 4, 512], P(None, 'tp'), may hold values from -3 to 3
- conv_b: float32 [4, 4, 64], P(None, 'tp'), may hold values from -3 to 3
- conv_c: float32 [4, 4, 64], P(None, 'tp'), may hold values from -3 to 3
- grad_y: bfloat16 [4096, 4, 512], P(('groups', 'ctx'), 'tp'), parts along dimension 0, may hold values from -6 to 6
Outputs:
- y_out: bfloat16 [4096, 4, 512], P(('groups', 'ctx'), 'tp'), parts along dimension 0
- grad_x: bfloat16 [4096, 4, 512], P(('groups', 'ctx'), 'tp'), parts along dimension 0
- grad_b: bfloat16 [4096, 4, 64], P(('groups', 'ctx'), 'tp'), parts along dimension 0
- grad_c: bfloat16 [4096, 4, 64], P(('groups', 'ctx'), 'tp'), parts along dimension 0
- grad_dt: float32 [4096, 4, 8], P(('groups', 'ctx'), 'tp'), parts along dimension 0
There are 2 independent parts, one for each index of `groups`. A program takes and returns all parts, laid end to end along the dimension named above; an argument that names none is the same for every part. Nothing has to cross between parts.
All inputs are finite; a program needn't handle non-finite values.
Results may differ from a plain program's by a relative error of at most 0.013.
Values may be sent and summed in bfloat16 or wider, within the bound.
No kernel may reach another device: no remote copies, remote signals or barrier semaphores. Data moves between devices by JAX's collectives and lax.ppermute only.
A program may use at most 256 MiB of HBM per device.

v0:
```python
import jax
import jax.numpy as jnp
from jax import lax
from jax.sharding import PartitionSpec as P

HIGH = lax.Precision.HIGHEST


def from_behind(array, axis, by):
    count = lax.axis_size(axis)
    pairs = [(i, i + by) for i in range(count) if 0 <= i + by < count]
    return lax.ppermute(array, axis, pairs)


def carried_in(array, axis, join, neutral, backward):
    count = lax.axis_size(axis)
    place = lax.axis_index(axis)
    ahead = count - 1 - place if backward else place
    gathered = jax.tree.map(
        lambda a, kind: lax.all_gather(a.astype(kind), axis), array, (jnp.bfloat16, jnp.bfloat16)
    )
    state = jax.tree.map(lambda a, e: jnp.zeros_like(a) + jnp.asarray(e, a.dtype), array, neutral)

    def one(step, state):
        source = count - 1 - step if backward else step
        return join(
            state,
            jax.tree.map(
                lambda a, own: lax.dynamic_index_in_dim(a, source, 0, False).astype(own.dtype),
                gathered,
                array,
            ),
        )

    return lax.fori_loop(0, ahead, one, state)


def conv_forward(extended, weight):
    kernel_width = weight.shape[0]
    length = extended.shape[0] - kernel_width + 1
    running = weight[0] * extended[0:length].astype(jnp.float32)
    for tap_index in range(1, kernel_width):
        running = running + weight[tap_index] * extended[tap_index : tap_index + length].astype(
            jnp.float32
        )
    return running


def conv_backward(grad_out, running, weight):
    sigmoid_v = jax.nn.sigmoid(running)
    inner_grad = grad_out.astype(jnp.float32) * (sigmoid_v * (1.0 + running * (1.0 - sigmoid_v)))
    kernel_width = weight.shape[0]
    ext_len = inner_grad.shape[0] + kernel_width - 1
    padding = [(kernel_width - 1, kernel_width - 1)] + [(0, 0)] * (inner_grad.ndim - 1)
    padded = jnp.pad(inner_grad, padding)
    result = weight[0] * padded[kernel_width - 1 : kernel_width - 1 + ext_len]
    for tap_index in range(1, kernel_width):
        offset = kernel_width - 1 - tap_index
        result = result + weight[tap_index] * padded[offset : offset + ext_len]
    return result


def ssd_block(x_float, b_float, c_float, dt_raw, rate, dt_bias, skip):
    length, groups, channels = x_float.shape
    head_count = dt_raw.shape[2]
    head_size = channels // head_count
    step_size = jax.nn.softplus(dt_raw + dt_bias)
    cum_log = jnp.cumsum(-rate * step_size, axis=0)
    x_heads = x_float.reshape(length, groups, head_count, head_size)
    x_half = x_heads.astype(jnp.bfloat16)
    cum_heads = jnp.transpose(cum_log, (1, 2, 0))
    step_heads = jnp.transpose(step_size, (1, 2, 0))
    row_index = lax.broadcasted_iota(jnp.int32, (length, length), 0)
    col_index = lax.broadcasted_iota(jnp.int32, (length, length), 1)
    causal = row_index >= col_index
    decay_all = jnp.where(
        causal, jnp.exp(jnp.minimum(cum_heads[:, :, :, None] - cum_heads[:, :, None, :], 0.0)), 0.0
    )
    scores = jnp.einsum("tgn,sgn->gts", c_float, b_float, precision=HIGH)
    mixing = (scores[:, None] * decay_all * step_heads[:, :, None, :]).astype(jnp.bfloat16)
    y_local = jnp.einsum("ghts,sghp->tghp", mixing, x_half, preferred_element_type=jnp.float32)
    y_local = y_local + skip[None, :, :, None] * x_heads
    tail_weight = jnp.exp(cum_log[-1][None] - cum_log) * step_size
    weighted = (x_heads * tail_weight[..., None]).astype(jnp.bfloat16)
    state_end = jnp.einsum("sghp,sgn->ghpn", weighted.astype(jnp.float32), b_float, precision=HIGH)
    return (y_local, cum_log, state_end)


def carry_in(c_float, cum_log, state_in):
    carried = jnp.einsum("tgn,ghpn->tghp", c_float, state_in, precision=HIGH)
    return carried * jnp.exp(cum_log)[..., None]


def chain_join(earlier, latter):
    return (earlier[0] * latter[0], latter[0][:, :, None, None] * earlier[1] + latter[1])


def on_device(x_in, b_in, c_in, dt_in, rate, dt_bias, skip, conv_x, conv_b, conv_c, grad_y):
    kernel_width = conv_x.shape[0]
    halo_rows = kernel_width - 1
    length, groups, channels = x_in.shape
    head_count = dt_in.shape[2]
    head_size = channels // head_count
    state_size = b_in.shape[2]
    x_span = groups * channels
    b_span = groups * state_size
    outgoing = jnp.concatenate(
        [
            x_in[length - halo_rows :].reshape(halo_rows, x_span),
            b_in[length - halo_rows :].reshape(halo_rows, b_span),
            c_in[length - halo_rows :].reshape(halo_rows, b_span),
        ],
        1,
    )
    incoming = from_behind(outgoing, "ctx", 1)
    x_ext = jnp.concatenate([incoming[:, :x_span].reshape(halo_rows, groups, channels), x_in], 0)
    b_ext = jnp.concatenate(
        [incoming[:, x_span : x_span + b_span].reshape(halo_rows, groups, state_size), b_in], 0
    )
    c_ext = jnp.concatenate(
        [incoming[:, x_span + b_span :].reshape(halo_rows, groups, state_size), c_in], 0
    )
    x_running = conv_forward(x_ext, conv_x)
    b_running = conv_forward(b_ext, conv_b)
    c_running = conv_forward(c_ext, conv_c)
    x_float = jax.nn.silu(x_running).astype(jnp.bfloat16).astype(jnp.float32)
    b_float = jax.nn.silu(b_running).astype(jnp.bfloat16).astype(jnp.float32)
    c_float = jax.nn.silu(c_running).astype(jnp.bfloat16).astype(jnp.float32)

    def local_map(x_arg, b_arg, c_arg, dt_arg):
        return ssd_block(x_arg, b_arg, c_arg, dt_arg, rate, dt_bias, skip)

    (y_local, cum_log, state_end), local_pull = jax.vjp(local_map, x_float, b_float, c_float, dt_in)
    decay_total = jnp.exp(cum_log[-1])
    grad_heads = grad_y.astype(jnp.float32).reshape(length, groups, head_count, head_size)
    seed_state = jnp.einsum(
        "tghp,tgn->ghpn", jnp.exp(cum_log)[..., None] * grad_heads, c_float, precision=HIGH
    )
    identity = (jnp.ones_like(decay_total), jnp.zeros_like(state_end))
    state_in = carried_in((decay_total, state_end), "ctx", chain_join, identity, False)[1]
    adjoint = carried_in((decay_total, seed_state), "ctx", chain_join, identity, True)[1]

    def carry_map(c_arg, cum_arg):
        return carry_in(c_arg, cum_arg, state_in)

    y_carry, carry_pull = jax.vjp(carry_map, c_float, cum_log)
    y_out = (y_local + y_carry).reshape(length, groups, channels).astype(jnp.bfloat16)
    grad_c_carry, grad_cum_carry = carry_pull(grad_heads)
    end_term = jnp.sum(adjoint * state_in, axis=(2, 3)) * decay_total
    grad_cum = grad_cum_carry.at[length - 1].add(end_term)
    grad_x_conv, grad_b_part, grad_c_local, grad_dt = local_pull((grad_heads, grad_cum, adjoint))
    grad_c_part = grad_c_local + grad_c_carry
    grad_b_ext = conv_backward(grad_b_part.astype(jnp.bfloat16), b_running, conv_b)
    grad_c_ext = conv_backward(grad_c_part.astype(jnp.bfloat16), c_running, conv_c)
    grad_x_ext = conv_backward(grad_x_conv.astype(jnp.bfloat16), x_running, conv_x)
    leaving = jnp.concatenate(
        [
            grad_x_ext[:halo_rows].reshape(halo_rows, x_span),
            grad_b_ext[:halo_rows].reshape(halo_rows, b_span),
            grad_c_ext[:halo_rows].reshape(halo_rows, b_span),
        ],
        1,
    )
    returned = from_behind(leaving, "ctx", -1)
    back_x = returned[:, :x_span].reshape(halo_rows, groups, channels)
    back_b = returned[:, x_span : x_span + b_span].reshape(halo_rows, groups, state_size)
    back_c = returned[:, x_span + b_span :].reshape(halo_rows, groups, state_size)
    grad_x = grad_x_ext[halo_rows:].at[length - halo_rows :].add(back_x).astype(jnp.bfloat16)
    grad_b = grad_b_ext[halo_rows:].at[length - halo_rows :].add(back_b).astype(jnp.bfloat16)
    grad_c = grad_c_ext[halo_rows:].at[length - halo_rows :].add(back_c).astype(jnp.bfloat16)
    return (y_out, grad_x, grad_b, grad_c, grad_dt)


def solution(mesh):
    return jax.shard_map(
        on_device,
        mesh=mesh,
        in_specs=(
            P(("groups", "ctx"), "tp", None),
            P(("groups", "ctx"), "tp", None),
            P(("groups", "ctx"), "tp", None),
            P(("groups", "ctx"), "tp", None),
            P("tp", None),
            P("tp", None),
            P("tp", None),
            P(None, "tp", None),
            P(None, "tp", None),
            P(None, "tp", None),
            P(("groups", "ctx"), "tp", None),
        ),
        out_specs=(
            P(("groups", "ctx"), "tp", None),
            P(("groups", "ctx"), "tp", None),
            P(("groups", "ctx"), "tp", None),
            P(("groups", "ctx"), "tp", None),
            P(("groups", "ctx"), "tp", None),
        ),
        check_vma=False,
    )
```

profile of v0, /device:TPU:26, one launch (start us, length us, event | category | flops | bytes accessed | tf_op | source)
XLA Modules:
  0.0 174.8 jit_solution(16487108078618479898)
XLA Ops:
  7.2 0.9 slice.271
  8.2 0.9 slice.272
  9.1 0.7 slice_bitcast_fusion.1
  9.9 1.3 collective-permute-start
  11.2 0.7 slice_bitcast_fusion.9
  11.9 0.7 neg.30
  13.2 0.8 multiply_bitcast_fusion
  14.0 1.2 reduce-window.14
  15.6 0.8 fusion.96
  16.5 0.7 slice_bitcast_fusion.13
  17.2 1.3 copy.93
  18.8 2.2 %multiply_convert_fusion.1 = (bf16[256,2,64]{0,2,1:T(8,128)(2,1)S(1)}, f32[256,2,64]{0,2,1:T(8,128)}, bf16[256,2,64]{0,2,1:T(8,128)(2,1)S(1)}, f32[256,2,64]{0,2,1:T(8,128)}) fusion(bf16[256,2,64]{0,2,1:T(8,128)(2,1)} %param.24, f32[2,64]{1,0:T(2,128)S(1)} %get-tuple-element.271, bf16[3,2,64]{0,2,1:T(8,128)(2,1)S(1)} %bitcast.253, ...), kind=kLoop, calls=%fused_computation.97 | loop fusion | flops 1638400 | bytes 529920 | tf_op jit(solution)/shard_map/convert_element_type | solution.py:127
  21.0 1.4 fusion.50
  22.6 16.1 %all_gather.18 = bf16[8,2,8]{2,1,0:T(2,128)(2,1)S(1)} all-gather(bf16[1,2,8]{2,1,0:T(2,128)(2,1)S(1)} %copy.92), channel_id=1, replica_groups=mesh['groups'=2,'ctx'=8,'tp'=2] {'ctx'}, dimensions={0}, use_global_device_ids=true | all-gather | bytes 288 | tf_op jit(solution)/shard_map/all_gather | solution.py:20
  39.6 32.0 %all-gather.7.cloned.1.call-done = bf16[16,8,64,64]{3,2,1,0:T(8,128)(2,1)} async-done(((bf16[2,8,64,64]{3,2,1,0:T(8,128)(2,1)}), bf16[16,8,64,64]{3,2,1,0:T(8,128)(2,1)}) %all-gather.7.cloned.1.call-update) | async-done | bytes 1048592 | tf_op jit(solution)/shard_map/all_gather | solution.py:20
  72.3 1.6 fusion.45
  74.0 1.3 copy.94
  75.3 3.8 %multiply_multiply_fusion = (f32[256,2,512]{2,1,0:T(2,128)S(1)}, f32[256,2,512]{2,1,0:T(2,128)S(1)}) fusion(f32[256,2,512]{2,1,0:T(2,128)} %copy.94, bf16[256,2,512]{2,1,0:T(2,128)(2,1)S(1)} %copy-done.3, f32[2,512]{1,0:T(2,128)S(1)} %get-tuple-element.262, bf16[259,2,512]{2,1,0:T(2,128)(2,1)S(1)} %constant_dynamic-update-slice_fusion, ...), kind=kLoop, calls=%fused_computation.66 | loop fusion | flops 4980736 | bytes 5259264 | tf_op jit(solution)/shard_map/mul | solution.py:51
  79.2 1.1 multiply_convert_fusion
  80.8 1.0 convolution_convert_fusion.2
  81.8 0.6 convolution_bitcast_fusion.2
  82.6 5.7 %fusion.18 = (f32[2,8,256]{2,1,0:T(8,128)}, f32[2,8,256]{2,1,0:T(8,128)}, f32[2,8,256]{2,1,0:T(8,128)}, f32[2,256,256]{2,1,0:T(8,128)S(1)}) fusion(f32[2,8,256]{2,1,0:T(8,128)S(1)} %get-tuple-element.266, f32[2,8,256]{2,1,0:T(8,128)S(1)} %get-tuple-element.258, f32[2,256,256]{2,1,0:T(8,128)S(1)} %copy-done.7, pred[256,256]{1,0:T(8,128)(4,1)} %copy-done.15, ...), kind=kOutput, calls=%fused_computation.31 | convolution fusion | flops 156094464 | bytes 2244608 | tf_op jit(solution)/shard_map/transpose(jvp(ghts,sghp->tghp))/dot_general | solution.py:81
  88.2 0.8 copy-done.4
  89.7 0.7 slice.349
  90.4 0.7 copy.97
  91.1 1.3 multiply_add_fusion
  92.4 1.2 slice.343
  93.6 0.6 copy.119
  94.4 42.9 %all-gather.5.cloned.1.call-done = bf16[16,8,64,64]{3,2,1,0:T(8,128)(2,1)} async-done(((bf16[2,8,64,64]{3,2,1,0:T(8,128)(2,1)}), bf16[16,8,64,64]{3,2,1,0:T(8,128)(2,1)}) %all-gather.5.cloned.1.call-update) | async-done | bytes 1048592 | tf_op jit(solution)/shard_map/all_gather | solution.py:20
  137.3 8.3 %while.30 = (s32[]{:T(128)}, f32[2,8,64,64]{3,2,1,0:T(8,128)S(1)}, s32[]{:T(128)}, bf16[8,2,8]{2,1,0:T(2,128)(2,1)S(1)}, bf16[8,2,8,64,64]{4,3,2,1,0:T(8,128)(2,1)}, /*index=5*/s32[]{:T(128)}, s32[]{:T(128)}, s32[]{:T(128)}) while((s32[]{:T(128)}, f32[2,8,64,64]{3,2,1,0:T(8,128)S(1)}, s32[]{:T(128)}, bf16[8,2,8]{2,1,0:T(2,128)(2,1)S(1)}, ...), condition=%wide.region_3.4_spmd, body=%wide.region_2.3_spmd.sunk | while | flops 196629 | bytes 655647 | solution.py:35
  137.3 1.1 convert_add_fusion.4
  138.5 1.1 convert_add_fusion.4
  139.7 1.1 convert_add_fusion.4
  140.8 1.1 convert_add_fusion.4
  142.0 1.1 convert_add_fusion.4
  143.1 1.1 convert_add_fusion.4
  144.3 1.1 convert_add_fusion.4
  145.6 2.2 %fusion.63 = (f32[256,2,8]{0,2,1:T(8,128)}, f32[256,2,8,64]{0,3,2,1:T(8,128)}) fusion(bf16[256,2,512]{0,2,1:T(8,128)(2,1)S(1)} %copy.93, f32[2,8,64,64]{3,2,1,0:T(8,128)S(1)} %get-tuple-element.181, bf16[256,2,64]{0,2,1:T(8,128)(2,1)S(1)} %get-tuple-element.279), kind=kOutput, calls=%fused_computation.65 | convolution fusion | flops 202108928 | bytes 1916928 | tf_op jit(solution)/shard_map/jvp(tgn,ghpn->tghp)/dot_general | solution.py:90
  148.1 1.1 convolution_bitcast_fusion.3
  149.3 0.9 fusion.102
  150.5 0.8 fusion.95
  151.3 5.0 %reduce-window.16 = f32[8,2,2,128]{3,0,1,2:T(8,128)S(1)} reduce-window(f32[8,2,2,128]{3,0,1,2:T(8,128)S(1)} %copy.103, f32[]{:T(128)} %constant.174.clone.1), window={size=1x1x1x128 pad=0_0x0_0x0_0x0_127}, to_apply=%region_14.15 | reduce-window | flops 520192 | bytes 32772 | tf_op jit(solution)/shard_map/reduce-window.2
  156.4 1.3 fusion.58
  158.1 2.2 %collective-permute-start.1 = (f32[3,1280]{1,0:T(4,128)S(1)}, f32[3,1280]{1,0:T(4,128)S(1)}, u32[]{:S(2)}, u32[]{:S(2)}) collective-permute-start(f32[3,1280]{1,0:T(4,128)S(1)} %pad_maximum_fusion.2), channel_id=1, source_target_pairs={{2,0},{4,2},{6,4},{8,6},{10,8},{12,10},{14,12},{3,1},{5,3},{7,5},{... | collective-permute-start | bytes 46088 | tf_op jit(solution)/shard_map/ppermute | solution.py:12
  160.5 2.7 %fusion.30 = bf16[256,2,8,64]{0,3,2,1:T(8,128)(2,1)S(1)} fusion(bf16[256,2,8,64]{0,3,2,1:T(8,128)(2,1)S(1)} %bitcast.243, f32[2,8,256]{2,1,0:T(8,128)S(1)} %copy-done.28, f32[2,8,256]{2,1,0:T(8,128)S(1)} %copy-done.24, f32[2,256,256]{2,1,0:T(8,128)S(1)} %copy-done.8, pred[256,256]{1,0:T(8,128)(4,1)S(1)} %copy-done.16, ...), kind=kOutput, calls=%fused_computation.39 | convolution fusion | flops 142082048 | bytes 2736192 | tf_op jit(solution)/shard_map/jvp(ghts,sghp->tghp)/dot_general | solution.py:81
  163.3 0.7 fusion.92
  164.1 1.2 copy.107
  166.6 1.3 fusion.97
  (171 shorter events, 7.5 us)
Async XLA Ops:
  7.2 31.7 %copy-start.3 = (bf16[256,2,512]{2,1,0:T(2,128)(2,1)S(1)}, bf16[256,2,512]{2,1,0:T(2,128)(2,1)}, u32[]{:S(2)}) copy-start(bf16[256,2,512]{2,1,0:T(2,128)(2,1)} %param.23) | copy-start | bytes 1572868
  7.2 31.6 %copy-start.26 = (f32[4,2,512]{2,1,0:T(2,128)S(1)}, f32[4,2,512]{2,1,0:T(2,128)}, u32[]{:S(2)}) copy-start(f32[4,2,512]{2,1,0:T(2,128)} %param.30) | copy-start | bytes 49156
  7.2 64.4 %all-gather.7.cloned.1.call-start = ((), (), s32[]{:S(2)}) async-start(), calls=%async_computation.1 | async-start | bytes 2359296 | tf_op jit(solution)/shard_map/all_gather | solution.py:20
  9.9 8.6 %collective-permute-start = (bf16[3,1280]{1,0:T(4,128)(2,1)S(1)}, bf16[3,1280]{1,0:T(4,128)(2,1)S(1)}, u32[]{:S(2)}, u32[]{:S(2)}) collective-permute-start(bf16[3,1280]{1,0:T(4,128)(2,1)S(1)} %pad_maximum_fusion.3), channel_id=1, source_target_pairs={{0,2},{2,4},{4,6},{6,8},{8,10},{10,12},{12,14},{1,3},{3,5},{5,7},{... | collective-permute-start | bytes 23048 | tf_op jit(solution)/shard_map/ppermute | solution.py:12
  11.9 27.3 %copy-start.39 = (f32[2,64]{1,0:T(2,128)}, f32[2,64]{1,0:T(2,128)S(1)}, u32[]{:S(2)}) copy-start(f32[2,64]{1,0:T(2,128)S(1)} %get-tuple-element.269) | copy-start | bytes 1540
  11.9 27.3 %copy-start.41 = (f32[2,64]{1,0:T(2,128)}, f32[2,64]{1,0:T(2,128)S(1)}, u32[]{:S(2)}) copy-start(f32[2,64]{1,0:T(2,128)S(1)} %get-tuple-element.270) | copy-start | bytes 1540
  11.9 59.6 %copy-start.43 = (f32[2,64]{1,0:T(2,128)}, f32[2,64]{1,0:T(2,128)S(1)}, u32[]{:S(2)}) copy-start(f32[2,64]{1,0:T(2,128)S(1)} %get-tuple-element.271) | copy-start | bytes 1540
  11.9 59.6 %copy-start.45 = (f32[2,64]{1,0:T(2,128)}, f32[2,64]{1,0:T(2,128)S(1)}, u32[]{:S(2)}) copy-start(f32[2,64]{1,0:T(2,128)S(1)} %get-tuple-element.272) | copy-start | bytes 1540
  15.5 23.8 %copy-start.11 = (f32[256,2,8]{0,2,1:T(8,128)}, f32[256,2,8]{0,2,1:T(8,128)S(1)}, u32[]{:S(2)}) copy-start(f32[256,2,8]{0,2,1:T(8,128)S(1)} %get-tuple-element.265) | copy-start | bytes 49156
  15.5 67.0 %copy-start.23 = (f32[2,8,256]{2,1,0:T(8,128)}, f32[2,8,256]{2,1,0:T(8,128)S(1)}, u32[]{:S(2)}) copy-start(f32[2,8,256]{2,1,0:T(8,128)S(1)} %get-tuple-element.266) | copy-start | bytes 49156
  15.6 3.0 %copy-start.21 = (f32[2,8]{1,0:T(2,128)}, f32[2,8]{1,0:T(2,128)S(1)}, u32[]{:S(2)}) copy-start(f32[2,8]{1,0:T(2,128)S(1)} %slice_reduce_fusion) | copy-start | bytes 196
  16.4 66.0 %copy-start.27 = (f32[2,8,256]{2,1,0:T(8,128)}, f32[2,8,256]{2,1,0:T(8,128)S(1)}, u32[]{:S(2)}) copy-start(f32[2,8,256]{2,1,0:T(8,128)S(1)} %get-tuple-element.258) | copy-start | bytes 49156
  17.2 22.3 %copy-start.31 = (f32[2,64]{1,0:T(2,128)}, f32[2,64]{1,0:T(2,128)S(1)}, u32[]{:S(2)}) copy-start(f32[2,64]{1,0:T(2,128)S(1)} %get-tuple-element.273) | copy-start | bytes 1540
  17.2 22.3 %copy-start.33 = (f32[2,64]{1,0:T(2,128)}, f32[2,64]{1,0:T(2,128)S(1)}, u32[]{:S(2)}) copy-start(f32[2,64]{1,0:T(2,128)S(1)} %get-tuple-element.274) | copy-start | bytes 1540
  17.2 22.3 %copy-start.35 = (f32[2,64]{1,0:T(2,128)}, f32[2,64]{1,0:T(2,128)S(1)}, u32[]{:S(2)}) copy-start(f32[2,64]{1,0:T(2,128)S(1)} %get-tuple-element.275) | copy-start | bytes 1540
  17.2 22.4 %copy-start.37 = (f32[2,64]{1,0:T(2,128)}, f32[2,64]{1,0:T(2,128)S(1)}, u32[]{:S(2)}) copy-start(f32[2,64]{1,0:T(2,128)S(1)} %get-tuple-element.276) | copy-start | bytes 1540
  22.4 114.9 %all-gather.5.cloned.1.call-start = ((), (), s32[]{:S(2)}) async-start(), calls=%async_computation | async-start | bytes 2359296 | tf_op jit(solution)/shard_map/all_gather | solution.py:20
  38.7 33.5 %copy-start.15 = (pred[256,256]{1,0:T(8,128)(4,1)}, pred[256,256]{1,0:T(8,128)(4,1)S(1)}, u32[]{:S(2)}) copy-start(pred[256,256]{1,0:T(8,128)(4,1)S(1)} %iota_compare_fusion) | copy-start | bytes 196612
  39.6 32.7 %copy-start.6 = (f32[2,256,256]{2,1,0:T(8,128)}, f32[2,256,256]{2,1,0:T(8,128)S(1)}, u32[]{:S(2)}) copy-start(f32[2,256,256]{2,1,0:T(8,128)S(1)} %fusion.105) | copy-start | bytes 1572868
  72.2 1.7 copy-start
  80.8 1.7 copy-start.7
  82.5 6.5 %copy-start.9 = (f32[256,2,64]{0,2,1:T(8,128)S(1)}, f32[256,2,64]{0,2,1:T(8,128)}, u32[]{:S(2)}) copy-start(f32[256,2,64]{0,2,1:T(8,128)} %get-tuple-element.252) | copy-start | bytes 393220
  82.5 6.9 %copy-start.40 = (f32[2,64]{1,0:T(2,128)S(1)}, f32[2,64]{1,0:T(2,128)}, u32[]{:S(2)}) copy-start(f32[2,64]{1,0:T(2,128)} %copy-done.39) | copy-start | bytes 1540
  82.5 6.9 %copy-start.42 = (f32[2,64]{1,0:T(2,128)S(1)}, f32[2,64]{1,0:T(2,128)}, u32[]{:S(2)}) copy-start(f32[2,64]{1,0:T(2,128)} %copy-done.41) | copy-start | bytes 1540
  82.5 6.9 %copy-start.44 = (f32[2,64]{1,0:T(2,128)S(1)}, f32[2,64]{1,0:T(2,128)}, u32[]{:S(2)}) copy-start(f32[2,64]{1,0:T(2,128)} %copy-done.43) | copy-start | bytes 1540
  82.6 6.8 %copy-start.46 = (f32[2,64]{1,0:T(2,128)S(1)}, f32[2,64]{1,0:T(2,128)}, u32[]{:S(2)}) copy-start(f32[2,64]{1,0:T(2,128)} %copy-done.45) | copy-start | bytes 1540
  91.1 3.1 %copy-start.1 = (f32[256,2,8,64]{0,3,2,1:T(8,128)S(1)}, f32[256,2,8,64]{0,3,2,1:T(8,128)}, u32[]{:S(2)}) copy-start(f32[256,2,8,64]{0,3,2,1:T(8,128)} %copy-done) | copy-start | bytes 3145732
  145.6 3.7 %copy-start.10 = (f32[256,2,8]{0,2,1:T(8,128)S(1)}, f32[256,2,8]{0,2,1:T(8,128)}, u32[]{:S(2)}) copy-start(f32[256,2,8]{0,2,1:T(8,128)} %param.26) | copy-start | bytes 49156
  145.6 3.6 %copy-start.20 = (f32[2,8]{1,0:T(2,128)S(1)}, f32[2,8]{1,0:T(2,128)}, u32[]{:S(2)}) copy-start(f32[2,8]{1,0:T(2,128)} %param.28) | copy-start | bytes 196
  145.6 10.8 %copy-start.5 = (f32[2,256,256]{2,1,0:T(8,128)S(1)}, f32[2,256,256]{2,1,0:T(8,128)}, u32[]{:S(2)}) copy-start(f32[2,256,256]{2,1,0:T(8,128)} %copy-done.4) | copy-start | bytes 1572868
  147.9 2.4 %copy-start.12 = (f32[256,2,8]{0,2,1:T(8,128)S(1)}, f32[256,2,8]{0,2,1:T(8,128)}, u32[]{:S(2)}) copy-start(f32[256,2,8]{0,2,1:T(8,128)} %copy-done.11) | copy-start | bytes 49156
  147.9 10.3 %copy-start.14 = (f32[1,3,2,512]{3,1,2,0:T(4,128)S(1)}, f32[1,3,2,512]{3,1,2,0:T(4,128)}, u32[]{:S(2)}) copy-start(f32[1,3,2,512]{3,1,2,0:T(4,128)} %copy.119) | copy-start | bytes 36868
  147.9 12.5 %copy-start.8 = (f32[2,256,256]{2,1,0:T(8,128)S(1)}, f32[2,256,256]{2,1,0:T(8,128)}, u32[]{:S(2)}) copy-start(f32[2,256,256]{2,1,0:T(8,128)} %copy-done.6) | copy-start | bytes 1572868
  148.0 9.7 %copy-start.32 = (f32[2,64]{1,0:T(2,128)S(1)}, f32[2,64]{1,0:T(2,128)}, u32[]{:S(2)}) copy-start(f32[2,64]{1,0:T(2,128)} %copy-done.31) | copy-start | bytes 1540
  148.0 9.7 %copy-start.34 = (f32[2,64]{1,0:T(2,128)S(1)}, f32[2,64]{1,0:T(2,128)}, u32[]{:S(2)}) copy-start(f32[2,64]{1,0:T(2,128)} %copy-done.33) | copy-start | bytes 1540
  148.0 9.7 %copy-start.36 = (f32[2,64]{1,0:T(2,128)S(1)}, f32[2,64]{1,0:T(2,128)}, u32[]{:S(2)}) copy-start(f32[2,64]{1,0:T(2,128)} %copy-done.35) | copy-start | bytes 1540
  148.0 9.7 %copy-start.38 = (f32[2,64]{1,0:T(2,128)S(1)}, f32[2,64]{1,0:T(2,128)}, u32[]{:S(2)}) copy-start(f32[2,64]{1,0:T(2,128)} %copy-done.37) | copy-start | bytes 1540
  148.1 10.1 %copy-start.47 = (f32[3,128]{1,0:T(4,128)S(1)}, f32[3,128]{1,0:T(4,128)}, u32[]{:S(2)}) copy-start(f32[3,128]{1,0:T(4,128)} %copy.97) | copy-start | bytes 4612
  148.1 12.3 %copy-start.16 = (pred[256,256]{1,0:T(8,128)(4,1)S(1)}, pred[256,256]{1,0:T(8,128)(4,1)}, u32[]{:S(2)}) copy-start(pred[256,256]{1,0:T(8,128)(4,1)} %copy-done.15) | copy-start | bytes 196612
  148.1 12.3 %copy-start.24 = (f32[2,8,256]{2,1,0:T(8,128)S(1)}, f32[2,8,256]{2,1,0:T(8,128)}, u32[]{:S(2)}) copy-start(f32[2,8,256]{2,1,0:T(8,128)} %copy-done.23) | copy-start | bytes 49156
  148.1 12.3 %copy-start.28 = (f32[2,8,256]{2,1,0:T(8,128)S(1)}, f32[2,8,256]{2,1,0:T(8,128)}, u32[]{:S(2)}) copy-start(f32[2,8,256]{2,1,0:T(8,128)} %copy-done.27) | copy-start | bytes 49156
  148.1 12.3 %copy-start.49 = (f32[2,8]{1,0:T(2,128)S(1)}, f32[2,8]{1,0:T(2,128)}, u32[]{:S(2)}) copy-start(f32[2,8]{1,0:T(2,128)} %param.29) | copy-start | bytes 196
  158.1 7.1 %collective-permute-start.1 = (f32[3,1280]{1,0:T(4,128)S(1)}, f32[3,1280]{1,0:T(4,128)S(1)}, u32[]{:S(2)}, u32[]{:S(2)}) collective-permute-start(f32[3,1280]{1,0:T(4,128)S(1)} %pad_maximum_fusion.2), channel_id=1, source_target_pairs={{2,0},{4,2},{6,4},{8,6},{10,8},{12,10},{14,12},{3,1},{5,3},{7,5},{... | collective-permute-start | bytes 46088 | tf_op jit(solution)/shard_map/ppermute | solution.py:12
  160.4 2.8 %copy-start.22 = (f32[2,8]{1,0:T(2,128)S(1)}, f32[2,8]{1,0:T(2,128)}, u32[]{:S(2)}) copy-start(f32[2,8]{1,0:T(2,128)} %copy-done.21) | copy-start | bytes 196
  160.4 2.8 %copy-start.25 = (f32[2,8,256]{2,1,0:T(8,128)S(1)}, f32[2,8,256]{2,1,0:T(8,128)}, u32[]{:S(2)}) copy-start(f32[2,8,256]{2,1,0:T(8,128)} %get-tuple-element.225) | copy-start | bytes 49156
  160.4 2.8 %copy-start.30 = (f32[2,8]{1,0:T(2,128)S(1)}, f32[2,8]{1,0:T(2,128)}, u32[]{:S(2)}) copy-start(f32[2,8]{1,0:T(2,128)} %copy-done.29) | copy-start | bytes 196
  160.5 5.6 %copy-start.17 = (bf16[256,2,64]{0,2,1:T(8,128)(2,1)S(1)}, bf16[256,2,64]{0,2,1:T(8,128)(2,1)}, u32[]{:S(2)}) copy-start(bf16[256,2,64]{0,2,1:T(8,128)(2,1)} %slice.349) | copy-start | bytes 196612
  166.1 1.9 %copy-start.19 = (bf16[256,2,64]{0,2,1:T(8,128)(2,1)}, bf16[256,2,64]{0,2,1:T(8,128)(2,1)S(1)}, u32[]{:S(2)}) copy-start(bf16[256,2,64]{0,2,1:T(8,128)(2,1)S(1)} %scatter-add.16) | copy-start | bytes 196612
  (6 other events, 6.0 us)
Sparse Core Ops, SparseCore 0:
  22.5 48.9 all-gather.6
  82.6 54.6 all-gather.4
where the time goes:
time: 176 us; the launch traced here: 175 us
  waiting for transfers between devices  74.9 us (43%)
  other arithmetic  29.8 us (17%)
  matrix products  18.7 us (11%)
  local copies, waits for them, and re-layouts  16.4 us (9%)
  blocking collectives  16.1 us (9%)
  between operations  14.9 us (8%)
  starting transfers between devices  3.59 us (2%)
    all_gather x2, waiting for transfers between devices, carried_in(): lax.all_gather(a.astype(kind), axis)  74.8 us
    all_gather x1, blocking collectives, carried_in(): lax.all_gather(a.astype(kind), axis)  16.1 us
    dot_general x3, matrix products, ssd_block(): jnp.einsum('ghts,sghp->tghp', mixing, x_half, preferred_element_type=jnp....  10 us
    another operation x7, other arithmetic  7.9 us
    add x7, other arithmetic, chain_join(): latter[0][:, :, None, None] * earlier[1] + latter[1]  7.78 us
    unnamed x107, local copies, waits for them, and re-layouts  5.48 us
    mul x1, other arithmetic, conv_backward(): grad_out.astype(jnp.float32)  3.82 us
  transfers between devices with their start and end apart: 4, of which 2 were waited for; matrix products, arithmetic and copies ran while one was open for 13% of the time, Pallas kernels for 0%

commit v1 on v0

--- a/solution.py
+++ b/solution.py
@@ -12,27 +12,26 @@
     return lax.ppermute(array, axis, pairs)
 
 
-def carried_in(array, axis, join, neutral, backward):
+def scanned_in(decay, state, axis, backward):
     count = lax.axis_size(axis)
-    place = lax.axis_index(axis)
-    ahead = count - 1 - place if backward else place
-    gathered = jax.tree.map(
-        lambda a, kind: lax.all_gather(a.astype(kind), axis), array, (jnp.bfloat16, jnp.bfloat16)
-    )
-    state = jax.tree.map(lambda a, e: jnp.zeros_like(a) + jnp.asarray(e, a.dtype), array, neutral)
+    sign = -1 if backward else 1
 
-    def one(step, state):
-        source = count - 1 - step if backward else step
-        return join(
-            state,
-            jax.tree.map(
-                lambda a, own: lax.dynamic_index_in_dim(a, source, 0, False).astype(own.dtype),
-                gathered,
-                array,
-            ),
-        )
+    def shift(tree, by):
+        pairs = [(i, i + sign * by) for i in range(count) if 0 <= i + sign * by < count]
+        return lax.ppermute(tree, axis, pairs)
 
-    return lax.fori_loop(0, ahead, one, state)
+    before_decay, before_state = shift((decay, state), 1)
+    upto_decay = before_decay * decay
+    upto_state = decay[:, :, None, None] * before_state + state
+    by = 2
+    while by < count:
+        got_decay, got_state = shift((upto_decay, upto_state), by)
+        before_state = before_decay[:, :, None, None] * got_state + before_state
+        before_decay = before_decay * got_decay
+        upto_state = upto_decay[:, :, None, None] * got_state + upto_state
+        upto_decay = upto_decay * got_decay
+        by *= 2
+    return before_state
 
 
 def conv_forward(extended, weight):
@@ -91,10 +90,6 @@
     return carried * jnp.exp(cum_log)[..., None]
 
 
-def chain_join(earlier, latter):
-    return (earlier[0] * latter[0], latter[0][:, :, None, None] * earlier[1] + latter[1])
-
-
 def on_device(x_in, b_in, c_in, dt_in, rate, dt_bias, skip, conv_x, conv_b, conv_c, grad_y):
     kernel_width = conv_x.shape[0]
     halo_rows = kernel_width - 1
@@ -136,9 +131,8 @@
     seed_state = jnp.einsum(
         "tghp,tgn->ghpn", jnp.exp(cum_log)[..., None] * grad_heads, c_float, precision=HIGH
     )
-    identity = (jnp.ones_like(decay_total), jnp.zeros_like(state_end))
-    state_in = carried_in((decay_total, state_end), "ctx", chain_join, identity, False)[1]
-    adjoint = carried_in((decay_total, seed_state), "ctx", chain_join, identity, True)[1]
+    state_in = scanned_in(decay_total, state_end, "ctx", False)
+    adjoint = scanned_in(decay_total, seed_state, "ctx", True)
 
     def carry_map(c_arg, cum_arg):
         return carry_in(c_arg, cum_arg, state_in)

time: 176 us -> 143 us (0.81)
  the two profiles are of different devices: /device:TPU:26 before, /device:TPU:28 now
where the time goes in v1:
time: 143 us; the launch traced here: 142 us
  waiting for transfers between devices  50 us (35%)
  starting transfers between devices  33.5 us (23%)
  other arithmetic  25.7 us (18%)
  local copies, waits for them, and re-layouts  16.9 us (12%)
  matrix products  14.5 us (10%)
  between operations  1.66 us (1%)
    ppermute x10, waiting for transfers between devices, shift(): return lax.ppermute(tree, axis, pairs)  50 us
    ppermute x10, starting transfers between devices, shift(): return lax.ppermute(tree, axis, pairs)  25.9 us
    dot_general x3, matrix products, ssd_block(): jnp.einsum('ghts,sghp->tghp', mixing, x_half, preferred_element_type=jnp....  8.96 us
    ppermute x2, starting transfers between devices, from_behind(): return lax.ppermute(array, axis, pairs)  7.65 us
    another operation x6, other arithmetic  7.07 us
    unnamed x117, local copies, waits for them, and re-layouts  5.11 us
  transfers between devices with their start and end apart: 12, of which 5 were waited for; matrix products, arithmetic and copies ran while one was open for 16% of the time, Pallas kernels for 0%

profile of v1, /device:TPU:28, one launch (start us, length us, event | category | flops | bytes accessed | tf_op | source)
XLA Modules:
  0.0 142.3 jit_solution(675865944955540369)
XLA Ops:
  0.6 0.9 slice.272
  1.6 0.9 slice.271
  2.6 0.7 slice_bitcast_fusion.1
  3.3 3.4 %collective-permute-start = (bf16[3,1280]{1,0:T(4,128)(2,1)S(1)}, bf16[3,1280]{1,0:T(4,128)(2,1)S(1)}, u32[]{:S(2)}, u32[]{:S(2)}) collective-permute-start(bf16[3,1280]{1,0:T(4,128)(2,1)S(1)} %pad_maximum_fusion.3), channel_id=1, source_target_pairs={{0,2},{2,4},{4,6},{6,8},{8,10},{10,12},{12,14},{1,3},{3,5},{5,7},{... | collective-permute-start | bytes 23048 | tf_op jit(solution)/shard_map/ppermute | solution.py:12
  6.7 0.7 neg.30
  7.4 0.8 multiply_bitcast_fusion
  8.2 1.2 reduce-window.14
  10.4 0.8 fusion.89
  11.3 0.7 slice_bitcast_fusion.13
  12.0 0.7 slice_bitcast_fusion.5
  12.8 0.7 slice_bitcast_fusion.9
  13.6 1.3 copy.88
  15.1 0.9 multiply_convert_fusion.2
  16.7 3.3 %collective-permute-start.8 = (f32[2,8,64,64]{3,2,1,0:T(8,128)S(1)}, f32[2,8,64,64]{3,2,1,0:T(8,128)}, u32[]{:S(2)}, u32[]{:S(2)}) collective-permute-start(f32[2,8,64,64]{3,2,1,0:T(8,128)S(1)} %fusion.37), channel_id=1, source_target_pairs={{2,0},{4,2},{6,4},{8,6},{10,8},{12,10},{14,12},{3,1},{5,3},{7,5},{... | collective-permute-start | bytes 786440 | tf_op jit(solution)/shard_map/ppermute | solution.py:21
  20.5 2.4 %multiply_convert_fusion = (bf16[256,2,512]{2,1,0:T(2,128)(2,1)S(1)}, f32[256,2,512]{2,1,0:T(2,128)S(1)}) fusion(bf16[256,2,512]{2,1,0:T(2,128)(2,1)S(1)} %copy-done, f32[2,512]{1,0:T(2,128)S(1)} %get-tuple-element.98, bf16[259,2,512]{2,1,0:T(2,128)(2,1)S(1)} %constant_dynamic-update-slice_fusion, f32[2,512]{1,0:T(2,128)S(1)} %get-tuple-element.99, ...), kind=kLoop, calls=%fused_computation.60 | loop fusion | flops 4194304 | bytes 3686400 | tf_op jit(solution)/shard_map/convert_element_type | solution.py:121
  24.3 3.3 %collective-permute-start.3 = (f32[2,8,64,64]{3,2,1,0:T(8,128)S(1)}, f32[2,8,64,64]{3,2,1,0:T(8,128)S(1)}, u32[]{:S(2)}, u32[]{:S(2)}) collective-permute-start(f32[2,8,64,64]{3,2,1,0:T(8,128)S(1)} %fusion.59), channel_id=1, source_target_pairs={{0,2},{2,4},{4,6},{6,8},{8,10},{10,12},{12,14},{1,3},{3,5},{5,7},{... | collective-permute-start | bytes 786440 | tf_op jit(solution)/shard_map/ppermute | solution.py:21
  27.6 15.7 %collective-permute-done.8 = f32[2,8,64,64]{3,2,1,0:T(8,128)} collective-permute-done((f32[2,8,64,64]{3,2,1,0:T(8,128)S(1)}, f32[2,8,64,64]{3,2,1,0:T(8,128)}, u32[]{:S(2)}, u32[]{:S(2)}) %collective-permute-start.8) | collective-permute-done | bytes 262176 | tf_op jit(solution)/shard_map/ppermute | solution.py:21
  43.3 1.2 multiply_add_fusion.5
  44.6 2.4 %collective-permute-start.9 = (f32[2,8,64,64]{3,2,1,0:T(8,128)S(1)}, f32[2,8,64,64]{3,2,1,0:T(8,128)S(1)}, u32[]{:S(2)}, u32[]{:S(2)}) collective-permute-start(f32[2,8,64,64]{3,2,1,0:T(8,128)S(1)} %get-tuple-element.113), channel_id=1, source_target_pairs={{4,0},{6,2},{8,4},{10,6},{12,8},{14,10},{5,1},{7,3},{9,5},{11,7},{... | collective-permute-start | bytes 786440 | tf_op jit(solution)/shard_map/ppermute | solution.py:21
  46.9 4.1 %collective-permute-start.6 = (f32[2,8]{1,0:T(2,128)S(1)}, f32[2,8]{1,0:T(2,128)S(1)}, u32[]{:S(2)}, u32[]{:S(2)}) collective-permute-start(f32[2,8]{1,0:T(2,128)S(1)} %exp.47), channel_id=1, source_target_pairs={{2,0},{4,2},{6,4},{8,6},{10,8},{12,10},{14,12},{3,1},{5,3},{7,5},{... | collective-permute-start | bytes 200 | tf_op jit(solution)/shard_map/ppermute | solution.py:21
  51.1 1.9 %collective-permute-start.1 = (f32[2,8]{1,0:T(2,128)S(1)}, f32[2,8]{1,0:T(2,128)S(1)}, u32[]{:S(2)}, u32[]{:S(2)}) collective-permute-start(f32[2,8]{1,0:T(2,128)S(1)} %exp.47), channel_id=1, source_target_pairs={{0,2},{2,4},{4,6},{6,8},{8,10},{10,12},{12,14},{1,3},{3,5},{5,7},{... | collective-permute-start | bytes 200 | tf_op jit(solution)/shard_map/ppermute | solution.py:21
  53.0 5.2 %collective-permute-done.6 = f32[2,8]{1,0:T(2,128)S(1)} collective-permute-done((f32[2,8]{1,0:T(2,128)S(1)}, f32[2,8]{1,0:T(2,128)S(1)}, u32[]{:S(2)}, u32[]{:S(2)}) %collective-permute-start.6) | collective-permute-done | bytes 96 | tf_op jit(solution)/shard_map/ppermute | solution.py:21
  58.2 1.3 collective-permute-start.4
  59.6 4.5 %collective-permute-start.10 = (f32[2,8,64,64]{3,2,1,0:T(8,128)S(1)}, f32[2,8,64,64]{3,2,1,0:T(8,128)S(1)}, u32[]{:S(2)}, u32[]{:S(2)}) collective-permute-start(f32[2,8,64,64]{3,2,1,0:T(8,128)S(1)} %multiply_add_fusion.2), channel_id=1, source_target_pairs={{8,0},{10,2},{12,4},{14,6},{9,1},{11,3},{13,5},{15,7},{24,16},{26,... | collective-permute-start | bytes 786440 | tf_op jit(solution)/shard_map/ppermute | solution.py:21
  64.1 8.8 %collective-permute-done.4 = f32[2,8,64,64]{3,2,1,0:T(8,128)S(1)} collective-permute-done((f32[2,8,64,64]{3,2,1,0:T(8,128)S(1)}, f32[2,8,64,64]{3,2,1,0:T(8,128)S(1)}, u32[]{:S(2)}, u32[]{:S(2)}) %collective-permute-start.4) | collective-permute-done | bytes 262176 | tf_op jit(solution)/shard_map/ppermute | solution.py:21
  73.0 1.3 collective-permute-start.5
  74.3 2.4 %collective-permute-start.7 = (f32[2,8]{1,0:T(2,128)S(1)}, f32[2,8]{1,0:T(2,128)S(1)}, u32[]{:S(2)}, u32[]{:S(2)}) collective-permute-start(f32[2,8]{1,0:T(2,128)S(1)} %get-tuple-element.111), channel_id=1, source_target_pairs={{4,0},{6,2},{8,4},{10,6},{12,8},{14,10},{5,1},{7,3},{9,5},{11,7},{... | collective-permute-start | bytes 200 | tf_op jit(solution)/shard_map/ppermute | solution.py:21
  76.7 1.5 %collective-permute-start.2 = (f32[2,8]{1,0:T(2,128)S(1)}, f32[2,8]{1,0:T(2,128)S(1)}, u32[]{:S(2)}, u32[]{:S(2)}) collective-permute-start(f32[2,8]{1,0:T(2,128)S(1)} %get-tuple-element.110), channel_id=1, source_target_pairs={{0,4},{2,6},{4,8},{6,10},{8,12},{10,14},{1,5},{3,7},{5,9},{7,11},{... | collective-permute-start | bytes 200 | tf_op jit(solution)/shard_map/ppermute | solution.py:21
  78.2 5.6 %collective-permute-done.2 = f32[2,8]{1,0:T(2,128)S(1)} collective-permute-done((f32[2,8]{1,0:T(2,128)S(1)}, f32[2,8]{1,0:T(2,128)S(1)}, u32[]{:S(2)}, u32[]{:S(2)}) %collective-permute-start.2) | collective-permute-done | bytes 96 | tf_op jit(solution)/shard_map/ppermute | solution.py:21
  84.1 14.7 %collective-permute-done.5 = f32[2,8,64,64]{3,2,1,0:T(8,128)S(1)} collective-permute-done((f32[2,8,64,64]{3,2,1,0:T(8,128)S(1)}, f32[2,8,64,64]{3,2,1,0:T(8,128)S(1)}, u32[]{:S(2)}, u32[]{:S(2)}) %collective-permute-start.5) | collective-permute-done | bytes 262176 | tf_op jit(solution)/shard_map/ppermute | solution.py:21
  98.8 2.1 %multiply_reduce_fusion = (f32[2,8]{1,0:T(2,128)}, f32[2,8,64,64]{3,2,1,0:T(8,128)S(1)}, f32[2,8,64,64]{3,2,1,0:T(8,128)S(1)}) fusion(f32[2,8,64,64]{3,2,1,0:T(8,128)} %collective-permute-done.8, f32[2,8,64,64]{3,2,1,0:T(8,128)S(1)} %collective-permute-done.9, f32[2,8]{1,0:T(2,128)S(1)} %collective-permute-done.6, ...), kind=kLoop, calls=%fused_computation.64 | loop fusion | flops 655344 | bytes 2097472 | tf_op jit(solution)/shard_map/reduce_sum | solution.py:143
  102.3 1.2 fusion.97
  103.5 4.9 %fusion.18 = (f32[2,8,256]{2,1,0:T(8,128)}, f32[2,8,256]{2,1,0:T(8,128)}, f32[2,8,256]{2,1,0:T(8,128)}, f32[2,256,256]{2,1,0:T(8,128)S(1)}) fusion(f32[2,8,256]{2,1,0:T(8,128)S(1)} %copy-done.30, f32[2,8,256]{2,1,0:T(8,128)S(1)} %get-tuple-element.90, f32[2,256,256]{2,1,0:T(8,128)S(1)} %fusion.100, pred[256,256]{1,0:T(8,128)(4,1)S(1)} %iota_compare_fusion, ...), kind=kOutput, calls=%fused_computation.27 | convolution fusion | flops 156094464 | bytes 2244608 | tf_op jit(solution)/shard_map/transpose(jvp(ghts,sghp->tghp))/dot_general | solution.py:80
  108.4 1.0 fusion.101
  109.8 2.4 %add_convert_fusion = bf16[256,2,8,64]{0,3,2,1:T(8,128)(2,1)} fusion(f32[256,2,8,64]{0,3,2,1:T(8,128)S(1)} %get-tuple-element.117, f32[256,2,8]{0,2,1:T(8,128)S(1)} %copy-done.9, bf16[256,2,8,64]{0,3,2,1:T(8,128)(2,1)S(1)} %bitcast.224, f32[2,8]{1,0:T(2,128)S(1)} %copy-done.54, f32[2,8,256]{2,1,0:T(8,128)S(1)} %get-tuple-element.90, ...), kind=kOutput, calls=%fused_computation.59 | convolution fusion | flops 142082048 | bytes 2736192 | tf_op jit(solution)/shard_map/jvp(ghts,sghp->tghp)/dot_general | solution.py:80
  112.2 1.6 %fusion.52 = bf16[256,2,8,64]{0,3,2,1:T(8,128)(2,1)S(1)} fusion(f32[256,2,8,64]{0,3,2,1:T(8,128)S(1)} %get-tuple-element.115, f32[256,2,8]{0,2,1:T(8,128)S(1)} %get-tuple-element.94, f32[2,8]{1,0:T(2,128)S(1)} %copy-done.54, bf16[256,2,512]{0,2,1:T(8,128)(2,1)S(1)} %copy.88, bf16[2,8,64,256]{3,2,1,0:T(8,128)(2,1)S(1)} %bitcast.228, ...), kind=kOutput, calls=%fused_computation.56 | convolution fusion | flops 142606336 | bytes 3260480 | tf_op jit(solution)/shard_map/transpose(jvp(ghts,sghp->tghp))/dot_general | solution.py:80
  113.8 1.1 bitcast_convert_fusion
  115.0 2.3 %copy.89 = f32[256,2,512]{2,1,0:T(2,128)} copy(f32[256,2,512]{0,2,1:T(8,128)} %bitcast_convert_fusion) | data formatting | bytes 2097152 | tf_op jit(solution)/shard_map/convert_element_type | solution.py:50
  117.2 2.7 %multiply_multiply_fusion = f32[256,2,512]{2,1,0:T(2,128)S(1)} fusion(f32[256,2,512]{2,1,0:T(2,128)} %copy.89, f32[256,2,512]{2,1,0:T(2,128)S(1)} %get-tuple-element.87), kind=kLoop, calls=%fused_computation.58 | loop fusion | flops 2097152 | bytes 3145728 | tf_op jit(solution)/shard_map/mul | solution.py:50
  120.0 2.2 %multiply_add_fusion = f32[259,2,512]{2,1,0:T(2,128)} fusion(f32[256,2,512]{2,1,0:T(2,128)S(1)} %multiply_multiply_fusion, f32[2,512]{1,0:T(2,128)S(1)} %copy-done.23, f32[2,512]{1,0:T(2,128)S(1)} %copy-done.25, f32[2,512]{1,0:T(2,128)S(1)} %copy-done.21, f32[2,512]{1,0:T(2,128)S(1)} %copy-done.19), kind=kLoop, calls=%fused_computation.51 | loop fusion | flops 1856512 | bytes 2125824 | tf_op jit(solution)/shard_map/add | solution.py:58
  122.2 1.1 fusion.46
  124.9 0.8 slice_bitcast_fusion
  125.7 4.3 %collective-permute-start.11 = (f32[3,1280]{1,0:T(4,128)S(1)}, f32[3,1280]{1,0:T(4,128)S(1)}, u32[]{:S(2)}, u32[]{:S(2)}) collective-permute-start(f32[3,1280]{1,0:T(4,128)S(1)} %pad_maximum_fusion.2), channel_id=1, source_target_pairs={{2,0},{4,2},{6,4},{8,6},{10,8},{12,10},{14,12},{3,1},{5,3},{7,5},{... | collective-permute-start | bytes 46088 | tf_op jit(solution)/shard_map/ppermute | solution.py:12
  130.7 5.0 %reduce-window.16 = f32[8,2,2,128]{3,0,1,2:T(8,128)S(1)} reduce-window(f32[8,2,2,128]{3,0,1,2:T(8,128)S(1)} %copy.98, f32[]{:T(128)} %constant.120.clone.1), window={size=1x1x1x128 pad=0_0x0_0x0_0x0_127}, to_apply=%region_10.11 | reduce-window | flops 520192 | bytes 32772 | tf_op jit(solution)/shard_map/reduce-window.2
  135.8 0.7 fusion.85
  136.5 1.6 %slice.343 = bf16[256,2,512]{2,1,0:T(2,128)(2,1)S(1)} slice(f32[259,2,512]{2,1,0:T(2,128)} %multiply_add_fusion), slice={[3:259], [0:2], [0:512]} | slice | bytes 1048576 | tf_op jit(solution)/shard_map/slice | solution.py:162
  138.3 1.2 copy.102
  139.8 0.7 fusion.90
  (181 shorter events, 10.6 us)
Async XLA Ops:
  0.6 14.5 %copy-start.4 = (bf16[256,2,64]{0,2,1:T(8,128)(2,1)S(1)}, bf16[256,2,64]{0,2,1:T(8,128)(2,1)}, u32[]{:S(2)}) copy-start(bf16[256,2,64]{0,2,1:T(8,128)(2,1)} %param.21) | copy-start | bytes 196612
  3.3 11.6 %collective-permute-start = (bf16[3,1280]{1,0:T(4,128)(2,1)S(1)}, bf16[3,1280]{1,0:T(4,128)(2,1)S(1)}, u32[]{:S(2)}, u32[]{:S(2)}) collective-permute-start(bf16[3,1280]{1,0:T(4,128)(2,1)S(1)} %pad_maximum_fusion.3), channel_id=1, source_target_pairs={{0,2},{2,4},{4,6},{6,8},{8,10},{10,12},{12,14},{1,3},{3,5},{5,7},{... | collective-permute-start | bytes 23048 | tf_op jit(solution)/shard_map/ppermute | solution.py:12
  7.4 7.6 %copy-start.34 = (f32[2,8]{1,0:T(2,128)}, f32[2,8]{1,0:T(2,128)S(1)}, u32[]{:S(2)}) copy-start(f32[2,8]{1,0:T(2,128)S(1)} %neg.30) | copy-start | bytes 196
  9.6 92.6 %copy-start.16 = (f32[8,2,2]{0,1,2:T(2,128)}, f32[8,2,2]{0,1,2:T(2,128)S(1)}, u32[]{:S(2)}) copy-start(f32[8,2,2]{0,1,2:T(2,128)S(1)} %copy.86) | copy-start | bytes 388
  10.3 2.5 %copy-start.11 = (f32[256,2,8]{0,2,1:T(8,128)}, f32[256,2,8]{0,2,1:T(8,128)S(1)}, u32[]{:S(2)}) copy-start(f32[256,2,8]{0,2,1:T(8,128)S(1)} %get-tuple-element.93) | copy-start | bytes 49156
  10.4 91.8 %copy-start.26 = (f32[2,8]{1,0:T(2,128)}, f32[2,8]{1,0:T(2,128)S(1)}, u32[]{:S(2)}) copy-start(f32[2,8]{1,0:T(2,128)S(1)} %slice_reduce_fusion) | copy-start | bytes 196
  11.3 5.4 %copy-start.8 = (f32[256,2,8]{0,2,1:T(8,128)}, f32[256,2,8]{0,2,1:T(8,128)S(1)}, u32[]{:S(2)}) copy-start(f32[256,2,8]{0,2,1:T(8,128)S(1)} %get-tuple-element.95) | copy-start | bytes 49156
  12.0 4.6 %copy-start.44 = (f32[2,64]{1,0:T(2,128)}, f32[2,64]{1,0:T(2,128)S(1)}, u32[]{:S(2)}) copy-start(f32[2,64]{1,0:T(2,128)S(1)} %get-tuple-element.106) | copy-start | bytes 1540
  12.0 4.6 %copy-start.46 = (f32[2,64]{1,0:T(2,128)}, f32[2,64]{1,0:T(2,128)S(1)}, u32[]{:S(2)}) copy-start(f32[2,64]{1,0:T(2,128)S(1)} %get-tuple-element.107) | copy-start | bytes 1540
  12.0 4.6 %copy-start.48 = (f32[2,64]{1,0:T(2,128)}, f32[2,64]{1,0:T(2,128)S(1)}, u32[]{:S(2)}) copy-start(f32[2,64]{1,0:T(2,128)S(1)} %get-tuple-element.108) | copy-start | bytes 1540
  12.0 4.6 %copy-start.50 = (f32[2,64]{1,0:T(2,128)}, f32[2,64]{1,0:T(2,128)S(1)}, u32[]{:S(2)}) copy-start(f32[2,64]{1,0:T(2,128)S(1)} %get-tuple-element.109) | copy-start | bytes 1540
  12.8 7.7 %copy-start.18 = (f32[2,512]{1,0:T(2,128)}, f32[2,512]{1,0:T(2,128)S(1)}, u32[]{:S(2)}) copy-start(f32[2,512]{1,0:T(2,128)S(1)} %get-tuple-element.96) | copy-start | bytes 12292
  12.8 7.7 %copy-start.20 = (f32[2,512]{1,0:T(2,128)}, f32[2,512]{1,0:T(2,128)S(1)}, u32[]{:S(2)}) copy-start(f32[2,512]{1,0:T(2,128)S(1)} %get-tuple-element.97) | copy-start | bytes 12292
  12.8 7.7 %copy-start.22 = (f32[2,512]{1,0:T(2,128)}, f32[2,512]{1,0:T(2,128)S(1)}, u32[]{:S(2)}) copy-start(f32[2,512]{1,0:T(2,128)S(1)} %get-tuple-element.98) | copy-start | bytes 12292
  12.8 7.7 %copy-start.24 = (f32[2,512]{1,0:T(2,128)}, f32[2,512]{1,0:T(2,128)S(1)}, u32[]{:S(2)}) copy-start(f32[2,512]{1,0:T(2,128)S(1)} %get-tuple-element.99) | copy-start | bytes 12292
  13.5 10.1 %copy-start.36 = (f32[2,64]{1,0:T(2,128)}, f32[2,64]{1,0:T(2,128)S(1)}, u32[]{:S(2)}) copy-start(f32[2,64]{1,0:T(2,128)S(1)} %get-tuple-element.102) | copy-start | bytes 1540
  13.5 10.1 %copy-start.38 = (f32[2,64]{1,0:T(2,128)}, f32[2,64]{1,0:T(2,128)S(1)}, u32[]{:S(2)}) copy-start(f32[2,64]{1,0:T(2,128)S(1)} %get-tuple-element.103) | copy-start | bytes 1540
  13.5 10.1 %copy-start.40 = (f32[2,64]{1,0:T(2,128)}, f32[2,64]{1,0:T(2,128)S(1)}, u32[]{:S(2)}) copy-start(f32[2,64]{1,0:T(2,128)S(1)} %get-tuple-element.104) | copy-start | bytes 1540
  13.5 10.1 %copy-start.42 = (f32[2,64]{1,0:T(2,128)}, f32[2,64]{1,0:T(2,128)S(1)}, u32[]{:S(2)}) copy-start(f32[2,64]{1,0:T(2,128)S(1)} %get-tuple-element.105) | copy-start | bytes 1540
  13.6 6.5 %copy-start = (bf16[256,2,512]{2,1,0:T(2,128)(2,1)S(1)}, bf16[256,2,512]{2,1,0:T(2,128)(2,1)}, u32[]{:S(2)}) copy-start(bf16[256,2,512]{2,1,0:T(2,128)(2,1)} %param.19) | copy-start | bytes 1572868
  16.7 26.6 %collective-permute-start.8 = (f32[2,8,64,64]{3,2,1,0:T(8,128)S(1)}, f32[2,8,64,64]{3,2,1,0:T(8,128)}, u32[]{:S(2)}, u32[]{:S(2)}) collective-permute-start(f32[2,8,64,64]{3,2,1,0:T(8,128)S(1)} %fusion.37), channel_id=1, source_target_pairs={{2,0},{4,2},{6,4},{8,6},{10,8},{12,10},{14,12},{3,1},{5,3},{7,5},{... | collective-permute-start | bytes 786440 | tf_op jit(solution)/shard_map/ppermute | solution.py:21
  24.3 19.0 %collective-permute-start.3 = (f32[2,8,64,64]{3,2,1,0:T(8,128)S(1)}, f32[2,8,64,64]{3,2,1,0:T(8,128)S(1)}, u32[]{:S(2)}, u32[]{:S(2)}) collective-permute-start(f32[2,8,64,64]{3,2,1,0:T(8,128)S(1)} %fusion.59), channel_id=1, source_target_pairs={{0,2},{2,4},{4,6},{6,8},{8,10},{10,12},{12,14},{1,3},{3,5},{5,7},{... | collective-permute-start | bytes 786440 | tf_op jit(solution)/shard_map/ppermute | solution.py:21
  44.6 14.9 %collective-permute-start.9 = (f32[2,8,64,64]{3,2,1,0:T(8,128)S(1)}, f32[2,8,64,64]{3,2,1,0:T(8,128)S(1)}, u32[]{:S(2)}, u32[]{:S(2)}) collective-permute-start(f32[2,8,64,64]{3,2,1,0:T(8,128)S(1)} %get-tuple-element.113), channel_id=1, source_target_pairs={{4,0},{6,2},{8,4},{10,6},{12,8},{14,10},{5,1},{7,3},{9,5},{11,7},{... | collective-permute-start | bytes 786440 | tf_op jit(solution)/shard_map/ppermute | solution.py:21
  46.9 11.2 %collective-permute-start.6 = (f32[2,8]{1,0:T(2,128)S(1)}, f32[2,8]{1,0:T(2,128)S(1)}, u32[]{:S(2)}, u32[]{:S(2)}) collective-permute-start(f32[2,8]{1,0:T(2,128)S(1)} %exp.47), channel_id=1, source_target_pairs={{2,0},{4,2},{6,4},{8,6},{10,8},{12,10},{14,12},{3,1},{5,3},{7,5},{... | collective-permute-start | bytes 200 | tf_op jit(solution)/shard_map/ppermute | solution.py:21
  51.1 7.1 %collective-permute-start.1 = (f32[2,8]{1,0:T(2,128)S(1)}, f32[2,8]{1,0:T(2,128)S(1)}, u32[]{:S(2)}, u32[]{:S(2)}) collective-permute-start(f32[2,8]{1,0:T(2,128)S(1)} %exp.47), channel_id=1, source_target_pairs={{0,2},{2,4},{4,6},{6,8},{8,10},{10,12},{12,14},{1,3},{3,5},{5,7},{... | collective-permute-start | bytes 200 | tf_op jit(solution)/shard_map/ppermute | solution.py:21
  58.2 14.7 %collective-permute-start.4 = (f32[2,8,64,64]{3,2,1,0:T(8,128)S(1)}, f32[2,8,64,64]{3,2,1,0:T(8,128)S(1)}, u32[]{:S(2)}, u32[]{:S(2)}) collective-permute-start(f32[2,8,64,64]{3,2,1,0:T(8,128)S(1)} %get-tuple-element.112), channel_id=1, source_target_pairs={{0,4},{2,6},{4,8},{6,10},{8,12},{10,14},{1,5},{3,7},{5,9},{7,11},{... | collective-permute-start | bytes 786440 | tf_op jit(solution)/shard_map/ppermute | solution.py:21
  59.6 24.5 %collective-permute-start.10 = (f32[2,8,64,64]{3,2,1,0:T(8,128)S(1)}, f32[2,8,64,64]{3,2,1,0:T(8,128)S(1)}, u32[]{:S(2)}, u32[]{:S(2)}) collective-permute-start(f32[2,8,64,64]{3,2,1,0:T(8,128)S(1)} %multiply_add_fusion.2), channel_id=1, source_target_pairs={{8,0},{10,2},{12,4},{14,6},{9,1},{11,3},{13,5},{15,7},{24,16},{26,... | collective-permute-start | bytes 786440 | tf_op jit(solution)/shard_map/ppermute | solution.py:21
  73.0 25.8 %collective-permute-start.5 = (f32[2,8,64,64]{3,2,1,0:T(8,128)S(1)}, f32[2,8,64,64]{3,2,1,0:T(8,128)S(1)}, u32[]{:S(2)}, u32[]{:S(2)}) collective-permute-start(f32[2,8,64,64]{3,2,1,0:T(8,128)S(1)} %multiply_add_fusion.4), channel_id=1, source_target_pairs={{0,8},{2,10},{4,12},{6,14},{1,9},{3,11},{5,13},{7,15},{16,24},{18,... | collective-permute-start | bytes 786440 | tf_op jit(solution)/shard_map/ppermute | solution.py:21
  74.3 3.8 %collective-permute-start.7 = (f32[2,8]{1,0:T(2,128)S(1)}, f32[2,8]{1,0:T(2,128)S(1)}, u32[]{:S(2)}, u32[]{:S(2)}) collective-permute-start(f32[2,8]{1,0:T(2,128)S(1)} %get-tuple-element.111), channel_id=1, source_target_pairs={{4,0},{6,2},{8,4},{10,6},{12,8},{14,10},{5,1},{7,3},{9,5},{11,7},{... | collective-permute-start | bytes 200 | tf_op jit(solution)/shard_map/ppermute | solution.py:21
  76.7 7.1 %collective-permute-start.2 = (f32[2,8]{1,0:T(2,128)S(1)}, f32[2,8]{1,0:T(2,128)S(1)}, u32[]{:S(2)}, u32[]{:S(2)}) collective-permute-start(f32[2,8]{1,0:T(2,128)S(1)} %get-tuple-element.110), channel_id=1, source_target_pairs={{0,4},{2,6},{4,8},{6,10},{8,12},{10,14},{1,5},{3,7},{5,9},{7,11},{... | collective-permute-start | bytes 200 | tf_op jit(solution)/shard_map/ppermute | solution.py:21
  117.2 2.7 %copy-start.19 = (f32[2,512]{1,0:T(2,128)S(1)}, f32[2,512]{1,0:T(2,128)}, u32[]{:S(2)}) copy-start(f32[2,512]{1,0:T(2,128)} %copy-done.18) | copy-start | bytes 12292
  117.2 2.8 %copy-start.21 = (f32[2,512]{1,0:T(2,128)S(1)}, f32[2,512]{1,0:T(2,128)}, u32[]{:S(2)}) copy-start(f32[2,512]{1,0:T(2,128)} %copy-done.20) | copy-start | bytes 12292
  117.2 2.8 %copy-start.23 = (f32[2,512]{1,0:T(2,128)S(1)}, f32[2,512]{1,0:T(2,128)}, u32[]{:S(2)}) copy-start(f32[2,512]{1,0:T(2,128)} %copy-done.22) | copy-start | bytes 12292
  117.2 2.8 %copy-start.25 = (f32[2,512]{1,0:T(2,128)S(1)}, f32[2,512]{1,0:T(2,128)}, u32[]{:S(2)}) copy-start(f32[2,512]{1,0:T(2,128)} %copy-done.24) | copy-start | bytes 12292
  120.0 2.2 %copy-start.6 = (f32[256,2,64]{0,2,1:T(8,128)S(1)}, f32[256,2,64]{0,2,1:T(8,128)}, u32[]{:S(2)}) copy-start(f32[256,2,64]{0,2,1:T(8,128)} %get-tuple-element.83) | copy-start | bytes 393220
  123.7 6.2 %copy-start.52 = (f32[2,8]{1,0:T(2,128)S(1)}, f32[2,8]{1,0:T(2,128)}, u32[]{:S(2)}) copy-start(f32[2,8]{1,0:T(2,128)} %get-tuple-element.80) | copy-start | bytes 196
  123.7 6.3 %copy-start.53 = (f32[2,8]{1,0:T(2,128)S(1)}, f32[2,8]{1,0:T(2,128)}, u32[]{:S(2)}) copy-start(f32[2,8]{1,0:T(2,128)} %get-tuple-element.77) | copy-start | bytes 196
  123.7 6.4 %copy-start.12 = (f32[256,2,8]{0,2,1:T(8,128)S(1)}, f32[256,2,8]{0,2,1:T(8,128)}, u32[]{:S(2)}) copy-start(f32[256,2,8]{0,2,1:T(8,128)} %copy-done.11) | copy-start | bytes 49156
  123.7 6.8 %copy-start.15 = (f32[256,2,8]{0,2,1:T(8,128)S(1)}, f32[256,2,8]{0,2,1:T(8,128)}, u32[]{:S(2)}) copy-start(f32[256,2,8]{0,2,1:T(8,128)} %get-tuple-element.81) | copy-start | bytes 49156
  123.8 6.8 %copy-start.32 = (f32[2,8,256]{2,1,0:T(8,128)S(1)}, f32[2,8,256]{2,1,0:T(8,128)}, u32[]{:S(2)}) copy-start(f32[2,8,256]{2,1,0:T(8,128)} %get-tuple-element.73) | copy-start | bytes 49156
  123.8 6.8 %copy-start.33 = (f32[2,8,256]{2,1,0:T(8,128)S(1)}, f32[2,8,256]{2,1,0:T(8,128)}, u32[]{:S(2)}) copy-start(f32[2,8,256]{2,1,0:T(8,128)} %get-tuple-element.74) | copy-start | bytes 49156
  123.8 12.0 %copy-start.17 = (f32[8,2,2]{0,1,2:T(2,128)S(1)}, f32[8,2,2]{0,1,2:T(2,128)}, u32[]{:S(2)}) copy-start(f32[8,2,2]{0,1,2:T(2,128)} %copy-done.16) | copy-start | bytes 388
  123.8 12.0 %copy-start.27 = (f32[2,8]{1,0:T(2,128)S(1)}, f32[2,8]{1,0:T(2,128)}, u32[]{:S(2)}) copy-start(f32[2,8]{1,0:T(2,128)} %copy-done.26) | copy-start | bytes 196
  123.8 12.0 %copy-start.29 = (f32[2,8]{1,0:T(2,128)S(1)}, f32[2,8]{1,0:T(2,128)}, u32[]{:S(2)}) copy-start(f32[2,8]{1,0:T(2,128)} %param.24) | copy-start | bytes 196
  123.8 12.0 %copy-start.31 = (f32[2,8,256]{2,1,0:T(8,128)S(1)}, f32[2,8,256]{2,1,0:T(8,128)}, u32[]{:S(2)}) copy-start(f32[2,8,256]{2,1,0:T(8,128)} %get-tuple-element.75) | copy-start | bytes 49156
  123.8 12.0 %copy-start.35 = (f32[2,8]{1,0:T(2,128)S(1)}, f32[2,8]{1,0:T(2,128)}, u32[]{:S(2)}) copy-start(f32[2,8]{1,0:T(2,128)} %copy-done.34) | copy-start | bytes 196
  124.8 13.5 %copy-start.1 = (bf16[256,2,8,64]{0,3,2,1:T(8,128)(2,1)S(1)}, bf16[256,2,8,64]{0,3,2,1:T(8,128)(2,1)}, u32[]{:S(2)}) copy-start(bf16[256,2,8,64]{0,3,2,1:T(8,128)(2,1)} %add_convert_fusion) | copy-start | bytes 1572868
  125.7 13.8 %collective-permute-start.11 = (f32[3,1280]{1,0:T(4,128)S(1)}, f32[3,1280]{1,0:T(4,128)S(1)}, u32[]{:S(2)}, u32[]{:S(2)}) collective-permute-start(f32[3,1280]{1,0:T(4,128)S(1)} %pad_maximum_fusion.2), channel_id=1, source_target_pairs={{2,0},{4,2},{6,4},{8,6},{10,8},{12,10},{14,12},{3,1},{5,3},{7,5},{... | collective-permute-start | bytes 46088 | tf_op jit(solution)/shard_map/ppermute | solution.py:12
  (19 other events, 22.7 us)

commit v2 on v1

--- a/solution.py
+++ b/solution.py
@@ -15,23 +15,34 @@
 def scanned_in(decay, state, axis, backward):
     count = lax.axis_size(axis)
     sign = -1 if backward else 1
-
-    def shift(tree, by):
+    groups, heads, rows, cols = state.shape
+    lanes = 128
+
+    def shift(decay_part, state_part, by):
         pairs = [(i, i + sign * by) for i in range(count) if 0 <= i + sign * by < count]
-        return lax.ppermute(tree, axis, pairs)
-
-    before_decay, before_state = shift((decay, state), 1)
+        packed = jnp.concatenate(
+            [
+                state_part.reshape(groups, heads, rows * cols),
+                jnp.broadcast_to(decay_part[:, :, None], (groups, heads, lanes)),
+            ],
+            2,
+        ).astype(jnp.bfloat16)
+        got = lax.ppermute(packed, axis, pairs).astype(jnp.float32)
+        return got[:, :, rows * cols], got[:, :, : rows * cols]
+
+    flat = state.reshape(groups, heads, rows * cols)
+    before_decay, before_state = shift(decay, flat, 1)
     upto_decay = before_decay * decay
-    upto_state = decay[:, :, None, None] * before_state + state
+    upto_state = decay[:, :, None] * before_state + flat
     by = 2
     while by < count:
-        got_decay, got_state = shift((upto_decay, upto_state), by)
-        before_state = before_decay[:, :, None, None] * got_state + before_state
+        got_decay, got_state = shift(upto_decay, upto_state, by)
+        before_state = before_decay[:, :, None] * got_state + before_state
         before_decay = before_decay * got_decay
-        upto_state = upto_decay[:, :, None, None] * got_state + upto_state
+        upto_state = upto_decay[:, :, None] * got_state + upto_state
         upto_decay = upto_decay * got_decay
         by *= 2
-    return before_state
+    return before_state.reshape(groups, heads, rows, cols)
 
 
 def conv_forward(extended, weight):

time: 143 us -> 103 us (0.72)
  the two profiles are of different devices: /device:TPU:28 before, /device:TPU:0 now
where the time goes in v2:
time: 103 us; the launch traced here: 102 us
  starting transfers between devices  22.4 us (22%)
  waiting for transfers between devices  21 us (20%)
  other arithmetic  20.4 us (20%)
  matrix products  19 us (18%)
  local copies, waits for them, and re-layouts  17.7 us (17%)
  between operations  1.78 us (2%)
    ppermute x6, waiting for transfers between devices, shift(): got = lax.ppermute(packed, axis, pairs).astype(jnp.float32)  19.1 us
    ppermute x6, starting transfers between devices, shift(): got = lax.ppermute(packed, axis, pairs).astype(jnp.float32)  16.1 us
    dot_general x3, matrix products, ssd_block(): jnp.einsum('ghts,sghp->tghp', mixing, x_half, preferred_element_type=jnp....  10.7 us
    another operation x15, other arithmetic  8.33 us
    ppermute x2, starting transfers between devices, from_behind(): return lax.ppermute(array, axis, pairs)  6.27 us
    unnamed x147, local copies, waits for them, and re-layouts  5.34 us
    dot_general x2, matrix products, carry_in(): carried = jnp.einsum('tgn,ghpn->tghp', c_float, state_in, precision=HIGH)  3.39 us
    dot_general x3, matrix products, ssd_block(): jnp.einsum('sghp,sgn->ghpn', weighted.astype(jnp.float32), b_float, preci...  2.48 us
  transfers between devices with their start and end apart: 8, of which 7 were waited for; matrix products, arithmetic and copies ran while one was open for 13% of the time, Pallas kernels for 0%

profile of v2, /device:TPU:0, one launch (start us, length us, event | category | flops | bytes accessed | tf_op | source)
XLA Modules:
  0.0 102.2 jit_solution(4376101073909147540)
XLA Ops:
  0.7 0.7 slice_bitcast_fusion.1
  1.4 0.8 slice.307
  2.3 0.9 slice.308
  3.3 4.8 %collective-permute-start = (bf16[3,1280]{1,0:T(4,128)(2,1)S(1)}, bf16[3,1280]{1,0:T(4,128)(2,1)S(1)}, u32[]{:S(2)}, u32[]{:S(2)}) collective-permute-start(bf16[3,1280]{1,0:T(4,128)(2,1)S(1)} %pad_maximum_fusion.9), channel_id=1, source_target_pairs={{0,2},{2,4},{4,6},{6,8},{8,10},{10,12},{12,14},{1,3},{3,5},{5,7},{... | collective-permute-start | bytes 23048 | tf_op jit(solution)/shard_map/ppermute | solution.py:12
  8.1 0.7 neg.30
  8.8 0.7 slice_bitcast_fusion.9
  9.6 0.7 slice_bitcast_fusion.13
  10.3 0.8 multiply_bitcast_fusion
  11.2 1.2 %reduce-window.14 = f32[8,2,2,128]{3,0,1,2:T(8,128)S(1)} reduce-window(f32[8,2,2,128]{3,0,1,2:T(8,128)S(1)} %copy.180, f32[]{:T(128)} %constant.120.clone.1), window={size=1x1x1x128 pad=0_0x0_0x0_0x127_0}, to_apply=%region_0.1 | reduce-window | flops 520192 | bytes 32772 | tf_op jit(solution)/shard_map/reduce-window
  12.5 0.7 slice_bitcast_fusion.5
  13.3 0.7 bitcast_bitcast_fusion.1
  14.1 0.8 fusion.98
  15.6 1.3 %copy.185 = bf16[256,2,512]{0,2,1:T(8,128)(2,1)S(1)} copy(bf16[256,2,512]{2,1,0:T(2,128)(2,1)} %param.29) | data formatting | bytes 1048576 | tf_op args[10]
  17.2 1.0 multiply_convert_fusion.1
  18.3 0.7 fusion.49
  19.7 2.4 %multiply_convert_fusion = (bf16[256,2,512]{2,1,0:T(2,128)(2,1)S(1)}, f32[256,2,512]{2,1,0:T(2,128)S(1)}) fusion(bf16[256,2,512]{2,1,0:T(2,128)(2,1)S(1)} %copy-done, f32[2,512]{1,0:T(2,128)S(1)} %get-tuple-element.116, bf16[259,2,512]{2,1,0:T(2,128)(2,1)S(1)} %constant_dynamic-update-slice_fusion, f32[2,512]{1,0:T(2,128)S(1)} %get-tuple-element.117, ...), kind=kLoop, calls=%fused_computation.61 | loop fusion | flops 4194304 | bytes 3686400 | tf_op jit(solution)/shard_map/convert_element_type | solution.py:132
  23.2 0.7 broadcast_in_dim.32
  24.0 3.5 %collective-permute-start.1 = (bf16[2,8,4224]{2,1,0:T(8,128)(2,1)S(1)}, bf16[2,8,4224]{2,1,0:T(8,128)(2,1)S(1)}, u32[]{:S(2)}, u32[]{:S(2)}) collective-permute-start(bf16[2,8,4224]{2,1,0:T(8,128)(2,1)S(1)} %get-tuple-element.120), channel_id=1, source_target_pairs={{0,2},{2,4},{4,6},{6,8},{8,10},{10,12},{12,14},{1,3},{3,5},{5,7},{... | collective-permute-start | bytes 405512 | tf_op jit(solution)/shard_map/ppermute | solution.py:30
  27.5 1.3 %collective-permute-start.4 = (bf16[2,8,4224]{2,1,0:T(8,128)(2,1)S(1)}, bf16[2,8,4224]{2,1,0:T(8,128)(2,1)S(1)}, u32[]{:S(2)}, u32[]{:S(2)}) collective-permute-start(bf16[2,8,4224]{2,1,0:T(8,128)(2,1)S(1)} %get-tuple-element.121), channel_id=1, source_target_pairs={{2,0},{4,2},{6,4},{8,6},{10,8},{12,10},{14,12},{3,1},{5,3},{7,5},{... | collective-permute-start | bytes 405512 | tf_op jit(solution)/shard_map/ppermute | solution.py:30
  28.8 1.2 %collective-permute-done.1 = bf16[2,8,4224]{2,1,0:T(8,128)(2,1)S(1)} collective-permute-done((bf16[2,8,4224]{2,1,0:T(8,128)(2,1)S(1)}, bf16[2,8,4224]{2,1,0:T(8,128)(2,1)S(1)}, u32[]{:S(2)}, u32[]{:S(2)}) %collective-permute-start.1) | collective-permute-done | bytes 135200 | tf_op jit(solution)/shard_map/ppermute | solution.py:30
  30.1 4.2 %collective-permute-done.4 = bf16[2,8,4224]{2,1,0:T(8,128)(2,1)S(1)} collective-permute-done((bf16[2,8,4224]{2,1,0:T(8,128)(2,1)S(1)}, bf16[2,8,4224]{2,1,0:T(8,128)(2,1)S(1)}, u32[]{:S(2)}, u32[]{:S(2)}) %collective-permute-start.4) | collective-permute-done | bytes 135200 | tf_op jit(solution)/shard_map/ppermute | solution.py:30
  34.7 3.9 %collective-permute-start.2 = (bf16[2,8,4224]{2,1,0:T(8,128)(2,1)S(1)}, bf16[2,8,4224]{2,1,0:T(8,128)(2,1)S(1)}, u32[]{:S(2)}, u32[]{:S(2)}) collective-permute-start(bf16[2,8,4224]{2,1,0:T(8,128)(2,1)S(1)} %pad_maximum_fusion.2), channel_id=1, source_target_pairs={{0,4},{2,6},{4,8},{6,10},{8,12},{10,14},{1,5},{3,7},{5,9},{7,11},{... | collective-permute-start | bytes 405512 | tf_op jit(solution)/shard_map/ppermute | solution.py:30
  38.5 0.7 iota_compare_fusion
  39.2 1.9 %collective-permute-done.2 = bf16[2,8,4224]{2,1,0:T(8,128)(2,1)S(1)} collective-permute-done((bf16[2,8,4224]{2,1,0:T(8,128)(2,1)S(1)}, bf16[2,8,4224]{2,1,0:T(8,128)(2,1)S(1)}, u32[]{:S(2)}, u32[]{:S(2)}) %collective-permute-start.2) | collective-permute-done | bytes 135200 | tf_op jit(solution)/shard_map/ppermute | solution.py:30
  41.3 1.3 %collective-permute-start.5 = (bf16[2,8,4224]{2,1,0:T(8,128)(2,1)S(1)}, bf16[2,8,4224]{2,1,0:T(8,128)(2,1)S(1)}, u32[]{:S(2)}, u32[]{:S(2)}) collective-permute-start(bf16[2,8,4224]{2,1,0:T(8,128)(2,1)S(1)} %pad_maximum_fusion.4), channel_id=1, source_target_pairs={{4,0},{6,2},{8,4},{10,6},{12,8},{14,10},{5,1},{7,3},{9,5},{11,7},{... | collective-permute-start | bytes 405512 | tf_op jit(solution)/shard_map/ppermute | solution.py:30
  42.6 1.1 %fusion.112 = f32[2,256,256]{2,1,0:T(8,128)} fusion(bf16[256,2,64]{0,2,1:T(8,128)(2,1)S(1)} %get-tuple-element.138, bf16[256,2,64]{0,2,1:T(8,128)(2,1)S(1)} %get-tuple-element.100), kind=kOutput, calls=%fused_computation.197 | convolution fusion | flops 16777216 | bytes 655360 | tf_op jit(solution)/shard_map/jvp(tgn,sgn->gts)/dot_general | solution.py:89
  43.7 5.0 %collective-permute-done.5 = bf16[2,8,4224]{2,1,0:T(8,128)(2,1)S(1)} collective-permute-done((bf16[2,8,4224]{2,1,0:T(8,128)(2,1)S(1)}, bf16[2,8,4224]{2,1,0:T(8,128)(2,1)S(1)}, u32[]{:S(2)}, u32[]{:S(2)}) %collective-permute-start.5) | collective-permute-done | bytes 135200 | tf_op jit(solution)/shard_map/ppermute | solution.py:30
  49.1 4.9 %collective-permute-start.3 = (bf16[2,8,4224]{2,1,0:T(8,128)(2,1)S(1)}, bf16[2,8,4224]{2,1,0:T(8,128)(2,1)S(1)}, u32[]{:S(2)}, u32[]{:S(2)}) collective-permute-start(bf16[2,8,4224]{2,1,0:T(8,128)(2,1)S(1)} %pad_maximum_fusion.3), channel_id=1, source_target_pairs={{0,8},{2,10},{4,12},{6,14},{1,9},{3,11},{5,13},{7,15},{16,24},{18,... | collective-permute-start | bytes 405512 | tf_op jit(solution)/shard_map/ppermute | solution.py:30
  54.1 1.3 %collective-permute-start.6 = (bf16[2,8,4224]{2,1,0:T(8,128)(2,1)S(1)}, bf16[2,8,4224]{2,1,0:T(8,128)(2,1)S(1)}, u32[]{:S(2)}, u32[]{:S(2)}) collective-permute-start(bf16[2,8,4224]{2,1,0:T(8,128)(2,1)S(1)} %pad_maximum_fusion.5), channel_id=1, source_target_pairs={{8,0},{10,2},{12,4},{14,6},{9,1},{11,3},{13,5},{15,7},{24,16},{26,... | collective-permute-start | bytes 405512 | tf_op jit(solution)/shard_map/ppermute | solution.py:30
  55.6 1.0 collective-permute-done.3
  56.6 5.8 %collective-permute-done.6 = bf16[2,8,4224]{2,1,0:T(8,128)(2,1)S(1)} collective-permute-done((bf16[2,8,4224]{2,1,0:T(8,128)(2,1)S(1)}, bf16[2,8,4224]{2,1,0:T(8,128)(2,1)S(1)}, u32[]{:S(2)}, u32[]{:S(2)}) %collective-permute-start.6) | collective-permute-done | bytes 135200 | tf_op jit(solution)/shard_map/ppermute | solution.py:30
  62.4 0.8 multiply_reduce_fusion
  63.5 1.8 %convolution_bitcast_fusion.3 = f32[2,256,64]{1,2,0:T(8,128)S(1)} fusion(f32[2,8,64,64]{3,2,1,0:T(8,128)S(1)} %reshape.271, bf16[256,2,8,64]{0,3,2,1:T(8,128)(2,1)S(1)} %bitcast.232, f32[256,2,8]{0,2,1:T(8,128)} %copy-done.12), kind=kOutput, calls=%fused_computation.47 | convolution fusion | flops 201850880 | bytes 933888 | tf_op jit(solution)/shard_map/transpose(jvp(tgn,ghpn->tghp))/dot_general | solution.py:100
  65.3 1.6 %fusion.62 = (f32[256,2,8]{0,2,1:T(8,128)S(1)}, f32[256,2,8,64]{0,3,2,1:T(8,128)}) fusion(bf16[256,2,512]{0,2,1:T(8,128)(2,1)S(1)} %copy.185, f32[2,8,64,64]{3,2,1,0:T(8,128)S(1)} %reshape.271, bf16[256,2,64]{0,2,1:T(8,128)(2,1)S(1)} %get-tuple-element.138), kind=kOutput, calls=%fused_computation.59 | convolution fusion | flops 202108928 | bytes 1916928 | tf_op jit(solution)/shard_map/jvp(tgn,ghpn->tghp)/dot_general | solution.py:100
  67.8 1.6 %fusion.60 = (f32[256,2,8]{0,2,1:T(8,128)S(1)}, f32[256,2,8,64]{0,3,2,1:T(8,128)}) fusion(bf16[256,2,512]{0,2,1:T(8,128)(2,1)S(1)} %copy.177, f32[2,8,64,64]{3,2,1,0:T(8,128)S(1)} %reshape.275, bf16[256,2,64]{0,2,1:T(8,128)(2,1)S(1)} %get-tuple-element.100), kind=kOutput, calls=%fused_computation.57 | convolution fusion | flops 202633216 | bytes 1916928 | tf_op jit(solution)/shard_map/transpose(jvp(sghp,sgn->ghpn))/dot_general | solution.py:95
  70.0 5.9 %fusion.18 = (f32[2,8,256]{2,1,0:T(8,128)S(1)}, f32[2,8,256]{2,1,0:T(8,128)S(1)}, f32[2,8,256]{2,1,0:T(8,128)}, f32[2,256,256]{2,1,0:T(8,128)S(1)}) fusion(f32[2,8,256]{2,1,0:T(8,128)S(1)} %copy-done.45, f32[2,8,256]{2,1,0:T(8,128)S(1)} %get-tuple-element.108, f32[2,256,256]{2,1,0:T(8,128)} %fusion.112, pred[256,256]{1,0:T(8,128)(4,1)S(1)} %copy-done.25, ...), kind=kOutput, calls=%fused_computation.27 | convolution fusion | flops 156094464 | bytes 2244608 | tf_op jit(solution)/shard_map/transpose(jvp(ghts,sghp->tghp))/dot_general | solution.py:91
  75.9 2.3 %fusion.45 = bf16[256,2,8,64]{0,3,2,1:T(8,128)(2,1)} fusion(bf16[2,8,64,256]{3,2,1,0:T(8,128)(2,1)S(1)} %bitcast.235, f32[2,8,256]{2,1,0:T(8,128)S(1)} %get-tuple-element.108, f32[2,8,256]{2,1,0:T(8,128)S(1)} %copy-done.45, f32[2,256,256]{2,1,0:T(8,128)S(1)} %copy-done.6, pred[256,256]{1,0:T(8,128)(4,1)S(1)} %copy-done.25, ...), kind=kOutput, calls=%fused_computation.40 | convolution fusion | flops 142606336 | bytes 3260480 | tf_op jit(solution)/shard_map/transpose(jvp(ghts,sghp->tghp))/dot_general | solution.py:91
  78.3 2.4 %fusion.30 = bf16[256,2,8,64]{0,3,2,1:T(8,128)(2,1)} fusion(bf16[256,2,8,64]{0,3,2,1:T(8,128)(2,1)S(1)} %bitcast.239, f32[2,8,256]{2,1,0:T(8,128)S(1)} %get-tuple-element.108, f32[2,8,256]{2,1,0:T(8,128)S(1)} %copy-done.45, f32[2,256,256]{2,1,0:T(8,128)S(1)} %copy-done.6, pred[256,256]{1,0:T(8,128)(4,1)S(1)} %copy-done.25, ...), kind=kOutput, calls=%fused_computation.35 | convolution fusion | flops 142082048 | bytes 2736192 | tf_op jit(solution)/shard_map/jvp(ghts,sghp->tghp)/dot_general | solution.py:91
  81.3 5.0 %reduce-window.16 = f32[8,2,2,128]{3,0,1,2:T(8,128)S(1)} reduce-window(f32[8,2,2,128]{3,0,1,2:T(8,128)S(1)} %copy.196, f32[]{:T(128)} %constant.120.clone.1), window={size=1x1x1x128 pad=0_0x0_0x0_0x0_127}, to_apply=%region_10.11 | reduce-window | flops 520192 | bytes 32772 | tf_op jit(solution)/shard_map/reduce-window.2
  88.4 0.7 copy.191
  89.1 0.7 copy.190
  90.5 1.5 %multiply_multiply_fusion = f32[256,2,512]{2,1,0:T(2,128)S(1)} fusion(f32[256,2,512]{2,1,0:T(2,128)S(1)} %copy.187, f32[256,2,512]{2,1,0:T(2,128)S(1)} %get-tuple-element.105), kind=kLoop, calls=%fused_computation.60 | loop fusion | flops 2097152 | bytes 3145728 | tf_op jit(solution)/shard_map/mul | solution.py:61
  92.2 1.3 %multiply_add_fusion = f32[259,2,512]{2,1,0:T(2,128)S(1)} fusion(f32[256,2,512]{2,1,0:T(2,128)S(1)} %multiply_multiply_fusion, f32[2,512]{1,0:T(2,128)S(1)} %copy-done.36, f32[2,512]{1,0:T(2,128)S(1)} %copy-done.38, f32[2,512]{1,0:T(2,128)S(1)} %copy-done.34, f32[2,512]{1,0:T(2,128)S(1)} %copy-done.32), kind=kLoop, calls=%fused_computation.55 | loop fusion | flops 1856512 | bytes 2125824 | tf_op jit(solution)/shard_map/add | solution.py:69
  93.6 1.4 %collective-permute-start.7 = (f32[3,1280]{1,0:T(4,128)S(1)}, f32[3,1280]{1,0:T(4,128)S(1)}, u32[]{:S(2)}, u32[]{:S(2)}) collective-permute-start(f32[3,1280]{1,0:T(4,128)S(1)} %pad_maximum_fusion.8), channel_id=1, source_target_pairs={{2,0},{4,2},{6,4},{8,6},{10,8},{12,10},{14,12},{3,1},{5,3},{7,5},{... | collective-permute-start | bytes 46088 | tf_op jit(solution)/shard_map/ppermute | solution.py:12
  95.1 0.7 fusion.94
  96.4 1.2 %copy.200 = bf16[256,2,512]{2,1,0:T(2,128)(2,1)} copy(bf16[256,2,512]{0,2,1:T(8,128)(2,1)S(1)} %bitcast.240) | data formatting | bytes 1048576
  97.5 1.8 %collective-permute-done.7 = f32[3,1280]{1,0:T(4,128)S(1)} collective-permute-done((f32[3,1280]{1,0:T(4,128)S(1)}, f32[3,1280]{1,0:T(4,128)S(1)}, u32[]{:S(2)}, u32[]{:S(2)}) %collective-permute-start.7) | collective-permute-done | bytes 15392 | tf_op jit(solution)/shard_map/ppermute | solution.py:12
  101.4 0.8 copy-done.8
  (225 shorter events, 12.2 us)
Async XLA Ops:
  0.6 16.6 %copy-start.19 = (bf16[256,2,64]{0,2,1:T(8,128)(2,1)S(1)}, bf16[256,2,64]{0,2,1:T(8,128)(2,1)}, u32[]{:S(2)}) copy-start(bf16[256,2,64]{0,2,1:T(8,128)(2,1)} %param.20) | copy-start | bytes 196612
  0.6 16.6 %copy-start.18 = (bf16[256,2,64]{0,2,1:T(8,128)(2,1)S(1)}, bf16[256,2,64]{0,2,1:T(8,128)(2,1)}, u32[]{:S(2)}) copy-start(bf16[256,2,64]{0,2,1:T(8,128)(2,1)} %param.21) | copy-start | bytes 196612
  3.3 13.6 %collective-permute-start = (bf16[3,1280]{1,0:T(4,128)(2,1)S(1)}, bf16[3,1280]{1,0:T(4,128)(2,1)S(1)}, u32[]{:S(2)}, u32[]{:S(2)}) collective-permute-start(bf16[3,1280]{1,0:T(4,128)(2,1)S(1)} %pad_maximum_fusion.9), channel_id=1, source_target_pairs={{0,2},{2,4},{4,6},{6,8},{8,10},{10,12},{12,14},{1,3},{3,5},{5,7},{... | collective-permute-start | bytes 23048 | tf_op jit(solution)/shard_map/ppermute | solution.py:12
  8.8 8.0 %copy-start.47 = (f32[2,8]{1,0:T(2,128)}, f32[2,8]{1,0:T(2,128)S(1)}, u32[]{:S(2)}) copy-start(f32[2,8]{1,0:T(2,128)S(1)} %neg.30) | copy-start | bytes 196
  9.6 8.7 %copy-start.57 = (f32[2,64]{1,0:T(2,128)}, f32[2,64]{1,0:T(2,128)S(1)}, u32[]{:S(2)}) copy-start(f32[2,64]{1,0:T(2,128)S(1)} %get-tuple-element.122) | copy-start | bytes 1540
  9.6 8.7 %copy-start.59 = (f32[2,64]{1,0:T(2,128)}, f32[2,64]{1,0:T(2,128)S(1)}, u32[]{:S(2)}) copy-start(f32[2,64]{1,0:T(2,128)S(1)} %get-tuple-element.123) | copy-start | bytes 1540
  9.6 8.7 %copy-start.61 = (f32[2,64]{1,0:T(2,128)}, f32[2,64]{1,0:T(2,128)S(1)}, u32[]{:S(2)}) copy-start(f32[2,64]{1,0:T(2,128)S(1)} %get-tuple-element.124) | copy-start | bytes 1540
  9.6 8.7 %copy-start.63 = (f32[2,64]{1,0:T(2,128)}, f32[2,64]{1,0:T(2,128)S(1)}, u32[]{:S(2)}) copy-start(f32[2,64]{1,0:T(2,128)S(1)} %get-tuple-element.125) | copy-start | bytes 1540
  10.3 8.6 %copy-start.49 = (f32[2,64]{1,0:T(2,128)}, f32[2,64]{1,0:T(2,128)S(1)}, u32[]{:S(2)}) copy-start(f32[2,64]{1,0:T(2,128)S(1)} %get-tuple-element.126) | copy-start | bytes 1540
  10.3 8.6 %copy-start.51 = (f32[2,64]{1,0:T(2,128)}, f32[2,64]{1,0:T(2,128)S(1)}, u32[]{:S(2)}) copy-start(f32[2,64]{1,0:T(2,128)S(1)} %get-tuple-element.127) | copy-start | bytes 1540
  10.3 8.6 %copy-start.53 = (f32[2,64]{1,0:T(2,128)}, f32[2,64]{1,0:T(2,128)S(1)}, u32[]{:S(2)}) copy-start(f32[2,64]{1,0:T(2,128)S(1)} %get-tuple-element.128) | copy-start | bytes 1540
  10.3 8.6 %copy-start.55 = (f32[2,64]{1,0:T(2,128)}, f32[2,64]{1,0:T(2,128)S(1)}, u32[]{:S(2)}) copy-start(f32[2,64]{1,0:T(2,128)S(1)} %get-tuple-element.129) | copy-start | bytes 1540
  12.5 4.6 %copy-start.28 = (f32[8,2,2]{0,1,2:T(2,128)}, f32[8,2,2]{0,1,2:T(2,128)S(1)}, u32[]{:S(2)}) copy-start(f32[8,2,2]{0,1,2:T(2,128)S(1)} %copy.182) | copy-start | bytes 388
  13.3 6.4 %copy-start.31 = (f32[2,512]{1,0:T(2,128)}, f32[2,512]{1,0:T(2,128)S(1)}, u32[]{:S(2)}) copy-start(f32[2,512]{1,0:T(2,128)S(1)} %get-tuple-element.114) | copy-start | bytes 12292
  13.3 6.4 %copy-start.33 = (f32[2,512]{1,0:T(2,128)}, f32[2,512]{1,0:T(2,128)S(1)}, u32[]{:S(2)}) copy-start(f32[2,512]{1,0:T(2,128)S(1)} %get-tuple-element.115) | copy-start | bytes 12292
  13.3 6.4 %copy-start.35 = (f32[2,512]{1,0:T(2,128)}, f32[2,512]{1,0:T(2,128)S(1)}, u32[]{:S(2)}) copy-start(f32[2,512]{1,0:T(2,128)S(1)} %get-tuple-element.116) | copy-start | bytes 12292
  13.3 6.4 %copy-start.37 = (f32[2,512]{1,0:T(2,128)}, f32[2,512]{1,0:T(2,128)S(1)}, u32[]{:S(2)}) copy-start(f32[2,512]{1,0:T(2,128)S(1)} %get-tuple-element.117) | copy-start | bytes 12292
  14.0 3.2 %copy-start.22 = (f32[256,2,8]{0,2,1:T(8,128)}, f32[256,2,8]{0,2,1:T(8,128)S(1)}, u32[]{:S(2)}) copy-start(f32[256,2,8]{0,2,1:T(8,128)S(1)} %get-tuple-element.112) | copy-start | bytes 49156
  14.1 3.1 %copy-start.39 = (f32[2,8]{1,0:T(2,128)}, f32[2,8]{1,0:T(2,128)S(1)}, u32[]{:S(2)}) copy-start(f32[2,8]{1,0:T(2,128)S(1)} %slice_reduce_fusion) | copy-start | bytes 196
  15.0 4.0 %copy-start.12 = (f32[256,2,8]{0,2,1:T(8,128)}, f32[256,2,8]{0,2,1:T(8,128)S(1)}, u32[]{:S(2)}) copy-start(f32[256,2,8]{0,2,1:T(8,128)S(1)} %get-tuple-element.111) | copy-start | bytes 49156
  15.0 7.7 %copy-start.14 = (f32[256,2,8]{0,2,1:T(8,128)}, f32[256,2,8]{0,2,1:T(8,128)S(1)}, u32[]{:S(2)}) copy-start(f32[256,2,8]{0,2,1:T(8,128)S(1)} %get-tuple-element.110) | copy-start | bytes 49156
  23.2 6.8 %copy-start.44 = (f32[2,8]{1,0:T(2,128)S(1)}, f32[2,8]{1,0:T(2,128)}, u32[]{:S(2)}) copy-start(f32[2,8]{1,0:T(2,128)} %get-tuple-element.132) | copy-start | bytes 196
  23.2 11.2 %copy-start.23 = (f32[256,2,8]{0,2,1:T(8,128)S(1)}, f32[256,2,8]{0,2,1:T(8,128)}, u32[]{:S(2)}) copy-start(f32[256,2,8]{0,2,1:T(8,128)} %copy-done.22) | copy-start | bytes 49156
  24.0 6.0 %collective-permute-start.1 = (bf16[2,8,4224]{2,1,0:T(8,128)(2,1)S(1)}, bf16[2,8,4224]{2,1,0:T(8,128)(2,1)S(1)}, u32[]{:S(2)}, u32[]{:S(2)}) collective-permute-start(bf16[2,8,4224]{2,1,0:T(8,128)(2,1)S(1)} %get-tuple-element.120), channel_id=1, source_target_pairs={{0,2},{2,4},{4,6},{6,8},{8,10},{10,12},{12,14},{1,3},{3,5},{5,7},{... | collective-permute-start | bytes 405512 | tf_op jit(solution)/shard_map/ppermute | solution.py:30
  27.5 6.9 %collective-permute-start.4 = (bf16[2,8,4224]{2,1,0:T(8,128)(2,1)S(1)}, bf16[2,8,4224]{2,1,0:T(8,128)(2,1)S(1)}, u32[]{:S(2)}, u32[]{:S(2)}) collective-permute-start(bf16[2,8,4224]{2,1,0:T(8,128)(2,1)S(1)} %get-tuple-element.121), channel_id=1, source_target_pairs={{2,0},{4,2},{6,4},{8,6},{10,8},{12,10},{14,12},{3,1},{5,3},{7,5},{... | collective-permute-start | bytes 405512 | tf_op jit(solution)/shard_map/ppermute | solution.py:30
  34.7 6.4 %collective-permute-start.2 = (bf16[2,8,4224]{2,1,0:T(8,128)(2,1)S(1)}, bf16[2,8,4224]{2,1,0:T(8,128)(2,1)S(1)}, u32[]{:S(2)}, u32[]{:S(2)}) collective-permute-start(bf16[2,8,4224]{2,1,0:T(8,128)(2,1)S(1)} %pad_maximum_fusion.2), channel_id=1, source_target_pairs={{0,4},{2,6},{4,8},{6,10},{8,12},{10,14},{1,5},{3,7},{5,9},{7,11},{... | collective-permute-start | bytes 405512 | tf_op jit(solution)/shard_map/ppermute | solution.py:30
  41.3 7.3 %collective-permute-start.5 = (bf16[2,8,4224]{2,1,0:T(8,128)(2,1)S(1)}, bf16[2,8,4224]{2,1,0:T(8,128)(2,1)S(1)}, u32[]{:S(2)}, u32[]{:S(2)}) collective-permute-start(bf16[2,8,4224]{2,1,0:T(8,128)(2,1)S(1)} %pad_maximum_fusion.4), channel_id=1, source_target_pairs={{4,0},{6,2},{8,4},{10,6},{12,8},{14,10},{5,1},{7,3},{9,5},{11,7},{... | collective-permute-start | bytes 405512 | tf_op jit(solution)/shard_map/ppermute | solution.py:30
  49.1 7.5 %collective-permute-start.3 = (bf16[2,8,4224]{2,1,0:T(8,128)(2,1)S(1)}, bf16[2,8,4224]{2,1,0:T(8,128)(2,1)S(1)}, u32[]{:S(2)}, u32[]{:S(2)}) collective-permute-start(bf16[2,8,4224]{2,1,0:T(8,128)(2,1)S(1)} %pad_maximum_fusion.3), channel_id=1, source_target_pairs={{0,8},{2,10},{4,12},{6,14},{1,9},{3,11},{5,13},{7,15},{16,24},{18,... | collective-permute-start | bytes 405512 | tf_op jit(solution)/shard_map/ppermute | solution.py:30
  54.1 8.3 %collective-permute-start.6 = (bf16[2,8,4224]{2,1,0:T(8,128)(2,1)S(1)}, bf16[2,8,4224]{2,1,0:T(8,128)(2,1)S(1)}, u32[]{:S(2)}, u32[]{:S(2)}) collective-permute-start(bf16[2,8,4224]{2,1,0:T(8,128)(2,1)S(1)} %pad_maximum_fusion.5), channel_id=1, source_target_pairs={{8,0},{10,2},{12,4},{14,6},{9,1},{11,3},{13,5},{15,7},{24,16},{26,... | collective-permute-start | bytes 405512 | tf_op jit(solution)/shard_map/ppermute | solution.py:30
  70.0 5.9 %copy-start.2 = (f32[256,2,8,64]{0,3,2,1:T(8,128)S(1)}, f32[256,2,8,64]{0,3,2,1:T(8,128)}, u32[]{:S(2)}) copy-start(f32[256,2,8,64]{0,3,2,1:T(8,128)} %get-tuple-element.135) | copy-start | bytes 3145732
  70.0 5.9 %copy-start.6 = (f32[2,256,256]{2,1,0:T(8,128)S(1)}, f32[2,256,256]{2,1,0:T(8,128)}, u32[]{:S(2)}) copy-start(f32[2,256,256]{2,1,0:T(8,128)} %fusion.112) | copy-start | bytes 1572868
  70.0 5.9 %copy-start.69 = (f32[2,8]{1,0:T(2,128)S(1)}, f32[2,8]{1,0:T(2,128)}, u32[]{:S(2)}) copy-start(f32[2,8]{1,0:T(2,128)} %param.25) | copy-start | bytes 196
  78.3 8.7 %copy-start.9 = (f32[256,2,64]{0,2,1:T(8,128)S(1)}, f32[256,2,64]{0,2,1:T(8,128)}, u32[]{:S(2)}) copy-start(f32[256,2,64]{0,2,1:T(8,128)} %get-tuple-element.101) | copy-start | bytes 393220
  80.7 6.6 %copy-start.58 = (f32[2,64]{1,0:T(2,128)S(1)}, f32[2,64]{1,0:T(2,128)}, u32[]{:S(2)}) copy-start(f32[2,64]{1,0:T(2,128)} %copy-done.57) | copy-start | bytes 1540
  80.7 6.6 %copy-start.60 = (f32[2,64]{1,0:T(2,128)S(1)}, f32[2,64]{1,0:T(2,128)}, u32[]{:S(2)}) copy-start(f32[2,64]{1,0:T(2,128)} %copy-done.59) | copy-start | bytes 1540
  80.7 6.6 %copy-start.62 = (f32[2,64]{1,0:T(2,128)S(1)}, f32[2,64]{1,0:T(2,128)}, u32[]{:S(2)}) copy-start(f32[2,64]{1,0:T(2,128)} %copy-done.61) | copy-start | bytes 1540
  80.7 6.7 %copy-start.64 = (f32[2,64]{1,0:T(2,128)S(1)}, f32[2,64]{1,0:T(2,128)}, u32[]{:S(2)}) copy-start(f32[2,64]{1,0:T(2,128)} %copy-done.63) | copy-start | bytes 1540
  92.1 2.9 %copy-start.11 = (f32[256,2,8]{0,2,1:T(8,128)S(1)}, f32[256,2,8]{0,2,1:T(8,128)}, u32[]{:S(2)}) copy-start(f32[256,2,8]{0,2,1:T(8,128)} %param.22) | copy-start | bytes 49156
  92.1 2.9 %copy-start.17 = (f32[256,2,8]{0,2,1:T(8,128)S(1)}, f32[256,2,8]{0,2,1:T(8,128)}, u32[]{:S(2)}) copy-start(f32[256,2,8]{0,2,1:T(8,128)} %copy-done.16) | copy-start | bytes 49156
  92.1 2.9 %copy-start.21 = (f32[8,2,2,128]{3,0,1,2:T(8,128)S(1)}, f32[8,2,2,128]{3,0,1,2:T(8,128)}, u32[]{:S(2)}) copy-start(f32[8,2,2,128]{3,0,1,2:T(8,128)} %copy-done.20) | copy-start | bytes 49156
  92.1 2.9 %copy-start.30 = (f32[8,2,2]{0,1,2:T(2,128)S(1)}, f32[8,2,2]{0,1,2:T(2,128)}, u32[]{:S(2)}) copy-start(f32[8,2,2]{0,1,2:T(2,128)} %copy-done.28) | copy-start | bytes 388
  92.1 2.9 %copy-start.41 = (f32[2,8]{1,0:T(2,128)S(1)}, f32[2,8]{1,0:T(2,128)}, u32[]{:S(2)}) copy-start(f32[2,8]{1,0:T(2,128)} %copy-done.39) | copy-start | bytes 196
  92.1 2.9 %copy-start.43 = (f32[2,8]{1,0:T(2,128)S(1)}, f32[2,8]{1,0:T(2,128)}, u32[]{:S(2)}) copy-start(f32[2,8]{1,0:T(2,128)} %param.24) | copy-start | bytes 196
  92.1 2.9 %copy-start.46 = (f32[2,8,256]{2,1,0:T(8,128)S(1)}, f32[2,8,256]{2,1,0:T(8,128)}, u32[]{:S(2)}) copy-start(f32[2,8,256]{2,1,0:T(8,128)} %get-tuple-element.85) | copy-start | bytes 49156
  92.2 2.9 %copy-start.48 = (f32[2,8]{1,0:T(2,128)S(1)}, f32[2,8]{1,0:T(2,128)}, u32[]{:S(2)}) copy-start(f32[2,8]{1,0:T(2,128)} %copy-done.47) | copy-start | bytes 196
  92.2 2.9 %copy-start.67 = (f32[8,2,2]{0,1,2:T(2,128)S(1)}, f32[8,2,2]{0,1,2:T(2,128)}, u32[]{:S(2)}) copy-start(f32[8,2,2]{0,1,2:T(2,128)} %copy.198) | copy-start | bytes 388
  92.2 3.6 %copy-start.4 = (f32[259,2,64]{0,2,1:T(8,128)S(1)}, f32[259,2,64]{0,2,1:T(8,128)}, u32[]{:S(2)}) copy-start(f32[259,2,64]{0,2,1:T(8,128)} %copy-done.3) | copy-start | bytes 397828
  93.6 5.8 %collective-permute-start.7 = (f32[3,1280]{1,0:T(4,128)S(1)}, f32[3,1280]{1,0:T(4,128)S(1)}, u32[]{:S(2)}, u32[]{:S(2)}) collective-permute-start(f32[3,1280]{1,0:T(4,128)S(1)} %pad_maximum_fusion.8), channel_id=1, source_target_pairs={{2,0},{4,2},{6,4},{8,6},{10,8},{12,10},{14,12},{3,1},{5,3},{7,5},{... | collective-permute-start | bytes 46088 | tf_op jit(solution)/shard_map/ppermute | solution.py:12
  (30 other events, 46.8 us)

commit v3 on v2

--- a/solution.py
+++ b/solution.py
@@ -70,12 +70,16 @@
     return result
 
 
-def ssd_block(x_float, b_float, c_float, dt_raw, rate, dt_bias, skip):
+def ssd_cum(dt_raw, rate, dt_bias):
+    step_size = jax.nn.softplus(dt_raw + dt_bias)
+    return step_size, jnp.cumsum(-rate * step_size, axis=0)
+
+
+def ssd_mix(x_float, b_float, c_float, dt_raw, rate, dt_bias, skip):
     length, groups, channels = x_float.shape
     head_count = dt_raw.shape[2]
     head_size = channels // head_count
-    step_size = jax.nn.softplus(dt_raw + dt_bias)
-    cum_log = jnp.cumsum(-rate * step_size, axis=0)
+    step_size, cum_log = ssd_cum(dt_raw, rate, dt_bias)
     x_heads = x_float.reshape(length, groups, head_count, head_size)
     x_half = x_heads.astype(jnp.bfloat16)
     cum_heads = jnp.transpose(cum_log, (1, 2, 0))
@@ -89,11 +93,19 @@
     scores = jnp.einsum("tgn,sgn->gts", c_float, b_float, precision=HIGH)
     mixing = (scores[:, None] * decay_all * step_heads[:, :, None, :]).astype(jnp.bfloat16)
     y_local = jnp.einsum("ghts,sghp->tghp", mixing, x_half, preferred_element_type=jnp.float32)
-    y_local = y_local + skip[None, :, :, None] * x_heads
+    return y_local + skip[None, :, :, None] * x_heads
+
+
+def ssd_state(x_float, b_float, dt_raw, rate, dt_bias):
+    length, groups, channels = x_float.shape
+    head_count = dt_raw.shape[2]
+    head_size = channels // head_count
+    step_size, cum_log = ssd_cum(dt_raw, rate, dt_bias)
+    x_heads = x_float.reshape(length, groups, head_count, head_size)
     tail_weight = jnp.exp(cum_log[-1][None] - cum_log) * step_size
     weighted = (x_heads * tail_weight[..., None]).astype(jnp.bfloat16)
     state_end = jnp.einsum("sghp,sgn->ghpn", weighted.astype(jnp.float32), b_float, precision=HIGH)
-    return (y_local, cum_log, state_end)
+    return (cum_log, state_end)
 
 
 def carry_in(c_float, cum_log, state_in):
@@ -133,10 +145,14 @@
     b_float = jax.nn.silu(b_running).astype(jnp.bfloat16).astype(jnp.float32)
     c_float = jax.nn.silu(c_running).astype(jnp.bfloat16).astype(jnp.float32)
 
-    def local_map(x_arg, b_arg, c_arg, dt_arg):
-        return ssd_block(x_arg, b_arg, c_arg, dt_arg, rate, dt_bias, skip)
-
-    (y_local, cum_log, state_end), local_pull = jax.vjp(local_map, x_float, b_float, c_float, dt_in)
+    def mix_map(x_arg, b_arg, c_arg, dt_arg):
+        return ssd_mix(x_arg, b_arg, c_arg, dt_arg, rate, dt_bias, skip)
+
+    def state_map(x_arg, b_arg, dt_arg):
+        return ssd_state(x_arg, b_arg, dt_arg, rate, dt_bias)
+
+    (cum_log, state_end), state_pull = jax.vjp(state_map, x_float, b_float, dt_in)
+    y_local, mix_pull = jax.vjp(mix_map, x_float, b_float, c_float, dt_in)
     decay_total = jnp.exp(cum_log[-1])
     grad_heads = grad_y.astype(jnp.float32).reshape(length, groups, head_count, head_size)
     seed_state = jnp.einsum(
@@ -153,8 +169,12 @@
     grad_c_carry, grad_cum_carry = carry_pull(grad_heads)
     end_term = jnp.sum(adjoint * state_in, axis=(2, 3)) * decay_total
     grad_cum = grad_cum_carry.at[length - 1].add(end_term)
-    grad_x_conv, grad_b_part, grad_c_local, grad_dt = local_pull((grad_heads, grad_cum, adjoint))
-    grad_c_part = grad_c_local + grad_c_carry
+    mix_x, mix_b, mix_c, mix_dt = mix_pull(grad_heads)
+    state_x, state_b, state_dt = state_pull((grad_cum, adjoint))
+    grad_x_conv = mix_x + state_x
+    grad_b_part = mix_b + state_b
+    grad_dt = mix_dt + state_dt
+    grad_c_part = mix_c + grad_c_carry
     grad_b_ext = conv_backward(grad_b_part.astype(jnp.bfloat16), b_running, conv_b)
     grad_c_ext = conv_backward(grad_c_part.astype(jnp.bfloat16), c_running, conv_c)
     grad_x_ext = conv_backward(grad_x_conv.astype(jnp.bfloat16), x_running, conv_x)

time: 103 us -> 109 us (1.058)
  other arithmetic: 20.4 us -> 26 us
    another operation x15 -> x18, other arithmetic: 8.33 us -> 13.3 us
where the time goes in v3:
time: 109 us; the launch traced here: 108 us
  other arithmetic  26 us (24%)
  starting transfers between devices  22.6 us (21%)
  waiting for transfers between devices  20.8 us (19%)
  matrix products  19.7 us (18%)
  local copies, waits for them, and re-layouts  17.6 us (16%)
  between operations  1.77 us (2%)
    ppermute x6, waiting for transfers between devices, shift(): got = lax.ppermute(packed, axis, pairs).astype(jnp.float32)  18.9 us
    ppermute x6, starting transfers between devices, shift(): got = lax.ppermute(packed, axis, pairs).astype(jnp.float32)  16.3 us
    another operation x18, other arithmetic  13.3 us
    dot_general x3, matrix products, ssd_mix(): jnp.einsum('ghts,sghp->tghp', mixing, x_half, preferred_element_type=jnp....  10.7 us
    ppermute x2, starting transfers between devices, from_behind(): return lax.ppermute(array, axis, pairs)  6.27 us
    unnamed x147, local copies, waits for them, and re-layouts  5.7 us
    dot_general x2, matrix products, carry_in(): carried = jnp.einsum('tgn,ghpn->tghp', c_float, state_in, precision=HIGH)  3.4 us
    dot_general x3, matrix products, ssd_state(): jnp.einsum('sghp,sgn->ghpn', weighted.astype(jnp.float32), b_float, preci...  3.21 us
  transfers between devices with their start and end apart: 8, of which 7 were waited for; matrix products, arithmetic and copies ran while one was open for 13% of the time, Pallas kernels for 0%

profile of v3, /device:TPU:0, one launch (start us, length us, event | category | flops | bytes accessed | tf_op | source)
XLA Modules:
  0.0 108.4 jit_solution(4351594571450909468)
XLA Ops:
  0.7 0.7 slice_bitcast_fusion.1
  1.4 0.8 slice.313
  2.3 0.9 slice.314
  3.3 4.8 %collective-permute-start = (bf16[3,1280]{1,0:T(4,128)(2,1)S(1)}, bf16[3,1280]{1,0:T(4,128)(2,1)S(1)}, u32[]{:S(2)}, u32[]{:S(2)}) collective-permute-start(bf16[3,1280]{1,0:T(4,128)(2,1)S(1)} %pad_maximum_fusion.9), channel_id=1, source_target_pairs={{0,2},{2,4},{4,6},{6,8},{8,10},{10,12},{12,14},{1,3},{3,5},{5,7},{... | collective-permute-start | bytes 23048 | tf_op jit(solution)/shard_map/ppermute | solution.py:12
  8.1 0.7 neg.30
  8.8 0.7 slice_bitcast_fusion.9
  9.6 0.7 slice_bitcast_fusion.13
  10.3 0.8 multiply_bitcast_fusion
  11.2 1.2 %reduce-window.20 = f32[8,2,2,128]{3,0,1,2:T(8,128)S(1)} reduce-window(f32[8,2,2,128]{3,0,1,2:T(8,128)S(1)} %copy.198, f32[]{:T(128)} %constant.122.clone.1), window={size=1x1x1x128 pad=0_0x0_0x0_0x127_0}, to_apply=%region_0.2 | reduce-window | flops 520192 | bytes 32772 | tf_op jit(solution)/shard_map/reduce-window
  12.5 0.7 slice_bitcast_fusion.5
  13.3 0.7 bitcast_bitcast_fusion.2
  14.2 1.4 %fusion.102 = (f32[256,2,8]{0,2,1:T(8,128)}, f32[256,2,8]{0,2,1:T(8,128)S(1)}) fusion(f32[2,8]{1,0:T(2,128)S(1)} %slice_reduce_fusion, f32[256,2,8]{0,2,1:T(8,128)} %param.23, f32[2,8]{1,0:T(2,128)} %param.25, f32[8,2,2,128]{3,0,1,2:T(8,128)S(1)} %reduce-window.20, f32[8,2,2]{0,1,2:T(2,128)S(1)} %copy.200), kind=kLoop, calls=%fused_computation.157 | loop fusion | flops 40960 | bytes 65792 | tf_op jit(solution)/shard_map/jvp()/mul | solution.py:105
  16.1 1.3 %copy.203 = bf16[256,2,512]{0,2,1:T(8,128)(2,1)S(1)} copy(bf16[256,2,512]{2,1,0:T(2,128)(2,1)} %param.30) | data formatting | bytes 1048576 | tf_op args[10]
  17.8 1.0 multiply_convert_fusion.1
  20.3 2.4 %multiply_convert_fusion = (bf16[256,2,512]{2,1,0:T(2,128)(2,1)S(1)}, f32[256,2,512]{2,1,0:T(2,128)S(1)}) fusion(bf16[256,2,512]{2,1,0:T(2,128)(2,1)S(1)} %copy-done, f32[2,512]{1,0:T(2,128)S(1)} %get-tuple-element.120, bf16[259,2,512]{2,1,0:T(2,128)(2,1)S(1)} %constant_dynamic-update-slice_fusion, f32[2,512]{1,0:T(2,128)S(1)} %get-tuple-element.121, ...), kind=kLoop, calls=%fused_computation.61 | loop fusion | flops 4194304 | bytes 3686400 | tf_op jit(solution)/shard_map/convert_element_type | solution.py:144
  23.3 1.0 fusion.68
  24.5 0.7 broadcast_in_dim.32
  25.3 3.5 %collective-permute-start.1 = (bf16[2,8,4224]{2,1,0:T(8,128)(2,1)S(1)}, bf16[2,8,4224]{2,1,0:T(8,128)(2,1)S(1)}, u32[]{:S(2)}, u32[]{:S(2)}) collective-permute-start(bf16[2,8,4224]{2,1,0:T(8,128)(2,1)S(1)} %get-tuple-element.124), channel_id=1, source_target_pairs={{0,2},{2,4},{4,6},{6,8},{8,10},{10,12},{12,14},{1,3},{3,5},{5,7},{... | collective-permute-start | bytes 405512 | tf_op jit(solution)/shard_map/ppermute | solution.py:30
  28.7 1.3 %collective-permute-start.4 = (bf16[2,8,4224]{2,1,0:T(8,128)(2,1)S(1)}, bf16[2,8,4224]{2,1,0:T(8,128)(2,1)S(1)}, u32[]{:S(2)}, u32[]{:S(2)}) collective-permute-start(bf16[2,8,4224]{2,1,0:T(8,128)(2,1)S(1)} %get-tuple-element.125), channel_id=1, source_target_pairs={{2,0},{4,2},{6,4},{8,6},{10,8},{12,10},{14,12},{3,1},{5,3},{7,5},{... | collective-permute-start | bytes 405512 | tf_op jit(solution)/shard_map/ppermute | solution.py:30
  30.0 1.2 %collective-permute-done.1 = bf16[2,8,4224]{2,1,0:T(8,128)(2,1)S(1)} collective-permute-done((bf16[2,8,4224]{2,1,0:T(8,128)(2,1)S(1)}, bf16[2,8,4224]{2,1,0:T(8,128)(2,1)S(1)}, u32[]{:S(2)}, u32[]{:S(2)}) %collective-permute-start.1) | collective-permute-done | bytes 135200 | tf_op jit(solution)/shard_map/ppermute | solution.py:30
  31.4 4.2 %collective-permute-done.4 = bf16[2,8,4224]{2,1,0:T(8,128)(2,1)S(1)} collective-permute-done((bf16[2,8,4224]{2,1,0:T(8,128)(2,1)S(1)}, bf16[2,8,4224]{2,1,0:T(8,128)(2,1)S(1)}, u32[]{:S(2)}, u32[]{:S(2)}) %collective-permute-start.4) | collective-permute-done | bytes 135200 | tf_op jit(solution)/shard_map/ppermute | solution.py:30
  36.0 3.8 %collective-permute-start.2 = (bf16[2,8,4224]{2,1,0:T(8,128)(2,1)S(1)}, bf16[2,8,4224]{2,1,0:T(8,128)(2,1)S(1)}, u32[]{:S(2)}, u32[]{:S(2)}) collective-permute-start(bf16[2,8,4224]{2,1,0:T(8,128)(2,1)S(1)} %pad_maximum_fusion.2), channel_id=1, source_target_pairs={{0,4},{2,6},{4,8},{6,10},{8,12},{10,14},{1,5},{3,7},{5,9},{7,11},{... | collective-permute-start | bytes 405512 | tf_op jit(solution)/shard_map/ppermute | solution.py:30
  39.8 0.7 iota_compare_fusion
  40.5 1.9 %collective-permute-done.2 = bf16[2,8,4224]{2,1,0:T(8,128)(2,1)S(1)} collective-permute-done((bf16[2,8,4224]{2,1,0:T(8,128)(2,1)S(1)}, bf16[2,8,4224]{2,1,0:T(8,128)(2,1)S(1)}, u32[]{:S(2)}, u32[]{:S(2)}) %collective-permute-start.2) | collective-permute-done | bytes 135200 | tf_op jit(solution)/shard_map/ppermute | solution.py:30
  42.6 1.3 %collective-permute-start.5 = (bf16[2,8,4224]{2,1,0:T(8,128)(2,1)S(1)}, bf16[2,8,4224]{2,1,0:T(8,128)(2,1)S(1)}, u32[]{:S(2)}, u32[]{:S(2)}) collective-permute-start(bf16[2,8,4224]{2,1,0:T(8,128)(2,1)S(1)} %pad_maximum_fusion.4), channel_id=1, source_target_pairs={{4,0},{6,2},{8,4},{10,6},{12,8},{14,10},{5,1},{7,3},{9,5},{11,7},{... | collective-permute-start | bytes 405512 | tf_op jit(solution)/shard_map/ppermute | solution.py:30
  43.9 1.1 fusion.116
  45.0 5.0 %collective-permute-done.5 = bf16[2,8,4224]{2,1,0:T(8,128)(2,1)S(1)} collective-permute-done((bf16[2,8,4224]{2,1,0:T(8,128)(2,1)S(1)}, bf16[2,8,4224]{2,1,0:T(8,128)(2,1)S(1)}, u32[]{:S(2)}, u32[]{:S(2)}) %collective-permute-start.5) | collective-permute-done | bytes 135200 | tf_op jit(solution)/shard_map/ppermute | solution.py:30
  50.4 4.9 %collective-permute-start.3 = (bf16[2,8,4224]{2,1,0:T(8,128)(2,1)S(1)}, bf16[2,8,4224]{2,1,0:T(8,128)(2,1)S(1)}, u32[]{:S(2)}, u32[]{:S(2)}) collective-permute-start(bf16[2,8,4224]{2,1,0:T(8,128)(2,1)S(1)} %pad_maximum_fusion.3), channel_id=1, source_target_pairs={{0,8},{2,10},{4,12},{6,14},{1,9},{3,11},{5,13},{7,15},{16,24},{18,... | collective-permute-start | bytes 405512 | tf_op jit(solution)/shard_map/ppermute | solution.py:30
  55.4 1.5 %collective-permute-start.6 = (bf16[2,8,4224]{2,1,0:T(8,128)(2,1)S(1)}, bf16[2,8,4224]{2,1,0:T(8,128)(2,1)S(1)}, u32[]{:S(2)}, u32[]{:S(2)}) collective-permute-start(bf16[2,8,4224]{2,1,0:T(8,128)(2,1)S(1)} %pad_maximum_fusion.5), channel_id=1, source_target_pairs={{8,0},{10,2},{12,4},{14,6},{9,1},{11,3},{13,5},{15,7},{24,16},{26,... | collective-permute-start | bytes 405512 | tf_op jit(solution)/shard_map/ppermute | solution.py:30
  57.1 0.8 collective-permute-done.3
  57.8 5.8 %collective-permute-done.6 = bf16[2,8,4224]{2,1,0:T(8,128)(2,1)S(1)} collective-permute-done((bf16[2,8,4224]{2,1,0:T(8,128)(2,1)S(1)}, bf16[2,8,4224]{2,1,0:T(8,128)(2,1)S(1)}, u32[]{:S(2)}, u32[]{:S(2)}) %collective-permute-start.6) | collective-permute-done | bytes 135200 | tf_op jit(solution)/shard_map/ppermute | solution.py:30
  63.7 0.8 multiply_reduce_fusion
  64.7 1.8 %convolution_bitcast_fusion.3 = f32[2,256,64]{1,2,0:T(8,128)S(1)} fusion(f32[2,8,64,64]{3,2,1,0:T(8,128)S(1)} %reshape.286, bf16[256,2,8,64]{0,3,2,1:T(8,128)(2,1)S(1)} %bitcast.259, f32[256,2,8]{0,2,1:T(8,128)} %copy-done.12), kind=kOutput, calls=%fused_computation.48 | convolution fusion | flops 201850880 | bytes 933888 | tf_op jit(solution)/shard_map/transpose(jvp(tgn,ghpn->tghp))/dot_general | solution.py:112
  66.5 1.6 %fusion.64 = (f32[256,2,8]{0,2,1:T(8,128)S(1)}, f32[256,2,8,64]{0,3,2,1:T(8,128)}) fusion(bf16[256,2,512]{0,2,1:T(8,128)(2,1)S(1)} %copy.203, f32[2,8,64,64]{3,2,1,0:T(8,128)S(1)} %reshape.286, bf16[256,2,64]{0,2,1:T(8,128)(2,1)S(1)} %get-tuple-element.142), kind=kOutput, calls=%fused_computation.59 | convolution fusion | flops 202108928 | bytes 1916928 | tf_op jit(solution)/shard_map/jvp(tgn,ghpn->tghp)/dot_general | solution.py:112
  69.0 1.6 %fusion.63 = (f32[256,2,8]{0,2,1:T(8,128)S(1)}, f32[256,2,8,64]{0,3,2,1:T(8,128)}) fusion(bf16[256,2,512]{0,2,1:T(8,128)(2,1)S(1)} %copy.195, f32[2,8,64,64]{3,2,1,0:T(8,128)S(1)} %reshape.290, bf16[256,2,64]{0,2,1:T(8,128)(2,1)S(1)} %get-tuple-element.104), kind=kOutput, calls=%fused_computation.58 | convolution fusion | flops 202633216 | bytes 1916928 | tf_op jit(solution)/shard_map/transpose(jvp(sghp,sgn->ghpn))/dot_general | solution.py:107
  71.0 5.9 %fusion.18 = (f32[2,8,256]{2,1,0:T(8,128)S(1)}, f32[2,8,256]{2,1,0:T(8,128)S(1)}, f32[2,8,256]{2,1,0:T(8,128)}, f32[2,256,256]{2,1,0:T(8,128)S(1)}) fusion(f32[2,8,256]{2,1,0:T(8,128)S(1)} %copy-done.46, f32[2,8,256]{2,1,0:T(8,128)S(1)} %get-tuple-element.112, f32[2,256,256]{2,1,0:T(8,128)} %fusion.116, pred[256,256]{1,0:T(8,128)(4,1)S(1)} %copy-done.26, ...), kind=kOutput, calls=%fused_computation.27 | convolution fusion | flops 156094464 | bytes 2244608 | tf_op jit(solution)/shard_map/transpose(jvp(ghts,sghp->tghp))/dot_general | solution.py:95
  76.9 2.3 %fusion.48 = bf16[256,2,8,64]{0,3,2,1:T(8,128)(2,1)} fusion(bf16[2,8,64,256]{3,2,1,0:T(8,128)(2,1)S(1)} %bitcast.262, f32[2,8,256]{2,1,0:T(8,128)S(1)} %get-tuple-element.112, f32[2,8,256]{2,1,0:T(8,128)S(1)} %copy-done.46, f32[2,256,256]{2,1,0:T(8,128)S(1)} %copy-done.6, pred[256,256]{1,0:T(8,128)(4,1)S(1)} %copy-done.26, ...), kind=kOutput, calls=%fused_computation.41 | convolution fusion | flops 142606336 | bytes 3260480 | tf_op jit(solution)/shard_map/transpose(jvp(ghts,sghp->tghp))/dot_general | solution.py:95
  79.2 2.4 %fusion.30 = bf16[256,2,8,64]{0,3,2,1:T(8,128)(2,1)} fusion(bf16[256,2,8,64]{0,3,2,1:T(8,128)(2,1)S(1)} %bitcast.266, f32[2,8,256]{2,1,0:T(8,128)S(1)} %get-tuple-element.112, f32[2,8,256]{2,1,0:T(8,128)S(1)} %copy-done.46, f32[2,256,256]{2,1,0:T(8,128)S(1)} %copy-done.6, pred[256,256]{1,0:T(8,128)(4,1)S(1)} %copy-done.26, ...), kind=kOutput, calls=%fused_computation.35 | convolution fusion | flops 142082048 | bytes 2736192 | tf_op jit(solution)/shard_map/jvp(ghts,sghp->tghp)/dot_general | solution.py:95
  81.7 5.0 %reduce-window.24 = f32[8,2,2,128]{3,0,1,2:T(8,128)S(1)} reduce-window(f32[8,2,2,128]{3,0,1,2:T(8,128)S(1)} %copy_bitcast_fusion, f32[]{:T(128)} %constant.122.clone.1), window={size=1x1x1x128 pad=0_0x0_0x0_0x0_127}, to_apply=%region_6.8 | reduce-window | flops 520192 | bytes 32772 | tf_op jit(solution)/shard_map/reduce-window.2
  88.0 5.0 %reduce-window.26 = f32[8,2,2,128]{3,0,1,2:T(8,128)S(1)} reduce-window(f32[8,2,2,128]{3,0,1,2:T(8,128)S(1)} %copy.218, f32[]{:T(128)} %constant.122.clone.1), window={size=1x1x1x128 pad=0_0x0_0x0_0x0_127}, to_apply=%region_12.14 | reduce-window | flops 520192 | bytes 32772 | tf_op jit(solution)/shard_map/reduce-window.4
  95.1 0.7 copy-done.3
  96.8 1.5 %multiply_multiply_fusion = f32[256,2,512]{2,1,0:T(2,128)S(1)} fusion(f32[256,2,512]{2,1,0:T(2,128)S(1)} %copy.205, f32[256,2,512]{2,1,0:T(2,128)S(1)} %get-tuple-element.109), kind=kLoop, calls=%fused_computation.60 | loop fusion | flops 2097152 | bytes 3145728 | tf_op jit(solution)/shard_map/mul | solution.py:61
  98.4 1.3 %multiply_add_fusion = f32[259,2,512]{2,1,0:T(2,128)S(1)} fusion(f32[256,2,512]{2,1,0:T(2,128)S(1)} %multiply_multiply_fusion, f32[2,512]{1,0:T(2,128)S(1)} %copy-done.37, f32[2,512]{1,0:T(2,128)S(1)} %copy-done.39, f32[2,512]{1,0:T(2,128)S(1)} %copy-done.35, f32[2,512]{1,0:T(2,128)S(1)} %copy-done.33), kind=kLoop, calls=%fused_computation.56 | loop fusion | flops 1856512 | bytes 2125824 | tf_op jit(solution)/shard_map/add | solution.py:69
  99.8 1.4 %collective-permute-start.7 = (f32[3,1280]{1,0:T(4,128)S(1)}, f32[3,1280]{1,0:T(4,128)S(1)}, u32[]{:S(2)}, u32[]{:S(2)}) collective-permute-start(f32[3,1280]{1,0:T(4,128)S(1)} %pad_maximum_fusion.8), channel_id=1, source_target_pairs={{2,0},{4,2},{6,4},{8,6},{10,8},{12,10},{14,12},{3,1},{5,3},{7,5},{... | collective-permute-start | bytes 46088 | tf_op jit(solution)/shard_map/ppermute | solution.py:12
  101.3 0.7 fusion.96
  102.6 1.2 %copy.222 = bf16[256,2,512]{2,1,0:T(2,128)(2,1)} copy(bf16[256,2,512]{0,2,1:T(8,128)(2,1)S(1)} %bitcast.267) | data formatting | bytes 1048576
  103.8 1.8 %collective-permute-done.7 = f32[3,1280]{1,0:T(4,128)S(1)} collective-permute-done((f32[3,1280]{1,0:T(4,128)S(1)}, f32[3,1280]{1,0:T(4,128)S(1)}, u32[]{:S(2)}, u32[]{:S(2)}) %collective-permute-start.7) | collective-permute-done | bytes 15392 | tf_op jit(solution)/shard_map/ppermute | solution.py:12
  107.6 0.8 copy-done.8
  (231 shorter events, 13.2 us)
Async XLA Ops:
  0.6 17.2 %copy-start.18 = (bf16[256,2,64]{0,2,1:T(8,128)(2,1)S(1)}, bf16[256,2,64]{0,2,1:T(8,128)(2,1)}, u32[]{:S(2)}) copy-start(bf16[256,2,64]{0,2,1:T(8,128)(2,1)} %param.21) | copy-start | bytes 196612
  0.6 17.1 %copy-start.17 = (bf16[256,2,64]{0,2,1:T(8,128)(2,1)S(1)}, bf16[256,2,64]{0,2,1:T(8,128)(2,1)}, u32[]{:S(2)}) copy-start(bf16[256,2,64]{0,2,1:T(8,128)(2,1)} %param.22) | copy-start | bytes 196612
  3.3 14.2 %collective-permute-start = (bf16[3,1280]{1,0:T(4,128)(2,1)S(1)}, bf16[3,1280]{1,0:T(4,128)(2,1)S(1)}, u32[]{:S(2)}, u32[]{:S(2)}) collective-permute-start(bf16[3,1280]{1,0:T(4,128)(2,1)S(1)} %pad_maximum_fusion.9), channel_id=1, source_target_pairs={{0,2},{2,4},{4,6},{6,8},{8,10},{10,12},{12,14},{1,3},{3,5},{5,7},{... | collective-permute-start | bytes 23048 | tf_op jit(solution)/shard_map/ppermute | solution.py:12
  9.6 9.2 %copy-start.58 = (f32[2,64]{1,0:T(2,128)}, f32[2,64]{1,0:T(2,128)S(1)}, u32[]{:S(2)}) copy-start(f32[2,64]{1,0:T(2,128)S(1)} %get-tuple-element.126) | copy-start | bytes 1540
  9.6 9.2 %copy-start.60 = (f32[2,64]{1,0:T(2,128)}, f32[2,64]{1,0:T(2,128)S(1)}, u32[]{:S(2)}) copy-start(f32[2,64]{1,0:T(2,128)S(1)} %get-tuple-element.127) | copy-start | bytes 1540
  9.6 9.2 %copy-start.62 = (f32[2,64]{1,0:T(2,128)}, f32[2,64]{1,0:T(2,128)S(1)}, u32[]{:S(2)}) copy-start(f32[2,64]{1,0:T(2,128)S(1)} %get-tuple-element.128) | copy-start | bytes 1540
  9.6 9.2 %copy-start.64 = (f32[2,64]{1,0:T(2,128)}, f32[2,64]{1,0:T(2,128)S(1)}, u32[]{:S(2)}) copy-start(f32[2,64]{1,0:T(2,128)S(1)} %get-tuple-element.129) | copy-start | bytes 1540
  10.3 9.2 %copy-start.50 = (f32[2,64]{1,0:T(2,128)}, f32[2,64]{1,0:T(2,128)S(1)}, u32[]{:S(2)}) copy-start(f32[2,64]{1,0:T(2,128)S(1)} %get-tuple-element.130) | copy-start | bytes 1540
  10.3 9.2 %copy-start.52 = (f32[2,64]{1,0:T(2,128)}, f32[2,64]{1,0:T(2,128)S(1)}, u32[]{:S(2)}) copy-start(f32[2,64]{1,0:T(2,128)S(1)} %get-tuple-element.131) | copy-start | bytes 1540
  10.3 9.2 %copy-start.54 = (f32[2,64]{1,0:T(2,128)}, f32[2,64]{1,0:T(2,128)S(1)}, u32[]{:S(2)}) copy-start(f32[2,64]{1,0:T(2,128)S(1)} %get-tuple-element.132) | copy-start | bytes 1540
  10.3 9.2 %copy-start.56 = (f32[2,64]{1,0:T(2,128)}, f32[2,64]{1,0:T(2,128)S(1)}, u32[]{:S(2)}) copy-start(f32[2,64]{1,0:T(2,128)S(1)} %get-tuple-element.133) | copy-start | bytes 1540
  12.5 5.0 %copy-start.29 = (f32[8,2,2]{0,1,2:T(2,128)}, f32[8,2,2]{0,1,2:T(2,128)S(1)}, u32[]{:S(2)}) copy-start(f32[8,2,2]{0,1,2:T(2,128)S(1)} %copy.200) | copy-start | bytes 388
  13.3 7.0 %copy-start.32 = (f32[2,512]{1,0:T(2,128)}, f32[2,512]{1,0:T(2,128)S(1)}, u32[]{:S(2)}) copy-start(f32[2,512]{1,0:T(2,128)S(1)} %get-tuple-element.118) | copy-start | bytes 12292
  13.3 7.0 %copy-start.34 = (f32[2,512]{1,0:T(2,128)}, f32[2,512]{1,0:T(2,128)S(1)}, u32[]{:S(2)}) copy-start(f32[2,512]{1,0:T(2,128)S(1)} %get-tuple-element.119) | copy-start | bytes 12292
  13.3 7.0 %copy-start.36 = (f32[2,512]{1,0:T(2,128)}, f32[2,512]{1,0:T(2,128)S(1)}, u32[]{:S(2)}) copy-start(f32[2,512]{1,0:T(2,128)S(1)} %get-tuple-element.120) | copy-start | bytes 12292
  13.3 7.0 %copy-start.38 = (f32[2,512]{1,0:T(2,128)}, f32[2,512]{1,0:T(2,128)S(1)}, u32[]{:S(2)}) copy-start(f32[2,512]{1,0:T(2,128)S(1)} %get-tuple-element.121) | copy-start | bytes 12292
  14.0 5.5 %copy-start.23 = (f32[256,2,8]{0,2,1:T(8,128)}, f32[256,2,8]{0,2,1:T(8,128)S(1)}, u32[]{:S(2)}) copy-start(f32[256,2,8]{0,2,1:T(8,128)S(1)} %get-tuple-element.116) | copy-start | bytes 49156
  14.1 3.3 %copy-start.40 = (f32[2,8]{1,0:T(2,128)}, f32[2,8]{1,0:T(2,128)S(1)}, u32[]{:S(2)}) copy-start(f32[2,8]{1,0:T(2,128)S(1)} %slice_reduce_fusion) | copy-start | bytes 196
  15.6 4.7 %copy-start.12 = (f32[256,2,8]{0,2,1:T(8,128)}, f32[256,2,8]{0,2,1:T(8,128)S(1)}, u32[]{:S(2)}) copy-start(f32[256,2,8]{0,2,1:T(8,128)S(1)} %get-tuple-element.115) | copy-start | bytes 49156
  24.5 6.8 %copy-start.45 = (f32[2,8]{1,0:T(2,128)S(1)}, f32[2,8]{1,0:T(2,128)}, u32[]{:S(2)}) copy-start(f32[2,8]{1,0:T(2,128)} %get-tuple-element.136) | copy-start | bytes 196
  24.5 11.2 %copy-start.24 = (f32[256,2,8]{0,2,1:T(8,128)S(1)}, f32[256,2,8]{0,2,1:T(8,128)}, u32[]{:S(2)}) copy-start(f32[256,2,8]{0,2,1:T(8,128)} %copy-done.23) | copy-start | bytes 49156
  25.3 6.0 %collective-permute-start.1 = (bf16[2,8,4224]{2,1,0:T(8,128)(2,1)S(1)}, bf16[2,8,4224]{2,1,0:T(8,128)(2,1)S(1)}, u32[]{:S(2)}, u32[]{:S(2)}) collective-permute-start(bf16[2,8,4224]{2,1,0:T(8,128)(2,1)S(1)} %get-tuple-element.124), channel_id=1, source_target_pairs={{0,2},{2,4},{4,6},{6,8},{8,10},{10,12},{12,14},{1,3},{3,5},{5,7},{... | collective-permute-start | bytes 405512 | tf_op jit(solution)/shard_map/ppermute | solution.py:30
  28.7 6.9 %collective-permute-start.4 = (bf16[2,8,4224]{2,1,0:T(8,128)(2,1)S(1)}, bf16[2,8,4224]{2,1,0:T(8,128)(2,1)S(1)}, u32[]{:S(2)}, u32[]{:S(2)}) collective-permute-start(bf16[2,8,4224]{2,1,0:T(8,128)(2,1)S(1)} %get-tuple-element.125), channel_id=1, source_target_pairs={{2,0},{4,2},{6,4},{8,6},{10,8},{12,10},{14,12},{3,1},{5,3},{7,5},{... | collective-permute-start | bytes 405512 | tf_op jit(solution)/shard_map/ppermute | solution.py:30
  36.0 6.4 %collective-permute-start.2 = (bf16[2,8,4224]{2,1,0:T(8,128)(2,1)S(1)}, bf16[2,8,4224]{2,1,0:T(8,128)(2,1)S(1)}, u32[]{:S(2)}, u32[]{:S(2)}) collective-permute-start(bf16[2,8,4224]{2,1,0:T(8,128)(2,1)S(1)} %pad_maximum_fusion.2), channel_id=1, source_target_pairs={{0,4},{2,6},{4,8},{6,10},{8,12},{10,14},{1,5},{3,7},{5,9},{7,11},{... | collective-permute-start | bytes 405512 | tf_op jit(solution)/shard_map/ppermute | solution.py:30
  42.6 7.3 %collective-permute-start.5 = (bf16[2,8,4224]{2,1,0:T(8,128)(2,1)S(1)}, bf16[2,8,4224]{2,1,0:T(8,128)(2,1)S(1)}, u32[]{:S(2)}, u32[]{:S(2)}) collective-permute-start(bf16[2,8,4224]{2,1,0:T(8,128)(2,1)S(1)} %pad_maximum_fusion.4), channel_id=1, source_target_pairs={{4,0},{6,2},{8,4},{10,6},{12,8},{14,10},{5,1},{7,3},{9,5},{11,7},{... | collective-permute-start | bytes 405512 | tf_op jit(solution)/shard_map/ppermute | solution.py:30
  50.4 7.5 %collective-permute-start.3 = (bf16[2,8,4224]{2,1,0:T(8,128)(2,1)S(1)}, bf16[2,8,4224]{2,1,0:T(8,128)(2,1)S(1)}, u32[]{:S(2)}, u32[]{:S(2)}) collective-permute-start(bf16[2,8,4224]{2,1,0:T(8,128)(2,1)S(1)} %pad_maximum_fusion.3), channel_id=1, source_target_pairs={{0,8},{2,10},{4,12},{6,14},{1,9},{3,11},{5,13},{7,15},{16,24},{18,... | collective-permute-start | bytes 405512 | tf_op jit(solution)/shard_map/ppermute | solution.py:30
  55.4 8.3 %collective-permute-start.6 = (bf16[2,8,4224]{2,1,0:T(8,128)(2,1)S(1)}, bf16[2,8,4224]{2,1,0:T(8,128)(2,1)S(1)}, u32[]{:S(2)}, u32[]{:S(2)}) collective-permute-start(bf16[2,8,4224]{2,1,0:T(8,128)(2,1)S(1)} %pad_maximum_fusion.5), channel_id=1, source_target_pairs={{8,0},{10,2},{12,4},{14,6},{9,1},{11,3},{13,5},{15,7},{24,16},{26,... | collective-permute-start | bytes 405512 | tf_op jit(solution)/shard_map/ppermute | solution.py:30
  70.6 6.2 %copy-start.15 = (f32[256,2,8]{0,2,1:T(8,128)}, f32[256,2,8]{0,2,1:T(8,128)S(1)}, u32[]{:S(2)}) copy-start(f32[256,2,8]{0,2,1:T(8,128)S(1)} %get-tuple-element.138) | copy-start | bytes 49156
  70.9 5.9 %copy-start.2 = (f32[256,2,8,64]{0,3,2,1:T(8,128)S(1)}, f32[256,2,8,64]{0,3,2,1:T(8,128)}, u32[]{:S(2)}) copy-start(f32[256,2,8,64]{0,3,2,1:T(8,128)} %get-tuple-element.139) | copy-start | bytes 3145732
  70.9 5.9 %copy-start.6 = (f32[2,256,256]{2,1,0:T(8,128)S(1)}, f32[2,256,256]{2,1,0:T(8,128)}, u32[]{:S(2)}) copy-start(f32[2,256,256]{2,1,0:T(8,128)} %fusion.116) | copy-start | bytes 1572868
  70.9 5.9 %copy-start.69 = (f32[2,8]{1,0:T(2,128)S(1)}, f32[2,8]{1,0:T(2,128)}, u32[]{:S(2)}) copy-start(f32[2,8]{1,0:T(2,128)} %param.26) | copy-start | bytes 196
  79.2 8.2 %copy-start.25 = (f32[256,2,8]{0,2,1:T(8,128)S(1)}, f32[256,2,8]{0,2,1:T(8,128)}, u32[]{:S(2)}) copy-start(f32[256,2,8]{0,2,1:T(8,128)} %copy-done.23) | copy-start | bytes 49156
  79.2 14.5 %copy-start.9 = (f32[256,2,64]{0,2,1:T(8,128)S(1)}, f32[256,2,64]{0,2,1:T(8,128)}, u32[]{:S(2)}) copy-start(f32[256,2,64]{0,2,1:T(8,128)} %get-tuple-element.105) | copy-start | bytes 393220
  81.7 12.4 %copy-start.59 = (f32[2,64]{1,0:T(2,128)S(1)}, f32[2,64]{1,0:T(2,128)}, u32[]{:S(2)}) copy-start(f32[2,64]{1,0:T(2,128)} %copy-done.58) | copy-start | bytes 1540
  81.7 12.4 %copy-start.61 = (f32[2,64]{1,0:T(2,128)S(1)}, f32[2,64]{1,0:T(2,128)}, u32[]{:S(2)}) copy-start(f32[2,64]{1,0:T(2,128)} %copy-done.60) | copy-start | bytes 1540
  81.7 12.4 %copy-start.63 = (f32[2,64]{1,0:T(2,128)S(1)}, f32[2,64]{1,0:T(2,128)}, u32[]{:S(2)}) copy-start(f32[2,64]{1,0:T(2,128)} %copy-done.62) | copy-start | bytes 1540
  81.7 12.4 %copy-start.65 = (f32[2,64]{1,0:T(2,128)S(1)}, f32[2,64]{1,0:T(2,128)}, u32[]{:S(2)}) copy-start(f32[2,64]{1,0:T(2,128)} %copy-done.64) | copy-start | bytes 1540
  86.7 7.0 %copy-start.19 = (f32[8,2,2,128]{3,0,1,2:T(8,128)}, f32[8,2,2,128]{3,0,1,2:T(8,128)S(1)}, u32[]{:S(2)}) copy-start(f32[8,2,2,128]{3,0,1,2:T(8,128)S(1)} %reduce-window.24) | copy-start | bytes 49156
  98.3 2.9 %copy-start.11 = (f32[256,2,8]{0,2,1:T(8,128)S(1)}, f32[256,2,8]{0,2,1:T(8,128)}, u32[]{:S(2)}) copy-start(f32[256,2,8]{0,2,1:T(8,128)} %param.23) | copy-start | bytes 49156
  98.3 2.9 %copy-start.16 = (f32[256,2,8]{0,2,1:T(8,128)S(1)}, f32[256,2,8]{0,2,1:T(8,128)}, u32[]{:S(2)}) copy-start(f32[256,2,8]{0,2,1:T(8,128)} %copy-done.15) | copy-start | bytes 49156
  98.3 2.9 %copy-start.20 = (f32[8,2,2,128]{3,0,1,2:T(8,128)S(1)}, f32[8,2,2,128]{3,0,1,2:T(8,128)}, u32[]{:S(2)}) copy-start(f32[8,2,2,128]{3,0,1,2:T(8,128)} %copy-done.19) | copy-start | bytes 49156
  98.3 2.9 %copy-start.22 = (f32[8,2,2,128]{3,0,1,2:T(8,128)S(1)}, f32[8,2,2,128]{3,0,1,2:T(8,128)}, u32[]{:S(2)}) copy-start(f32[8,2,2,128]{3,0,1,2:T(8,128)} %copy-done.21) | copy-start | bytes 49156
  98.3 2.9 %copy-start.31 = (f32[8,2,2]{0,1,2:T(2,128)S(1)}, f32[8,2,2]{0,1,2:T(2,128)}, u32[]{:S(2)}) copy-start(f32[8,2,2]{0,1,2:T(2,128)} %copy-done.29) | copy-start | bytes 388
  98.4 2.9 %copy-start.42 = (f32[2,8]{1,0:T(2,128)S(1)}, f32[2,8]{1,0:T(2,128)}, u32[]{:S(2)}) copy-start(f32[2,8]{1,0:T(2,128)} %copy-done.40) | copy-start | bytes 196
  98.4 2.9 %copy-start.44 = (f32[2,8]{1,0:T(2,128)S(1)}, f32[2,8]{1,0:T(2,128)}, u32[]{:S(2)}) copy-start(f32[2,8]{1,0:T(2,128)} %param.25) | copy-start | bytes 196
  98.4 2.9 %copy-start.47 = (f32[2,8,256]{2,1,0:T(8,128)S(1)}, f32[2,8,256]{2,1,0:T(8,128)}, u32[]{:S(2)}) copy-start(f32[2,8,256]{2,1,0:T(8,128)} %get-tuple-element.89) | copy-start | bytes 49156
  98.4 3.6 %copy-start.4 = (f32[259,2,64]{0,2,1:T(8,128)S(1)}, f32[259,2,64]{0,2,1:T(8,128)}, u32[]{:S(2)}) copy-start(f32[259,2,64]{0,2,1:T(8,128)} %copy-done.3) | copy-start | bytes 397828
  99.8 5.8 %collective-permute-start.7 = (f32[3,1280]{1,0:T(4,128)S(1)}, f32[3,1280]{1,0:T(4,128)S(1)}, u32[]{:S(2)}, u32[]{:S(2)}) collective-permute-start(f32[3,1280]{1,0:T(4,128)S(1)} %pad_maximum_fusion.8), channel_id=1, source_target_pairs={{2,0},{4,2},{6,4},{8,6},{10,8},{12,10},{14,12},{3,1},{5,3},{7,5},{... | collective-permute-start | bytes 46088 | tf_op jit(solution)/shard_map/ppermute | solution.py:12
  (30 other events, 49.3 us)

commit v4 on v3

--- a/solution.py
+++ b/solution.py
@@ -12,37 +12,47 @@
     return lax.ppermute(array, axis, pairs)
 
 
-def scanned_in(decay, state, axis, backward):
+def scanned_pair(decay, forward_state, backward_state, axis, riders):
     count = lax.axis_size(axis)
-    sign = -1 if backward else 1
-    groups, heads, rows, cols = state.shape
+    groups, heads, rows, cols = forward_state.shape
     lanes = 128
 
-    def shift(decay_part, state_part, by):
+    def shift(decay_part, state_part, by, sign):
         pairs = [(i, i + sign * by) for i in range(count) if 0 <= i + sign * by < count]
         packed = jnp.concatenate(
-            [
-                state_part.reshape(groups, heads, rows * cols),
-                jnp.broadcast_to(decay_part[:, :, None], (groups, heads, lanes)),
-            ],
-            2,
+            [state_part, jnp.broadcast_to(decay_part[:, :, None], (groups, heads, lanes))], 2
         ).astype(jnp.bfloat16)
-        got = lax.ppermute(packed, axis, pairs).astype(jnp.float32)
+        return lax.ppermute(packed, axis, pairs)
+
+    def unpack(got):
+        got = got.astype(jnp.float32)
         return got[:, :, rows * cols], got[:, :, : rows * cols]
 
-    flat = state.reshape(groups, heads, rows * cols)
-    before_decay, before_state = shift(decay, flat, 1)
-    upto_decay = before_decay * decay
-    upto_state = decay[:, :, None] * before_state + flat
-    by = 2
+    def fold(window, got_decay, got_state):
+        before_decay, before_state, upto_decay, upto_state = window
+        return (
+            before_decay * got_decay,
+            before_decay[:, :, None] * got_state + before_state,
+            upto_decay * got_decay,
+            upto_decay[:, :, None] * got_state + upto_state,
+        )
+
+    flats = [s.reshape(groups, heads, rows * cols) for s in (forward_state, backward_state)]
+    windows = [
+        (jnp.ones_like(decay), jnp.zeros_like(flat), decay, flat) for flat in flats
+    ]
+    tied = list(riders)
+    by = 1
+    step = 0
     while by < count:
-        got_decay, got_state = shift(upto_decay, upto_state, by)
-        before_state = before_decay[:, :, None] * got_state + before_state
-        before_decay = before_decay * got_decay
-        upto_state = upto_decay[:, :, None] * got_state + upto_state
-        upto_decay = upto_decay * got_decay
+        got = [shift(w[2], w[3], by, sign) for w, sign in zip(windows, (1, -1))]
+        if step < len(tied):
+            got, tied[step] = lax.optimization_barrier((got, tied[step]))
+        windows = [fold(w, *unpack(g)) for w, g in zip(windows, got)]
         by *= 2
-    return before_state.reshape(groups, heads, rows, cols)
+        step += 1
+    state_in, adjoint = [w[1].reshape(groups, heads, rows, cols) for w in windows]
+    return state_in, adjoint, tied
 
 
 def conv_forward(extended, weight):
@@ -71,8 +81,13 @@
 
 
 def ssd_cum(dt_raw, rate, dt_bias):
+    length = dt_raw.shape[0]
     step_size = jax.nn.softplus(dt_raw + dt_bias)
-    return step_size, jnp.cumsum(-rate * step_size, axis=0)
+    row_index = lax.broadcasted_iota(jnp.int32, (length, length), 0)
+    col_index = lax.broadcasted_iota(jnp.int32, (length, length), 1)
+    lower = (row_index >= col_index).astype(jnp.float32)
+    cum_log = jnp.einsum("ts,sgh->tgh", lower, -rate * step_size, precision=HIGH)
+    return step_size, cum_log
 
 
 def ssd_mix(x_float, b_float, c_float, dt_raw, rate, dt_bias, skip):
@@ -158,8 +173,11 @@
     seed_state = jnp.einsum(
         "tghp,tgn->ghpn", jnp.exp(cum_log)[..., None] * grad_heads, c_float, precision=HIGH
     )
-    state_in = scanned_in(decay_total, state_end, "ctx", False)
-    adjoint = scanned_in(decay_total, seed_state, "ctx", True)
+    mix_x, mix_b, mix_c, mix_dt = mix_pull(grad_heads)
+    state_in, adjoint, riders = scanned_pair(
+        decay_total, state_end, seed_state, "ctx", [y_local, mix_x, (mix_b, mix_c, mix_dt)]
+    )
+    y_local, mix_x, (mix_b, mix_c, mix_dt) = riders
 
     def carry_map(c_arg, cum_arg):
         return carry_in(c_arg, cum_arg, state_in)
@@ -169,7 +187,6 @@
     grad_c_carry, grad_cum_carry = carry_pull(grad_heads)
     end_term = jnp.sum(adjoint * state_in, axis=(2, 3)) * decay_total
     grad_cum = grad_cum_carry.at[length - 1].add(end_term)
-    mix_x, mix_b, mix_c, mix_dt = mix_pull(grad_heads)
     state_x, state_b, state_dt = state_pull((grad_cum, adjoint))
     grad_x_conv = mix_x + state_x
     grad_b_part = mix_b + state_b

time: 109 us -> 102 us (0.936)
  other arithmetic: 26 us -> 16.8 us
  waiting for transfers between devices: 20.8 us -> 12.8 us
  local copies, waits for them, and re-layouts: 17.6 us -> 23.2 us
  starting transfers between devices: 22.6 us -> 24.9 us
  matrix products: 19.7 us -> 21.7 us
    another operation x18 -> x7, other arithmetic: 13.3 us -> 0.5 us
    ppermute x6, waiting for transfers between devices: 18.9 us -> 11.3 us  [shift(): return lax.ppermute(packed, axis, pairs)]
    reshape x4 -> x5, local copies, waits for them, and re-layouts: 0.8 us -> 5.15 us  [the longest x1 2.32 us: ssd_state(): x_heads = x_float.reshape(length, groups, head_count, head_size)]
    ppermute x6, starting transfers between devices: 16.3 us -> 18.7 us  [shift(): return lax.ppermute(packed, axis, pairs)]
    optimization_barrier x0 -> x1, local copies, waits for them, and re-layouts: none -> 2.26 us  [scanned_pair(): got, tied[step] = lax.optimization_barrier((got, tied[step]))]
    unnamed x0 -> x3, matrix products: none -> 1.96 us
    mul x1 -> x3, other arithmetic: 1.51 us -> 3.15 us  [conv_backward(): grad_out.astype(jnp.float32)]
    dot_general x3, matrix products: 3.21 us -> 4.81 us  [ssd_state(): jnp.einsum('sghp,sgn->ghpn', weighted.astype(jnp.float32), b_float, preci...]
  transfers between devices with their start and end apart: 8 -> 8, of which waited for: 7 -> 5; matrix products, arithmetic and copies ran while one was open for 13% -> 15% of each run, Pallas kernels for 0% -> 0%
where the time goes in v4:
time: 102 us; the launch traced here: 101 us
  starting transfers between devices  24.9 us (24%)
  local copies, waits for them, and re-layouts  23.2 us (23%)
  matrix products  21.7 us (21%)
  other arithmetic  16.8 us (16%)
  waiting for transfers between devices  12.8 us (13%)
  between operations  1.73 us (2%)
    ppermute x6, starting transfers between devices, shift(): return lax.ppermute(packed, axis, pairs)  18.7 us
    ppermute x6, waiting for transfers between devices, shift(): return lax.ppermute(packed, axis, pairs)  11.3 us
    dot_general x3, matrix products, ssd_mix(): jnp.einsum('ghts,sghp->tghp', mixing, x_half, preferred_element_type=jnp....  9.69 us
    ppermute x2, starting transfers between devices, from_behind(): return lax.ppermute(array, axis, pairs)  6.14 us
    unnamed x135, local copies, waits for them, and re-layouts  5.75 us
    dot_general x3, matrix products, ssd_state(): jnp.einsum('sghp,sgn->ghpn', weighted.astype(jnp.float32), b_float, preci...  4.81 us
    mul x3, other arithmetic, conv_backward(): grad_out.astype(jnp.float32)  3.15 us
    add x3, other arithmetic, conv_backward(): result = result + weight[tap_index] * padded[offset:offset + ext_len]  2.55 us
  transfers between devices with their start and end apart: 8, of which 5 were waited for; matrix products, arithmetic and copies ran while one was open for 15% of the time, Pallas kernels for 0%

profile of v4, /device:TPU:0, one launch (start us, length us, event | category | flops | bytes accessed | tf_op | source)
XLA Modules:
  0.0 101.0 jit_solution(1778250348658816108)
XLA Ops:
  0.6 0.8 slice_bitcast_fusion.1
  1.4 0.8 slice.295
  2.3 0.9 slice.296
  3.3 4.8 %collective-permute-start = (bf16[3,1280]{1,0:T(4,128)(2,1)S(1)}, bf16[3,1280]{1,0:T(4,128)(2,1)S(1)}, u32[]{:S(2)}, u32[]{:S(2)}) collective-permute-start(bf16[3,1280]{1,0:T(4,128)(2,1)S(1)} %pad_maximum_fusion.9), channel_id=1, source_target_pairs={{0,2},{2,4},{4,6},{6,8},{8,10},{10,12},{12,14},{1,3},{3,5},{5,7},{... | collective-permute-start | bytes 23048 | tf_op jit(solution)/shard_map/ppermute | solution.py:12
  8.1 0.7 neg.28
  8.8 0.9 fusion.56
  10.0 0.8 fusion.107
  10.8 0.7 slice_bitcast_fusion.13
  11.6 0.7 slice_bitcast_fusion.9
  12.4 0.7 slice_bitcast_fusion.5
  13.2 1.3 %copy.122 = bf16[256,2,512]{0,2,1:T(8,128)(2,1)S(1)} copy(bf16[256,2,512]{2,1,0:T(2,128)(2,1)} %param.30) | data formatting | bytes 1048576 | tf_op args[10]
  15.2 2.4 %multiply_convert_fusion = (bf16[256,2,512]{2,1,0:T(2,128)(2,1)S(1)}, f32[256,2,512]{2,1,0:T(2,128)S(1)}) fusion(bf16[256,2,512]{2,1,0:T(2,128)(2,1)S(1)} %copy-done.2, f32[2,512]{1,0:T(2,128)S(1)} %get-tuple-element.138, bf16[259,2,512]{2,1,0:T(2,128)(2,1)S(1)} %constant_dynamic-update-slice_fusion, f32[2,512]{1,0:T(2,128)S(1)} %get-tuple-element.139, ...), kind=kLoop, calls=%fused_computation.59 | loop fusion | flops 4194304 | bytes 3686400 | tf_op jit(solution)/shard_map/convert_element_type | solution.py:159
  18.5 1.1 %multiply_convert_fusion.1 = (bf16[256,2,64]{0,2,1:T(8,128)(2,1)S(1)}, f32[256,2,64]{0,2,1:T(8,128)}, bf16[256,2,64]{0,2,1:T(8,128)(2,1)S(1)}, f32[256,2,64]{0,2,1:T(8,128)}) fusion(bf16[256,2,64]{0,2,1:T(8,128)(2,1)S(1)} %copy-done.16, f32[2,64]{1,0:T(2,128)S(1)} %get-tuple-element.146, bf16[3,2,64]{0,2,1:T(8,128)(2,1)S(1)} %bitcast.205, ...), kind=kLoop, calls=%fused_computation.107 | loop fusion | flops 1638400 | bytes 529920 | tf_op jit(solution)/shard_map/convert_element_type | solution.py:161
  20.3 4.8 %fusion.18 = (f32[2,8,256]{2,1,0:T(8,128)}, f32[2,8,256]{2,1,0:T(8,128)}, f32[2,8,256]{2,1,0:T(8,128)}, f32[2,256,256]{2,1,0:T(8,128)S(1)}) fusion(f32[2,8,256]{2,1,0:T(8,128)S(1)} %bitcast.199, f32[2,8,256]{2,1,0:T(8,128)S(1)} %get-tuple-element.131, f32[2,256,256]{2,1,0:T(8,128)S(1)} %fusion.111, pred[256,256]{1,0:T(8,128)(4,1)S(1)} %iota_compare_fusion, ...), kind=kOutput, calls=%fused_computation.27 | convolution fusion | flops 156094464 | bytes 2244608 | tf_op jit(solution)/shard_map/transpose(jvp(ghts,sghp->tghp))/dot_general | solution.py:110
  25.1 2.5 %fusion.22 = f32[256,2,8,64]{0,3,2,1:T(8,128)} fusion(bf16[256,2,8,64]{0,3,2,1:T(8,128)(2,1)S(1)} %bitcast.188, f32[2,8,256]{2,1,0:T(8,128)S(1)} %get-tuple-element.131, f32[2,8,256]{2,1,0:T(8,128)S(1)} %bitcast.200, f32[2,256,256]{2,1,0:T(8,128)S(1)} %fusion.111, pred[256,256]{1,0:T(8,128)(4,1)S(1)} %iota_compare_fusion, f32[2,8]{1,0:T(2,128)S(1)} %copy-done.60), kind=kOutput, calls=%fused_computation.30 | convolution fusion | flops 141295616 | bytes 2195520 | tf_op jit(solution)/shard_map/jvp(ghts,sghp->tghp)/dot_general | solution.py:110
  27.6 2.4 %fusion.36 = f32[256,2,8,64]{0,3,2,1:T(8,128)} fusion(bf16[2,8,64,256]{3,2,1,0:T(8,128)(2,1)S(1)} %bitcast.184, f32[2,8,256]{2,1,0:T(8,128)S(1)} %get-tuple-element.131, f32[2,8,256]{2,1,0:T(8,128)S(1)} %bitcast.201, f32[2,256,256]{2,1,0:T(8,128)S(1)} %fusion.111, pred[256,256]{1,0:T(8,128)(4,1)S(1)} %iota_compare_fusion, ...), kind=kOutput, calls=%fused_computation.37 | convolution fusion | flops 141819904 | bytes 2719808 | tf_op jit(solution)/shard_map/transpose(jvp(ghts,sghp->tghp))/dot_general | solution.py:110
  30.8 1.9 %fusion.54 = f32[2,8,64,64]{3,2,1,0:T(8,128)} fusion(bf16[256,2,8,64]{0,3,2,1:T(8,128)(2,1)S(1)} %bitcast.189, f32[256,2,8]{0,2,1:T(8,128)S(1)} %get-tuple-element.132, bf16[256,2,64]{0,2,1:T(8,128)(2,1)} %copy-done.3), kind=kOutput, calls=%fused_computation.65 | convolution fusion | flops 34340864 | bytes 868352 | tf_op jit(solution)/shard_map/jvp(sghp,sgn->ghpn)/dot_general | solution.py:122
  32.7 1.3 %reshape.250 = f32[2,8,4096]{2,1,0:T(8,128)S(1)} reshape(f32[2,8,64,64]{3,2,1,0:T(8,128)} %fusion.54) | data formatting | bytes 524288 | tf_op jit(solution)/shard_map/reshape | solution.py:40
  34.1 1.3 %collective-permute-start.2 = (bf16[2,8,4224]{2,1,0:T(8,128)(2,1)S(1)}, bf16[2,8,4224]{2,1,0:T(8,128)(2,1)S(1)}, u32[]{:S(2)}, u32[]{:S(2)}) collective-permute-start(bf16[2,8,4224]{2,1,0:T(8,128)(2,1)S(1)} %get-tuple-element.142), channel_id=1, source_target_pairs={{2,0},{4,2},{6,4},{8,6},{10,8},{12,10},{14,12},{3,1},{5,3},{7,5},{... | collective-permute-start | bytes 405512 | tf_op jit(solution)/shard_map/ppermute | solution.py:25
  35.4 4.6 %collective-permute-start.1 = (bf16[2,8,4224]{2,1,0:T(8,128)(2,1)S(1)}, bf16[2,8,4224]{2,1,0:T(8,128)(2,1)S(1)}, u32[]{:S(2)}, u32[]{:S(2)}) collective-permute-start(bf16[2,8,4224]{2,1,0:T(8,128)(2,1)S(1)} %get-tuple-element.143), channel_id=1, source_target_pairs={{0,2},{2,4},{4,6},{6,8},{8,10},{10,12},{12,14},{1,3},{3,5},{5,7},{... | collective-permute-start | bytes 405512 | tf_op jit(solution)/shard_map/ppermute | solution.py:25
  40.0 1.1 %convolution_bitcast_fusion.2 = f32[256,2,64]{0,2,1:T(8,128)} fusion(f32[2,256,256]{2,1,0:T(8,128)S(1)} %get-tuple-element.107, bf16[256,2,64]{0,2,1:T(8,128)(2,1)S(1)} %copy-done.4), kind=kOutput, calls=%fused_computation.41 | convolution fusion | flops 100663296 | bytes 720896 | tf_op jit(solution)/shard_map/transpose(jvp(tgn,sgn->gts))/dot_general | solution.py:108
  41.0 1.0 convolution_bitcast_fusion.3
  42.0 1.9 %collective-permute-done.1 = bf16[2,8,4224]{2,1,0:T(8,128)(2,1)S(1)} collective-permute-done((bf16[2,8,4224]{2,1,0:T(8,128)(2,1)S(1)}, bf16[2,8,4224]{2,1,0:T(8,128)(2,1)S(1)}, u32[]{:S(2)}, u32[]{:S(2)}) %collective-permute-start.1) | collective-permute-done | bytes 135200 | tf_op jit(solution)/shard_map/ppermute | solution.py:25
  44.5 4.8 %collective-permute-start.3 = (bf16[2,8,4224]{2,1,0:T(8,128)(2,1)S(1)}, bf16[2,8,4224]{2,1,0:T(8,128)(2,1)S(1)}, u32[]{:S(2)}, u32[]{:S(2)}) collective-permute-start(bf16[2,8,4224]{2,1,0:T(8,128)(2,1)S(1)} %pad_maximum_fusion.2), channel_id=1, source_target_pairs={{0,4},{2,6},{4,8},{6,10},{8,12},{10,14},{1,5},{3,7},{5,9},{7,11},{... | collective-permute-start | bytes 405512 | tf_op jit(solution)/shard_map/ppermute | solution.py:25
  49.4 1.3 %collective-permute-start.4 = (bf16[2,8,4224]{2,1,0:T(8,128)(2,1)S(1)}, bf16[2,8,4224]{2,1,0:T(8,128)(2,1)S(1)}, u32[]{:S(2)}, u32[]{:S(2)}) collective-permute-start(bf16[2,8,4224]{2,1,0:T(8,128)(2,1)S(1)} %pad_maximum_fusion.3), channel_id=1, source_target_pairs={{4,0},{6,2},{8,4},{10,6},{12,8},{14,10},{5,1},{7,3},{9,5},{11,7},{... | collective-permute-start | bytes 405512 | tf_op jit(solution)/shard_map/ppermute | solution.py:25
  50.8 0.8 fusion.46
  51.9 4.5 %collective-permute-done.4 = bf16[2,8,4224]{2,1,0:T(8,128)(2,1)S(1)} collective-permute-done((bf16[2,8,4224]{2,1,0:T(8,128)(2,1)S(1)}, bf16[2,8,4224]{2,1,0:T(8,128)(2,1)S(1)}, u32[]{:S(2)}, u32[]{:S(2)}) %collective-permute-start.4) | collective-permute-done | bytes 135200 | tf_op jit(solution)/shard_map/ppermute | solution.py:25
  57.1 5.2 %collective-permute-start.5 = (bf16[2,8,4224]{2,1,0:T(8,128)(2,1)S(1)}, bf16[2,8,4224]{2,1,0:T(8,128)(2,1)}, u32[]{:S(2)}, u32[]{:S(2)}) collective-permute-start(bf16[2,8,4224]{2,1,0:T(8,128)(2,1)S(1)} %pad_maximum_fusion.4), channel_id=1, source_target_pairs={{0,8},{2,10},{4,12},{6,14},{1,9},{3,11},{5,13},{7,15},{16,24},{18,... | collective-permute-start | bytes 405512 | tf_op jit(solution)/shard_map/ppermute | solution.py:25
  62.3 0.7 pad_maximum_fusion.5
  63.0 1.6 %collective-permute-start.6 = (bf16[2,8,4224]{2,1,0:T(8,128)(2,1)}, bf16[2,8,4224]{2,1,0:T(8,128)(2,1)}, u32[]{:S(2)}, u32[]{:S(2)}) collective-permute-start(bf16[2,8,4224]{2,1,0:T(8,128)(2,1)} %pad_maximum_fusion.5), channel_id=1, source_target_pairs={{8,0},{10,2},{12,4},{14,6},{9,1},{11,3},{13,5},{15,7},{24,16},{26,... | collective-permute-start | bytes 405512 | tf_op jit(solution)/shard_map/ppermute | solution.py:25
  64.7 2.3 %copy.126 = f32[256,2,512]{2,1,0:T(2,128)} copy(f32[256,2,512]{0,2,1:T(8,128)} %bitcast.193) | data formatting | bytes 2097152 | tf_op jit(solution)/shard_map/optimization_barrier | solution.py:50
  67.0 4.7 %collective-permute-done.6 = bf16[2,8,4224]{2,1,0:T(8,128)(2,1)} collective-permute-done((bf16[2,8,4224]{2,1,0:T(8,128)(2,1)}, bf16[2,8,4224]{2,1,0:T(8,128)(2,1)}, u32[]{:S(2)}, u32[]{:S(2)}) %collective-permute-start.6) | collective-permute-done | bytes 135200 | tf_op jit(solution)/shard_map/ppermute | solution.py:25
  71.7 1.9 %multiply_reduce_fusion = (f32[2,8]{1,0:T(2,128)S(1)}, f32[2,8,4096]{2,1,0:T(8,128)}, f32[2,8,4096]{2,1,0:T(8,128)}) fusion(f32[2,8,4224]{2,1,0:T(8,128)S(1)} %convert_element_type.165, f32[2,8,4224]{2,1,0:T(8,128)S(1)} %copy-done.1, f32[2,8]{1,0:T(2,128)S(1)} %get-tuple-element.109, bf16[2,8,4224]{2,1,0:T(8,128)(2,1)} %collective-permute-done.6, ...), kind=kLoop, calls=%fused_computation.66 | loop fusion | flops 786416 | bytes 1835328 | tf_op jit(solution)/shard_map/reduce_sum | solution.py:188
  73.6 1.2 %reshape.257 = f32[2,8,64,64]{3,2,1,0:T(8,128)S(1)} reshape(f32[2,8,4096]{2,1,0:T(8,128)} %get-tuple-element.117) | data formatting | bytes 524288 | tf_op jit(solution)/shard_map/reshape | solution.py:54
  75.4 2.3 %fusion.49 = (f32[256,2,8]{0,2,1:T(8,128)}, f32[256,2,8,64]{0,3,2,1:T(8,128)}) fusion(bf16[256,2,512]{0,2,1:T(8,128)(2,1)S(1)} %copy.120, f32[256,2,8]{0,2,1:T(8,128)S(1)} %get-tuple-element.132, f32[2,8,64,64]{3,2,1,0:T(8,128)S(1)} %reshape.257, bf16[256,2,64]{0,2,1:T(8,128)(2,1)S(1)} %copy-done.5), kind=kOutput, calls=%fused_computation.54 | convolution fusion | flops 202895360 | bytes 1933312 | tf_op jit(solution)/shard_map/transpose(jvp(sghp,sgn->ghpn))/dot_general | solution.py:122
  77.9 1.7 %convolution_bitcast_fusion.4 = f32[256,2,64]{0,2,1:T(8,128)} fusion(f32[2,8,64,64]{3,2,1,0:T(8,128)S(1)} %reshape.256, bf16[256,2,8,64]{0,3,2,1:T(8,128)(2,1)S(1)} %bitcast.186, f32[256,2,8]{0,2,1:T(8,128)S(1)} %get-tuple-element.133), kind=kOutput, calls=%fused_computation.43 | convolution fusion | flops 201850880 | bytes 933888 | tf_op jit(solution)/shard_map/transpose(jvp(tgn,ghpn->tghp))/dot_general | solution.py:127
  80.2 0.7 copy.134
  81.0 2.3 %copy.127 = f32[256,2,512]{2,1,0:T(2,128)} copy(f32[256,2,512]{0,2,1:T(8,128)} %bitcast.191) | data formatting | bytes 2097152 | tf_op jit(solution)/shard_map/transpose(jvp())/reshape | solution.py:119
  83.7 0.7 copy.130
  84.4 1.0 fusion.67
  85.4 0.7 copy.131
  86.1 1.6 %fusion.50 = (f32[256,2,8]{0,2,1:T(8,128)S(1)}, bf16[256,2,8,64]{0,3,2,1:T(8,128)(2,1)S(1)}) fusion(f32[256,2,8,64]{0,3,2,1:T(8,128)S(1)} %convolution_bitcast_fusion, bf16[256,2,512]{0,2,1:T(8,128)(2,1)S(1)} %copy.122, f32[256,2,8,64]{0,3,2,1:T(8,128)} %fusion.22, f32[256,2,8]{0,2,1:T(8,128)S(1)} %get-tuple-element.133), kind=kLoop, calls=%fused_computation.55 | loop fusion | flops 1568768 | bytes 3178496 | tf_op jit(solution)/shard_map/transpose(jvp())/reduce_sum | solution.py:128
  88.0 3.0 %multiply_multiply_fusion = f32[256,2,512]{2,1,0:T(2,128)S(1)} fusion(f32[256,2,512]{2,1,0:T(2,128)S(1)} %get-tuple-element.124, f32[256,2,512]{2,1,0:T(2,128)} %copy.126, f32[256,2,512]{2,1,0:T(2,128)} %copy.127), kind=kLoop, calls=%fused_computation.56 | loop fusion | flops 2883584 | bytes 4194304 | tf_op jit(solution)/shard_map/mul | solution.py:71
  91.2 1.3 %multiply_add_fusion = f32[259,2,512]{2,1,0:T(2,128)S(1)} fusion(f32[256,2,512]{2,1,0:T(2,128)S(1)} %multiply_multiply_fusion, f32[2,512]{1,0:T(2,128)S(1)} %copy-done.30, f32[2,512]{1,0:T(2,128)S(1)} %copy-done.32, f32[2,512]{1,0:T(2,128)S(1)} %copy-done.28, f32[2,512]{1,0:T(2,128)S(1)} %copy-done.26), kind=kLoop, calls=%fused_computation.52 | loop fusion | flops 1856512 | bytes 2125824 | tf_op jit(solution)/shard_map/add | solution.py:79
  92.6 1.3 %collective-permute-start.7 = (f32[3,1280]{1,0:T(4,128)S(1)}, f32[3,1280]{1,0:T(4,128)S(1)}, u32[]{:S(2)}, u32[]{:S(2)}) collective-permute-start(f32[3,1280]{1,0:T(4,128)S(1)} %pad_maximum_fusion.8), channel_id=1, source_target_pairs={{2,0},{4,2},{6,4},{8,6},{10,8},{12,10},{14,12},{3,1},{5,3},{7,5},{... | collective-permute-start | bytes 46088 | tf_op jit(solution)/shard_map/ppermute | solution.py:12
  95.0 1.2 %copy.136 = bf16[256,2,512]{2,1,0:T(2,128)(2,1)} copy(bf16[256,2,512]{0,2,1:T(8,128)(2,1)S(1)} %bitcast.192) | data formatting | bytes 1048576
  96.8 1.5 %collective-permute-done.7 = f32[3,1280]{1,0:T(4,128)S(1)} collective-permute-done((f32[3,1280]{1,0:T(4,128)S(1)}, f32[3,1280]{1,0:T(4,128)S(1)}, u32[]{:S(2)}, u32[]{:S(2)}) %collective-permute-start.7) | collective-permute-done | bytes 15392 | tf_op jit(solution)/shard_map/ppermute | solution.py:12
  100.3 0.8 copy-done.7
  (202 shorter events, 11.2 us)
Async XLA Ops:
  0.6 14.2 %copy-start.2 = (bf16[256,2,512]{2,1,0:T(2,128)(2,1)S(1)}, bf16[256,2,512]{2,1,0:T(2,128)(2,1)}, u32[]{:S(2)}) copy-start(bf16[256,2,512]{2,1,0:T(2,128)(2,1)} %param.20) | copy-start | bytes 1572868
  3.3 11.2 %collective-permute-start = (bf16[3,1280]{1,0:T(4,128)(2,1)S(1)}, bf16[3,1280]{1,0:T(4,128)(2,1)S(1)}, u32[]{:S(2)}, u32[]{:S(2)}) collective-permute-start(bf16[3,1280]{1,0:T(4,128)(2,1)S(1)} %pad_maximum_fusion.9), channel_id=1, source_target_pairs={{0,2},{2,4},{4,6},{6,8},{8,10},{10,12},{12,14},{1,3},{3,5},{5,7},{... | collective-permute-start | bytes 23048 | tf_op jit(solution)/shard_map/ppermute | solution.py:12
  9.8 46.8 %copy-start.13 = (f32[256,16]{0,1}, f32[256,16]{0,1:S(1)}, u32[]{:S(2)}) copy-start(f32[256,16]{0,1:S(1)} %fusion.56) | copy-start | bytes 49156
  10.0 34.2 %copy-start.50 = (f32[2,8]{1,0:T(2,128)}, f32[2,8]{1,0:T(2,128)S(1)}, u32[]{:S(2)}) copy-start(f32[2,8]{1,0:T(2,128)S(1)} %get-tuple-element.156) | copy-start | bytes 196
  11.6 6.7 %copy-start.42 = (f32[2,64]{1,0:T(2,128)}, f32[2,64]{1,0:T(2,128)S(1)}, u32[]{:S(2)}) copy-start(f32[2,64]{1,0:T(2,128)S(1)} %get-tuple-element.148) | copy-start | bytes 1540
  11.6 6.7 %copy-start.44 = (f32[2,64]{1,0:T(2,128)}, f32[2,64]{1,0:T(2,128)S(1)}, u32[]{:S(2)}) copy-start(f32[2,64]{1,0:T(2,128)S(1)} %get-tuple-element.149) | copy-start | bytes 1540
  11.6 6.7 %copy-start.46 = (f32[2,64]{1,0:T(2,128)}, f32[2,64]{1,0:T(2,128)S(1)}, u32[]{:S(2)}) copy-start(f32[2,64]{1,0:T(2,128)S(1)} %get-tuple-element.150) | copy-start | bytes 1540
  11.6 6.7 %copy-start.48 = (f32[2,64]{1,0:T(2,128)}, f32[2,64]{1,0:T(2,128)S(1)}, u32[]{:S(2)}) copy-start(f32[2,64]{1,0:T(2,128)S(1)} %get-tuple-element.151) | copy-start | bytes 1540
  12.3 5.9 %copy-start.38 = (f32[2,64]{1,0:T(2,128)}, f32[2,64]{1,0:T(2,128)S(1)}, u32[]{:S(2)}) copy-start(f32[2,64]{1,0:T(2,128)S(1)} %get-tuple-element.144) | copy-start | bytes 1540
  12.3 6.0 %copy-start.39 = (f32[2,64]{1,0:T(2,128)}, f32[2,64]{1,0:T(2,128)S(1)}, u32[]{:S(2)}) copy-start(f32[2,64]{1,0:T(2,128)S(1)} %get-tuple-element.145) | copy-start | bytes 1540
  12.3 6.0 %copy-start.40 = (f32[2,64]{1,0:T(2,128)}, f32[2,64]{1,0:T(2,128)S(1)}, u32[]{:S(2)}) copy-start(f32[2,64]{1,0:T(2,128)S(1)} %get-tuple-element.146) | copy-start | bytes 1540
  12.3 6.0 %copy-start.41 = (f32[2,64]{1,0:T(2,128)}, f32[2,64]{1,0:T(2,128)S(1)}, u32[]{:S(2)}) copy-start(f32[2,64]{1,0:T(2,128)S(1)} %get-tuple-element.147) | copy-start | bytes 1540
  20.2 4.8 %copy-start.60 = (f32[2,8]{1,0:T(2,128)S(1)}, f32[2,8]{1,0:T(2,128)}, u32[]{:S(2)}) copy-start(f32[2,8]{1,0:T(2,128)} %param.26) | copy-start | bytes 196
  32.7 7.2 %copy-start.4 = (bf16[256,2,64]{0,2,1:T(8,128)(2,1)S(1)}, bf16[256,2,64]{0,2,1:T(8,128)(2,1)}, u32[]{:S(2)}) copy-start(bf16[256,2,64]{0,2,1:T(8,128)(2,1)} %copy-done.3) | copy-start | bytes 196612
  34.1 7.9 %collective-permute-start.2 = (bf16[2,8,4224]{2,1,0:T(8,128)(2,1)S(1)}, bf16[2,8,4224]{2,1,0:T(8,128)(2,1)S(1)}, u32[]{:S(2)}, u32[]{:S(2)}) collective-permute-start(bf16[2,8,4224]{2,1,0:T(8,128)(2,1)S(1)} %get-tuple-element.142), channel_id=1, source_target_pairs={{2,0},{4,2},{6,4},{8,6},{10,8},{12,10},{14,12},{3,1},{5,3},{7,5},{... | collective-permute-start | bytes 405512 | tf_op jit(solution)/shard_map/ppermute | solution.py:25
  35.4 8.5 %collective-permute-start.1 = (bf16[2,8,4224]{2,1,0:T(8,128)(2,1)S(1)}, bf16[2,8,4224]{2,1,0:T(8,128)(2,1)S(1)}, u32[]{:S(2)}, u32[]{:S(2)}) collective-permute-start(bf16[2,8,4224]{2,1,0:T(8,128)(2,1)S(1)} %get-tuple-element.143), channel_id=1, source_target_pairs={{0,2},{2,4},{4,6},{6,8},{8,10},{10,12},{12,14},{1,3},{3,5},{5,7},{... | collective-permute-start | bytes 405512 | tf_op jit(solution)/shard_map/ppermute | solution.py:25
  43.9 6.8 %copy-start.22 = (f32[256,2,8]{0,2,1:T(8,128)S(1)}, f32[256,2,8]{0,2,1:T(8,128)}, u32[]{:S(2)}) copy-start(f32[256,2,8]{0,2,1:T(8,128)} %param.23) | copy-start | bytes 49156
  44.0 6.8 %copy-start.54 = (f32[2,8]{1,0:T(2,128)S(1)}, f32[2,8]{1,0:T(2,128)}, u32[]{:S(2)}) copy-start(f32[2,8]{1,0:T(2,128)} %param.25) | copy-start | bytes 196
  44.0 6.8 %copy-start.58 = (f32[2,8]{1,0:T(2,128)S(1)}, f32[2,8]{1,0:T(2,128)}, u32[]{:S(2)}) copy-start(f32[2,8]{1,0:T(2,128)} %copy-done.57) | copy-start | bytes 196
  44.0 6.8 %copy-start.61 = (f32[2,8,256]{2,1,0:T(8,128)S(1)}, f32[2,8,256]{2,1,0:T(8,128)}, u32[]{:S(2)}) copy-start(f32[2,8,256]{2,1,0:T(8,128)} %get-tuple-element.104) | copy-start | bytes 49156
  44.0 6.8 %copy-start.62 = (f32[2,8,256]{2,1,0:T(8,128)S(1)}, f32[2,8,256]{2,1,0:T(8,128)}, u32[]{:S(2)}) copy-start(f32[2,8,256]{2,1,0:T(8,128)} %get-tuple-element.105) | copy-start | bytes 49156
  44.0 6.8 %copy-start.63 = (f32[2,8,256]{2,1,0:T(8,128)S(1)}, f32[2,8,256]{2,1,0:T(8,128)}, u32[]{:S(2)}) copy-start(f32[2,8,256]{2,1,0:T(8,128)} %get-tuple-element.106) | copy-start | bytes 49156
  44.4 12.0 %copy-start.51 = (f32[2,8]{1,0:T(2,128)S(1)}, f32[2,8]{1,0:T(2,128)}, u32[]{:S(2)}) copy-start(f32[2,8]{1,0:T(2,128)} %copy-done.50) | copy-start | bytes 196
  44.5 7.4 %collective-permute-start.3 = (bf16[2,8,4224]{2,1,0:T(8,128)(2,1)S(1)}, bf16[2,8,4224]{2,1,0:T(8,128)(2,1)S(1)}, u32[]{:S(2)}, u32[]{:S(2)}) collective-permute-start(bf16[2,8,4224]{2,1,0:T(8,128)(2,1)S(1)} %pad_maximum_fusion.2), channel_id=1, source_target_pairs={{0,4},{2,6},{4,8},{6,10},{8,12},{10,14},{1,5},{3,7},{5,9},{7,11},{... | collective-permute-start | bytes 405512 | tf_op jit(solution)/shard_map/ppermute | solution.py:25
  49.4 6.9 %collective-permute-start.4 = (bf16[2,8,4224]{2,1,0:T(8,128)(2,1)S(1)}, bf16[2,8,4224]{2,1,0:T(8,128)(2,1)S(1)}, u32[]{:S(2)}, u32[]{:S(2)}) collective-permute-start(bf16[2,8,4224]{2,1,0:T(8,128)(2,1)S(1)} %pad_maximum_fusion.3), channel_id=1, source_target_pairs={{4,0},{6,2},{8,4},{10,6},{12,8},{14,10},{5,1},{7,3},{9,5},{11,7},{... | collective-permute-start | bytes 405512 | tf_op jit(solution)/shard_map/ppermute | solution.py:25
  57.1 9.9 %collective-permute-start.5 = (bf16[2,8,4224]{2,1,0:T(8,128)(2,1)S(1)}, bf16[2,8,4224]{2,1,0:T(8,128)(2,1)}, u32[]{:S(2)}, u32[]{:S(2)}) collective-permute-start(bf16[2,8,4224]{2,1,0:T(8,128)(2,1)S(1)} %pad_maximum_fusion.4), channel_id=1, source_target_pairs={{0,8},{2,10},{4,12},{6,14},{1,9},{3,11},{5,13},{7,15},{16,24},{18,... | collective-permute-start | bytes 405512 | tf_op jit(solution)/shard_map/ppermute | solution.py:25
  63.0 4.0 %copy-start.1 = (f32[2,8,4224]{2,1,0:T(8,128)S(1)}, f32[2,8,4224]{2,1,0:T(8,128)}, u32[]{:S(2)}) copy-start(f32[2,8,4224]{2,1,0:T(8,128)} %copy-done) | copy-start | bytes 811012
  63.0 8.7 %collective-permute-start.6 = (bf16[2,8,4224]{2,1,0:T(8,128)(2,1)}, bf16[2,8,4224]{2,1,0:T(8,128)(2,1)}, u32[]{:S(2)}, u32[]{:S(2)}) collective-permute-start(bf16[2,8,4224]{2,1,0:T(8,128)(2,1)} %pad_maximum_fusion.5), channel_id=1, source_target_pairs={{8,0},{10,2},{12,4},{14,6},{9,1},{11,3},{13,5},{15,7},{24,16},{26,... | collective-permute-start | bytes 405512 | tf_op jit(solution)/shard_map/ppermute | solution.py:25
  80.2 3.1 %copy-start.10 = (f32[256,2,64]{0,2,1:T(8,128)S(1)}, f32[256,2,64]{0,2,1:T(8,128)}, u32[]{:S(2)}) copy-start(f32[256,2,64]{0,2,1:T(8,128)} %get-tuple-element.159) | copy-start | bytes 393220
  80.2 3.1 %copy-start.12 = (f32[256,2,64]{0,2,1:T(8,128)S(1)}, f32[256,2,64]{0,2,1:T(8,128)}, u32[]{:S(2)}) copy-start(f32[256,2,64]{0,2,1:T(8,128)} %convolution_bitcast_fusion.3) | copy-start | bytes 393220
  80.9 2.4 %copy-start.45 = (f32[2,64]{1,0:T(2,128)S(1)}, f32[2,64]{1,0:T(2,128)}, u32[]{:S(2)}) copy-start(f32[2,64]{1,0:T(2,128)} %copy-done.44) | copy-start | bytes 1540
  80.9 2.5 %copy-start.47 = (f32[2,64]{1,0:T(2,128)S(1)}, f32[2,64]{1,0:T(2,128)}, u32[]{:S(2)}) copy-start(f32[2,64]{1,0:T(2,128)} %copy-done.46) | copy-start | bytes 1540
  80.9 2.5 %copy-start.49 = (f32[2,64]{1,0:T(2,128)S(1)}, f32[2,64]{1,0:T(2,128)}, u32[]{:S(2)}) copy-start(f32[2,64]{1,0:T(2,128)} %copy-done.48) | copy-start | bytes 1540
  80.9 3.4 %copy-start.8 = (f32[256,2,64]{0,2,1:T(8,128)S(1)}, f32[256,2,64]{0,2,1:T(8,128)}, u32[]{:S(2)}) copy-start(f32[256,2,64]{0,2,1:T(8,128)} %convolution_bitcast_fusion.4) | copy-start | bytes 393220
  80.9 3.4 %copy-start.9 = (f32[256,2,64]{0,2,1:T(8,128)S(1)}, f32[256,2,64]{0,2,1:T(8,128)}, u32[]{:S(2)}) copy-start(f32[256,2,64]{0,2,1:T(8,128)} %get-tuple-element.120) | copy-start | bytes 393220
  81.0 3.4 %copy-start.11 = (f32[256,2,64]{0,2,1:T(8,128)S(1)}, f32[256,2,64]{0,2,1:T(8,128)}, u32[]{:S(2)}) copy-start(f32[256,2,64]{0,2,1:T(8,128)} %convolution_bitcast_fusion.2) | copy-start | bytes 393220
  88.0 3.0 %copy-start.26 = (f32[2,512]{1,0:T(2,128)S(1)}, f32[2,512]{1,0:T(2,128)}, u32[]{:S(2)}) copy-start(f32[2,512]{1,0:T(2,128)} %copy-done.25) | copy-start | bytes 12292
  88.0 3.0 %copy-start.28 = (f32[2,512]{1,0:T(2,128)S(1)}, f32[2,512]{1,0:T(2,128)}, u32[]{:S(2)}) copy-start(f32[2,512]{1,0:T(2,128)} %copy-done.27) | copy-start | bytes 12292
  88.0 3.1 %copy-start.30 = (f32[2,512]{1,0:T(2,128)S(1)}, f32[2,512]{1,0:T(2,128)}, u32[]{:S(2)}) copy-start(f32[2,512]{1,0:T(2,128)} %copy-done.29) | copy-start | bytes 12292
  88.0 3.1 %copy-start.32 = (f32[2,512]{1,0:T(2,128)S(1)}, f32[2,512]{1,0:T(2,128)}, u32[]{:S(2)}) copy-start(f32[2,512]{1,0:T(2,128)} %copy-done.31) | copy-start | bytes 12292
  91.1 2.7 %copy-start.15 = (f32[256,16]{0,1:S(1)}, f32[256,16]{0,1}, u32[]{:S(2)}) copy-start(f32[256,16]{0,1} %copy-done.13) | copy-start | bytes 49156
  91.1 2.7 %copy-start.33 = (f32[1,2,8]{0,2,1:T(8,128)S(1)}, f32[1,2,8]{0,2,1:T(8,128)}, u32[]{:S(2)}) copy-start(f32[1,2,8]{0,2,1:T(8,128)} %copy.134) | copy-start | bytes 196
  91.1 3.0 %copy-start.19 = (f32[256,2,8]{0,2,1:T(8,128)S(1)}, f32[256,2,8]{0,2,1:T(8,128)}, u32[]{:S(2)}) copy-start(f32[256,2,8]{0,2,1:T(8,128)} %get-tuple-element.127) | copy-start | bytes 49156
  91.2 3.0 %copy-start.24 = (f32[256,2,8]{0,2,1:T(8,128)S(1)}, f32[256,2,8]{0,2,1:T(8,128)}, u32[]{:S(2)}) copy-start(f32[256,2,8]{0,2,1:T(8,128)} %param.23) | copy-start | bytes 49156
  91.2 3.0 %copy-start.36 = (f32[2,8]{1,0:T(2,128)S(1)}, f32[2,8]{1,0:T(2,128)}, u32[]{:S(2)}) copy-start(f32[2,8]{1,0:T(2,128)} %copy-done.34) | copy-start | bytes 196
  91.2 3.0 %copy-start.56 = (f32[2,8]{1,0:T(2,128)S(1)}, f32[2,8]{1,0:T(2,128)}, u32[]{:S(2)}) copy-start(f32[2,8]{1,0:T(2,128)} %param.25) | copy-start | bytes 196
  91.2 3.0 %copy-start.59 = (f32[2,8]{1,0:T(2,128)S(1)}, f32[2,8]{1,0:T(2,128)}, u32[]{:S(2)}) copy-start(f32[2,8]{1,0:T(2,128)} %copy-done.57) | copy-start | bytes 196
  92.6 5.7 %collective-permute-start.7 = (f32[3,1280]{1,0:T(4,128)S(1)}, f32[3,1280]{1,0:T(4,128)S(1)}, u32[]{:S(2)}, u32[]{:S(2)}) collective-permute-start(f32[3,1280]{1,0:T(4,128)S(1)} %pad_maximum_fusion.8), channel_id=1, source_target_pairs={{2,0},{4,2},{6,4},{8,6},{10,8},{12,10},{14,12},{3,1},{5,3},{7,5},{... | collective-permute-start | bytes 46088 | tf_op jit(solution)/shard_map/ppermute | solution.py:12
  (24 other events, 36.2 us)

commit v5 on v4

--- a/solution.py
+++ b/solution.py
@@ -17,11 +17,13 @@
     groups, heads, rows, cols = forward_state.shape
     lanes = 128
 
-    def shift(decay_part, state_part, by, sign):
-        pairs = [(i, i + sign * by) for i in range(count) if 0 <= i + sign * by < count]
-        packed = jnp.concatenate(
+    def pack(decay_part, state_part):
+        return jnp.concatenate(
             [state_part, jnp.broadcast_to(decay_part[:, :, None], (groups, heads, lanes))], 2
         ).astype(jnp.bfloat16)
+
+    def shift(packed, by, sign):
+        pairs = [(i, i + sign * by) for i in range(count) if 0 <= i + sign * by < count]
         return lax.ppermute(packed, axis, pairs)
 
     def unpack(got):
@@ -41,13 +43,19 @@
     windows = [
         (jnp.ones_like(decay), jnp.zeros_like(flat), decay, flat) for flat in flats
     ]
-    tied = list(riders)
+    tied = []
     by = 1
     step = 0
     while by < count:
-        got = [shift(w[2], w[3], by, sign) for w, sign in zip(windows, (1, -1))]
-        if step < len(tied):
-            got, tied[step] = lax.optimization_barrier((got, tied[step]))
+        sent = [pack(w[2], w[3]) for w in windows]
+        if step < len(riders):
+            work, arguments = riders[step]
+            sent, arguments = lax.optimization_barrier((sent, arguments))
+        got = [shift(s, by, sign) for s, sign in zip(sent, (1, -1))]
+        if step < len(riders):
+            done = work(*arguments)
+            got, done = lax.optimization_barrier((got, done))
+            tied.append(done)
         windows = [fold(w, *unpack(g)) for w, g in zip(windows, got)]
         by *= 2
         step += 1
@@ -167,17 +175,15 @@
         return ssd_state(x_arg, b_arg, dt_arg, rate, dt_bias)
 
     (cum_log, state_end), state_pull = jax.vjp(state_map, x_float, b_float, dt_in)
-    y_local, mix_pull = jax.vjp(mix_map, x_float, b_float, c_float, dt_in)
     decay_total = jnp.exp(cum_log[-1])
     grad_heads = grad_y.astype(jnp.float32).reshape(length, groups, head_count, head_size)
     seed_state = jnp.einsum(
         "tghp,tgn->ghpn", jnp.exp(cum_log)[..., None] * grad_heads, c_float, precision=HIGH
     )
+
+    y_local, mix_pull = jax.vjp(mix_map, x_float, b_float, c_float, dt_in)
     mix_x, mix_b, mix_c, mix_dt = mix_pull(grad_heads)
-    state_in, adjoint, riders = scanned_pair(
-        decay_total, state_end, seed_state, "ctx", [y_local, mix_x, (mix_b, mix_c, mix_dt)]
-    )
-    y_local, mix_x, (mix_b, mix_c, mix_dt) = riders
+    state_in, adjoint, _ = scanned_pair(decay_total, state_end, seed_state, "ctx", [])
 
     def carry_map(c_arg, cum_arg):
         return carry_in(c_arg, cum_arg, state_in)

time: 102 us -> 96.4 us (0.945)
  waiting for transfers between devices: 12.8 us -> 20.8 us
  local copies, waits for them, and re-layouts: 23.2 us -> 16.8 us
  other arithmetic: 16.8 us -> 13.4 us
  starting transfers between devices: 24.9 us -> 22.4 us
  matrix products: 21.7 us -> 20.4 us
    ppermute x6, waiting for transfers between devices: 11.3 us -> 19.5 us  [shift(): return lax.ppermute(packed, axis, pairs)]
    ppermute x6, starting transfers between devices: 18.7 us -> 16.3 us  [shift(): return lax.ppermute(packed, axis, pairs)]
    reshape x1 -> x0, local copies, waits for them, and re-layouts: 2.32 us -> none  [ssd_state(): x_heads = x_float.reshape(length, groups, head_count, head_size)]
    dot_general x3, matrix products: 4.81 us -> 2.52 us  [ssd_state(): jnp.einsum('sghp,sgn->ghpn', weighted.astype(jnp.float32), b_float, preci...]
    optimization_barrier x1 -> x0, local copies, waits for them, and re-layouts: 2.26 us -> none  [scanned_pair(): got, tied[step] = lax.optimization_barrier((got, tied[step]))]
    mul x3 -> x1, other arithmetic: 3.15 us -> 1.51 us  [conv_backward(): grad_out.astype(jnp.float32)]
    convert_element_type x0 -> x1, local copies, waits for them, and re-layouts: none -> 1.54 us  [conv_backward(): grad_out.astype(jnp.float32)]
    reduce_sum x1, other arithmetic: 1.93 us -> 0.82 us  [on_device(): end_term = jnp.sum(adjoint * state_in, axis=(2, 3)) * decay_total]
  transfers between devices with their start and end apart: 8 -> 8, of which waited for: 5 -> 7; matrix products, arithmetic and copies ran while one was open for 15% -> 12% of each run, Pallas kernels for 0% -> 0%
where the time goes in v5:
time: 96.4 us; the launch traced here: 95.6 us
  starting transfers between devices  22.4 us (23%)
  waiting for transfers between devices  20.8 us (22%)
  matrix products  20.4 us (21%)
  local copies, waits for them, and re-layouts  16.8 us (17%)
  other arithmetic  13.4 us (14%)
  between operations  1.79 us (2%)
    ppermute x6, waiting for transfers between devices, shift(): return lax.ppermute(packed, axis, pairs)  19.5 us
    ppermute x6, starting transfers between devices, shift(): return lax.ppermute(packed, axis, pairs)  16.3 us
    dot_general x3, matrix products, ssd_mix(): jnp.einsum('ghts,sghp->tghp', mixing, x_half, preferred_element_type=jnp....  10.8 us
    ppermute x2, starting transfers between devices, from_behind(): return lax.ppermute(array, axis, pairs)  6.14 us
    unnamed x129, local copies, waits for them, and re-layouts  5.13 us
    dot_general x2, matrix products, carry_in(): carried = jnp.einsum('tgn,ghpn->tghp', c_float, state_in, precision=HIGH)  2.66 us
    dot_general x3, matrix products, ssd_state(): jnp.einsum('sghp,sgn->ghpn', weighted.astype(jnp.float32), b_float, preci...  2.52 us
    convert_element_type x1, other arithmetic, on_device(): x_float = jax.nn.silu(x_running).astype(jnp.bfloat16).astype(jnp.float32)  2.42 us
  transfers between devices with their start and end apart: 8, of which 7 were waited for; matrix products, arithmetic and copies ran while one was open for 12% of the time, Pallas kernels for 0%

profile of v5, /device:TPU:0, one launch (start us, length us, event | category | flops | bytes accessed | tf_op | source)
XLA Modules:
  0.0 95.6 jit_solution(10338459830410624071)
XLA Ops:
  0.7 0.7 slice_bitcast_fusion.1
  1.4 0.8 slice.295
  2.3 0.9 slice.296
  3.3 4.8 %collective-permute-start = (bf16[3,1280]{1,0:T(4,128)(2,1)S(1)}, bf16[3,1280]{1,0:T(4,128)(2,1)S(1)}, u32[]{:S(2)}, u32[]{:S(2)}) collective-permute-start(bf16[3,1280]{1,0:T(4,128)(2,1)S(1)} %pad_maximum_fusion.9), channel_id=1, source_target_pairs={{0,2},{2,4},{4,6},{6,8},{8,10},{10,12},{12,14},{1,3},{3,5},{5,7},{... | collective-permute-start | bytes 23048 | tf_op jit(solution)/shard_map/ppermute | solution.py:12
  8.1 0.7 neg.30
  8.8 0.7 slice_bitcast_fusion.9
  9.6 0.7 slice_bitcast_fusion.13
  10.3 0.9 fusion.76
  11.5 0.7 slice_bitcast_fusion.5
  12.3 0.8 fusion.113
  13.1 0.6 fusion.130
  13.7 1.3 %copy.120 = bf16[256,2,512]{0,2,1:T(8,128)(2,1)S(1)} copy(bf16[256,2,512]{2,1,0:T(2,128)(2,1)} %param.30) | data formatting | bytes 1048576 | tf_op args[10]
  15.3 1.1 %multiply_convert_fusion.1 = (bf16[256,2,64]{0,2,1:T(8,128)(2,1)S(1)}, f32[256,2,64]{0,2,1:T(8,128)}, bf16[256,2,64]{0,2,1:T(8,128)(2,1)S(1)}, f32[256,2,64]{0,2,1:T(8,128)}) fusion(bf16[256,2,64]{0,2,1:T(8,128)(2,1)S(1)} %copy-done.11, f32[2,64]{1,0:T(2,128)S(1)} %get-tuple-element.120, bf16[3,2,64]{0,2,1:T(8,128)(2,1)S(1)} %bitcast.222, ...), kind=kLoop, calls=%fused_computation.113 | loop fusion | flops 1638400 | bytes 529920 | tf_op jit(solution)/shard_map/convert_element_type | solution.py:168
  16.4 0.6 fusion.52
  17.8 2.4 %multiply_convert_fusion = (bf16[256,2,512]{2,1,0:T(2,128)(2,1)S(1)}, f32[256,2,512]{2,1,0:T(2,128)S(1)}) fusion(bf16[256,2,512]{2,1,0:T(2,128)(2,1)S(1)} %copy-done, f32[2,512]{1,0:T(2,128)S(1)} %get-tuple-element.112, bf16[259,2,512]{2,1,0:T(2,128)(2,1)S(1)} %constant_dynamic-update-slice_fusion, f32[2,512]{1,0:T(2,128)S(1)} %get-tuple-element.113, ...), kind=kLoop, calls=%fused_computation.69 | loop fusion | flops 4194304 | bytes 3686400 | tf_op jit(solution)/shard_map/convert_element_type | solution.py:167
  21.6 3.5 %collective-permute-start.1 = (bf16[2,8,4224]{2,1,0:T(8,128)(2,1)S(1)}, bf16[2,8,4224]{2,1,0:T(8,128)(2,1)S(1)}, u32[]{:S(2)}, u32[]{:S(2)}) collective-permute-start(bf16[2,8,4224]{2,1,0:T(8,128)(2,1)S(1)} %get-tuple-element.116), channel_id=1, source_target_pairs={{0,2},{2,4},{4,6},{6,8},{8,10},{10,12},{12,14},{1,3},{3,5},{5,7},{... | collective-permute-start | bytes 405512 | tf_op jit(solution)/shard_map/ppermute | solution.py:27
  25.0 1.3 %collective-permute-start.4 = (bf16[2,8,4224]{2,1,0:T(8,128)(2,1)S(1)}, bf16[2,8,4224]{2,1,0:T(8,128)(2,1)S(1)}, u32[]{:S(2)}, u32[]{:S(2)}) collective-permute-start(bf16[2,8,4224]{2,1,0:T(8,128)(2,1)S(1)} %get-tuple-element.117), channel_id=1, source_target_pairs={{2,0},{4,2},{6,4},{8,6},{10,8},{12,10},{14,12},{3,1},{5,3},{7,5},{... | collective-permute-start | bytes 405512 | tf_op jit(solution)/shard_map/ppermute | solution.py:27
  26.3 1.2 %collective-permute-done.1 = bf16[2,8,4224]{2,1,0:T(8,128)(2,1)S(1)} collective-permute-done((bf16[2,8,4224]{2,1,0:T(8,128)(2,1)S(1)}, bf16[2,8,4224]{2,1,0:T(8,128)(2,1)S(1)}, u32[]{:S(2)}, u32[]{:S(2)}) %collective-permute-start.1) | collective-permute-done | bytes 135200 | tf_op jit(solution)/shard_map/ppermute | solution.py:27
  27.7 4.2 %collective-permute-done.4 = bf16[2,8,4224]{2,1,0:T(8,128)(2,1)S(1)} collective-permute-done((bf16[2,8,4224]{2,1,0:T(8,128)(2,1)S(1)}, bf16[2,8,4224]{2,1,0:T(8,128)(2,1)S(1)}, u32[]{:S(2)}, u32[]{:S(2)}) %collective-permute-start.4) | collective-permute-done | bytes 135200 | tf_op jit(solution)/shard_map/ppermute | solution.py:27
  32.2 3.9 %collective-permute-start.2 = (bf16[2,8,4224]{2,1,0:T(8,128)(2,1)S(1)}, bf16[2,8,4224]{2,1,0:T(8,128)(2,1)S(1)}, u32[]{:S(2)}, u32[]{:S(2)}) collective-permute-start(bf16[2,8,4224]{2,1,0:T(8,128)(2,1)S(1)} %pad_maximum_fusion.2), channel_id=1, source_target_pairs={{0,4},{2,6},{4,8},{6,10},{8,12},{10,14},{1,5},{3,7},{5,9},{7,11},{... | collective-permute-start | bytes 405512 | tf_op jit(solution)/shard_map/ppermute | solution.py:27
  36.2 2.5 %collective-permute-done.2 = bf16[2,8,4224]{2,1,0:T(8,128)(2,1)S(1)} collective-permute-done((bf16[2,8,4224]{2,1,0:T(8,128)(2,1)S(1)}, bf16[2,8,4224]{2,1,0:T(8,128)(2,1)S(1)}, u32[]{:S(2)}, u32[]{:S(2)}) %collective-permute-start.2) | collective-permute-done | bytes 135200 | tf_op jit(solution)/shard_map/ppermute | solution.py:27
  38.9 1.3 %collective-permute-start.5 = (bf16[2,8,4224]{2,1,0:T(8,128)(2,1)S(1)}, bf16[2,8,4224]{2,1,0:T(8,128)(2,1)S(1)}, u32[]{:S(2)}, u32[]{:S(2)}) collective-permute-start(bf16[2,8,4224]{2,1,0:T(8,128)(2,1)S(1)} %pad_maximum_fusion.4), channel_id=1, source_target_pairs={{4,0},{6,2},{8,4},{10,6},{12,8},{14,10},{5,1},{7,3},{9,5},{11,7},{... | collective-permute-start | bytes 405512 | tf_op jit(solution)/shard_map/ppermute | solution.py:27
  40.2 1.1 %fusion.131 = f32[2,256,256]{2,1,0:T(8,128)} fusion(bf16[256,2,64]{0,2,1:T(8,128)(2,1)S(1)} %get-tuple-element.134, bf16[256,2,64]{0,2,1:T(8,128)(2,1)S(1)} %get-tuple-element.97), kind=kOutput, calls=%fused_computation.208 | convolution fusion | flops 16777216 | bytes 655360 | tf_op jit(solution)/shard_map/jvp(tgn,sgn->gts)/dot_general | solution.py:116
  41.3 5.0 %collective-permute-done.5 = bf16[2,8,4224]{2,1,0:T(8,128)(2,1)S(1)} collective-permute-done((bf16[2,8,4224]{2,1,0:T(8,128)(2,1)S(1)}, bf16[2,8,4224]{2,1,0:T(8,128)(2,1)S(1)}, u32[]{:S(2)}, u32[]{:S(2)}) %collective-permute-start.5) | collective-permute-done | bytes 135200 | tf_op jit(solution)/shard_map/ppermute | solution.py:27
  46.7 4.9 %collective-permute-start.3 = (bf16[2,8,4224]{2,1,0:T(8,128)(2,1)S(1)}, bf16[2,8,4224]{2,1,0:T(8,128)(2,1)S(1)}, u32[]{:S(2)}, u32[]{:S(2)}) collective-permute-start(bf16[2,8,4224]{2,1,0:T(8,128)(2,1)S(1)} %pad_maximum_fusion.3), channel_id=1, source_target_pairs={{0,8},{2,10},{4,12},{6,14},{1,9},{3,11},{5,13},{7,15},{16,24},{18,... | collective-permute-start | bytes 405512 | tf_op jit(solution)/shard_map/ppermute | solution.py:27
  51.7 1.5 %collective-permute-start.6 = (bf16[2,8,4224]{2,1,0:T(8,128)(2,1)S(1)}, bf16[2,8,4224]{2,1,0:T(8,128)(2,1)S(1)}, u32[]{:S(2)}, u32[]{:S(2)}) collective-permute-start(bf16[2,8,4224]{2,1,0:T(8,128)(2,1)S(1)} %pad_maximum_fusion.5), channel_id=1, source_target_pairs={{8,0},{10,2},{12,4},{14,6},{9,1},{11,3},{13,5},{15,7},{24,16},{26,... | collective-permute-start | bytes 405512 | tf_op jit(solution)/shard_map/ppermute | solution.py:27
  53.4 0.8 collective-permute-done.3
  54.1 5.8 %collective-permute-done.6 = bf16[2,8,4224]{2,1,0:T(8,128)(2,1)S(1)} collective-permute-done((bf16[2,8,4224]{2,1,0:T(8,128)(2,1)S(1)}, bf16[2,8,4224]{2,1,0:T(8,128)(2,1)S(1)}, u32[]{:S(2)}, u32[]{:S(2)}) %collective-permute-start.6) | collective-permute-done | bytes 135200 | tf_op jit(solution)/shard_map/ppermute | solution.py:27
  60.0 0.8 multiply_reduce_fusion
  61.0 1.1 %convolution_bitcast_fusion.3 = f32[2,256,64]{1,2,0:T(8,128)S(1)} fusion(f32[2,8,64,64]{3,2,1,0:T(8,128)S(1)} %reshape.254, bf16[256,2,8,64]{0,3,2,1:T(8,128)(2,1)S(1)} %bitcast.202, f32[256,2,8]{0,2,1:T(8,128)S(1)} %get-tuple-element.109), kind=kOutput, calls=%fused_computation.48 | convolution fusion | flops 201850880 | bytes 933888 | tf_op jit(solution)/shard_map/transpose(jvp(tgn,ghpn->tghp))/dot_general | solution.py:135
  62.1 1.6 %fusion.70 = (f32[256,2,8]{0,2,1:T(8,128)S(1)}, f32[256,2,8,64]{0,3,2,1:T(8,128)}) fusion(bf16[256,2,512]{0,2,1:T(8,128)(2,1)S(1)} %copy.120, f32[2,8,64,64]{3,2,1,0:T(8,128)S(1)} %reshape.254, bf16[256,2,64]{0,2,1:T(8,128)(2,1)S(1)} %get-tuple-element.134), kind=kOutput, calls=%fused_computation.67 | convolution fusion | flops 202108928 | bytes 1916928 | tf_op jit(solution)/shard_map/jvp(tgn,ghpn->tghp)/dot_general | solution.py:135
  63.9 0.6 convolution_bitcast_fusion.1
  64.6 1.6 %fusion.69 = (f32[256,2,8]{0,2,1:T(8,128)S(1)}, f32[256,2,8,64]{0,3,2,1:T(8,128)}) fusion(bf16[256,2,512]{0,2,1:T(8,128)(2,1)S(1)} %copy.116, f32[2,8,64,64]{3,2,1,0:T(8,128)S(1)} %reshape.258, bf16[256,2,64]{0,2,1:T(8,128)(2,1)S(1)} %get-tuple-element.97), kind=kOutput, calls=%fused_computation.66 | convolution fusion | flops 202633216 | bytes 1916928 | tf_op jit(solution)/shard_map/transpose(jvp(sghp,sgn->ghpn))/dot_general | solution.py:130
  66.2 0.7 copy.129
  66.9 1.3 %fusion.114 = (f32[2,8]{1,0:T(2,128)}, f32[2,8,256]{2,1,0:T(8,128)S(1)}, f32[256,2,8]{0,2,1:T(8,128)}) fusion(f32[256,2,8]{0,2,1:T(8,128)S(1)} %get-tuple-element.130, f32[2,8]{1,0:T(2,128)S(1)} %copy-done.31, f32[256,16]{0,1:S(1)} %fusion.76, f32[256,2,8]{0,2,1:T(8,128)S(1)} %copy-done.17, f32[2,8]{1,0:T(2,128)S(1)} %copy-done.50, ...), kind=kLoop, calls=%fused_computation.160 | loop fusion | flops 49136 | bytes 98496 | tf_op jit(solution)/shard_map/transpose(jvp())/reduce_sum | solution.py:128
  68.2 5.9 %fusion.18 = (f32[2,8,256]{2,1,0:T(8,128)}, f32[2,8,256]{2,1,0:T(8,128)}, f32[2,8,256]{2,1,0:T(8,128)}, f32[2,256,256]{2,1,0:T(8,128)S(1)}) fusion(f32[2,8,256]{2,1,0:T(8,128)S(1)} %bitcast.218, f32[2,8,256]{2,1,0:T(8,128)S(1)} %get-tuple-element.106, f32[2,256,256]{2,1,0:T(8,128)} %fusion.131, pred[256,256]{1,0:T(8,128)(4,1)S(1)} %iota_compare_fusion, ...), kind=kOutput, calls=%fused_computation.27 | convolution fusion | flops 156094464 | bytes 2244608 | tf_op jit(solution)/shard_map/transpose(jvp(ghts,sghp->tghp))/dot_general | solution.py:118
  74.1 2.3 %fusion.48 = bf16[256,2,8,64]{0,3,2,1:T(8,128)(2,1)} fusion(bf16[2,8,64,256]{3,2,1,0:T(8,128)(2,1)S(1)} %bitcast.205, f32[2,8,256]{2,1,0:T(8,128)S(1)} %get-tuple-element.106, f32[2,8,256]{2,1,0:T(8,128)S(1)} %bitcast.219, f32[2,256,256]{2,1,0:T(8,128)S(1)} %copy-done.4, pred[256,256]{1,0:T(8,128)(4,1)S(1)} %iota_compare_fusion, ...), kind=kOutput, calls=%fused_computation.41 | convolution fusion | flops 142606336 | bytes 3260480 | tf_op jit(solution)/shard_map/transpose(jvp(ghts,sghp->tghp))/dot_general | solution.py:118
  76.5 2.6 %fusion.30 = bf16[256,2,8,64]{0,3,2,1:T(8,128)(2,1)S(1)} fusion(bf16[256,2,8,64]{0,3,2,1:T(8,128)(2,1)S(1)} %bitcast.209, f32[2,8,256]{2,1,0:T(8,128)S(1)} %get-tuple-element.106, f32[2,8,256]{2,1,0:T(8,128)S(1)} %bitcast.220, f32[2,256,256]{2,1,0:T(8,128)S(1)} %copy-done.4, pred[256,256]{1,0:T(8,128)(4,1)} %copy-done.14, ...), kind=kOutput, calls=%fused_computation.35 | convolution fusion | flops 142082048 | bytes 2736192 | tf_op jit(solution)/shard_map/jvp(ghts,sghp->tghp)/dot_general | solution.py:118
  79.1 0.7 copy.130
  81.4 1.1 %bitcast_convert_fusion = f32[256,2,512]{0,2,1:T(8,128)} fusion(bf16[256,2,8,64]{0,3,2,1:T(8,128)(2,1)S(1)} %copy-done.3), kind=kLoop, calls=%fused_computation.72 | loop fusion | flops 262144 | bytes 1572864 | tf_op jit(solution)/shard_map/convert_element_type | solution.py:79
  82.5 1.5 %copy.122 = f32[256,2,512]{2,1,0:T(2,128)S(1)} copy(f32[256,2,512]{0,2,1:T(8,128)} %bitcast_convert_fusion) | data formatting | bytes 2097152 | tf_op jit(solution)/shard_map/convert_element_type | solution.py:79
  84.1 1.5 %multiply_multiply_fusion = f32[256,2,512]{2,1,0:T(2,128)S(1)} fusion(f32[256,2,512]{2,1,0:T(2,128)S(1)} %copy.122, f32[256,2,512]{2,1,0:T(2,128)S(1)} %get-tuple-element.102), kind=kLoop, calls=%fused_computation.68 | loop fusion | flops 2097152 | bytes 3145728 | tf_op jit(solution)/shard_map/mul | solution.py:79
  85.7 1.3 %multiply_add_fusion = f32[259,2,512]{2,1,0:T(2,128)S(1)} fusion(f32[256,2,512]{2,1,0:T(2,128)S(1)} %multiply_multiply_fusion, f32[2,512]{1,0:T(2,128)S(1)} %copy-done.24, f32[2,512]{1,0:T(2,128)S(1)} %copy-done.26, f32[2,512]{1,0:T(2,128)S(1)} %copy-done.22, f32[2,512]{1,0:T(2,128)S(1)} %copy-done.20), kind=kLoop, calls=%fused_computation.64 | loop fusion | flops 1856512 | bytes 2125824 | tf_op jit(solution)/shard_map/add | solution.py:87
  87.1 1.3 %collective-permute-start.7 = (f32[3,1280]{1,0:T(4,128)S(1)}, f32[3,1280]{1,0:T(4,128)S(1)}, u32[]{:S(2)}, u32[]{:S(2)}) collective-permute-start(f32[3,1280]{1,0:T(4,128)S(1)} %pad_maximum_fusion.8), channel_id=1, source_target_pairs={{2,0},{4,2},{6,4},{8,6},{10,8},{12,10},{14,12},{3,1},{5,3},{7,5},{... | collective-permute-start | bytes 46088 | tf_op jit(solution)/shard_map/ppermute | solution.py:12
  88.9 0.9 fusion.64
  90.3 1.2 %copy.131 = bf16[256,2,512]{2,1,0:T(2,128)(2,1)} copy(bf16[256,2,512]{0,2,1:T(8,128)(2,1)S(1)} %bitcast.210) | data formatting | bytes 1048576
  91.5 1.3 %collective-permute-done.7 = f32[3,1280]{1,0:T(4,128)S(1)} collective-permute-done((f32[3,1280]{1,0:T(4,128)S(1)}, f32[3,1280]{1,0:T(4,128)S(1)}, u32[]{:S(2)}, u32[]{:S(2)}) %collective-permute-start.7) | collective-permute-done | bytes 15392 | tf_op jit(solution)/shard_map/ppermute | solution.py:12
  94.8 0.8 copy-done.5
  (193 shorter events, 9.0 us)
Async XLA Ops:
  0.6 14.7 %copy-start.11 = (bf16[256,2,64]{0,2,1:T(8,128)(2,1)S(1)}, bf16[256,2,64]{0,2,1:T(8,128)(2,1)}, u32[]{:S(2)}) copy-start(bf16[256,2,64]{0,2,1:T(8,128)(2,1)} %param.21) | copy-start | bytes 196612
  0.6 14.6 %copy-start.10 = (bf16[256,2,64]{0,2,1:T(8,128)(2,1)S(1)}, bf16[256,2,64]{0,2,1:T(8,128)(2,1)}, u32[]{:S(2)}) copy-start(bf16[256,2,64]{0,2,1:T(8,128)(2,1)} %param.22) | copy-start | bytes 196612
  3.3 11.7 %collective-permute-start = (bf16[3,1280]{1,0:T(4,128)(2,1)S(1)}, bf16[3,1280]{1,0:T(4,128)(2,1)S(1)}, u32[]{:S(2)}, u32[]{:S(2)}) collective-permute-start(bf16[3,1280]{1,0:T(4,128)(2,1)S(1)} %pad_maximum_fusion.9), channel_id=1, source_target_pairs={{0,2},{2,4},{4,6},{6,8},{8,10},{10,12},{12,14},{1,3},{3,5},{5,7},{... | collective-permute-start | bytes 23048 | tf_op jit(solution)/shard_map/ppermute | solution.py:12
  8.8 2.4 %copy-start.55 = (f32[2,8]{1,0:T(2,128)}, f32[2,8]{1,0:T(2,128)S(1)}, u32[]{:S(2)}) copy-start(f32[2,8]{1,0:T(2,128)S(1)} %neg.30) | copy-start | bytes 196
  9.6 7.5 %copy-start.41 = (f32[2,64]{1,0:T(2,128)}, f32[2,64]{1,0:T(2,128)S(1)}, u32[]{:S(2)}) copy-start(f32[2,64]{1,0:T(2,128)S(1)} %get-tuple-element.118) | copy-start | bytes 1540
  9.6 7.5 %copy-start.43 = (f32[2,64]{1,0:T(2,128)}, f32[2,64]{1,0:T(2,128)S(1)}, u32[]{:S(2)}) copy-start(f32[2,64]{1,0:T(2,128)S(1)} %get-tuple-element.119) | copy-start | bytes 1540
  9.6 7.5 %copy-start.45 = (f32[2,64]{1,0:T(2,128)}, f32[2,64]{1,0:T(2,128)S(1)}, u32[]{:S(2)}) copy-start(f32[2,64]{1,0:T(2,128)S(1)} %get-tuple-element.120) | copy-start | bytes 1540
  9.6 7.5 %copy-start.47 = (f32[2,64]{1,0:T(2,128)}, f32[2,64]{1,0:T(2,128)S(1)}, u32[]{:S(2)}) copy-start(f32[2,64]{1,0:T(2,128)S(1)} %get-tuple-element.121) | copy-start | bytes 1540
  10.3 6.8 %copy-start.33 = (f32[2,64]{1,0:T(2,128)}, f32[2,64]{1,0:T(2,128)S(1)}, u32[]{:S(2)}) copy-start(f32[2,64]{1,0:T(2,128)S(1)} %get-tuple-element.122) | copy-start | bytes 1540
  10.3 6.8 %copy-start.35 = (f32[2,64]{1,0:T(2,128)}, f32[2,64]{1,0:T(2,128)S(1)}, u32[]{:S(2)}) copy-start(f32[2,64]{1,0:T(2,128)S(1)} %get-tuple-element.123) | copy-start | bytes 1540
  10.3 6.8 %copy-start.37 = (f32[2,64]{1,0:T(2,128)}, f32[2,64]{1,0:T(2,128)S(1)}, u32[]{:S(2)}) copy-start(f32[2,64]{1,0:T(2,128)S(1)} %get-tuple-element.124) | copy-start | bytes 1540
  10.3 6.8 %copy-start.39 = (f32[2,64]{1,0:T(2,128)}, f32[2,64]{1,0:T(2,128)S(1)}, u32[]{:S(2)}) copy-start(f32[2,64]{1,0:T(2,128)S(1)} %get-tuple-element.125) | copy-start | bytes 1540
  11.5 3.5 %copy-start.30 = (f32[2,8]{1,0:T(2,128)}, f32[2,8]{1,0:T(2,128)S(1)}, u32[]{:S(2)}) copy-start(f32[2,8]{1,0:T(2,128)S(1)} %slice_reduce_fusion) | copy-start | bytes 196
  12.2 5.6 %copy-start.19 = (f32[2,512]{1,0:T(2,128)}, f32[2,512]{1,0:T(2,128)S(1)}, u32[]{:S(2)}) copy-start(f32[2,512]{1,0:T(2,128)S(1)} %get-tuple-element.110) | copy-start | bytes 12292
  12.2 5.6 %copy-start.21 = (f32[2,512]{1,0:T(2,128)}, f32[2,512]{1,0:T(2,128)S(1)}, u32[]{:S(2)}) copy-start(f32[2,512]{1,0:T(2,128)S(1)} %get-tuple-element.111) | copy-start | bytes 12292
  12.2 5.6 %copy-start.23 = (f32[2,512]{1,0:T(2,128)}, f32[2,512]{1,0:T(2,128)S(1)}, u32[]{:S(2)}) copy-start(f32[2,512]{1,0:T(2,128)S(1)} %get-tuple-element.112) | copy-start | bytes 12292
  12.2 5.6 %copy-start.25 = (f32[2,512]{1,0:T(2,128)}, f32[2,512]{1,0:T(2,128)S(1)}, u32[]{:S(2)}) copy-start(f32[2,512]{1,0:T(2,128)S(1)} %get-tuple-element.113) | copy-start | bytes 12292
  13.1 47.9 %copy-start.8 = (f32[256,2,8]{0,2,1:T(8,128)}, f32[256,2,8]{0,2,1:T(8,128)S(1)}, u32[]{:S(2)}) copy-start(f32[256,2,8]{0,2,1:T(8,128)S(1)} %get-tuple-element.109) | copy-start | bytes 49156
  21.1 6.5 %copy-start.29 = (f32[2,8]{1,0:T(2,128)S(1)}, f32[2,8]{1,0:T(2,128)}, u32[]{:S(2)}) copy-start(f32[2,8]{1,0:T(2,128)} %get-tuple-element.128) | copy-start | bytes 196
  21.6 6.0 %collective-permute-start.1 = (bf16[2,8,4224]{2,1,0:T(8,128)(2,1)S(1)}, bf16[2,8,4224]{2,1,0:T(8,128)(2,1)S(1)}, u32[]{:S(2)}, u32[]{:S(2)}) collective-permute-start(bf16[2,8,4224]{2,1,0:T(8,128)(2,1)S(1)} %get-tuple-element.116), channel_id=1, source_target_pairs={{0,2},{2,4},{4,6},{6,8},{8,10},{10,12},{12,14},{1,3},{3,5},{5,7},{... | collective-permute-start | bytes 405512 | tf_op jit(solution)/shard_map/ppermute | solution.py:27
  25.0 6.9 %collective-permute-start.4 = (bf16[2,8,4224]{2,1,0:T(8,128)(2,1)S(1)}, bf16[2,8,4224]{2,1,0:T(8,128)(2,1)S(1)}, u32[]{:S(2)}, u32[]{:S(2)}) collective-permute-start(bf16[2,8,4224]{2,1,0:T(8,128)(2,1)S(1)} %get-tuple-element.117), channel_id=1, source_target_pairs={{2,0},{4,2},{6,4},{8,6},{10,8},{12,10},{14,12},{3,1},{5,3},{7,5},{... | collective-permute-start | bytes 405512 | tf_op jit(solution)/shard_map/ppermute | solution.py:27
  32.2 6.4 %collective-permute-start.2 = (bf16[2,8,4224]{2,1,0:T(8,128)(2,1)S(1)}, bf16[2,8,4224]{2,1,0:T(8,128)(2,1)S(1)}, u32[]{:S(2)}, u32[]{:S(2)}) collective-permute-start(bf16[2,8,4224]{2,1,0:T(8,128)(2,1)S(1)} %pad_maximum_fusion.2), channel_id=1, source_target_pairs={{0,4},{2,6},{4,8},{6,10},{8,12},{10,14},{1,5},{3,7},{5,9},{7,11},{... | collective-permute-start | bytes 405512 | tf_op jit(solution)/shard_map/ppermute | solution.py:27
  36.1 37.9 %copy-start.14 = (pred[256,256]{1,0:T(8,128)(4,1)}, pred[256,256]{1,0:T(8,128)(4,1)S(1)}, u32[]{:S(2)}) copy-start(pred[256,256]{1,0:T(8,128)(4,1)S(1)} %iota_compare_fusion) | copy-start | bytes 196612
  38.9 7.3 %collective-permute-start.5 = (bf16[2,8,4224]{2,1,0:T(8,128)(2,1)S(1)}, bf16[2,8,4224]{2,1,0:T(8,128)(2,1)S(1)}, u32[]{:S(2)}, u32[]{:S(2)}) collective-permute-start(bf16[2,8,4224]{2,1,0:T(8,128)(2,1)S(1)} %pad_maximum_fusion.4), channel_id=1, source_target_pairs={{4,0},{6,2},{8,4},{10,6},{12,8},{14,10},{5,1},{7,3},{9,5},{11,7},{... | collective-permute-start | bytes 405512 | tf_op jit(solution)/shard_map/ppermute | solution.py:27
  46.7 7.5 %collective-permute-start.3 = (bf16[2,8,4224]{2,1,0:T(8,128)(2,1)S(1)}, bf16[2,8,4224]{2,1,0:T(8,128)(2,1)S(1)}, u32[]{:S(2)}, u32[]{:S(2)}) collective-permute-start(bf16[2,8,4224]{2,1,0:T(8,128)(2,1)S(1)} %pad_maximum_fusion.3), channel_id=1, source_target_pairs={{0,8},{2,10},{4,12},{6,14},{1,9},{3,11},{5,13},{7,15},{16,24},{18,... | collective-permute-start | bytes 405512 | tf_op jit(solution)/shard_map/ppermute | solution.py:27
  51.7 8.3 %collective-permute-start.6 = (bf16[2,8,4224]{2,1,0:T(8,128)(2,1)S(1)}, bf16[2,8,4224]{2,1,0:T(8,128)(2,1)S(1)}, u32[]{:S(2)}, u32[]{:S(2)}) collective-permute-start(bf16[2,8,4224]{2,1,0:T(8,128)(2,1)S(1)} %pad_maximum_fusion.5), channel_id=1, source_target_pairs={{8,0},{10,2},{12,4},{14,6},{9,1},{11,3},{13,5},{15,7},{24,16},{26,... | collective-permute-start | bytes 405512 | tf_op jit(solution)/shard_map/ppermute | solution.py:27
  66.2 7.9 %copy-start.12 = (f32[256,2,8]{0,2,1:T(8,128)}, f32[256,2,8]{0,2,1:T(8,128)S(1)}, u32[]{:S(2)}) copy-start(f32[256,2,8]{0,2,1:T(8,128)S(1)} %get-tuple-element.130) | copy-start | bytes 49156
  68.2 5.9 %copy-start.2 = (f32[256,2,8,64]{0,3,2,1:T(8,128)S(1)}, f32[256,2,8,64]{0,3,2,1:T(8,128)}, u32[]{:S(2)}) copy-start(f32[256,2,8,64]{0,3,2,1:T(8,128)} %get-tuple-element.131) | copy-start | bytes 3145732
  68.2 5.9 %copy-start.4 = (f32[2,256,256]{2,1,0:T(8,128)S(1)}, f32[2,256,256]{2,1,0:T(8,128)}, u32[]{:S(2)}) copy-start(f32[2,256,256]{2,1,0:T(8,128)} %fusion.131) | copy-start | bytes 1572868
  68.2 5.9 %copy-start.57 = (f32[2,8]{1,0:T(2,128)S(1)}, f32[2,8]{1,0:T(2,128)}, u32[]{:S(2)}) copy-start(f32[2,8]{1,0:T(2,128)} %param.26) | copy-start | bytes 196
  76.4 2.6 %copy-start.53 = (f32[2,8]{1,0:T(2,128)S(1)}, f32[2,8]{1,0:T(2,128)}, u32[]{:S(2)}) copy-start(f32[2,8]{1,0:T(2,128)} %get-tuple-element.105) | copy-start | bytes 196
  76.5 3.3 %copy-start.7 = (f32[256,2,64]{0,2,1:T(8,128)S(1)}, f32[256,2,64]{0,2,1:T(8,128)}, u32[]{:S(2)}) copy-start(f32[256,2,64]{0,2,1:T(8,128)} %get-tuple-element.98) | copy-start | bytes 393220
  76.5 3.7 %copy-start.42 = (f32[2,64]{1,0:T(2,128)S(1)}, f32[2,64]{1,0:T(2,128)}, u32[]{:S(2)}) copy-start(f32[2,64]{1,0:T(2,128)} %copy-done.41) | copy-start | bytes 1540
  76.5 3.7 %copy-start.44 = (f32[2,64]{1,0:T(2,128)S(1)}, f32[2,64]{1,0:T(2,128)}, u32[]{:S(2)}) copy-start(f32[2,64]{1,0:T(2,128)} %copy-done.43) | copy-start | bytes 1540
  76.5 3.7 %copy-start.46 = (f32[2,64]{1,0:T(2,128)S(1)}, f32[2,64]{1,0:T(2,128)}, u32[]{:S(2)}) copy-start(f32[2,64]{1,0:T(2,128)} %copy-done.45) | copy-start | bytes 1540
  76.5 3.7 %copy-start.48 = (f32[2,64]{1,0:T(2,128)S(1)}, f32[2,64]{1,0:T(2,128)}, u32[]{:S(2)}) copy-start(f32[2,64]{1,0:T(2,128)} %copy-done.47) | copy-start | bytes 1540
  85.6 2.8 %copy-start.27 = (f32[256,2,8]{0,2,1:T(8,128)S(1)}, f32[256,2,8]{0,2,1:T(8,128)}, u32[]{:S(2)}) copy-start(f32[256,2,8]{0,2,1:T(8,128)} %get-tuple-element.107) | copy-start | bytes 49156
  85.6 2.7 %copy-start.28 = (f32[1,2,8]{0,2,1:T(8,128)S(1)}, f32[1,2,8]{0,2,1:T(8,128)}, u32[]{:S(2)}) copy-start(f32[1,2,8]{0,2,1:T(8,128)} %copy.129) | copy-start | bytes 196
  85.6 3.0 %copy-start.56 = (f32[2,8]{1,0:T(2,128)S(1)}, f32[2,8]{1,0:T(2,128)}, u32[]{:S(2)}) copy-start(f32[2,8]{1,0:T(2,128)} %copy-done.55) | copy-start | bytes 196
  85.7 3.0 %copy-start.58 = (f32[2,8,256]{2,1,0:T(8,128)S(1)}, f32[2,8,256]{2,1,0:T(8,128)}, u32[]{:S(2)}) copy-start(f32[2,8,256]{2,1,0:T(8,128)} %get-tuple-element.82) | copy-start | bytes 49156
  85.7 3.0 %copy-start.59 = (f32[2,8,256]{2,1,0:T(8,128)S(1)}, f32[2,8,256]{2,1,0:T(8,128)}, u32[]{:S(2)}) copy-start(f32[2,8,256]{2,1,0:T(8,128)} %get-tuple-element.83) | copy-start | bytes 49156
  85.7 3.0 %copy-start.60 = (f32[2,8,256]{2,1,0:T(8,128)S(1)}, f32[2,8,256]{2,1,0:T(8,128)}, u32[]{:S(2)}) copy-start(f32[2,8,256]{2,1,0:T(8,128)} %get-tuple-element.84) | copy-start | bytes 49156
  85.7 3.2 %copy-start.13 = (f32[256,2,8]{0,2,1:T(8,128)S(1)}, f32[256,2,8]{0,2,1:T(8,128)}, u32[]{:S(2)}) copy-start(f32[256,2,8]{0,2,1:T(8,128)} %copy-done.12) | copy-start | bytes 49156
  85.7 3.2 %copy-start.18 = (f32[256,2,8]{0,2,1:T(8,128)S(1)}, f32[256,2,8]{0,2,1:T(8,128)}, u32[]{:S(2)}) copy-start(f32[256,2,8]{0,2,1:T(8,128)} %param.23) | copy-start | bytes 49156
  85.7 3.2 %copy-start.32 = (f32[2,8]{1,0:T(2,128)S(1)}, f32[2,8]{1,0:T(2,128)}, u32[]{:S(2)}) copy-start(f32[2,8]{1,0:T(2,128)} %copy-done.30) | copy-start | bytes 196
  85.7 3.2 %copy-start.49 = (f32[1,2,8]{0,2,1:T(8,128)S(1)}, f32[1,2,8]{0,2,1:T(8,128)}, u32[]{:S(2)}) copy-start(f32[1,2,8]{0,2,1:T(8,128)} %copy.130) | copy-start | bytes 196
  85.7 3.2 %copy-start.51 = (f32[2,8]{1,0:T(2,128)S(1)}, f32[2,8]{1,0:T(2,128)}, u32[]{:S(2)}) copy-start(f32[2,8]{1,0:T(2,128)} %param.25) | copy-start | bytes 196
  87.1 5.7 %collective-permute-start.7 = (f32[3,1280]{1,0:T(4,128)S(1)}, f32[3,1280]{1,0:T(4,128)S(1)}, u32[]{:S(2)}, u32[]{:S(2)}) collective-permute-start(f32[3,1280]{1,0:T(4,128)S(1)} %pad_maximum_fusion.8), channel_id=1, source_target_pairs={{2,0},{4,2},{6,4},{8,6},{10,8},{12,10},{14,12},{3,1},{5,3},{7,5},{... | collective-permute-start | bytes 46088 | tf_op jit(solution)/shard_map/ppermute | solution.py:12
  (21 other events, 30.5 us)

commit v6 on v4

--- a/solution.py
+++ b/solution.py
@@ -1,58 +1,61 @@
+import functools
 import jax
 import jax.numpy as jnp
 from jax import lax
-from jax.sharding import PartitionSpec as P
+from jax.sharding import Mesh, PartitionSpec as P
 
 HIGH = lax.Precision.HIGHEST
 
 
 def from_behind(array, axis, by):
-    count = lax.axis_size(axis)
+    count = 2 ** len(axis)
     pairs = [(i, i + by) for i in range(count) if 0 <= i + by < count]
     return lax.ppermute(array, axis, pairs)
 
 
-def scanned_pair(decay, forward_state, backward_state, axis, riders):
-    count = lax.axis_size(axis)
+def butterfly_pair(decay, forward_state, backward_state, bit_axes):
     groups, heads, rows, cols = forward_state.shape
+    span = rows * cols
     lanes = 128
 
-    def shift(decay_part, state_part, by, sign):
-        pairs = [(i, i + sign * by) for i in range(count) if 0 <= i + sign * by < count]
+    def join(earlier, later):
+        return (earlier[0] * later[0], later[0][:, :, None] * earlier[1] + later[1])
+
+    ones = jnp.ones_like(decay)
+    zeros = jnp.zeros((groups, heads, span), jnp.float32)
+    front = (decay, forward_state.reshape(groups, heads, span))
+    back = (decay, backward_state.reshape(groups, heads, span))
+    before = (ones, zeros)
+    after = (ones, zeros)
+    for axis in reversed(bit_axes):
+        upper = lax.axis_index(axis) == 1
         packed = jnp.concatenate(
-            [state_part, jnp.broadcast_to(decay_part[:, :, None], (groups, heads, lanes))], 2
+            [front[1], back[1], jnp.broadcast_to(front[0][:, :, None], (groups, heads, lanes))], 2
         ).astype(jnp.bfloat16)
-        return lax.ppermute(packed, axis, pairs)
-
-    def unpack(got):
-        got = got.astype(jnp.float32)
-        return got[:, :, rows * cols], got[:, :, : rows * cols]
-
-    def fold(window, got_decay, got_state):
-        before_decay, before_state, upto_decay, upto_state = window
-        return (
-            before_decay * got_decay,
-            before_decay[:, :, None] * got_state + before_state,
-            upto_decay * got_decay,
-            upto_decay[:, :, None] * got_state + upto_state,
-        )
-
-    flats = [s.reshape(groups, heads, rows * cols) for s in (forward_state, backward_state)]
-    windows = [
-        (jnp.ones_like(decay), jnp.zeros_like(flat), decay, flat) for flat in flats
-    ]
-    tied = list(riders)
-    by = 1
-    step = 0
-    while by < count:
-        got = [shift(w[2], w[3], by, sign) for w, sign in zip(windows, (1, -1))]
-        if step < len(tied):
-            got, tied[step] = lax.optimization_barrier((got, tied[step]))
-        windows = [fold(w, *unpack(g)) for w, g in zip(windows, got)]
-        by *= 2
-        step += 1
-    state_in, adjoint = [w[1].reshape(groups, heads, rows, cols) for w in windows]
-    return state_in, adjoint, tied
+        both = lax.all_gather(packed, axis)
+        other = jnp.where(upper, both[0], both[1]).astype(jnp.float32)
+        other_decay = other[:, :, 2 * span]
+        other_front = (other_decay, other[:, :, :span])
+        other_back = (other_decay, other[:, :, span : 2 * span])
+        before = jax.tree.map(
+            lambda joined, kept: jnp.where(upper, joined, kept), join(other_front, before), before
+        )
+        after = jax.tree.map(
+            lambda joined, kept: jnp.where(upper, kept, joined), join(other_back, after), after
+        )
+        front = jax.tree.map(
+            lambda low, high: jnp.where(upper, low, high),
+            join(other_front, front),
+            join(front, other_front),
+        )
+        back = jax.tree.map(
+            lambda low, high: jnp.where(upper, low, high),
+            join(back, other_back),
+            join(other_back, back),
+        )
+    state_in = before[1].reshape(groups, heads, rows, cols)
+    adjoint = after[1].reshape(groups, heads, rows, cols)
+    return state_in, adjoint
 
 
 def conv_forward(extended, weight):
@@ -128,7 +131,7 @@
     return carried * jnp.exp(cum_log)[..., None]
 
 
-def on_device(x_in, b_in, c_in, dt_in, rate, dt_bias, skip, conv_x, conv_b, conv_c, grad_y):
+def on_device(bit_axes, x_in, b_in, c_in, dt_in, rate, dt_bias, skip, conv_x, conv_b, conv_c, grad_y):
     kernel_width = conv_x.shape[0]
     halo_rows = kernel_width - 1
     length, groups, channels = x_in.shape
@@ -145,7 +148,7 @@
         ],
         1,
     )
-    incoming = from_behind(outgoing, "ctx", 1)
+    incoming = from_behind(outgoing, bit_axes, 1)
     x_ext = jnp.concatenate([incoming[:, :x_span].reshape(halo_rows, groups, channels), x_in], 0)
     b_ext = jnp.concatenate(
         [incoming[:, x_span : x_span + b_span].reshape(halo_rows, groups, state_size), b_in], 0
@@ -167,17 +170,15 @@
         return ssd_state(x_arg, b_arg, dt_arg, rate, dt_bias)
 
     (cum_log, state_end), state_pull = jax.vjp(state_map, x_float, b_float, dt_in)
-    y_local, mix_pull = jax.vjp(mix_map, x_float, b_float, c_float, dt_in)
     decay_total = jnp.exp(cum_log[-1])
     grad_heads = grad_y.astype(jnp.float32).reshape(length, groups, head_count, head_size)
     seed_state = jnp.einsum(
         "tghp,tgn->ghpn", jnp.exp(cum_log)[..., None] * grad_heads, c_float, precision=HIGH
     )
+
+    y_local, mix_pull = jax.vjp(mix_map, x_float, b_float, c_float, dt_in)
     mix_x, mix_b, mix_c, mix_dt = mix_pull(grad_heads)
-    state_in, adjoint, riders = scanned_pair(
-        decay_total, state_end, seed_state, "ctx", [y_local, mix_x, (mix_b, mix_c, mix_dt)]
-    )
-    y_local, mix_x, (mix_b, mix_c, mix_dt) = riders
+    state_in, adjoint = butterfly_pair(decay_total, state_end, seed_state, bit_axes)
 
     def carry_map(c_arg, cum_arg):
         return carry_in(c_arg, cum_arg, state_in)
@@ -203,7 +204,7 @@
         ],
         1,
     )
-    returned = from_behind(leaving, "ctx", -1)
+    returned = from_behind(leaving, bit_axes, -1)
     back_x = returned[:, :x_span].reshape(halo_rows, groups, channels)
     back_b = returned[:, x_span : x_span + b_span].reshape(halo_rows, groups, state_size)
     back_c = returned[:, x_span + b_span :].reshape(halo_rows, groups, state_size)
@@ -214,28 +215,33 @@
 
 
 def solution(mesh):
+    groups, count, parts = mesh.devices.shape
+    bits = count.bit_length() - 1
+    assert 2**bits == count
+    bit_axes = tuple("ctx_%d" % k for k in reversed(range(bits)))
+    split = Mesh(mesh.devices.reshape((groups,) + (2,) * bits + (parts,)), ("groups",) + bit_axes + ("tp",))
     return jax.shard_map(
-        on_device,
-        mesh=mesh,
+        functools.partial(on_device, bit_axes),
+        mesh=split,
         in_specs=(
-            P(("groups", "ctx"), "tp", None),
-            P(("groups", "ctx"), "tp", None),
-            P(("groups", "ctx"), "tp", None),
-            P(("groups", "ctx"), "tp", None),
+            P(("groups",) + bit_axes, "tp", None),
+            P(("groups",) + bit_axes, "tp", None),
+            P(("groups",) + bit_axes, "tp", None),
+            P(("groups",) + bit_axes, "tp", None),
             P("tp", None),
             P("tp", None),
             P("tp", None),
             P(None, "tp", None),
             P(None, "tp", None),
             P(None, "tp", None),
-            P(("groups", "ctx"), "tp", None),
+            P(("groups",) + bit_axes, "tp", None),
         ),
         out_specs=(
-            P(("groups", "ctx"), "tp", None),
-            P(("groups", "ctx"), "tp", None),
-            P(("groups", "ctx"), "tp", None),
-            P(("groups", "ctx"), "tp", None),
-            P(("groups", "ctx"), "tp", None),
+            P(("groups",) + bit_axes, "tp", None),
+            P(("groups",) + bit_axes, "tp", None),
+            P(("groups",) + bit_axes, "tp", None),
+            P(("groups",) + bit_axes, "tp", None),
+            P(("groups",) + bit_axes, "tp", None),
         ),
         check_vma=False,
     )

time: 102 us -> 225 us (2.21)
  local copies, waits for them, and re-layouts: 23.2 us -> 98.8 us
  other arithmetic: 16.8 us -> 66.7 us
  blocking collectives: 0 us -> 29.7 us
  starting transfers between devices: 24.9 us -> 6.14 us
  waiting for transfers between devices: 12.8 us -> 0.01 us
    slice x1 -> x10, local copies, waits for them, and re-layouts: 0.22 us -> 40.4 us  [the longest x9 40.3 us: butterfly_pair(): other = jnp.where(upper, both[0], both[1]).astype(jnp.float32)]
    all_gather x0 -> x3, blocking collectives: none -> 29.7 us  [butterfly_pair(): both = lax.all_gather(packed, axis)]
    convert_element_type x5, other arithmetic: 1.16 us -> 21.3 us  [the longest x3 20.8 us: butterfly_pair(): other = jnp.where(upper, both[0], both[1]).astype(jnp.float32)]
    ppermute x6 -> x0, starting transfers between devices: 18.7 us -> none  [shift(): return lax.ppermute(packed, axis, pairs)]
    concatenate x5, other arithmetic: 0.75 us -> 19.4 us  [butterfly_pair(): jnp.concatenate([front[1], back[1], jnp.broadcast_to(front[0][:, :, None]...]
    concatenate x0 -> x6, local copies, waits for them, and re-layouts: none -> 18 us  [butterfly_pair(): jnp.concatenate([front[1], back[1], jnp.broadcast_to(front[0][:, :, None]...]
    reshape x5 -> x4, local copies, waits for them, and re-layouts: 5.15 us -> 19.6 us  [the longest x1 5.5 us: butterfly_pair(): state_in = before[1].reshape(groups, heads, rows, cols)]
    ppermute x6 -> x0, waiting for transfers between devices: 11.3 us -> none  [shift(): return lax.ppermute(packed, axis, pairs)]
  transfers between devices with their start and end apart: 8 -> 2, of which waited for: 5 -> 0; matrix products, arithmetic and copies ran while one was open for 15% -> 6% of each run, Pallas kernels for 0% -> 0%
where the time goes in v6:
time: 225 us; the launch traced here: 223 us
  local copies, waits for them, and re-layouts  98.8 us (44%)
  other arithmetic  66.7 us (30%)
  blocking collectives  29.7 us (13%)
  matrix products  20.1 us (9%)
  starting transfers between devices  6.14 us (3%)
    slice x9, local copies, waits for them, and re-layouts, butterfly_pair(): other = jnp.where(upper, both[0], both[1]).astype(jnp.float32)  40.3 us
    all_gather x3, blocking collectives, butterfly_pair(): both = lax.all_gather(packed, axis)  29.7 us
    convert_element_type x3, other arithmetic, butterfly_pair(): other = jnp.where(upper, both[0], both[1]).astype(jnp.float32)  20.8 us
    concatenate x5, other arithmetic, butterfly_pair(): jnp.concatenate([front[1], back[1], jnp.broadcast_to(front[0][:, :, None]...  19.4 us
    concatenate x6, local copies, waits for them, and re-layouts, butterfly_pair(): jnp.concatenate([front[1], back[1], jnp.broadcast_to(front[0][:, :, None]...  18 us
    dot_general x3, matrix products, ssd_mix(): jnp.einsum('ghts,sghp->tghp', mixing, x_half, preferred_element_type=jnp....  11.8 us
    reduce_sum x1, other arithmetic, on_device(): end_term = jnp.sum(adjoint * state_in, axis=(2, 3)) * decay_total  11.1 us
    unnamed x167, local copies, waits for them, and re-layouts  7.45 us
  transfers between devices with their start and end apart: 2, of which 0 were waited for; matrix products, arithmetic and copies ran while one was open for 6% of the time, Pallas kernels for 0%

profile of v6, /device:TPU:0, one launch (start us, length us, event | category | flops | bytes accessed | tf_op | source)
XLA Modules:
  0.0 223.3 jit_solution(10010660869728640911)
XLA Ops:
  0.7 0.9 slice.301
  1.6 0.9 slice.302
  3.3 4.8 %collective-permute-start = (bf16[3,1280]{1,0:T(4,128)(2,1)S(1)}, bf16[3,1280]{1,0:T(4,128)(2,1)S(1)}, u32[]{:S(2)}, u32[]{:S(2)}) collective-permute-start(bf16[3,1280]{1,0:T(4,128)(2,1)S(1)} %pad_maximum_fusion.6), channel_id=1, source_target_pairs={{0,2},{2,4},{4,6},{6,8},{8,10},{10,12},{12,14},{1,3},{3,5},{5,7},{... | collective-permute-start | bytes 23048 | tf_op jit(solution)/shard_map/ppermute | solution.py:13
  8.8 0.9 fusion.88
  10.0 0.8 fusion.123
  14.3 1.3 copy.61
  16.0 1.5 constant_dynamic-update-slice_fusion
  17.4 4.3 %multiply_convert_fusion = (bf16[256,2,512]{2,1,0:T(2,128)(2,1)S(1)}, f32[256,2,512]{2,1,0:T(2,128)}) fusion(bf16[256,2,512]{2,1,0:T(2,128)(2,1)} %param.20, f32[2,512]{1,0:T(2,128)S(1)} %get-tuple-element.119, bf16[259,2,512]{2,1,0:T(2,128)(2,1)S(1)} %constant_dynamic-update-slice_fusion, f32[2,512]{1,0:T(2,128)S(1)} %get-tuple-element.120, ...), kind=kLoop, calls=%fused_computation.99 | loop fusion | flops 4194304 | bytes 3686400 | tf_op jit(solution)/shard_map/convert_element_type | solution.py:162
  23.4 1.1 fusion.153
  25.5 8.5 %all_gather.12 = bf16[2,2,8,8320]{3,2,1,0:T(8,128)(2,1)S(1)} all-gather(bf16[1,2,8,8320]{3,2,1,0:T(8,128)(2,1)S(1)} %pad_maximum_fusion), channel_id=1, replica_groups=mesh['groups'=2,'ctx_2'=2,'ctx_1'=2,'ctx_0'=2,'tp'=2] {'ctx_0'}, dimensions={0}, use_global_device_ids=true | all-gather | bytes 798720 | tf_op jit(solution)/shard_map/all_gather | solution.py:35
  34.1 6.7 %copy.62 = bf16[1,2,8,8320]{2,1,3,0:T(2,128)(2,1)} copy(bf16[1,2,8,8320]{3,2,1,0:T(8,128)(2,1)S(1)} %get-tuple-element.109) | data formatting | bytes 532480 | tf_op jit(solution)/shard_map/slice | solution.py:36
  40.8 6.7 %copy.63 = bf16[1,2,8,8320]{2,1,3,0:T(2,128)(2,1)} copy(bf16[1,2,8,8320]{3,2,1,0:T(8,128)(2,1)S(1)} %get-tuple-element.108) | data formatting | bytes 532480 | tf_op jit(solution)/shard_map/slice | solution.py:36
  47.4 4.3 %copy.94 = f32[2,8,64,64]{1,0,3,2:T(2,128)} copy(f32[2,8,64,64]{3,2,1,0:T(8,128)S(1)} %get-tuple-element.136) | data formatting | bytes 524288 | tf_op jit(solution)/shard_map/reshape | solution.py:26
  51.8 4.3 %copy.95 = f32[2,8,64,64]{1,0,3,2:T(2,128)} copy(f32[2,8,64,64]{3,2,1,0:T(8,128)S(1)} %get-tuple-element.134) | data formatting | bytes 524288 | tf_op jit(solution)/shard_map/reshape | solution.py:27
  56.1 6.7 %fusion.3 = f32[2,8,8320]{1,0,2:T(2,128)S(1)} fusion(bf16[1,2,8,8320]{2,1,3,0:T(2,128)(2,1)} %copy.62, bf16[1,2,8,8320]{2,1,3,0:T(2,128)(2,1)} %copy.63, pred[]{:T(512)S(6)} %eq.20), kind=kLoop, calls=%fused_computation.13 | loop fusion | flops 266240 | bytes 1064961 | tf_op jit(solution)/shard_map/convert_element_type | solution.py:36
  63.4 9.9 %convert_bitcast_fusion.1 = (bf16[1,2,8,4096]{2,1,3,0:T(2,128)(2,1)}, f32[2,8,4096]{1,0,2:T(2,128)}, bf16[1,2,8,4096]{2,1,3,0:T(2,128)(2,1)S(1)}, f32[2,8,4096]{1,0,2:T(2,128)}) fusion(f32[2,8]{1,0:T(2,128)S(1)} %get-tuple-element.103, f32[2,8,64,64]{1,0,3,2:T(2,128)S(1)} %copy-done.5, f32[2,8,8320]{1,0,2:T(2,128)S(1)} %fusion.3, f32[2,8]{1,0:T(2,128)S(1)} %copy-done.70, ...), kind=kLoop, calls=%fused_computation.44 | loop fusion | flops 786432 | bytes 1835137 | tf_op jit(solution)/shard_map/concatenate | solution.py:32
  73.3 5.2 %copy.68 = bf16[1,2,8,4096]{3,2,1,0:T(8,128)(2,1)} copy(bf16[1,2,8,4096]{2,1,3,0:T(2,128)(2,1)} %get-tuple-element.81) | data formatting | bytes 262144 | tf_op jit(solution)/shard_map/concatenate | solution.py:32
  78.5 3.5 %copy.69 = bf16[1,2,8,4096]{3,2,1,0:T(8,128)(2,1)} copy(bf16[1,2,8,4096]{2,1,3,0:T(2,128)(2,1)S(1)} %get-tuple-element.98) | data formatting | bytes 262144 | tf_op jit(solution)/shard_map/concatenate | solution.py:32
  82.8 1.0 pad_maximum_fusion.1
  83.8 7.6 %all_gather.13 = bf16[2,2,8,8320]{3,2,1,0:T(8,128)(2,1)S(1)} all-gather(bf16[1,2,8,8320]{3,2,1,0:T(8,128)(2,1)S(1)} %pad_maximum_fusion.1), channel_id=1, replica_groups=mesh['groups'=2,'ctx_2'=2,'ctx_1'=2,'ctx_0'=2,'tp'=2] {'ctx_1'}, dimensions={0}, use_global_device_ids=true | all-gather | bytes 798720 | tf_op jit(solution)/shard_map/all_gather | solution.py:35
  91.5 6.7 %copy.70 = bf16[1,2,8,8320]{2,1,3,0:T(2,128)(2,1)} copy(bf16[1,2,8,8320]{3,2,1,0:T(8,128)(2,1)S(1)} %get-tuple-element.107) | data formatting | bytes 532480 | tf_op jit(solution)/shard_map/slice | solution.py:36
  98.2 6.7 %copy.71 = bf16[1,2,8,8320]{2,1,3,0:T(2,128)(2,1)} copy(bf16[1,2,8,8320]{3,2,1,0:T(8,128)(2,1)S(1)} %get-tuple-element.106) | data formatting | bytes 532480 | tf_op jit(solution)/shard_map/slice | solution.py:36
  104.9 6.7 %fusion.1 = f32[2,8,8320]{1,0,2:T(2,128)S(1)} fusion(bf16[1,2,8,8320]{2,1,3,0:T(2,128)(2,1)} %copy.70, bf16[1,2,8,8320]{2,1,3,0:T(2,128)(2,1)} %copy.71, pred[]{:T(512)S(6)} %eq.19), kind=kLoop, calls=%fused_computation.11 | loop fusion | flops 266240 | bytes 1064961 | tf_op jit(solution)/shard_map/convert_element_type | solution.py:36
  111.6 1.7 fusion.129
  113.2 7.5 %fusion.23 = (bf16[1,2,8,4096]{2,1,3,0:T(2,128)(2,1)}, bf16[1,2,8,4096]{2,1,3,0:T(2,128)(2,1)S(1)}) fusion(f32[2,8,4096]{1,0,2:T(2,128)S(1)} %copy-done.3, f32[2,8]{1,0:T(2,128)S(1)} %get-tuple-element.100, f32[2,8,8320]{1,0,2:T(2,128)S(1)} %fusion.1, f32[2,8]{1,0:T(2,128)S(1)} %copy-done.71, pred[]{:T(512)S(6)} %eq.19, f32[2,8,4096]{1,0,2:T(2,128)S(1)} %copy-done.4), kind=kLoop, calls=%fused_computation.45 | loop fusion | flops 786432 | bytes 1310849 | tf_op jit(solution)/shard_map/concatenate | solution.py:32
  120.8 5.2 %copy.72 = bf16[1,2,8,4096]{3,2,1,0:T(8,128)(2,1)} copy(bf16[1,2,8,4096]{2,1,3,0:T(2,128)(2,1)} %get-tuple-element.96) | data formatting | bytes 262144 | tf_op jit(solution)/shard_map/concatenate | solution.py:32
  126.0 3.5 %copy.73 = bf16[1,2,8,4096]{3,2,1,0:T(8,128)(2,1)} copy(bf16[1,2,8,4096]{2,1,3,0:T(2,128)(2,1)S(1)} %get-tuple-element.97) | data formatting | bytes 262144 | tf_op jit(solution)/shard_map/concatenate | solution.py:32
  130.2 1.0 pad_maximum_fusion.2
  131.2 13.5 %all_gather.14 = bf16[2,2,8,8320]{3,2,1,0:T(8,128)(2,1)S(1)} all-gather(bf16[1,2,8,8320]{3,2,1,0:T(8,128)(2,1)S(1)} %pad_maximum_fusion.2), channel_id=1, replica_groups=mesh['groups'=2,'ctx_2'=2,'ctx_1'=2,'ctx_0'=2,'tp'=2] {'ctx_2'}, dimensions={0}, use_global_device_ids=true | all-gather | bytes 798720 | tf_op jit(solution)/shard_map/all_gather | solution.py:35
  144.7 6.7 %copy.74 = bf16[1,2,8,8320]{2,1,3,0:T(2,128)(2,1)} copy(bf16[1,2,8,8320]{3,2,1,0:T(8,128)(2,1)S(1)} %get-tuple-element.105) | data formatting | bytes 532480 | tf_op jit(solution)/shard_map/slice | solution.py:36
  151.5 6.7 %copy.75 = bf16[1,2,8,8320]{2,1,3,0:T(2,128)(2,1)} copy(bf16[1,2,8,8320]{3,2,1,0:T(8,128)(2,1)S(1)} %get-tuple-element.104) | data formatting | bytes 532480 | tf_op jit(solution)/shard_map/slice | solution.py:36
  158.2 7.5 %fusion.5 = f32[2,8,8320]{1,0,2:T(2,128)S(1)} fusion(bf16[1,2,8,8320]{2,1,3,0:T(2,128)(2,1)} %copy.74, bf16[1,2,8,8320]{2,1,3,0:T(2,128)(2,1)} %copy.75, pred[]{:T(512)S(6)} %eq.18), kind=kLoop, calls=%fused_computation.15 | loop fusion | flops 266240 | bytes 1064961 | tf_op jit(solution)/shard_map/convert_element_type | solution.py:36
  165.8 11.1 %multiply_reduce_fusion = (f32[2,8]{1,0:T(2,128)S(1)}, f32[2,8,4096]{1,0,2:T(2,128)}, f32[2,8,4096]{1,0,2:T(2,128)}) fusion(f32[2,8,8320]{1,0,2:T(2,128)S(1)} %fusion.5, f32[2,8]{1,0:T(2,128)S(1)} %copy-done.65, f32[2,8,8320]{1,0,2:T(2,128)S(1)} %copy-done.2, f32[2,8]{1,0:T(2,128)S(1)} %copy-done.66, f32[2,8,8320]{1,0,2:T(2,128)S(1)} %bitcast.263, ...), kind=kLoop, calls=%fused_computation.40 | loop fusion | flops 1048560 | bytes 2097475 | tf_op jit(solution)/shard_map/reduce_sum | solution.py:189
  176.9 5.5 %copy.79 = f32[2,8,64,64]{2,3,1,0:T(8,128)S(1)} copy(f32[2,8,64,64]{1,0,3,2:T(2,128)} %bitcast.265) | data formatting | bytes 524288 | tf_op jit(solution)/shard_map/reshape | solution.py:57
  183.6 5.5 %copy.80 = f32[2,8,64,64]{2,3,1,0:T(8,128)S(1)} copy(f32[2,8,64,64]{1,0,3,2:T(2,128)} %bitcast.264) | data formatting | bytes 524288 | tf_op jit(solution)/shard_map/reshape | solution.py:56
  189.0 1.7 fusion.82
  190.7 0.9 convolution_bitcast_fusion.3
  193.8 5.8 %fusion.30 = (f32[2,8,256]{2,1,0:T(8,128)}, f32[2,8,256]{2,1,0:T(8,128)}, f32[2,8,256]{2,1,0:T(8,128)}, f32[2,256,256]{2,1,0:T(8,128)S(1)}) fusion(f32[2,8,256]{2,1,0:T(8,128)S(1)} %bitcast.282, f32[2,8,256]{2,1,0:T(8,128)S(1)} %get-tuple-element.113, f32[2,256,256]{2,1,0:T(8,128)} %fusion.153, pred[256,256]{1,0:T(8,128)(4,1)S(1)} %copy-done.24, ...), kind=kOutput, calls=%fused_computation.57 | convolution fusion | flops 156094464 | bytes 2244608 | tf_op jit(solution)/shard_map/transpose(jvp(ghts,sghp->tghp))/dot_general | solution.py:113
  202.4 2.8 %fusion.60 = bf16[256,2,8,64]{0,3,2,1:T(8,128)(2,1)S(1)} fusion(bf16[2,8,64,256]{3,2,1,0:T(8,128)(2,1)S(1)} %bitcast.270, f32[2,8,256]{2,1,0:T(8,128)} %copy-done.43, f32[2,8,256]{2,1,0:T(8,128)} %bitcast.281, f32[2,256,256]{2,1,0:T(8,128)} %fusion.153, pred[256,256]{1,0:T(8,128)(4,1)} %iota_compare_fusion, bf16[256,2,8,64]{0,3,2,1:T(8,128)(2,1)S(1)} %bitcast.269, ...), kind=kOutput, calls=%fused_computation.71 | convolution fusion | flops 142606336 | bytes 3260480 | tf_op jit(solution)/shard_map/transpose(jvp(ghts,sghp->tghp))/dot_general | solution.py:113
  205.3 1.3 copy.78
  206.7 2.8 %multiply_multiply_fusion = f32[256,2,512]{2,1,0:T(2,128)S(1)} fusion(f32[256,2,512]{2,1,0:T(2,128)} %copy.78, f32[256,2,512]{2,1,0:T(2,128)S(1)} %copy-done.7), kind=kLoop, calls=%fused_computation.98 | loop fusion | flops 2097152 | bytes 3145728 | tf_op jit(solution)/shard_map/mul | solution.py:74
  209.5 1.3 multiply_add_fusion
  210.8 1.0 copy-done.8
  211.8 1.3 collective-permute-start.1
  213.3 3.2 %fusion.42 = bf16[256,2,8,64]{0,3,2,1:T(8,128)(2,1)} fusion(bf16[256,2,8,64]{0,3,2,1:T(8,128)(2,1)S(1)} %bitcast.274, f32[2,8,256]{2,1,0:T(8,128)} %copy-done.43, f32[2,8,256]{2,1,0:T(8,128)S(1)} %bitcast.283, f32[2,256,256]{2,1,0:T(8,128)S(1)} %copy-done.13, pred[256,256]{1,0:T(8,128)(4,1)S(1)} %copy-done.25, f32[256,2,8,64]{0,3,2,1:T(8,128)S(1)} %copy-done.10, ...), kind=kOutput, calls=%fused_computation.65 | convolution fusion | flops 142082048 | bytes 2736192 | tf_op jit(solution)/shard_map/jvp(ghts,sghp->tghp)/dot_general | solution.py:113
  217.0 0.9 fusion.76
  218.5 2.0 copy.87
  222.5 0.8 copy-done.14
  (226 shorter events, 19.4 us)
Async XLA Ops:
  0.6 21.7 %copy-start.18 = (bf16[256,2,64]{0,2,1:T(8,128)(2,1)S(1)}, bf16[256,2,64]{0,2,1:T(8,128)(2,1)}, u32[]{:S(2)}) copy-start(bf16[256,2,64]{0,2,1:T(8,128)(2,1)} %param.21) | copy-start | bytes 196612
  0.6 21.7 %copy-start.17 = (bf16[256,2,64]{0,2,1:T(8,128)(2,1)S(1)}, bf16[256,2,64]{0,2,1:T(8,128)(2,1)}, u32[]{:S(2)}) copy-start(bf16[256,2,64]{0,2,1:T(8,128)(2,1)} %param.22) | copy-start | bytes 196612
  3.3 12.3 %collective-permute-start = (bf16[3,1280]{1,0:T(4,128)(2,1)S(1)}, bf16[3,1280]{1,0:T(4,128)(2,1)S(1)}, u32[]{:S(2)}, u32[]{:S(2)}) collective-permute-start(bf16[3,1280]{1,0:T(4,128)(2,1)S(1)} %pad_maximum_fusion.6), channel_id=1, source_target_pairs={{0,2},{2,4},{4,6},{6,8},{8,10},{10,12},{12,14},{1,3},{3,5},{5,7},{... | collective-permute-start | bytes 23048 | tf_op jit(solution)/shard_map/ppermute | solution.py:13
  9.8 12.9 %copy-start.19 = (f32[256,16]{0,1}, f32[256,16]{0,1:S(1)}, u32[]{:S(2)}) copy-start(f32[256,16]{0,1:S(1)} %fusion.88) | copy-start | bytes 49156
  10.0 52.8 %copy-start.44 = (f32[2,8]{1,0:T(2,128)}, f32[2,8]{1,0:T(2,128)S(1)}, u32[]{:S(2)}) copy-start(f32[2,8]{1,0:T(2,128)S(1)} %get-tuple-element.77) | copy-start | bytes 196
  10.8 12.2 %copy-start.15 = (f32[256,2,8]{0,2,1:T(8,128)}, f32[256,2,8]{0,2,1:T(8,128)S(1)}, u32[]{:S(2)}) copy-start(f32[256,2,8]{0,2,1:T(8,128)S(1)} %get-tuple-element.115) | copy-start | bytes 49156
  12.2 10.9 %copy-start.54 = (f32[2,64]{1,0:T(2,128)}, f32[2,64]{1,0:T(2,128)S(1)}, u32[]{:S(2)}) copy-start(f32[2,64]{1,0:T(2,128)S(1)} %get-tuple-element.123) | copy-start | bytes 1540
  12.2 10.9 %copy-start.56 = (f32[2,64]{1,0:T(2,128)}, f32[2,64]{1,0:T(2,128)S(1)}, u32[]{:S(2)}) copy-start(f32[2,64]{1,0:T(2,128)S(1)} %get-tuple-element.124) | copy-start | bytes 1540
  12.2 10.9 %copy-start.58 = (f32[2,64]{1,0:T(2,128)}, f32[2,64]{1,0:T(2,128)S(1)}, u32[]{:S(2)}) copy-start(f32[2,64]{1,0:T(2,128)S(1)} %get-tuple-element.125) | copy-start | bytes 1540
  12.2 10.9 %copy-start.60 = (f32[2,64]{1,0:T(2,128)}, f32[2,64]{1,0:T(2,128)S(1)}, u32[]{:S(2)}) copy-start(f32[2,64]{1,0:T(2,128)S(1)} %get-tuple-element.126) | copy-start | bytes 1540
  12.9 10.2 %copy-start.46 = (f32[2,64]{1,0:T(2,128)}, f32[2,64]{1,0:T(2,128)S(1)}, u32[]{:S(2)}) copy-start(f32[2,64]{1,0:T(2,128)S(1)} %get-tuple-element.127) | copy-start | bytes 1540
  12.9 10.2 %copy-start.48 = (f32[2,64]{1,0:T(2,128)}, f32[2,64]{1,0:T(2,128)S(1)}, u32[]{:S(2)}) copy-start(f32[2,64]{1,0:T(2,128)S(1)} %get-tuple-element.128) | copy-start | bytes 1540
  12.9 10.2 %copy-start.50 = (f32[2,64]{1,0:T(2,128)}, f32[2,64]{1,0:T(2,128)S(1)}, u32[]{:S(2)}) copy-start(f32[2,64]{1,0:T(2,128)S(1)} %get-tuple-element.129) | copy-start | bytes 1540
  12.9 10.2 %copy-start.52 = (f32[2,64]{1,0:T(2,128)}, f32[2,64]{1,0:T(2,128)S(1)}, u32[]{:S(2)}) copy-start(f32[2,64]{1,0:T(2,128)S(1)} %get-tuple-element.130) | copy-start | bytes 1540
  13.7 9.0 %copy-start.30 = (f32[2,512]{1,0:T(2,128)}, f32[2,512]{1,0:T(2,128)S(1)}, u32[]{:S(2)}) copy-start(f32[2,512]{1,0:T(2,128)S(1)} %get-tuple-element.117) | copy-start | bytes 12292
  13.7 9.0 %copy-start.32 = (f32[2,512]{1,0:T(2,128)}, f32[2,512]{1,0:T(2,128)S(1)}, u32[]{:S(2)}) copy-start(f32[2,512]{1,0:T(2,128)S(1)} %get-tuple-element.118) | copy-start | bytes 12292
  13.7 9.0 %copy-start.34 = (f32[2,512]{1,0:T(2,128)}, f32[2,512]{1,0:T(2,128)S(1)}, u32[]{:S(2)}) copy-start(f32[2,512]{1,0:T(2,128)S(1)} %get-tuple-element.119) | copy-start | bytes 12292
  13.7 9.1 %copy-start.36 = (f32[2,512]{1,0:T(2,128)}, f32[2,512]{1,0:T(2,128)S(1)}, u32[]{:S(2)}) copy-start(f32[2,512]{1,0:T(2,128)S(1)} %get-tuple-element.120) | copy-start | bytes 12292
  56.1 7.3 %copy-start.5 = (f32[2,8,64,64]{1,0,3,2:T(2,128)S(1)}, f32[2,8,64,64]{1,0,3,2:T(2,128)}, u32[]{:S(2)}) copy-start(f32[2,8,64,64]{1,0,3,2:T(2,128)} %copy.94) | copy-start | bytes 786436
  56.1 7.3 %copy-start.6 = (f32[2,8,64,64]{1,0,3,2:T(2,128)S(1)}, f32[2,8,64,64]{1,0,3,2:T(2,128)}, u32[]{:S(2)}) copy-start(f32[2,8,64,64]{1,0,3,2:T(2,128)} %copy.95) | copy-start | bytes 786436
  56.1 7.3 %copy-start.70 = (f32[2,8]{1,0:T(2,128)S(1)}, f32[2,8]{1,0:T(2,128)}, u32[]{:S(2)}) copy-start(f32[2,8]{1,0:T(2,128)} %get-tuple-element.131) | copy-start | bytes 196
  62.8 10.6 %copy-start = (f32[2,8,8320]{1,0,2:T(2,128)}, f32[2,8,8320]{1,0,2:T(2,128)S(1)}, u32[]{:S(2)}) copy-start(f32[2,8,8320]{1,0,2:T(2,128)S(1)} %fusion.3) | copy-start | bytes 1597444
  104.9 8.4 %copy-start.3 = (f32[2,8,4096]{1,0,2:T(2,128)S(1)}, f32[2,8,4096]{1,0,2:T(2,128)}, u32[]{:S(2)}) copy-start(f32[2,8,4096]{1,0,2:T(2,128)} %get-tuple-element.82) | copy-start | bytes 786436
  104.9 8.4 %copy-start.4 = (f32[2,8,4096]{1,0,2:T(2,128)S(1)}, f32[2,8,4096]{1,0,2:T(2,128)}, u32[]{:S(2)}) copy-start(f32[2,8,4096]{1,0,2:T(2,128)} %get-tuple-element.99) | copy-start | bytes 786436
  104.9 8.4 %copy-start.71 = (f32[2,8]{1,0:T(2,128)S(1)}, f32[2,8]{1,0:T(2,128)}, u32[]{:S(2)}) copy-start(f32[2,8]{1,0:T(2,128)} %get-tuple-element.86) | copy-start | bytes 196
  111.5 9.2 %copy-start.1 = (f32[2,8,8320]{1,0,2:T(2,128)}, f32[2,8,8320]{1,0,2:T(2,128)S(1)}, u32[]{:S(2)}) copy-start(f32[2,8,8320]{1,0,2:T(2,128)S(1)} %fusion.1) | copy-start | bytes 1597444
  151.5 14.3 %slice-start = ((s8[8519680]{0:T(1024)(128)(4,1)}), s8[131072]{0:T(1024)(128)(4,1)S(1)}, s32[]{:S(2)}) async-start(s8[8519680]{0:T(1024)(128)(4,1)} %bitcast.262), calls=%async_computation | async-start | bytes 262144
  158.2 7.6 %slice-start.1 = ((s8[8519680]{0:T(1024)(128)(4,1)}), s8[4194304]{0:T(1024)(128)(4,1)S(1)}, s32[]{:S(2)}) async-start(s8[8519680]{0:T(1024)(128)(4,1)} %bitcast.262), calls=%async_computation.1 | async-start | bytes 8388608
  158.2 7.6 %slice-start.2 = ((s8[8519680]{0:T(1024)(128)(4,1)}), s8[4194304]{0:T(1024)(128)(4,1)S(1)}, s32[]{:S(2)}) async-start(s8[8519680]{0:T(1024)(128)(4,1)} %bitcast.262), calls=%async_computation.2 | async-start | bytes 8388608
  158.2 7.6 %copy-start.2 = (f32[2,8,8320]{1,0,2:T(2,128)S(1)}, f32[2,8,8320]{1,0,2:T(2,128)}, u32[]{:S(2)}) copy-start(f32[2,8,8320]{1,0,2:T(2,128)} %copy-done.1) | copy-start | bytes 1597444
  158.2 7.6 %copy-start.64 = (f32[2,8]{1,0:T(2,128)S(1)}, f32[2,8]{1,0:T(2,128)}, u32[]{:S(2)}) copy-start(f32[2,8]{1,0:T(2,128)} %get-tuple-element.93) | copy-start | bytes 196
  158.2 7.6 %copy-start.65 = (f32[2,8]{1,0:T(2,128)S(1)}, f32[2,8]{1,0:T(2,128)}, u32[]{:S(2)}) copy-start(f32[2,8]{1,0:T(2,128)} %get-tuple-element.95) | copy-start | bytes 196
  158.2 7.6 %copy-start.66 = (f32[2,8]{1,0:T(2,128)S(1)}, f32[2,8]{1,0:T(2,128)}, u32[]{:S(2)}) copy-start(f32[2,8]{1,0:T(2,128)} %get-tuple-element.101) | copy-start | bytes 196
  158.2 7.6 %copy-start.67 = (f32[2,8]{1,0:T(2,128)S(1)}, f32[2,8]{1,0:T(2,128)}, u32[]{:S(2)}) copy-start(f32[2,8]{1,0:T(2,128)} %get-tuple-element.102) | copy-start | bytes 196
  183.1 9.2 %copy-start.22 = (f32[256,2,8]{0,2,1:T(8,128)}, f32[256,2,8]{0,2,1:T(8,128)S(1)}, u32[]{:S(2)}) copy-start(f32[256,2,8]{0,2,1:T(8,128)S(1)} %get-tuple-element.137) | copy-start | bytes 49156
  183.5 8.8 %copy-start.20 = (f32[256,16]{0,1:S(1)}, f32[256,16]{0,1}, u32[]{:S(2)}) copy-start(f32[256,16]{0,1} %copy-done.19) | copy-start | bytes 49156
  183.5 8.8 %copy-start.28 = (f32[256,2,8]{0,2,1:T(8,128)S(1)}, f32[256,2,8]{0,2,1:T(8,128)}, u32[]{:S(2)}) copy-start(f32[256,2,8]{0,2,1:T(8,128)} %param.23) | copy-start | bytes 49156
  183.5 8.8 %copy-start.41 = (f32[2,8]{1,0:T(2,128)S(1)}, f32[2,8]{1,0:T(2,128)}, u32[]{:S(2)}) copy-start(f32[2,8]{1,0:T(2,128)} %copy-done.40) | copy-start | bytes 196
  183.5 8.8 %copy-start.68 = (f32[2,8]{1,0:T(2,128)S(1)}, f32[2,8]{1,0:T(2,128)}, u32[]{:S(2)}) copy-start(f32[2,8]{1,0:T(2,128)} %param.25) | copy-start | bytes 196
  183.5 10.2 %copy-start.24 = (pred[256,256]{1,0:T(8,128)(4,1)S(1)}, pred[256,256]{1,0:T(8,128)(4,1)}, u32[]{:S(2)}) copy-start(pred[256,256]{1,0:T(8,128)(4,1)} %iota_compare_fusion) | copy-start | bytes 196612
  193.7 7.6 %copy-start.47 = (f32[2,64]{1,0:T(2,128)S(1)}, f32[2,64]{1,0:T(2,128)}, u32[]{:S(2)}) copy-start(f32[2,64]{1,0:T(2,128)} %copy-done.46) | copy-start | bytes 1540
  193.7 7.6 %copy-start.49 = (f32[2,64]{1,0:T(2,128)S(1)}, f32[2,64]{1,0:T(2,128)}, u32[]{:S(2)}) copy-start(f32[2,64]{1,0:T(2,128)} %copy-done.48) | copy-start | bytes 1540
  193.7 7.6 %copy-start.51 = (f32[2,64]{1,0:T(2,128)S(1)}, f32[2,64]{1,0:T(2,128)}, u32[]{:S(2)}) copy-start(f32[2,64]{1,0:T(2,128)} %copy-done.50) | copy-start | bytes 1540
  193.7 7.6 %copy-start.53 = (f32[2,64]{1,0:T(2,128)S(1)}, f32[2,64]{1,0:T(2,128)}, u32[]{:S(2)}) copy-start(f32[2,64]{1,0:T(2,128)} %copy-done.52) | copy-start | bytes 1540
  205.2 8.0 %copy-start.13 = (f32[2,256,256]{2,1,0:T(8,128)S(1)}, f32[2,256,256]{2,1,0:T(8,128)}, u32[]{:S(2)}) copy-start(f32[2,256,256]{2,1,0:T(8,128)} %fusion.153) | copy-start | bytes 1572868
  205.2 8.0 %copy-start.21 = (f32[256,16]{0,1:S(1)}, f32[256,16]{0,1}, u32[]{:S(2)}) copy-start(f32[256,16]{0,1} %copy-done.19) | copy-start | bytes 49156
  205.2 8.0 %copy-start.25 = (pred[256,256]{1,0:T(8,128)(4,1)S(1)}, pred[256,256]{1,0:T(8,128)(4,1)}, u32[]{:S(2)}) copy-start(pred[256,256]{1,0:T(8,128)(4,1)} %iota_compare_fusion) | copy-start | bytes 196612
  211.8 8.7 %collective-permute-start.1 = (f32[3,1280]{1,0:T(4,128)S(1)}, f32[3,1280]{1,0:T(4,128)S(1)}, u32[]{:S(2)}, u32[]{:S(2)}) collective-permute-start(f32[3,1280]{1,0:T(4,128)S(1)} %pad_maximum_fusion.5), channel_id=1, source_target_pairs={{2,0},{4,2},{6,4},{8,6},{10,8},{12,10},{14,12},{3,1},{5,3},{7,5},{... | collective-permute-start | bytes 46088 | tf_op jit(solution)/shard_map/ppermute | solution.py:13
  (34 other events, 138.6 us)

commit v7 on v5

--- a/solution.py
+++ b/solution.py
@@ -1,6 +1,7 @@
 import jax
 import jax.numpy as jnp
 from jax import lax
+from jax.experimental import pallas as pl
 from jax.sharding import PartitionSpec as P
 
 HIGH = lax.Precision.HIGHEST
@@ -119,6 +120,100 @@
     return y_local + skip[None, :, :, None] * x_heads
 
 
+def mix_kernel(x_ref, gy_ref, c_ref, b_ref, cum_col_ref, cum_row_ref, step_row_ref,
+               y_ref, dx_ref, ds_ref, dcum_t_ref, dcum_s_ref, dstep_ref):
+    groups = c_ref.shape[0]
+    length = x_ref.shape[0]
+    pairs = x_ref.shape[1] // (groups * 128)
+    row = lax.broadcasted_iota(jnp.int32, (length, length), 0)
+    col = lax.broadcasted_iota(jnp.int32, (length, length), 1)
+    causal = row >= col
+    lane = lax.broadcasted_iota(jnp.int32, (length, 128), 1)
+    low = lane < 64
+    for g in range(groups):
+        scores = lax.dot_general(c_ref[g], b_ref[g], (((1,), (1,)), ((), ())),
+                                 precision=HIGH, preferred_element_type=jnp.float32)
+        ds_acc = jnp.zeros((length, length), jnp.float32)
+        for k in range(pairs):
+            lanes = pl.ds(g * pairs * 128 + k * 128, 128)
+            xp = x_ref[:, lanes]
+            gp = gy_ref[:, lanes]
+            ys = []
+            dxs = []
+            for j in range(2):
+                gh = g * pairs * 2 + 2 * k + j
+                gap = cum_col_ref[:, pl.ds(gh, 1)] - cum_row_ref[pl.ds(gh, 1), :]
+                decay = jnp.where(causal, jnp.exp(jnp.where(causal, gap, 0.0)), 0.0)
+                step = step_row_ref[pl.ds(gh, 1), :]
+                sd = scores * decay
+                mixing = (sd * step).astype(jnp.bfloat16)
+                ys.append(jnp.dot(mixing, xp, preferred_element_type=jnp.float32))
+                gm = jnp.where(low if j == 0 else jnp.logical_not(low), gp, jnp.zeros_like(gp))
+                dmix = lax.dot_general(gm, xp, (((1,), (1,)), ((), ())),
+                                       preferred_element_type=jnp.float32)
+                dmix = dmix.astype(jnp.bfloat16).astype(jnp.float32)
+                dxs.append(lax.dot_general(mixing, gp, (((0,), (0,)), ((), ())),
+                                           preferred_element_type=jnp.float32))
+                dsd = dmix * step
+                ds_acc = ds_acc + dsd * decay
+                dgap = dsd * scores * decay
+                dcum_t_ref[:, pl.ds(gh, 1)] = jnp.sum(dgap, axis=1, keepdims=True)
+                dcum_s_ref[pl.ds(gh, 1), :] = -jnp.sum(dgap, axis=0, keepdims=True)
+                dstep_ref[pl.ds(gh, 1), :] = jnp.sum(dmix * sd, axis=0, keepdims=True)
+            y_ref[:, lanes] = jnp.where(low, ys[0], ys[1])
+            dx_ref[:, lanes] = jnp.where(low, dxs[0], dxs[1])
+        ds_ref[g] = ds_acc
+
+
+def mix_call(x_flat, gy_flat, c_groups, b_groups, cum_col, cum_row, step_row):
+    length, width = x_flat.shape
+    groups = c_groups.shape[0]
+    heads = cum_col.shape[1]
+    f32 = jnp.float32
+    out_shape = (
+        jax.ShapeDtypeStruct((length, width), f32),
+        jax.ShapeDtypeStruct((length, width), f32),
+        jax.ShapeDtypeStruct((groups, length, length), f32),
+        jax.ShapeDtypeStruct((length, heads), f32),
+        jax.ShapeDtypeStruct((heads, length), f32),
+        jax.ShapeDtypeStruct((heads, length), f32),
+    )
+    return pl.pallas_call(mix_kernel, out_shape=out_shape)(
+        x_flat, gy_flat, c_groups, b_groups, cum_col, cum_row, step_row)
+
+
+def mix_grads(x_float, b_float, c_float, dt_raw, grad_heads, rate, dt_bias, skip):
+    length, groups, channels = x_float.shape
+    heads = dt_raw.shape[2]
+    step_size, cum_log = ssd_cum(dt_raw, rate, dt_bias)
+    cum_col = cum_log.reshape(length, groups * heads)
+    grad_flat = grad_heads.reshape(length, groups * channels)
+    y_mix, dx_mix, d_scores, dcum_t, dcum_s, dstep = mix_call(
+        x_float.reshape(length, groups * channels).astype(jnp.bfloat16),
+        grad_flat.astype(jnp.bfloat16),
+        jnp.transpose(c_float, (1, 0, 2)),
+        jnp.transpose(b_float, (1, 0, 2)),
+        cum_col,
+        cum_col.T,
+        step_size.reshape(length, groups * heads).T,
+    )
+    skip_lanes = jnp.repeat(skip.reshape(groups * heads), channels // heads)[None, :]
+    y_local = (y_mix + skip_lanes * x_float.reshape(length, -1)).reshape(
+        length, groups, heads, channels // heads
+    )
+    grad_x = (dx_mix + skip_lanes * grad_flat).reshape(length, groups, channels)
+    grad_c = jnp.einsum("gts,sgn->tgn", d_scores, b_float, precision=HIGH)
+    grad_b = jnp.einsum("gts,tgn->sgn", d_scores, c_float, precision=HIGH)
+    grad_cum = (dcum_t + dcum_s.T).reshape(length, groups, heads)
+    row_index = lax.broadcasted_iota(jnp.int32, (length, length), 0)
+    col_index = lax.broadcasted_iota(jnp.int32, (length, length), 1)
+    lower = (row_index >= col_index).astype(jnp.float32)
+    grad_log = jnp.einsum("ts,tgh->sgh", lower, grad_cum, precision=HIGH)
+    grad_step = dstep.T.reshape(length, groups, heads) - rate * grad_log
+    grad_dt = grad_step * jax.nn.sigmoid(dt_raw + dt_bias)
+    return y_local, (grad_x, grad_b, grad_c, grad_dt)
+
+
 def ssd_state(x_float, b_float, dt_raw, rate, dt_bias):
     length, groups, channels = x_float.shape
     head_count = dt_raw.shape[2]
@@ -181,8 +276,9 @@
         "tghp,tgn->ghpn", jnp.exp(cum_log)[..., None] * grad_heads, c_float, precision=HIGH
     )
 
-    y_local, mix_pull = jax.vjp(mix_map, x_float, b_float, c_float, dt_in)
-    mix_x, mix_b, mix_c, mix_dt = mix_pull(grad_heads)
+    y_local, (mix_x, mix_b, mix_c, mix_dt) = mix_grads(
+        x_float, b_float, c_float, dt_in, grad_heads, rate, dt_bias, skip
+    )
     state_in, adjoint, _ = scanned_pair(decay_total, state_end, seed_state, "ctx", [])
 
     def carry_map(c_arg, cum_arg):

time: 96.4 us -> 123 us (1.28)
  local copies, waits for them, and re-layouts: 16.8 us -> 32.7 us
  other arithmetic: 13.4 us -> 27.4 us
  matrix products: 20.4 us -> 11.7 us
  Pallas kernels: 0 us -> 7.41 us
  waiting for transfers between devices: 20.8 us -> 16.2 us
  starting transfers between devices: 22.4 us -> 23.9 us
    dot_general x6 -> x2, matrix products: 12.6 us -> 0.72 us  [the longest x1 0.39 us: mix_grads(): grad_c = jnp.einsum('gts,sgn->tgn', d_scores, b_float, precision=HIGH)]
    pallas_call x0 -> x1, Pallas kernels: none -> 7.41 us  [mix_call(): pl.pallas_call(mix_kernel, out_shape=out_shape)]
    reshape x0 -> x8, local copies, waits for them, and re-layouts: none -> 5.49 us  [the longest x1 2.29 us: ssd_state(): x_heads = x_float.reshape(length, groups, head_count, head_size)]
    unnamed x129 -> x186, local copies, waits for them, and re-layouts: 5.13 us -> 9.5 us
    ppermute x6, waiting for transfers between devices: 19.5 us -> 16.2 us  [shift(): return lax.ppermute(packed, axis, pairs)]
    add x0 -> x1, other arithmetic: none -> 3.27 us  [mix_grads(): grad_x = (dx_mix + skip_lanes * grad_flat).reshape(length, groups, channels)]
    dot_general x3, matrix products: 2.52 us -> 5.11 us  [ssd_state(): jnp.einsum('sghp,sgn->ghpn', weighted.astype(jnp.float32), b_float, preci...]
    reshape x2, local copies, waits for them, and re-layouts: 0.43 us -> 2.22 us  [scanned_pair(): w[1].reshape(groups, heads, rows, cols)]
  transfers between devices with their start and end apart: 8 -> 8, of which waited for: 7 -> 5; matrix products, arithmetic and copies ran while one was open for 12% -> 18% of each run, Pallas kernels for 0% -> 0%
where the time goes in v7:
time: 123 us; the launch traced here: 121 us
  local copies, waits for them, and re-layouts  32.7 us (27%)
  other arithmetic  27.4 us (22%)
  starting transfers between devices  23.9 us (19%)
  waiting for transfers between devices  16.2 us (13%)
  matrix products  11.7 us (10%)
  Pallas kernels  7.41 us (6%)
  between operations  1.96 us (2%)
    ppermute x6, starting transfers between devices, shift(): return lax.ppermute(packed, axis, pairs)  17.6 us
    ppermute x6, waiting for transfers between devices, shift(): return lax.ppermute(packed, axis, pairs)  16.2 us
    unnamed x186, local copies, waits for them, and re-layouts  9.5 us
    pallas_call x1, Pallas kernels, mix_call(): pl.pallas_call(mix_kernel, out_shape=out_shape)  7.41 us
    ppermute x2, starting transfers between devices, from_behind(): return lax.ppermute(array, axis, pairs)  6.27 us
    dot_general x3, matrix products, ssd_state(): jnp.einsum('sghp,sgn->ghpn', weighted.astype(jnp.float32), b_float, preci...  5.11 us
    convert_element_type x1, other arithmetic, on_device(): x_float = jax.nn.silu(x_running).astype(jnp.bfloat16).astype(jnp.float32)  4.12 us
    dot_general x2, matrix products, carry_in(): carried = jnp.einsum('tgn,ghpn->tghp', c_float, state_in, precision=HIGH)  3.28 us
  transfers between devices with their start and end apart: 8, of which 5 were waited for; matrix products, arithmetic and copies ran while one was open for 18% of the time, Pallas kernels for 0%

profile of v7, /device:TPU:0, one launch (start us, length us, event | category | flops | bytes accessed | tf_op | source)
XLA Modules:
  0.0 121.3 jit_solution(11825030807943864753)
XLA Ops:
  1.4 0.8 slice.295
  2.3 0.9 slice.296
  3.3 4.8 %collective-permute-start = (bf16[3,1280]{1,0:T(4,128)(2,1)S(1)}, bf16[3,1280]{1,0:T(4,128)(2,1)S(1)}, u32[]{:S(2)}, u32[]{:S(2)}) collective-permute-start(bf16[3,1280]{1,0:T(4,128)(2,1)S(1)} %pad_maximum_fusion.9), channel_id=1, source_target_pairs={{0,2},{2,4},{4,6},{6,8},{8,10},{10,12},{12,14},{1,3},{3,5},{5,7},{... | collective-permute-start | bytes 23048 | tf_op jit(solution)/shard_map/ppermute | solution.py:13
  10.3 0.9 fusion.20
  11.5 0.8 slice_bitcast_fusion.5
  12.3 1.4 %fusion.41 = (f32[256,2,8]{0,2,1:T(8,128)}, f32[256,2,8]{0,2,1:T(8,128)S(1)}) fusion(f32[2,8]{1,0:T(2,128)S(1)} %slice_reduce_fusion, f32[256,16]{0,1:S(1)} %fusion.20, f32[256,2,8]{0,2,1:T(8,128)} %param.22, f32[2,8]{1,0:T(2,128)} %param.24), kind=kLoop, calls=%fused_computation.100 | loop fusion | flops 36864 | bytes 65664 | tf_op jit(solution)/shard_map/jvp()/mul | solution.py:223
  14.3 1.0 copy.197
  15.3 1.0 copy.194
  17.5 1.2 convert_bitcast_fusion
  20.3 4.1 %fusion.17 = (f32[256,2,512]{2,1,0:T(2,128)S(1)}, f32[256,2,512]{2,1,0:T(2,128)}) fusion(bf16[256,2,512]{2,1,0:T(2,128)(2,1)} %param.19, f32[2,512]{1,0:T(2,128)S(1)} %get-tuple-element.121, bf16[259,2,512]{2,1,0:T(2,128)(2,1)S(1)} %constant_dynamic-update-slice_fusion, f32[2,512]{1,0:T(2,128)S(1)} %get-tuple-element.122, ...), kind=kLoop, calls=%fused_computation.37 | loop fusion | flops 4456448 | bytes 4210688 | tf_op jit(solution)/shard_map/convert_element_type | solution.py:262
  25.2 1.1 fusion.21
  26.3 1.2 %reshape.255 = f32[2,8,4096]{2,1,0:T(8,128)S(1)} reshape(f32[2,8,64,64]{3,2,1,0:T(8,128)} %fusion.21) | data formatting | bytes 524288 | tf_op jit(solution)/shard_map/reshape | solution.py:43
  27.6 0.9 pad_maximum_fusion.1
  28.5 3.5 %collective-permute-start.1 = (bf16[2,8,4224]{2,1,0:T(8,128)(2,1)S(1)}, bf16[2,8,4224]{2,1,0:T(8,128)(2,1)S(1)}, u32[]{:S(2)}, u32[]{:S(2)}) collective-permute-start(bf16[2,8,4224]{2,1,0:T(8,128)(2,1)S(1)} %get-tuple-element.127), channel_id=1, source_target_pairs={{0,2},{2,4},{4,6},{6,8},{8,10},{10,12},{12,14},{1,3},{3,5},{5,7},{... | collective-permute-start | bytes 405512 | tf_op jit(solution)/shard_map/ppermute | solution.py:28
  32.0 1.4 %collective-permute-start.4 = (bf16[2,8,4224]{2,1,0:T(8,128)(2,1)S(1)}, bf16[2,8,4224]{2,1,0:T(8,128)(2,1)S(1)}, u32[]{:S(2)}, u32[]{:S(2)}) collective-permute-start(bf16[2,8,4224]{2,1,0:T(8,128)(2,1)S(1)} %get-tuple-element.128), channel_id=1, source_target_pairs={{2,0},{4,2},{6,4},{8,6},{10,8},{12,10},{14,12},{3,1},{5,3},{7,5},{... | collective-permute-start | bytes 405512 | tf_op jit(solution)/shard_map/ppermute | solution.py:28
  33.5 1.1 collective-permute-done.1
  34.7 4.4 %collective-permute-done.4 = bf16[2,8,4224]{2,1,0:T(8,128)(2,1)S(1)} collective-permute-done((bf16[2,8,4224]{2,1,0:T(8,128)(2,1)S(1)}, bf16[2,8,4224]{2,1,0:T(8,128)(2,1)S(1)}, u32[]{:S(2)}, u32[]{:S(2)}) %collective-permute-start.4) | collective-permute-done | bytes 135200 | tf_op jit(solution)/shard_map/ppermute | solution.py:28
  39.4 3.7 %collective-permute-start.2 = (bf16[2,8,4224]{2,1,0:T(8,128)(2,1)S(1)}, bf16[2,8,4224]{2,1,0:T(8,128)(2,1)S(1)}, u32[]{:S(2)}, u32[]{:S(2)}) collective-permute-start(bf16[2,8,4224]{2,1,0:T(8,128)(2,1)S(1)} %pad_maximum_fusion.2), channel_id=1, source_target_pairs={{0,4},{2,6},{4,8},{6,10},{8,12},{10,14},{1,5},{3,7},{5,9},{7,11},{... | collective-permute-start | bytes 405512 | tf_op jit(solution)/shard_map/ppermute | solution.py:28
  43.1 2.5 %collective-permute-done.2 = bf16[2,8,4224]{2,1,0:T(8,128)(2,1)S(1)} collective-permute-done((bf16[2,8,4224]{2,1,0:T(8,128)(2,1)S(1)}, bf16[2,8,4224]{2,1,0:T(8,128)(2,1)S(1)}, u32[]{:S(2)}, u32[]{:S(2)}) %collective-permute-start.2) | collective-permute-done | bytes 135200 | tf_op jit(solution)/shard_map/ppermute | solution.py:28
  45.7 0.8 add_convert_fusion.3
  47.2 1.3 %collective-permute-start.5 = (bf16[2,8,4224]{2,1,0:T(8,128)(2,1)}, bf16[2,8,4224]{2,1,0:T(8,128)(2,1)}, u32[]{:S(2)}, u32[]{:S(2)}) collective-permute-start(bf16[2,8,4224]{2,1,0:T(8,128)(2,1)} %pad_maximum_fusion.4), channel_id=1, source_target_pairs={{4,0},{6,2},{8,4},{10,6},{12,8},{14,10},{5,1},{7,3},{9,5},{11,7},{... | collective-permute-start | bytes 405512 | tf_op jit(solution)/shard_map/ppermute | solution.py:28
  48.5 1.4 %convert_element_type.145 = f32[256,2,512]{2,1,0:T(2,128)} convert(bf16[256,2,512]{2,1,0:T(2,128)(2,1)S(1)} %copy-done.19) | non-fusion elementwise | flops 262144 | bytes 1572864 | tf_op jit(solution)/shard_map/convert_element_type | solution.py:274
  51.4 1.4 %copy.249 = f32[32,8,2,512]{3,1,2,0:T(8,128)S(1)} copy(f32[32,8,2,512]{3,2,1,0:T(2,128)} %bitcast.182) | data formatting | bytes 2097152
  52.9 0.9 convert_element_type.146.gy_ref
  54.6 0.9 convert_element_type.144.x_ref
  55.4 1.0 convert_element_type.163
  56.9 6.4 %collective-permute-start.3 = (bf16[2,8,4224]{2,1,0:T(8,128)(2,1)S(1)}, bf16[2,8,4224]{2,1,0:T(8,128)(2,1)S(1)}, u32[]{:S(2)}, u32[]{:S(2)}) collective-permute-start(bf16[2,8,4224]{2,1,0:T(8,128)(2,1)S(1)} %pad_maximum_fusion.3), channel_id=1, source_target_pairs={{0,8},{2,10},{4,12},{6,14},{1,9},{3,11},{5,13},{7,15},{16,24},{18,... | collective-permute-start | bytes 405512 | tf_op jit(solution)/shard_map/ppermute | solution.py:28
  63.4 1.3 %collective-permute-start.6 = (bf16[2,8,4224]{2,1,0:T(8,128)(2,1)S(1)}, bf16[2,8,4224]{2,1,0:T(8,128)(2,1)S(1)}, u32[]{:S(2)}, u32[]{:S(2)}) collective-permute-start(bf16[2,8,4224]{2,1,0:T(8,128)(2,1)S(1)} %pad_maximum_fusion.5), channel_id=1, source_target_pairs={{8,0},{10,2},{12,4},{14,6},{9,1},{11,3},{13,5},{15,7},{24,16},{26,... | collective-permute-start | bytes 405512 | tf_op jit(solution)/shard_map/ppermute | solution.py:28
  64.9 1.0 collective-permute-done.3
  65.9 7.3 %collective-permute-done.6 = bf16[2,8,4224]{2,1,0:T(8,128)(2,1)S(1)} collective-permute-done((bf16[2,8,4224]{2,1,0:T(8,128)(2,1)S(1)}, bf16[2,8,4224]{2,1,0:T(8,128)(2,1)S(1)}, u32[]{:S(2)}, u32[]{:S(2)}) %collective-permute-start.6) | collective-permute-done | bytes 135200 | tf_op jit(solution)/shard_map/ppermute | solution.py:28
  73.1 1.6 %multiply_reduce_fusion.2 = (f32[2,8]{1,0:T(2,128)}, f32[2,8,4096]{2,1,0:T(8,128)}, f32[2,8,4096]{2,1,0:T(8,128)}) fusion(f32[2,8,4224]{2,1,0:T(8,128)S(1)} %copy-done.8, f32[2,8,4224]{2,1,0:T(8,128)S(1)} %convert_element_type.163, f32[2,8]{1,0:T(2,128)S(1)} %get-tuple-element.91, bf16[2,8,4224]{2,1,0:T(8,128)(2,1)S(1)} %collective-permute-done.6, ...), kind=kLoop, calls=%fused_computation.46 | loop fusion | flops 786416 | bytes 1835328 | tf_op jit(solution)/shard_map/reduce_sum | solution.py:290
  74.7 2.0 %reshape.260 = f32[2,8,64,64]{3,2,1,0:T(8,128)} reshape(f32[2,8,4096]{2,1,0:T(8,128)} %get-tuple-element.99) | data formatting | bytes 524288 | tf_op jit(solution)/shard_map/reshape | solution.py:63
  76.7 2.4 %convolution_bitcast_fusion.3 = f32[2,64,256]{2,1,0:T(8,128)} fusion(f32[2,8,64,64]{3,2,1,0:T(8,128)} %reshape.260, f32[256,2,8,64]{0,3,2,1:T(8,128)S(1)} %bitcast.174, f32[256,2,8]{0,2,1:T(8,128)} %get-tuple-element.117), kind=kOutput, calls=%fused_computation.10 | convolution fusion | flops 201850880 | bytes 1458176 | tf_op jit(solution)/shard_map/transpose(jvp(sghp,sgn->ghpn))/dot_general | solution.py:225
  79.1 1.6 %multiply_reduce_fusion.1 = (f32[256,2,8]{0,2,1:T(8,128)S(1)}, f32[256,2,8,64]{0,3,2,1:T(8,128)}) fusion(f32[256,2,512]{0,2,1:T(8,128)S(1)} %copy.201, f32[256,2,8]{0,2,1:T(8,128)S(1)} %copy-done.40, f32[2,8,64,64]{3,2,1,0:T(8,128)S(1)} %copy-done.6, bf16[256,2,64]{2,0,1:T(8,128)(2,1)S(1)} %copy-done.21), kind=kOutput, calls=%fused_computation.24 | convolution fusion | flops 202633216 | bytes 2457600 | tf_op jit(solution)/shard_map/transpose(jvp(sghp,sgn->ghpn))/dot_general | solution.py:225
  81.5 2.3 %copy.209 = f32[256,2,512]{2,1,0:T(2,128)} copy(f32[256,2,512]{0,2,1:T(8,128)} %bitcast.181) | data formatting | bytes 2097152 | tf_op jit(solution)/shard_map/transpose(jvp())/reshape | solution.py:222
  86.2 2.6 %convolution_bitcast_fusion.2 = f32[256,2,64]{2,0,1:T(8,128)} fusion(f32[2,8,64,64]{3,2,1,0:T(8,128)S(1)} %reshape.256, f32[256,2,8,64]{0,3,2,1:T(8,128)S(1)} %bitcast.172, f32[256,2,8]{0,2,1:T(8,128)S(1)} %copy-done.37), kind=kOutput, calls=%fused_computation.6 | convolution fusion | flops 201588736 | bytes 1458176 | tf_op jit(solution)/shard_map/transpose(jvp(tgn,ghpn->tghp))/dot_general | solution.py:230
  88.8 7.4 %shard_map.146 = (f32[256,1024]{1,0:T(8,128)}, f32[256,1024]{1,0:T(8,128)}, f32[2,256,256]{2,1,0:T(8,128)}, f32[256,16]{1,0:T(8,128)}, f32[16,256]{1,0:T(8,128)}, /*index=5*/f32[16,256]{1,0:T(8,128)}) custom-call(bf16[256,1024]{1,0:T(8,128)(2,1)} %convert_element_type.144.x_ref, bf16[256,1024]{1,0:T(8,128)(2,1)} %convert_element_type.146.gy_ref, ...), custom_call_target="tpu_custom_call" | custom-call | tf_op jit(solution)/shard_map/pallas_call | solution.py:181
  96.2 3.3 %multiply_add_fusion.1 = (f32[256,1024]{1,0:T(8,128)}, f32[256,1024]{1,0:T(8,128)}) fusion(f32[256,1024]{1,0:T(8,128)} %get-tuple-element.60, f32[256,1024]{1,0:T(8,128)S(1)} %bitcast.176, f32[1024]{0:T(1024)S(1)} %copy-done.57, f32[256,1024]{1,0:T(8,128)} %get-tuple-element.59, f32[256,1024]{1,0:T(8,128)S(1)} %bitcast.178), kind=kLoop, calls=%fused_computation.27 | loop fusion | flops 1048576 | bytes 6295552 | tf_op jit(solution)/shard_map/add | solution.py:204
  99.5 2.2 %reshape.257 = f32[256,2,512]{2,1,0:T(2,128)S(1)} reshape(f32[256,1024]{1,0:T(8,128)} %get-tuple-element.125) | data formatting | bytes 2097152 | tf_op jit(solution)/shard_map/reshape | solution.py:204
  101.7 2.7 %multiply_multiply_fusion = f32[256,2,512]{2,1,0:T(2,128)S(1)} fusion(f32[256,2,512]{2,1,0:T(2,128)} %get-tuple-element.108, f32[256,2,512]{2,1,0:T(2,128)S(1)} %reshape.257, f32[256,2,512]{2,1,0:T(2,128)S(1)} %copy-done.12), kind=kLoop, calls=%fused_computation.25 | loop fusion | flops 2883584 | bytes 4194304 | tf_op jit(solution)/shard_map/mul | solution.py:80
  104.5 1.3 %multiply_add_fusion = f32[259,2,512]{2,1,0:T(2,128)S(1)} fusion(f32[256,2,512]{2,1,0:T(2,128)S(1)} %multiply_multiply_fusion, f32[2,512]{1,0:T(2,128)S(1)} %copy-done.48, f32[2,512]{1,0:T(2,128)S(1)} %copy-done.50, f32[2,512]{1,0:T(2,128)S(1)} %get-tuple-element.120, f32[2,512]{1,0:T(2,128)S(1)} %get-tuple-element.119), kind=kLoop, calls=%fused_computation.21 | loop fusion | flops 1856512 | bytes 2125824 | tf_op jit(solution)/shard_map/add | solution.py:88
  107.0 1.0 copy.221
  108.5 1.4 %collective-permute-start.7 = (f32[3,1280]{1,0:T(4,128)S(1)}, f32[3,1280]{1,0:T(4,128)S(1)}, u32[]{:S(2)}, u32[]{:S(2)}) collective-permute-start(f32[3,1280]{1,0:T(4,128)S(1)} %pad_maximum_fusion.8), channel_id=1, source_target_pairs={{2,0},{4,2},{6,4},{8,6},{10,8},{12,10},{14,12},{3,1},{5,3},{7,5},{... | collective-permute-start | bytes 46088 | tf_op jit(solution)/shard_map/ppermute | solution.py:13
  110.0 1.6 %copy.200 = f32[256,1024]{0,1:T(8,128)S(1)} copy(f32[256,1024]{1,0:T(8,128)} %get-tuple-element.126) | data formatting | bytes 2097152 | tf_op jit(solution)/shard_map/add | solution.py:201
  113.0 0.9 fusion.9
  113.8 1.0 slice.392
  114.8 1.0 slice.389
  116.2 1.2 copy.224
  (264 shorter events, 21.8 us)
Async XLA Ops:
  0.6 15.6 %copy-start.18 = (bf16[256,2,512]{2,1,0:T(2,128)(2,1)S(1)}, bf16[256,2,512]{2,1,0:T(2,128)(2,1)}, u32[]{:S(2)}) copy-start(bf16[256,2,512]{2,1,0:T(2,128)(2,1)} %param.29) | copy-start | bytes 1572868
  3.3 13.5 %collective-permute-start = (bf16[3,1280]{1,0:T(4,128)(2,1)S(1)}, bf16[3,1280]{1,0:T(4,128)(2,1)S(1)}, u32[]{:S(2)}, u32[]{:S(2)}) collective-permute-start(bf16[3,1280]{1,0:T(4,128)(2,1)S(1)} %pad_maximum_fusion.9), channel_id=1, source_target_pairs={{0,2},{2,4},{4,6},{6,8},{8,10},{10,12},{12,14},{1,3},{3,5},{5,7},{... | collective-permute-start | bytes 23048 | tf_op jit(solution)/shard_map/ppermute | solution.py:13
  8.8 8.0 %copy-start.82 = (f32[2,8]{1,0:T(2,128)}, f32[2,8]{1,0:T(2,128)S(1)}, u32[]{:S(2)}) copy-start(f32[2,8]{1,0:T(2,128)S(1)} %neg.33) | copy-start | bytes 196
  9.6 7.9 %copy-start.58 = (f32[2,64]{1,0:T(2,128)}, f32[2,64]{1,0:T(2,128)S(1)}, u32[]{:S(2)}) copy-start(f32[2,64]{1,0:T(2,128)S(1)} %get-tuple-element.129) | copy-start | bytes 1540
  9.6 7.9 %copy-start.60 = (f32[2,64]{1,0:T(2,128)}, f32[2,64]{1,0:T(2,128)S(1)}, u32[]{:S(2)}) copy-start(f32[2,64]{1,0:T(2,128)S(1)} %get-tuple-element.130) | copy-start | bytes 1540
  9.6 7.9 %copy-start.62 = (f32[2,64]{1,0:T(2,128)}, f32[2,64]{1,0:T(2,128)S(1)}, u32[]{:S(2)}) copy-start(f32[2,64]{1,0:T(2,128)S(1)} %get-tuple-element.131) | copy-start | bytes 1540
  9.6 7.9 %copy-start.64 = (f32[2,64]{1,0:T(2,128)}, f32[2,64]{1,0:T(2,128)S(1)}, u32[]{:S(2)}) copy-start(f32[2,64]{1,0:T(2,128)S(1)} %get-tuple-element.132) | copy-start | bytes 1540
  10.3 7.2 %copy-start.66 = (f32[2,64]{1,0:T(2,128)}, f32[2,64]{1,0:T(2,128)S(1)}, u32[]{:S(2)}) copy-start(f32[2,64]{1,0:T(2,128)S(1)} %get-tuple-element.133) | copy-start | bytes 1540
  10.3 7.2 %copy-start.68 = (f32[2,64]{1,0:T(2,128)}, f32[2,64]{1,0:T(2,128)S(1)}, u32[]{:S(2)}) copy-start(f32[2,64]{1,0:T(2,128)S(1)} %get-tuple-element.134) | copy-start | bytes 1540
  10.3 7.2 %copy-start.70 = (f32[2,64]{1,0:T(2,128)}, f32[2,64]{1,0:T(2,128)S(1)}, u32[]{:S(2)}) copy-start(f32[2,64]{1,0:T(2,128)S(1)} %get-tuple-element.135) | copy-start | bytes 1540
  10.3 7.2 %copy-start.72 = (f32[2,64]{1,0:T(2,128)}, f32[2,64]{1,0:T(2,128)S(1)}, u32[]{:S(2)}) copy-start(f32[2,64]{1,0:T(2,128)S(1)} %get-tuple-element.136) | copy-start | bytes 1540
  11.3 4.0 %copy-start.25 = (f32[256,16]{0,1}, f32[256,16]{0,1:S(1)}, u32[]{:S(2)}) copy-start(f32[256,16]{0,1:S(1)} %fusion.20) | copy-start | bytes 49156
  11.5 5.5 %copy-start.54 = (f32[2,8]{1,0:T(2,128)}, f32[2,8]{1,0:T(2,128)S(1)}, u32[]{:S(2)}) copy-start(f32[2,8]{1,0:T(2,128)S(1)} %slice_reduce_fusion) | copy-start | bytes 196
  11.5 5.6 %copy-start.17 = (bf16[256,2,512]{2,1,0:T(2,128)(2,1)S(1)}, bf16[256,2,512]{2,1,0:T(2,128)(2,1)}, u32[]{:S(2)}) copy-start(bf16[256,2,512]{2,1,0:T(2,128)(2,1)} %param.19) | copy-start | bytes 1572868
  12.3 8.0 %copy-start.47 = (f32[2,512]{1,0:T(2,128)}, f32[2,512]{1,0:T(2,128)S(1)}, u32[]{:S(2)}) copy-start(f32[2,512]{1,0:T(2,128)S(1)} %get-tuple-element.121) | copy-start | bytes 12292
  12.3 8.0 %copy-start.49 = (f32[2,512]{1,0:T(2,128)}, f32[2,512]{1,0:T(2,128)S(1)}, u32[]{:S(2)}) copy-start(f32[2,512]{1,0:T(2,128)S(1)} %get-tuple-element.122) | copy-start | bytes 12292
  13.7 5.0 %copy-start.36 = (f32[256,2,8]{0,2,1:T(8,128)}, f32[256,2,8]{0,2,1:T(8,128)S(1)}, u32[]{:S(2)}) copy-start(f32[256,2,8]{0,2,1:T(8,128)S(1)} %get-tuple-element.118) | copy-start | bytes 49156
  18.7 6.3 %copy-start.20 = (bf16[256,2,64]{2,0,1:T(8,128)(2,1)}, bf16[256,2,64]{2,0,1:T(8,128)(2,1)S(1)}, u32[]{:S(2)}) copy-start(bf16[256,2,64]{2,0,1:T(8,128)(2,1)S(1)} %get-tuple-element.102) | copy-start | bytes 196612
  19.6 4.8 %copy-start.9 = (f32[2,8,4096]{2,1,0:T(8,128)}, f32[2,8,4096]{2,1,0:T(8,128)S(1)}, u32[]{:S(2)}) copy-start(f32[2,8,4096]{2,1,0:T(8,128)S(1)} %reshape.259) | copy-start | bytes 786436
  26.3 8.3 %copy-start.52 = (f32[2,8]{1,0:T(2,128)S(1)}, f32[2,8]{1,0:T(2,128)}, u32[]{:S(2)}) copy-start(f32[2,8]{1,0:T(2,128)} %get-tuple-element.139) | copy-start | bytes 196
  27.5 11.6 %copy-start.26 = (f32[256,16]{0,1:S(1)}, f32[256,16]{0,1}, u32[]{:S(2)}) copy-start(f32[256,16]{0,1} %copy-done.25) | copy-start | bytes 49156
  28.5 6.0 %collective-permute-start.1 = (bf16[2,8,4224]{2,1,0:T(8,128)(2,1)S(1)}, bf16[2,8,4224]{2,1,0:T(8,128)(2,1)S(1)}, u32[]{:S(2)}, u32[]{:S(2)}) collective-permute-start(bf16[2,8,4224]{2,1,0:T(8,128)(2,1)S(1)} %get-tuple-element.127), channel_id=1, source_target_pairs={{0,2},{2,4},{4,6},{6,8},{8,10},{10,12},{12,14},{1,3},{3,5},{5,7},{... | collective-permute-start | bytes 405512 | tf_op jit(solution)/shard_map/ppermute | solution.py:28
  32.0 13.6 %copy-start.10 = (f32[2,8,4096]{2,1,0:T(8,128)S(1)}, f32[2,8,4096]{2,1,0:T(8,128)}, u32[]{:S(2)}) copy-start(f32[2,8,4096]{2,1,0:T(8,128)} %copy-done.9) | copy-start | bytes 786436
  32.0 7.0 %collective-permute-start.4 = (bf16[2,8,4224]{2,1,0:T(8,128)(2,1)S(1)}, bf16[2,8,4224]{2,1,0:T(8,128)(2,1)S(1)}, u32[]{:S(2)}, u32[]{:S(2)}) collective-permute-start(bf16[2,8,4224]{2,1,0:T(8,128)(2,1)S(1)} %get-tuple-element.128), channel_id=1, source_target_pairs={{2,0},{4,2},{6,4},{8,6},{10,8},{12,10},{14,12},{3,1},{5,3},{7,5},{... | collective-permute-start | bytes 405512 | tf_op jit(solution)/shard_map/ppermute | solution.py:28
  39.1 7.4 %copy-start.7 = (f32[2,8,4224]{2,1,0:T(8,128)}, f32[2,8,4224]{2,1,0:T(8,128)S(1)}, u32[]{:S(2)}) copy-start(f32[2,8,4224]{2,1,0:T(8,128)S(1)} %convert_element_type.162) | copy-start | bytes 811012
  39.3 7.2 %copy-start.78 = (f32[2,8]{1,0:T(2,128)}, f32[2,8]{1,0:T(2,128)S(1)}, u32[]{:S(2)}) copy-start(f32[2,8]{1,0:T(2,128)S(1)} %get-tuple-element.96) | copy-start | bytes 196
  39.4 6.2 %collective-permute-start.2 = (bf16[2,8,4224]{2,1,0:T(8,128)(2,1)S(1)}, bf16[2,8,4224]{2,1,0:T(8,128)(2,1)S(1)}, u32[]{:S(2)}, u32[]{:S(2)}) collective-permute-start(bf16[2,8,4224]{2,1,0:T(8,128)(2,1)S(1)} %pad_maximum_fusion.2), channel_id=1, source_target_pairs={{0,4},{2,6},{4,8},{6,10},{8,12},{10,14},{1,5},{3,7},{5,9},{7,11},{... | collective-permute-start | bytes 405512 | tf_op jit(solution)/shard_map/ppermute | solution.py:28
  43.1 5.4 %copy-start.19 = (bf16[256,2,512]{2,1,0:T(2,128)(2,1)S(1)}, bf16[256,2,512]{2,1,0:T(2,128)(2,1)}, u32[]{:S(2)}) copy-start(bf16[256,2,512]{2,1,0:T(2,128)(2,1)} %param.29) | copy-start | bytes 1572868
  45.7 4.2 %copy-start.15 = (f32[2,8,4224]{2,1,0:T(8,128)}, f32[2,8,4224]{2,1,0:T(8,128)S(1)}, u32[]{:S(2)}) copy-start(f32[2,8,4224]{2,1,0:T(8,128)S(1)} %convert_element_type.159) | copy-start | bytes 811012
  46.5 3.4 %copy-start.86 = (f32[2,8]{1,0:T(2,128)S(1)}, f32[2,8]{1,0:T(2,128)}, u32[]{:S(2)}) copy-start(f32[2,8]{1,0:T(2,128)} %param.25) | copy-start | bytes 196
  47.2 8.2 %collective-permute-start.5 = (bf16[2,8,4224]{2,1,0:T(8,128)(2,1)}, bf16[2,8,4224]{2,1,0:T(8,128)(2,1)}, u32[]{:S(2)}, u32[]{:S(2)}) collective-permute-start(bf16[2,8,4224]{2,1,0:T(8,128)(2,1)} %pad_maximum_fusion.4), channel_id=1, source_target_pairs={{4,0},{6,2},{8,4},{10,6},{12,8},{14,10},{5,1},{7,3},{9,5},{11,7},{... | collective-permute-start | bytes 405512 | tf_op jit(solution)/shard_map/ppermute | solution.py:28
  56.9 9.0 %collective-permute-start.3 = (bf16[2,8,4224]{2,1,0:T(8,128)(2,1)S(1)}, bf16[2,8,4224]{2,1,0:T(8,128)(2,1)S(1)}, u32[]{:S(2)}, u32[]{:S(2)}) collective-permute-start(bf16[2,8,4224]{2,1,0:T(8,128)(2,1)S(1)} %pad_maximum_fusion.3), channel_id=1, source_target_pairs={{0,8},{2,10},{4,12},{6,14},{1,9},{3,11},{5,13},{7,15},{16,24},{18,... | collective-permute-start | bytes 405512 | tf_op jit(solution)/shard_map/ppermute | solution.py:28
  63.4 9.7 %collective-permute-start.6 = (bf16[2,8,4224]{2,1,0:T(8,128)(2,1)S(1)}, bf16[2,8,4224]{2,1,0:T(8,128)(2,1)S(1)}, u32[]{:S(2)}, u32[]{:S(2)}) collective-permute-start(bf16[2,8,4224]{2,1,0:T(8,128)(2,1)S(1)} %pad_maximum_fusion.5), channel_id=1, source_target_pairs={{8,0},{10,2},{12,4},{14,6},{9,1},{11,3},{13,5},{15,7},{24,16},{26,... | collective-permute-start | bytes 405512 | tf_op jit(solution)/shard_map/ppermute | solution.py:28
  74.7 4.4 %copy-start.21 = (bf16[256,2,64]{2,0,1:T(8,128)(2,1)S(1)}, bf16[256,2,64]{2,0,1:T(8,128)(2,1)}, u32[]{:S(2)}) copy-start(bf16[256,2,64]{2,0,1:T(8,128)(2,1)} %copy-done.20) | copy-start | bytes 196612
  74.7 4.4 %copy-start.40 = (f32[256,2,8]{0,2,1:T(8,128)S(1)}, f32[256,2,8]{0,2,1:T(8,128)}, u32[]{:S(2)}) copy-start(f32[256,2,8]{0,2,1:T(8,128)} %get-tuple-element.117) | copy-start | bytes 49156
  80.7 3.7 %copy-start.43 = (f32[256,2,8]{0,2,1:T(8,128)}, f32[256,2,8]{0,2,1:T(8,128)S(1)}, u32[]{:S(2)}) copy-start(f32[256,2,8]{0,2,1:T(8,128)S(1)} %get-tuple-element.111) | copy-start | bytes 49156
  80.8 3.0 %copy-start.55 = (f32[2,8]{1,0:T(2,128)S(1)}, f32[2,8]{1,0:T(2,128)}, u32[]{:S(2)}) copy-start(f32[2,8]{1,0:T(2,128)} %copy-done.54) | copy-start | bytes 196
  80.8 3.0 %copy-start.75 = (f32[2,8]{1,0:T(2,128)S(1)}, f32[2,8]{1,0:T(2,128)}, u32[]{:S(2)}) copy-start(f32[2,8]{1,0:T(2,128)} %param.24) | copy-start | bytes 196
  81.5 3.7 %copy-start.23 = (f32[2,8,4096]{2,1,0:T(8,128)S(1)}, f32[2,8,4096]{2,1,0:T(8,128)}, u32[]{:S(2)}) copy-start(f32[2,8,4096]{2,1,0:T(8,128)} %get-tuple-element.100) | copy-start | bytes 786436
  81.5 4.7 %copy-start.37 = (f32[256,2,8]{0,2,1:T(8,128)S(1)}, f32[256,2,8]{0,2,1:T(8,128)}, u32[]{:S(2)}) copy-start(f32[256,2,8]{0,2,1:T(8,128)} %copy-done.36) | copy-start | bytes 49156
  88.8 7.4 %copy-start.1 = (f32[32,8,2,512]{3,1,2,0:T(8,128)S(1)}, f32[32,8,2,512]{3,1,2,0:T(8,128)}, u32[]{:S(2)}) copy-start(f32[32,8,2,512]{3,1,2,0:T(8,128)} %copy-done) | copy-start | bytes 3145732
  88.8 7.4 %copy-start.57 = (f32[1024]{0:T(1024)S(1)}, f32[1024]{0:T(1024)}, u32[]{:S(2)}) copy-start(f32[1024]{0:T(1024)} %mul.501) | copy-start | bytes 12292
  106.9 3.1 %copy-start.30 = (f32[259,2,64]{2,0,1:T(8,128)}, f32[259,2,64]{2,0,1:T(8,128)S(1)}, u32[]{:S(2)}) copy-start(f32[259,2,64]{2,0,1:T(8,128)S(1)} %multiply_add_fusion.4) | copy-start | bytes 397828
  108.4 3.1 %copy-start.31 = (f32[259,2,64]{2,0,1:T(8,128)}, f32[259,2,64]{2,0,1:T(8,128)S(1)}, u32[]{:S(2)}) copy-start(f32[259,2,64]{2,0,1:T(8,128)S(1)} %multiply_add_fusion.5) | copy-start | bytes 397828
  108.5 3.0 %copy-start.5 = (f32[2,8,64,64]{3,2,1,0:T(8,128)S(1)}, f32[2,8,64,64]{3,2,1,0:T(8,128)}, u32[]{:S(2)}) copy-start(f32[2,8,64,64]{3,2,1,0:T(8,128)} %copy-done.4) | copy-start | bytes 786436
  108.5 3.0 %copy-start.38 = (f32[256,2,8]{0,2,1:T(8,128)S(1)}, f32[256,2,8]{0,2,1:T(8,128)}, u32[]{:S(2)}) copy-start(f32[256,2,8]{0,2,1:T(8,128)} %copy-done.36) | copy-start | bytes 49156
  108.5 8.8 %collective-permute-start.7 = (f32[3,1280]{1,0:T(4,128)S(1)}, f32[3,1280]{1,0:T(4,128)S(1)}, u32[]{:S(2)}, u32[]{:S(2)}) collective-permute-start(f32[3,1280]{1,0:T(4,128)S(1)} %pad_maximum_fusion.8), channel_id=1, source_target_pairs={{2,0},{4,2},{6,4},{8,6},{10,8},{12,10},{14,12},{3,1},{5,3},{7,5},{... | collective-permute-start | bytes 46088 | tf_op jit(solution)/shard_map/ppermute | solution.py:13
  112.4 3.4 %copy-start.14 = (f32[259,2,512]{2,1,0:T(2,128)S(1)}, f32[259,2,512]{2,1,0:T(2,128)}, u32[]{:S(2)}) copy-start(f32[259,2,512]{2,1,0:T(2,128)} %copy-done.13) | copy-start | bytes 3182596
  (47 other events, 72.5 us)

commit v8 on v4

--- a/solution.py
+++ b/solution.py
@@ -12,47 +12,44 @@
     return lax.ppermute(array, axis, pairs)
 
 
-def scanned_pair(decay, forward_state, backward_state, axis, riders):
+def butterfly_pair(decay, forward_state, backward_state, axis):
     count = lax.axis_size(axis)
+    place = lax.axis_index(axis)
     groups, heads, rows, cols = forward_state.shape
+    span = rows * cols
     lanes = 128
 
-    def shift(decay_part, state_part, by, sign):
-        pairs = [(i, i + sign * by) for i in range(count) if 0 <= i + sign * by < count]
+    def join(earlier, later):
+        return (earlier[0] * later[0], later[0][:, :, None] * earlier[1] + later[1])
+
+    def pick(flag, when_true, when_false):
+        return jax.tree.map(lambda a, b: jnp.where(flag, a, b), when_true, when_false)
+
+    ones = jnp.ones_like(decay)
+    zeros = jnp.zeros((groups, heads, span), jnp.float32)
+    front = (decay, forward_state.reshape(groups, heads, span))
+    back = (decay, backward_state.reshape(groups, heads, span))
+    before = (ones, zeros)
+    after = (ones, zeros)
+    bit = 1
+    while bit < count:
+        upper = (place // bit) % 2 == 1
         packed = jnp.concatenate(
-            [state_part, jnp.broadcast_to(decay_part[:, :, None], (groups, heads, lanes))], 2
+            [front[1], back[1], jnp.broadcast_to(front[0][:, :, None], (groups, heads, lanes))], 2
         ).astype(jnp.bfloat16)
-        return lax.ppermute(packed, axis, pairs)
-
-    def unpack(got):
-        got = got.astype(jnp.float32)
-        return got[:, :, rows * cols], got[:, :, : rows * cols]
-
-    def fold(window, got_decay, got_state):
-        before_decay, before_state, upto_decay, upto_state = window
-        return (
-            before_decay * got_decay,
-            before_decay[:, :, None] * got_state + before_state,
-            upto_decay * got_decay,
-            upto_decay[:, :, None] * got_state + upto_state,
-        )
-
-    flats = [s.reshape(groups, heads, rows * cols) for s in (forward_state, backward_state)]
-    windows = [
-        (jnp.ones_like(decay), jnp.zeros_like(flat), decay, flat) for flat in flats
-    ]
-    tied = list(riders)
-    by = 1
-    step = 0
-    while by < count:
-        got = [shift(w[2], w[3], by, sign) for w, sign in zip(windows, (1, -1))]
-        if step < len(tied):
-            got, tied[step] = lax.optimization_barrier((got, tied[step]))
-        windows = [fold(w, *unpack(g)) for w, g in zip(windows, got)]
-        by *= 2
-        step += 1
-    state_in, adjoint = [w[1].reshape(groups, heads, rows, cols) for w in windows]
-    return state_in, adjoint, tied
+        pairs = [(i, i ^ bit) for i in range(count)]
+        other = lax.ppermute(packed, axis, pairs).astype(jnp.float32)
+        other_decay = other[:, :, 2 * span]
+        other_front = (other_decay, other[:, :, :span])
+        other_back = (other_decay, other[:, :, span : 2 * span])
+        before = pick(upper, join(other_front, before), before)
+        after = pick(upper, after, join(other_back, after))
+        front = pick(upper, join(other_front, front), join(front, other_front))
+        back = pick(upper, join(back, other_back), join(other_back, back))
+        bit *= 2
+    state_in = before[1].reshape(groups, heads, rows, cols)
+    adjoint = after[1].reshape(groups, heads, rows, cols)
+    return state_in, adjoint
 
 
 def conv_forward(extended, weight):
@@ -167,17 +164,15 @@
         return ssd_state(x_arg, b_arg, dt_arg, rate, dt_bias)
 
     (cum_log, state_end), state_pull = jax.vjp(state_map, x_float, b_float, dt_in)
-    y_local, mix_pull = jax.vjp(mix_map, x_float, b_float, c_float, dt_in)
     decay_total = jnp.exp(cum_log[-1])
     grad_heads = grad_y.astype(jnp.float32).reshape(length, groups, head_count, head_size)
     seed_state = jnp.einsum(
         "tghp,tgn->ghpn", jnp.exp(cum_log)[..., None] * grad_heads, c_float, precision=HIGH
     )
+
+    y_local, mix_pull = jax.vjp(mix_map, x_float, b_float, c_float, dt_in)
     mix_x, mix_b, mix_c, mix_dt = mix_pull(grad_heads)
-    state_in, adjoint, riders = scanned_pair(
-        decay_total, state_end, seed_state, "ctx", [y_local, mix_x, (mix_b, mix_c, mix_dt)]
-    )
-    y_local, mix_x, (mix_b, mix_c, mix_dt) = riders
+    state_in, adjoint = butterfly_pair(decay_total, state_end, seed_state, "ctx")
 
     def carry_map(c_arg, cum_arg):
         return carry_in(c_arg, cum_arg, state_in)

time: 102 us -> 188 us (1.84)
  local copies, waits for them, and re-layouts: 23.2 us -> 80.7 us
  other arithmetic: 16.8 us -> 56.7 us
  starting transfers between devices: 24.9 us -> 12 us
  waiting for transfers between devices: 12.8 us -> 15.5 us
    select_n x0 -> x4, local copies, waits for them, and re-layouts: none -> 18.5 us  [pick(): jnp.where(flag, a, b)]
    select_n x0 -> x2, other arithmetic: none -> 14.9 us  [pick(): jnp.where(flag, a, b)]
    reshape x5 -> x6, local copies, waits for them, and re-layouts: 5.15 us -> 19.9 us  [the longest x1 5.47 us: butterfly_pair(): adjoint = after[1].reshape(groups, heads, rows, cols)]
    ppermute x0 -> x2, local copies, waits for them, and re-layouts: none -> 13.4 us  [butterfly_pair(): other = lax.ppermute(packed, axis, pairs).astype(jnp.float32)]
    reduce_sum x1, other arithmetic: 1.93 us -> 15.2 us  [on_device(): end_term = jnp.sum(adjoint * state_in, axis=(2, 3)) * decay_total]
    ppermute x6 -> x3, starting transfers between devices: 18.7 us -> 5.91 us  [butterfly_pair(): other = lax.ppermute(packed, axis, pairs).astype(jnp.float32)]
    convert_element_type x5, other arithmetic: 1.16 us -> 11.1 us  [the longest x3 10.6 us: butterfly_pair(): other = lax.ppermute(packed, axis, pairs).astype(jnp.float32)]
    mul x0 -> x2, local copies, waits for them, and re-layouts: none -> 8.7 us  [join(): return (earlier[0] * later[0], later[0][:, :, None] * earlier[1] + later[1])]
  transfers between devices with their start and end apart: 8 -> 5, of which waited for: 5 -> 2; matrix products, arithmetic and copies ran while one was open for 15% -> 12% of each run, Pallas kernels for 0% -> 0%
where the time goes in v8:
time: 188 us; the launch traced here: 187 us
  local copies, waits for them, and re-layouts  80.7 us (43%)
  other arithmetic  56.7 us (30%)
  matrix products  20.4 us (11%)
  waiting for transfers between devices  15.5 us (8%)
  starting transfers between devices  12 us (6%)
    select_n x4, local copies, waits for them, and re-layouts, pick(): jnp.where(flag, a, b)  18.5 us
    ppermute x3, waiting for transfers between devices, butterfly_pair(): other = lax.ppermute(packed, axis, pairs).astype(jnp.float32)  15.5 us
    reduce_sum x1, other arithmetic, on_device(): end_term = jnp.sum(adjoint * state_in, axis=(2, 3)) * decay_total  15.2 us
    select_n x2, other arithmetic, pick(): jnp.where(flag, a, b)  14.9 us
    ppermute x2, local copies, waits for them, and re-layouts, butterfly_pair(): other = lax.ppermute(packed, axis, pairs).astype(jnp.float32)  13.4 us
    dot_general x3, matrix products, ssd_mix(): jnp.einsum('ghts,sghp->tghp', mixing, x_half, preferred_element_type=jnp....  12 us
    convert_element_type x3, other arithmetic, butterfly_pair(): other = lax.ppermute(packed, axis, pairs).astype(jnp.float32)  10.6 us
    mul x2, local copies, waits for them, and re-layouts, join(): return (earlier[0] * later[0], later[0][:, :, None] * earlier[1] + later[1])  8.7 us
  transfers between devices with their start and end apart: 5, of which 2 were waited for; matrix products, arithmetic and copies ran while one was open for 12% of the time, Pallas kernels for 0%

profile of v8, /device:TPU:0, one launch (start us, length us, event | category | flops | bytes accessed | tf_op | source)
XLA Modules:
  0.0 187.1 jit_solution(8958274432626677509)
XLA Ops:
  0.7 0.9 slice.283
  1.6 0.9 slice.284
  3.3 4.8 %collective-permute-start = (bf16[3,1280]{1,0:T(4,128)(2,1)S(1)}, bf16[3,1280]{1,0:T(4,128)(2,1)S(1)}, u32[]{:S(2)}, u32[]{:S(2)}) collective-permute-start(bf16[3,1280]{1,0:T(4,128)(2,1)S(1)} %pad_maximum_fusion.6), channel_id=1, source_target_pairs={{0,2},{2,4},{4,6},{6,8},{8,10},{10,12},{12,14},{1,3},{3,5},{5,7},{... | collective-permute-start | bytes 23048 | tf_op jit(solution)/shard_map/ppermute | solution.py:12
  8.9 0.7 slice_bitcast_fusion.13
  9.7 0.7 slice_bitcast_fusion.5
  11.1 0.9 fusion.76
  12.3 0.8 fusion.111
  13.1 1.3 copy.61
  14.8 1.5 constant_dynamic-update-slice_fusion
  16.2 4.3 %multiply_convert_fusion = (bf16[256,2,512]{2,1,0:T(2,128)(2,1)S(1)}, f32[256,2,512]{2,1,0:T(2,128)}) fusion(bf16[256,2,512]{2,1,0:T(2,128)(2,1)} %param.20, f32[2,512]{1,0:T(2,128)S(1)} %get-tuple-element.113, bf16[259,2,512]{2,1,0:T(2,128)(2,1)S(1)} %constant_dynamic-update-slice_fusion, f32[2,512]{1,0:T(2,128)S(1)} %get-tuple-element.114, ...), kind=kLoop, calls=%fused_computation.78 | loop fusion | flops 4194304 | bytes 3686400 | tf_op jit(solution)/shard_map/convert_element_type | solution.py:156
  23.0 1.6 collective-permute-start.1
  24.6 4.3 %copy.63 = f32[2,8,4096]{1,0,2:T(2,128)} copy(f32[2,8,4096]{2,1,0:T(8,128)S(1)} %reshape.251) | data formatting | bytes 524288 | tf_op jit(solution)/shard_map/reshape | solution.py:30
  28.9 4.3 %copy.66 = f32[2,8,4096]{1,0,2:T(2,128)} copy(f32[2,8,4096]{2,1,0:T(8,128)S(1)} %reshape.254) | data formatting | bytes 524288 | tf_op jit(solution)/shard_map/reshape | solution.py:31
  33.3 6.7 %copy.62 = bf16[2,8,8320]{1,0,2:T(2,128)(2,1)} copy(bf16[2,8,8320]{2,1,0:T(8,128)(2,1)S(1)} %collective-permute-done.1) | data formatting | bytes 532480 | tf_op jit(solution)/shard_map/ppermute | solution.py:41
  39.9 5.4 %convert_element_type.164 = f32[2,8,8320]{1,0,2:T(2,128)S(1)} convert(bf16[2,8,8320]{1,0,2:T(2,128)(2,1)} %copy.62) | non-fusion elementwise | flops 133120 | bytes 798720 | tf_op jit(solution)/shard_map/convert_element_type | solution.py:41
  46.1 7.4 %add_select_fusion.7 = (f32[2,8,4096]{1,0,2:T(2,128)}, f32[2,8,4096]{1,0,2:T(2,128)}) fusion(f32[2,8,4096]{1,0,2:T(2,128)S(1)} %copy-done.4, pred[]{:T(512)S(6)} %eq.24, f32[2,8,8320]{1,0,2:T(2,128)S(1)} %convert_element_type.164, f32[2,8]{1,0:T(2,128)S(1)} %get-tuple-element.97, f32[2,8]{1,0:T(2,128)S(1)} %get-tuple-element.125, f32[2,8,4096]{1,0,2:T(2,128)S(1)} %copy-done.5), kind=kLoop, calls=%fused_computation.25 | loop fusion | flops 655360 | bytes 1572993 | tf_op jit(solution)/shard_map/jit(_where)/select_n | solution.py:26
  53.5 4.8 %copy.65 = bf16[2,8,4096]{2,1,0:T(8,128)(2,1)S(1)} copy(f32[2,8,4096]{1,0,2:T(2,128)} %get-tuple-element.94) | data formatting | bytes 393216 | tf_op jit(solution)/shard_map/jit(_where)/select_n | solution.py:26
  58.3 4.9 %copy.68 = bf16[2,8,4096]{2,1,0:T(8,128)(2,1)S(1)} copy(f32[2,8,4096]{1,0,2:T(2,128)} %get-tuple-element.95) | data formatting | bytes 393216 | tf_op jit(solution)/shard_map/jit(_where)/select_n | solution.py:26
  63.3 1.6 collective-permute-start.2
  64.9 6.0 %collective-permute-done.2 = bf16[2,8,8320]{2,1,0:T(8,128)(2,1)S(1)} collective-permute-done((bf16[2,8,8320]{2,1,0:T(8,128)(2,1)S(1)}, bf16[2,8,8320]{2,1,0:T(8,128)(2,1)S(1)}, u32[]{:S(2)}, u32[]{:S(2)}) %collective-permute-start.2) | collective-permute-done | bytes 266272 | tf_op jit(solution)/shard_map/ppermute | solution.py:41
  70.9 6.7 %copy.69 = bf16[2,8,8320]{1,0,2:T(2,128)(2,1)} copy(bf16[2,8,8320]{2,1,0:T(8,128)(2,1)S(1)} %collective-permute-done.2) | data formatting | bytes 532480 | tf_op jit(solution)/shard_map/ppermute | solution.py:41
  77.6 5.2 %convert_element_type.165 = f32[2,8,8320]{1,0,2:T(2,128)S(1)} convert(bf16[2,8,8320]{1,0,2:T(2,128)(2,1)} %copy.69) | non-fusion elementwise | flops 133120 | bytes 798720 | tf_op jit(solution)/shard_map/convert_element_type | solution.py:41
  82.8 1.6 fusion.117
  84.4 7.5 %add_select_fusion.5 = (bf16[2,8,4096]{1,0,2:T(2,128)(2,1)}, bf16[2,8,4096]{1,0,2:T(2,128)(2,1)S(1)}) fusion(f32[2,8,4096]{1,0,2:T(2,128)S(1)} %copy-done.2, pred[]{:T(512)S(6)} %eq.23, f32[2,8,8320]{1,0,2:T(2,128)S(1)} %convert_element_type.165, f32[2,8]{1,0:T(2,128)S(1)} %get-tuple-element.101, f32[2,8]{1,0:T(2,128)S(1)} %copy-done.65, ...), kind=kLoop, calls=%fused_computation.23 | loop fusion | flops 655360 | bytes 1310849 | tf_op jit(solution)/shard_map/jit(_where)/select_n | solution.py:26
  92.0 5.2 %copy.70 = bf16[2,8,4096]{2,1,0:T(8,128)(2,1)} copy(bf16[2,8,4096]{1,0,2:T(2,128)(2,1)} %get-tuple-element.92) | data formatting | bytes 262144 | tf_op jit(solution)/shard_map/jit(_where)/select_n | solution.py:26
  97.2 3.5 %copy.71 = bf16[2,8,4096]{2,1,0:T(8,128)(2,1)} copy(bf16[2,8,4096]{1,0,2:T(2,128)(2,1)S(1)} %get-tuple-element.93) | data formatting | bytes 262144 | tf_op jit(solution)/shard_map/jit(_where)/select_n | solution.py:26
  101.4 1.0 pad_maximum_fusion.2
  102.4 2.7 %collective-permute-start.3 = (bf16[2,8,8320]{2,1,0:T(8,128)(2,1)S(1)}, bf16[2,8,8320]{2,1,0:T(8,128)(2,1)S(1)}, u32[]{:S(2)}, u32[]{:S(2)}) collective-permute-start(bf16[2,8,8320]{2,1,0:T(8,128)(2,1)S(1)} %pad_maximum_fusion.2), channel_id=1, source_target_pairs={{0,8},{2,10},{4,12},{6,14},{8,0},{10,2},{12,4},{14,6},{1,9},{3,11}... | collective-permute-start | bytes 798728 | tf_op jit(solution)/shard_map/ppermute | solution.py:41
  105.1 1.1 fusion.134
  106.2 9.5 %collective-permute-done.3 = bf16[2,8,8320]{2,1,0:T(8,128)(2,1)S(1)} collective-permute-done((bf16[2,8,8320]{2,1,0:T(8,128)(2,1)S(1)}, bf16[2,8,8320]{2,1,0:T(8,128)(2,1)S(1)}, u32[]{:S(2)}, u32[]{:S(2)}) %collective-permute-start.3) | collective-permute-done | bytes 266272 | tf_op jit(solution)/shard_map/ppermute | solution.py:41
  116.5 4.3 %copy.73 = f32[2,8,4096]{1,0,2:T(2,128)} copy(f32[2,8,4096]{2,1,0:T(8,128)S(1)} %get-tuple-element.102) | data formatting | bytes 524288 | tf_op jit(solution)/shard_map/mul | solution.py:23
  120.8 4.4 %copy.76 = f32[2,8,4096]{1,0,2:T(2,128)} copy(f32[2,8,4096]{2,1,0:T(8,128)S(1)} %get-tuple-element.103) | data formatting | bytes 524288 | tf_op jit(solution)/shard_map/mul | solution.py:23
  125.2 15.2 %multiply_reduce_fusion = (f32[2,8]{1,0:T(2,128)S(1)}, f32[2,8,4096]{1,0,2:T(2,128)}, f32[2,8,4096]{1,0,2:T(2,128)}) fusion(f32[2,8,4096]{1,0,2:T(2,128)} %copy.76, f32[2,8,8320]{1,0,2:T(2,128)} %copy-done.1, f32[2,8]{1,0:T(2,128)S(1)} %copy-done.62, f32[2,8,8320]{1,0,2:T(2,128)} %copy-done, pred[]{:T(512)S(6)} %eq.24, pred[]{:T(512)S(6)} %eq.23, ...), kind=kLoop, calls=%fused_computation.21 | loop fusion | flops 917488 | bytes 2097347 | tf_op jit(solution)/shard_map/reduce_sum | solution.py:183
  140.5 5.5 %copy.79 = f32[2,8,64,64]{2,3,1,0:T(8,128)S(1)} copy(f32[2,8,64,64]{1,0,3,2:T(2,128)} %bitcast.216) | data formatting | bytes 524288 | tf_op jit(solution)/shard_map/reshape | solution.py:51
  147.1 5.5 %copy.80 = f32[2,8,64,64]{2,3,1,0:T(8,128)S(1)} copy(f32[2,8,64,64]{1,0,3,2:T(2,128)} %bitcast.215) | data formatting | bytes 524288 | tf_op jit(solution)/shard_map/reshape | solution.py:50
  152.6 1.7 fusion.70
  154.3 0.9 convolution_bitcast_fusion.3
  157.3 5.8 %fusion.18 = (f32[2,8,256]{2,1,0:T(8,128)}, f32[2,8,256]{2,1,0:T(8,128)}, f32[2,8,256]{2,1,0:T(8,128)}, f32[2,256,256]{2,1,0:T(8,128)S(1)}) fusion(f32[2,8,256]{2,1,0:T(8,128)S(1)} %bitcast.233, f32[2,8,256]{2,1,0:T(8,128)S(1)} %get-tuple-element.107, f32[2,256,256]{2,1,0:T(8,128)} %fusion.134, pred[256,256]{1,0:T(8,128)(4,1)S(1)} %iota_compare_fusion, ...), kind=kOutput, calls=%fused_computation.36 | convolution fusion | flops 156094464 | bytes 2244608 | tf_op jit(solution)/shard_map/transpose(jvp(ghts,sghp->tghp))/dot_general | solution.py:107
  165.9 2.8 %fusion.48 = bf16[256,2,8,64]{0,3,2,1:T(8,128)(2,1)S(1)} fusion(bf16[2,8,64,256]{3,2,1,0:T(8,128)(2,1)S(1)} %bitcast.225, f32[2,8,256]{2,1,0:T(8,128)} %copy-done.41, f32[2,8,256]{2,1,0:T(8,128)} %bitcast.232, f32[2,256,256]{2,1,0:T(8,128)} %fusion.134, pred[256,256]{1,0:T(8,128)(4,1)} %copy-done.22, bf16[256,2,8,64]{0,3,2,1:T(8,128)(2,1)S(1)} %bitcast.224, ...), kind=kOutput, calls=%fused_computation.50 | convolution fusion | flops 142606336 | bytes 3260480 | tf_op jit(solution)/shard_map/transpose(jvp(ghts,sghp->tghp))/dot_general | solution.py:107
  168.9 1.3 copy.78
  170.2 2.8 %multiply_multiply_fusion = f32[256,2,512]{2,1,0:T(2,128)S(1)} fusion(f32[256,2,512]{2,1,0:T(2,128)} %copy.78, f32[256,2,512]{2,1,0:T(2,128)S(1)} %copy-done.6), kind=kLoop, calls=%fused_computation.77 | loop fusion | flops 2097152 | bytes 3145728 | tf_op jit(solution)/shard_map/mul | solution.py:68
  173.1 1.3 multiply_add_fusion
  174.4 1.0 copy-done.7
  175.4 1.3 collective-permute-start.4
  176.9 3.4 %fusion.30 = bf16[256,2,8,64]{0,3,2,1:T(8,128)(2,1)} fusion(bf16[256,2,8,64]{0,3,2,1:T(8,128)(2,1)S(1)} %bitcast.220, f32[2,8,256]{2,1,0:T(8,128)S(1)} %copy-done.42, f32[2,8,256]{2,1,0:T(8,128)S(1)} %bitcast.234, f32[2,256,256]{2,1,0:T(8,128)} %fusion.134, pred[256,256]{1,0:T(8,128)(4,1)S(1)} %copy-done.23, f32[256,2,8,64]{0,3,2,1:T(8,128)S(1)} %copy-done.9, ...), kind=kOutput, calls=%fused_computation.44 | convolution fusion | flops 142082048 | bytes 2736192 | tf_op jit(solution)/shard_map/jvp(ghts,sghp->tghp)/dot_general | solution.py:107
  180.9 0.9 fusion.64
  182.3 2.0 %copy.87 = bf16[256,2,512]{2,1,0:T(2,128)(2,1)} copy(bf16[256,2,512]{0,2,1:T(8,128)(2,1)} %bitcast.226) | data formatting | bytes 1048576
  186.3 0.8 copy-done.12
  (210 shorter events, 16.6 us)
Async XLA Ops:
  0.6 20.4 %copy-start.16 = (bf16[256,2,64]{0,2,1:T(8,128)(2,1)S(1)}, bf16[256,2,64]{0,2,1:T(8,128)(2,1)}, u32[]{:S(2)}) copy-start(bf16[256,2,64]{0,2,1:T(8,128)(2,1)} %param.21) | copy-start | bytes 196612
  0.6 20.4 %copy-start.15 = (bf16[256,2,64]{0,2,1:T(8,128)(2,1)S(1)}, bf16[256,2,64]{0,2,1:T(8,128)(2,1)}, u32[]{:S(2)}) copy-start(bf16[256,2,64]{0,2,1:T(8,128)(2,1)} %param.22) | copy-start | bytes 196612
  3.3 11.1 %collective-permute-start = (bf16[3,1280]{1,0:T(4,128)(2,1)S(1)}, bf16[3,1280]{1,0:T(4,128)(2,1)S(1)}, u32[]{:S(2)}, u32[]{:S(2)}) collective-permute-start(bf16[3,1280]{1,0:T(4,128)(2,1)S(1)} %pad_maximum_fusion.6), channel_id=1, source_target_pairs={{0,2},{2,4},{4,6},{6,8},{8,10},{10,12},{12,14},{1,3},{3,5},{5,7},{... | collective-permute-start | bytes 23048 | tf_op jit(solution)/shard_map/ppermute | solution.py:12
  8.9 12.9 %copy-start.51 = (f32[2,64]{1,0:T(2,128)}, f32[2,64]{1,0:T(2,128)S(1)}, u32[]{:S(2)}) copy-start(f32[2,64]{1,0:T(2,128)S(1)} %get-tuple-element.117) | copy-start | bytes 1540
  8.9 12.9 %copy-start.53 = (f32[2,64]{1,0:T(2,128)}, f32[2,64]{1,0:T(2,128)S(1)}, u32[]{:S(2)}) copy-start(f32[2,64]{1,0:T(2,128)S(1)} %get-tuple-element.118) | copy-start | bytes 1540
  8.9 12.9 %copy-start.55 = (f32[2,64]{1,0:T(2,128)}, f32[2,64]{1,0:T(2,128)S(1)}, u32[]{:S(2)}) copy-start(f32[2,64]{1,0:T(2,128)S(1)} %get-tuple-element.119) | copy-start | bytes 1540
  8.9 12.9 %copy-start.57 = (f32[2,64]{1,0:T(2,128)}, f32[2,64]{1,0:T(2,128)S(1)}, u32[]{:S(2)}) copy-start(f32[2,64]{1,0:T(2,128)S(1)} %get-tuple-element.120) | copy-start | bytes 1540
  9.6 12.2 %copy-start.43 = (f32[2,64]{1,0:T(2,128)}, f32[2,64]{1,0:T(2,128)S(1)}, u32[]{:S(2)}) copy-start(f32[2,64]{1,0:T(2,128)S(1)} %get-tuple-element.121) | copy-start | bytes 1540
  9.6 12.2 %copy-start.45 = (f32[2,64]{1,0:T(2,128)}, f32[2,64]{1,0:T(2,128)S(1)}, u32[]{:S(2)}) copy-start(f32[2,64]{1,0:T(2,128)S(1)} %get-tuple-element.122) | copy-start | bytes 1540
  9.6 12.2 %copy-start.47 = (f32[2,64]{1,0:T(2,128)}, f32[2,64]{1,0:T(2,128)S(1)}, u32[]{:S(2)}) copy-start(f32[2,64]{1,0:T(2,128)S(1)} %get-tuple-element.123) | copy-start | bytes 1540
  9.7 12.2 %copy-start.49 = (f32[2,64]{1,0:T(2,128)}, f32[2,64]{1,0:T(2,128)S(1)}, u32[]{:S(2)}) copy-start(f32[2,64]{1,0:T(2,128)S(1)} %get-tuple-element.124) | copy-start | bytes 1540
  10.4 11.0 %copy-start.28 = (f32[2,512]{1,0:T(2,128)}, f32[2,512]{1,0:T(2,128)S(1)}, u32[]{:S(2)}) copy-start(f32[2,512]{1,0:T(2,128)S(1)} %get-tuple-element.111) | copy-start | bytes 12292
  10.4 11.0 %copy-start.30 = (f32[2,512]{1,0:T(2,128)}, f32[2,512]{1,0:T(2,128)S(1)}, u32[]{:S(2)}) copy-start(f32[2,512]{1,0:T(2,128)S(1)} %get-tuple-element.112) | copy-start | bytes 12292
  10.4 11.0 %copy-start.32 = (f32[2,512]{1,0:T(2,128)}, f32[2,512]{1,0:T(2,128)S(1)}, u32[]{:S(2)}) copy-start(f32[2,512]{1,0:T(2,128)S(1)} %get-tuple-element.113) | copy-start | bytes 12292
  10.4 11.0 %copy-start.34 = (f32[2,512]{1,0:T(2,128)}, f32[2,512]{1,0:T(2,128)S(1)}, u32[]{:S(2)}) copy-start(f32[2,512]{1,0:T(2,128)S(1)} %get-tuple-element.114) | copy-start | bytes 12292
  12.1 9.4 %copy-start.17 = (f32[256,16]{0,1}, f32[256,16]{0,1:S(1)}, u32[]{:S(2)}) copy-start(f32[256,16]{0,1:S(1)} %fusion.76) | copy-start | bytes 49156
  13.1 8.7 %copy-start.13 = (f32[256,2,8]{0,2,1:T(8,128)}, f32[256,2,8]{0,2,1:T(8,128)S(1)}, u32[]{:S(2)}) copy-start(f32[256,2,8]{0,2,1:T(8,128)S(1)} %get-tuple-element.109) | copy-start | bytes 49156
  23.0 10.2 %collective-permute-start.1 = (bf16[2,8,8320]{2,1,0:T(8,128)(2,1)S(1)}, bf16[2,8,8320]{2,1,0:T(8,128)(2,1)S(1)}, u32[]{:S(2)}, u32[]{:S(2)}) collective-permute-start(bf16[2,8,8320]{2,1,0:T(8,128)(2,1)S(1)} %pad_maximum_fusion), channel_id=1, source_target_pairs={{0,2},{2,0},{4,6},{6,4},{8,10},{10,8},{12,14},{14,12},{1,3},{3,1},... | collective-permute-start | bytes 798728 | tf_op jit(solution)/shard_map/ppermute | solution.py:41
  45.4 8.1 %copy-start = (f32[2,8,8320]{1,0,2:T(2,128)}, f32[2,8,8320]{1,0,2:T(2,128)S(1)}, u32[]{:S(2)}) copy-start(f32[2,8,8320]{1,0,2:T(2,128)S(1)} %convert_element_type.164) | copy-start | bytes 1597444
  63.3 7.6 %collective-permute-start.2 = (bf16[2,8,8320]{2,1,0:T(8,128)(2,1)S(1)}, bf16[2,8,8320]{2,1,0:T(8,128)(2,1)S(1)}, u32[]{:S(2)}, u32[]{:S(2)}) collective-permute-start(bf16[2,8,8320]{2,1,0:T(8,128)(2,1)S(1)} %pad_maximum_fusion.1), channel_id=1, source_target_pairs={{0,4},{2,6},{4,0},{6,2},{8,12},{10,14},{12,8},{14,10},{1,5},{3,7},... | collective-permute-start | bytes 798728 | tf_op jit(solution)/shard_map/ppermute | solution.py:41
  77.6 6.8 %copy-start.2 = (f32[2,8,4096]{1,0,2:T(2,128)S(1)}, f32[2,8,4096]{1,0,2:T(2,128)}, u32[]{:S(2)}) copy-start(f32[2,8,4096]{1,0,2:T(2,128)} %get-tuple-element.94) | copy-start | bytes 786436
  77.6 6.8 %copy-start.3 = (f32[2,8,4096]{1,0,2:T(2,128)S(1)}, f32[2,8,4096]{1,0,2:T(2,128)}, u32[]{:S(2)}) copy-start(f32[2,8,4096]{1,0,2:T(2,128)} %get-tuple-element.95) | copy-start | bytes 786436
  77.6 6.8 %copy-start.65 = (f32[2,8]{1,0:T(2,128)S(1)}, f32[2,8]{1,0:T(2,128)}, u32[]{:S(2)}) copy-start(f32[2,8]{1,0:T(2,128)} %get-tuple-element.99) | copy-start | bytes 196
  82.8 9.2 %copy-start.1 = (f32[2,8,8320]{1,0,2:T(2,128)}, f32[2,8,8320]{1,0,2:T(2,128)S(1)}, u32[]{:S(2)}) copy-start(f32[2,8,8320]{1,0,2:T(2,128)S(1)} %convert_element_type.165) | copy-start | bytes 1597444
  102.4 13.3 %collective-permute-start.3 = (bf16[2,8,8320]{2,1,0:T(8,128)(2,1)S(1)}, bf16[2,8,8320]{2,1,0:T(8,128)(2,1)S(1)}, u32[]{:S(2)}, u32[]{:S(2)}) collective-permute-start(bf16[2,8,8320]{2,1,0:T(8,128)(2,1)S(1)} %pad_maximum_fusion.2), channel_id=1, source_target_pairs={{0,8},{2,10},{4,12},{6,14},{8,0},{10,2},{12,4},{14,6},{1,9},{3,11}... | collective-permute-start | bytes 798728 | tf_op jit(solution)/shard_map/ppermute | solution.py:41
  105.1 52.2 %copy-start.22 = (pred[256,256]{1,0:T(8,128)(4,1)}, pred[256,256]{1,0:T(8,128)(4,1)S(1)}, u32[]{:S(2)}) copy-start(pred[256,256]{1,0:T(8,128)(4,1)S(1)} %iota_compare_fusion) | copy-start | bytes 196612
  116.5 8.7 %copy-start.61 = (f32[2,8]{1,0:T(2,128)S(1)}, f32[2,8]{1,0:T(2,128)}, u32[]{:S(2)}) copy-start(f32[2,8]{1,0:T(2,128)} %get-tuple-element.96) | copy-start | bytes 196
  116.5 8.7 %copy-start.62 = (f32[2,8]{1,0:T(2,128)S(1)}, f32[2,8]{1,0:T(2,128)}, u32[]{:S(2)}) copy-start(f32[2,8]{1,0:T(2,128)} %get-tuple-element.100) | copy-start | bytes 196
  146.6 9.2 %copy-start.20 = (f32[256,2,8]{0,2,1:T(8,128)}, f32[256,2,8]{0,2,1:T(8,128)S(1)}, u32[]{:S(2)}) copy-start(f32[256,2,8]{0,2,1:T(8,128)S(1)} %get-tuple-element.127) | copy-start | bytes 49156
  147.1 8.8 %copy-start.18 = (f32[256,16]{0,1:S(1)}, f32[256,16]{0,1}, u32[]{:S(2)}) copy-start(f32[256,16]{0,1} %copy-done.17) | copy-start | bytes 49156
  147.1 8.8 %copy-start.26 = (f32[256,2,8]{0,2,1:T(8,128)S(1)}, f32[256,2,8]{0,2,1:T(8,128)}, u32[]{:S(2)}) copy-start(f32[256,2,8]{0,2,1:T(8,128)} %param.23) | copy-start | bytes 49156
  147.1 8.8 %copy-start.39 = (f32[2,8]{1,0:T(2,128)S(1)}, f32[2,8]{1,0:T(2,128)}, u32[]{:S(2)}) copy-start(f32[2,8]{1,0:T(2,128)} %copy-done.38) | copy-start | bytes 196
  147.1 8.7 %copy-start.63 = (f32[2,8]{1,0:T(2,128)S(1)}, f32[2,8]{1,0:T(2,128)}, u32[]{:S(2)}) copy-start(f32[2,8]{1,0:T(2,128)} %param.25) | copy-start | bytes 196
  156.6 6.5 %copy-start.41 = (f32[2,8,256]{2,1,0:T(8,128)}, f32[2,8,256]{2,1,0:T(8,128)S(1)}, u32[]{:S(2)}) copy-start(f32[2,8,256]{2,1,0:T(8,128)S(1)} %get-tuple-element.107) | copy-start | bytes 49156
  157.2 6.2 %copy-start.54 = (f32[2,64]{1,0:T(2,128)S(1)}, f32[2,64]{1,0:T(2,128)}, u32[]{:S(2)}) copy-start(f32[2,64]{1,0:T(2,128)} %copy-done.53) | copy-start | bytes 1540
  157.2 6.2 %copy-start.56 = (f32[2,64]{1,0:T(2,128)S(1)}, f32[2,64]{1,0:T(2,128)}, u32[]{:S(2)}) copy-start(f32[2,64]{1,0:T(2,128)} %copy-done.55) | copy-start | bytes 1540
  157.2 6.2 %copy-start.58 = (f32[2,64]{1,0:T(2,128)S(1)}, f32[2,64]{1,0:T(2,128)}, u32[]{:S(2)}) copy-start(f32[2,64]{1,0:T(2,128)} %copy-done.57) | copy-start | bytes 1540
  157.3 7.6 %copy-start.44 = (f32[2,64]{1,0:T(2,128)S(1)}, f32[2,64]{1,0:T(2,128)}, u32[]{:S(2)}) copy-start(f32[2,64]{1,0:T(2,128)} %copy-done.43) | copy-start | bytes 1540
  157.3 7.6 %copy-start.46 = (f32[2,64]{1,0:T(2,128)S(1)}, f32[2,64]{1,0:T(2,128)}, u32[]{:S(2)}) copy-start(f32[2,64]{1,0:T(2,128)} %copy-done.45) | copy-start | bytes 1540
  157.3 7.6 %copy-start.48 = (f32[2,64]{1,0:T(2,128)S(1)}, f32[2,64]{1,0:T(2,128)}, u32[]{:S(2)}) copy-start(f32[2,64]{1,0:T(2,128)} %copy-done.47) | copy-start | bytes 1540
  157.3 7.6 %copy-start.50 = (f32[2,64]{1,0:T(2,128)S(1)}, f32[2,64]{1,0:T(2,128)}, u32[]{:S(2)}) copy-start(f32[2,64]{1,0:T(2,128)} %copy-done.49) | copy-start | bytes 1540
  168.7 6.7 %copy-start.59 = (f32[3,128]{1,0:T(4,128)S(1)}, f32[3,128]{1,0:T(4,128)}, u32[]{:S(2)}) copy-start(f32[3,128]{1,0:T(4,128)} %copy.81) | copy-start | bytes 4612
  168.7 8.0 %copy-start.19 = (f32[256,16]{0,1:S(1)}, f32[256,16]{0,1}, u32[]{:S(2)}) copy-start(f32[256,16]{0,1} %copy-done.17) | copy-start | bytes 49156
  168.8 8.0 %copy-start.23 = (pred[256,256]{1,0:T(8,128)(4,1)S(1)}, pred[256,256]{1,0:T(8,128)(4,1)}, u32[]{:S(2)}) copy-start(pred[256,256]{1,0:T(8,128)(4,1)} %copy-done.22) | copy-start | bytes 196612
  168.8 8.0 %copy-start.42 = (f32[2,8,256]{2,1,0:T(8,128)S(1)}, f32[2,8,256]{2,1,0:T(8,128)}, u32[]{:S(2)}) copy-start(f32[2,8,256]{2,1,0:T(8,128)} %copy-done.41) | copy-start | bytes 49156
  168.8 8.0 %copy-start.68 = (f32[2,8]{1,0:T(2,128)S(1)}, f32[2,8]{1,0:T(2,128)}, u32[]{:S(2)}) copy-start(f32[2,8]{1,0:T(2,128)} %param.26) | copy-start | bytes 196
  170.2 6.5 %copy-start.9 = (f32[256,2,8,64]{0,3,2,1:T(8,128)S(1)}, f32[256,2,8,64]{0,3,2,1:T(8,128)}, u32[]{:S(2)}) copy-start(f32[256,2,8,64]{0,3,2,1:T(8,128)} %get-tuple-element.130) | copy-start | bytes 3145732
  175.4 8.9 %collective-permute-start.4 = (f32[3,1280]{1,0:T(4,128)S(1)}, f32[3,1280]{1,0:T(4,128)S(1)}, u32[]{:S(2)}, u32[]{:S(2)}) collective-permute-start(f32[3,1280]{1,0:T(4,128)S(1)} %pad_maximum_fusion.5), channel_id=1, source_target_pairs={{2,0},{4,2},{6,4},{8,6},{10,8},{12,10},{14,12},{3,1},{5,3},{7,5},{... | collective-permute-start | bytes 46088 | tf_op jit(solution)/shard_map/ppermute | solution.py:12
  (29 other events, 105.4 us)

commit v9 on v8

--- a/solution.py
+++ b/solution.py
@@ -16,32 +16,34 @@
     count = lax.axis_size(axis)
     place = lax.axis_index(axis)
     groups, heads, rows, cols = forward_state.shape
+    width = groups * heads
     span = rows * cols
     lanes = 128
 
     def join(earlier, later):
-        return (earlier[0] * later[0], later[0][:, :, None] * earlier[1] + later[1])
+        return (earlier[0] * later[0], later[0] * earlier[1] + later[1])
 
     def pick(flag, when_true, when_false):
-        return jax.tree.map(lambda a, b: jnp.where(flag, a, b), when_true, when_false)
-
-    ones = jnp.ones_like(decay)
-    zeros = jnp.zeros((groups, heads, span), jnp.float32)
-    front = (decay, forward_state.reshape(groups, heads, span))
-    back = (decay, backward_state.reshape(groups, heads, span))
+        return jax.tree.map(lambda a, b: a * flag + b * (1.0 - flag), when_true, when_false)
+
+    decay_col = decay.reshape(width, 1)
+    ones = jnp.ones_like(decay_col)
+    zeros = jnp.zeros((width, span), jnp.float32)
+    front = (decay_col, forward_state.reshape(width, span))
+    back = (decay_col, backward_state.reshape(width, span))
     before = (ones, zeros)
     after = (ones, zeros)
     bit = 1
     while bit < count:
-        upper = (place // bit) % 2 == 1
+        upper = ((place // bit) % 2).astype(jnp.float32)
         packed = jnp.concatenate(
-            [front[1], back[1], jnp.broadcast_to(front[0][:, :, None], (groups, heads, lanes))], 2
+            [front[1], back[1], jnp.broadcast_to(front[0], (width, lanes))], 1
         ).astype(jnp.bfloat16)
         pairs = [(i, i ^ bit) for i in range(count)]
         other = lax.ppermute(packed, axis, pairs).astype(jnp.float32)
-        other_decay = other[:, :, 2 * span]
-        other_front = (other_decay, other[:, :, :span])
-        other_back = (other_decay, other[:, :, span : 2 * span])
+        other_decay = other[:, 2 * span : 2 * span + 1]
+        other_front = (other_decay, other[:, :span])
+        other_back = (other_decay, other[:, span : 2 * span])
         before = pick(upper, join(other_front, before), before)
         after = pick(upper, after, join(other_back, after))
         front = pick(upper, join(other_front, front), join(front, other_front))

time: 188 us -> 99.2 us (0.53)
  local copies, waits for them, and re-layouts: 80.7 us -> 18.6 us
  other arithmetic: 56.7 us -> 23 us
  waiting for transfers between devices: 15.5 us -> 21.6 us
    select_n x4 -> x0, local copies, waits for them, and re-layouts: 18.5 us -> none  [pick(): jnp.where(flag, a, b)]
    select_n x2 -> x0, other arithmetic: 14.9 us -> none  [pick(): jnp.where(flag, a, b)]
    ppermute x2 -> x0, local copies, waits for them, and re-layouts: 13.4 us -> none  [butterfly_pair(): other = lax.ppermute(packed, axis, pairs).astype(jnp.float32)]
    reduce_sum x1, other arithmetic: 15.2 us -> 2.3 us  [on_device(): end_term = jnp.sum(adjoint * state_in, axis=(2, 3)) * decay_total]
    mul x2 -> x0, local copies, waits for them, and re-layouts: 8.7 us -> none  [join(): return (earlier[0] * later[0], later[0][:, :, None] * earlier[1] + later[1])]
    reshape x4 -> x2, local copies, waits for them, and re-layouts: 9 us -> 0.37 us  [the longest x1 0.19 us: butterfly_pair(): front = (decay_col, forward_state.reshape(width, span))]
    convert_element_type x3, other arithmetic: 10.6 us -> 2.01 us  [butterfly_pair(): other = lax.ppermute(packed, axis, pairs).astype(jnp.float32)]
    reshape x1, local copies, waits for them, and re-layouts: 5.47 us -> 0.21 us  [butterfly_pair(): adjoint = after[1].reshape(groups, heads, rows, cols)]
  transfers between devices with their start and end apart: 5 -> 5, of which waited for: 2 -> 4; matrix products, arithmetic and copies ran while one was open for 12% -> 13% of each run, Pallas kernels for 0% -> 0%
where the time goes in v9:
time: 99.2 us; the launch traced here: 98.3 us
  other arithmetic  23 us (23%)
  waiting for transfers between devices  21.6 us (22%)
  matrix products  21.4 us (22%)
  local copies, waits for them, and re-layouts  18.6 us (19%)
  starting transfers between devices  12 us (12%)
  between operations  1.76 us (2%)
    ppermute x3, waiting for transfers between devices, butterfly_pair(): other = lax.ppermute(packed, axis, pairs).astype(jnp.float32)  20.3 us
    dot_general x3, matrix products, ssd_mix(): jnp.einsum('ghts,sghp->tghp', mixing, x_half, preferred_element_type=jnp....  10.3 us
    ppermute x2, starting transfers between devices, from_behind(): return lax.ppermute(array, axis, pairs)  6.14 us
    ppermute x3, starting transfers between devices, butterfly_pair(): other = lax.ppermute(packed, axis, pairs).astype(jnp.float32)  5.88 us
    unnamed x149, local copies, waits for them, and re-layouts  5.46 us
    another operation x7, other arithmetic  3.57 us
    dot_general x2, matrix products, carry_in(): carried = jnp.einsum('tgn,ghpn->tghp', c_float, state_in, precision=HIGH)  3.45 us
    dot_general x3, matrix products, ssd_state(): jnp.einsum('sghp,sgn->ghpn', weighted.astype(jnp.float32), b_float, preci...  3.29 us
  transfers between devices with their start and end apart: 5, of which 4 were waited for; matrix products, arithmetic and copies ran while one was open for 13% of the time, Pallas kernels for 0%

profile of v9, /device:TPU:0, one launch (start us, length us, event | category | flops | bytes accessed | tf_op | source)
XLA Modules:
  0.0 98.3 jit_solution(7368154128509787077)
XLA Ops:
  0.7 0.7 slice_bitcast_fusion.1
  1.4 0.8 slice.283
  2.3 0.9 slice.284
  3.3 4.8 %collective-permute-start = (bf16[3,1280]{1,0:T(4,128)(2,1)S(1)}, bf16[3,1280]{1,0:T(4,128)(2,1)S(1)}, u32[]{:S(2)}, u32[]{:S(2)}) collective-permute-start(bf16[3,1280]{1,0:T(4,128)(2,1)S(1)} %pad_maximum_fusion.6), channel_id=1, source_target_pairs={{0,2},{2,4},{4,6},{6,8},{8,10},{10,12},{12,14},{1,3},{3,5},{5,7},{... | collective-permute-start | bytes 23048 | tf_op jit(solution)/shard_map/ppermute | solution.py:12
  8.1 0.7 neg.30
  8.8 0.7 slice_bitcast_fusion.9
  9.6 0.9 fusion.82
  10.8 1.3 %slice_bitcast_fusion.5 = (f32[2,512]{1,0:T(2,128)S(1)}, f32[2,512]{1,0:T(2,128)S(1)}, f32[2,512]{1,0:T(2,128)}, f32[2,512]{1,0:T(2,128)}) fusion(f32[4,2,512]{2,1,0:T(2,128)} %param.27), kind=kLoop, calls=%fused_computation.190 | loop fusion | bytes 32768 | tf_op jit(solution)/shard_map/mul | solution.py:60
  12.1 1.4 %fusion.117 = (f32[256,2,8]{0,2,1:T(8,128)}, f32[256,2,8]{0,2,1:T(8,128)S(1)}) fusion(f32[2,8]{1,0:T(2,128)S(1)} %get-tuple-element.93, f32[256,16]{0,1:S(1)} %fusion.82, f32[256,2,8]{0,2,1:T(8,128)} %param.23, f32[2,8]{1,0:T(2,128)} %param.25), kind=kLoop, calls=%fused_computation.160 | loop fusion | flops 36864 | bytes 65664 | tf_op jit(solution)/shard_map/jvp()/mul | solution.py:119
  13.5 0.7 slice_bitcast_fusion.13
  14.9 1.3 %copy.107 = bf16[256,2,512]{0,2,1:T(8,128)(2,1)S(1)} copy(bf16[256,2,512]{2,1,0:T(2,128)(2,1)} %param.30) | data formatting | bytes 1048576 | tf_op args[10]
  16.5 1.1 %multiply_convert_fusion.1 = (bf16[256,2,64]{0,2,1:T(8,128)(2,1)S(1)}, f32[256,2,64]{0,2,1:T(8,128)}, bf16[256,2,64]{0,2,1:T(8,128)(2,1)S(1)}, f32[256,2,64]{0,2,1:T(8,128)}) fusion(bf16[256,2,64]{0,2,1:T(8,128)(2,1)S(1)} %copy-done.18, f32[2,64]{1,0:T(2,128)S(1)} %get-tuple-element.123, bf16[3,2,64]{0,2,1:T(8,128)(2,1)S(1)} %bitcast.217, ...), kind=kLoop, calls=%fused_computation.116 | loop fusion | flops 1638400 | bytes 529920 | tf_op jit(solution)/shard_map/convert_element_type | solution.py:159
  19.7 2.4 %multiply_convert_fusion = (bf16[256,2,512]{2,1,0:T(2,128)(2,1)S(1)}, f32[256,2,512]{2,1,0:T(2,128)S(1)}) fusion(bf16[256,2,512]{2,1,0:T(2,128)(2,1)S(1)} %copy-done.1, f32[2,512]{1,0:T(2,128)S(1)} %copy-done.30, bf16[259,2,512]{2,1,0:T(2,128)(2,1)S(1)} %constant_dynamic-update-slice_fusion, f32[2,512]{1,0:T(2,128)S(1)} %copy-done.32, ...), kind=kLoop, calls=%fused_computation.69 | loop fusion | flops 4194304 | bytes 3686400 | tf_op jit(solution)/shard_map/convert_element_type | solution.py:158
  22.7 1.0 %fusion.74 = f32[2,8,64,64]{3,2,1,0:T(8,128)S(1)} fusion(bf16[256,2,8,64]{0,3,2,1:T(8,128)(2,1)S(1)} %bitcast.201, f32[256,2,8]{0,2,1:T(8,128)} %get-tuple-element.113, bf16[256,2,64]{0,2,1:T(8,128)(2,1)S(1)} %get-tuple-element.98), kind=kOutput, calls=%fused_computation.75 | convolution fusion | flops 34340864 | bytes 868352 | tf_op jit(solution)/shard_map/jvp(sghp,sgn->ghpn)/dot_general | solution.py:121
  24.1 1.6 %collective-permute-start.1 = (bf16[16,8320]{1,0:T(8,128)(2,1)S(1)}, bf16[16,8320]{1,0:T(8,128)(2,1)S(1)}, u32[]{:S(2)}, u32[]{:S(2)}) collective-permute-start(bf16[16,8320]{1,0:T(8,128)(2,1)S(1)} %pad_maximum_fusion), channel_id=1, source_target_pairs={{0,2},{2,0},{4,6},{6,4},{8,10},{10,8},{12,14},{14,12},{1,3},{3,1},... | collective-permute-start | bytes 798728 | tf_op jit(solution)/shard_map/ppermute | solution.py:43
  25.7 6.3 %collective-permute-done.1 = bf16[16,8320]{1,0:T(8,128)(2,1)S(1)} collective-permute-done((bf16[16,8320]{1,0:T(8,128)(2,1)S(1)}, bf16[16,8320]{1,0:T(8,128)(2,1)S(1)}, u32[]{:S(2)}, u32[]{:S(2)}) %collective-permute-start.1) | collective-permute-done | bytes 266272 | tf_op jit(solution)/shard_map/ppermute | solution.py:43
  32.0 1.5 %fusion.124 = (f32[16]{0:T(128)}, f32[16]{0:T(128)S(1)}, f32[16]{0:T(128)}, f32[16]{0:T(128)S(1)}) fusion(f32[16,8320]{1,0:T(8,128)S(1)} %convert_element_type.173, f32[]{:T(128)S(6)} %sub.72, f32[]{:T(128)S(6)} %convert_element_type.174, f32[256,2,8]{0,2,1:T(8,128)} %bitcast.211, f32[]{:T(128)S(6)} %add.316), kind=kLoop, calls=%fused_computation.179 | loop fusion | flops 96 | bytes 396 | tf_op jit(solution)/shard_map/add | solution.py:27
  34.3 1.7 %collective-permute-start.2 = (bf16[16,8320]{1,0:T(8,128)(2,1)S(1)}, bf16[16,8320]{1,0:T(8,128)(2,1)}, u32[]{:S(2)}, u32[]{:S(2)}) collective-permute-start(bf16[16,8320]{1,0:T(8,128)(2,1)S(1)} %pad_maximum_fusion.1), channel_id=1, source_target_pairs={{0,4},{2,6},{4,0},{6,2},{8,12},{10,14},{12,8},{14,10},{1,5},{3,7},... | collective-permute-start | bytes 798728 | tf_op jit(solution)/shard_map/ppermute | solution.py:43
  36.0 5.4 %collective-permute-done.2 = bf16[16,8320]{1,0:T(8,128)(2,1)} collective-permute-done((bf16[16,8320]{1,0:T(8,128)(2,1)S(1)}, bf16[16,8320]{1,0:T(8,128)(2,1)}, u32[]{:S(2)}, u32[]{:S(2)}) %collective-permute-start.2) | collective-permute-done | bytes 266272 | tf_op jit(solution)/shard_map/ppermute | solution.py:43
  41.4 1.0 %convert_element_type.175 = f32[16,8320]{1,0:T(8,128)S(1)} convert(bf16[16,8320]{1,0:T(8,128)(2,1)} %collective-permute-done.2) | non-fusion elementwise | flops 133120 | bytes 798720 | tf_op jit(solution)/shard_map/convert_element_type | solution.py:43
  42.4 0.7 add_reduce_fusion
  43.1 0.9 fusion.126
  44.0 1.3 %add_convert_fusion.1 = (bf16[16,4096]{1,0:T(8,128)(2,1)S(1)}, bf16[16,4096]{1,0:T(8,128)(2,1)S(1)}) fusion(f32[16,8320]{1,0:T(8,128)S(1)} %convert_element_type.175, f32[]{:T(128)S(6)} %sub.74, f32[16]{0:T(128)S(1)} %get-tuple-element.92, f32[]{:T(128)S(6)} %convert_element_type.176, f32[16]{0:T(128)} %copy-done.62, f32[]{:T(128)S(6)} %sub.72, ...), kind=kLoop, calls=%fused_computation.89 | loop fusion | flops 1966080 | bytes 1835280 | tf_op jit(solution)/shard_map/convert.7
  45.4 0.7 pad_maximum_fusion.2
  46.1 2.6 %collective-permute-start.3 = (bf16[16,8320]{1,0:T(8,128)(2,1)}, bf16[16,8320]{1,0:T(8,128)(2,1)}, u32[]{:S(2)}, u32[]{:S(2)}) collective-permute-start(bf16[16,8320]{1,0:T(8,128)(2,1)} %pad_maximum_fusion.2), channel_id=1, source_target_pairs={{0,8},{2,10},{4,12},{6,14},{8,0},{10,2},{12,4},{14,6},{1,9},{3,11}... | collective-permute-start | bytes 798728 | tf_op jit(solution)/shard_map/ppermute | solution.py:43
  49.4 1.1 %fusion.140 = f32[2,256,256]{2,1,0:T(8,128)} fusion(bf16[256,2,64]{0,2,1:T(8,128)(2,1)S(1)} %get-tuple-element.133, bf16[256,2,64]{0,2,1:T(8,128)(2,1)S(1)} %get-tuple-element.98), kind=kOutput, calls=%fused_computation.211 | convolution fusion | flops 16777216 | bytes 655360 | tf_op jit(solution)/shard_map/jvp(tgn,sgn->gts)/dot_general | solution.py:107
  50.4 8.6 %collective-permute-done.3 = bf16[16,8320]{1,0:T(8,128)(2,1)} collective-permute-done((bf16[16,8320]{1,0:T(8,128)(2,1)}, bf16[16,8320]{1,0:T(8,128)(2,1)}, u32[]{:S(2)}, u32[]{:S(2)}) %collective-permute-start.3) | collective-permute-done | bytes 266272 | tf_op jit(solution)/shard_map/ppermute | solution.py:43
  59.0 1.0 %convert_element_type.177 = f32[16,8320]{1,0:T(8,128)S(1)} convert(bf16[16,8320]{1,0:T(8,128)(2,1)} %collective-permute-done.3) | non-fusion elementwise | flops 133120 | bytes 798720 | tf_op jit(solution)/shard_map/convert_element_type | solution.py:43
  60.0 2.3 %multiply_reduce_fusion = (f32[16]{0:T(128)}, f32[16,4096]{1,0:T(8,128)S(1)}, f32[16,4096]{1,0:T(8,128)}) fusion(f32[]{:T(128)S(6)} %sub.76, f32[16,8320]{1,0:T(8,128)S(1)} %convert_element_type.177, f32[16]{0:T(128)} %get-tuple-element.86, f32[]{:T(128)S(6)} %convert_element_type.178, f32[]{:T(128)S(6)} %sub.74, f32[16,8320]{1,0:T(8,128)S(1)} %convert_element_type.175, ...), kind=kLoop, calls=%fused_computation.87 | loop fusion | flops 1703920 | bytes 2097504 | tf_op jit(solution)/shard_map/reduce_sum | solution.py:185
  62.3 1.1 %reshape.256 = f32[2,8,64,64]{3,2,1,0:T(8,128)S(1)} reshape(f32[16,4096]{1,0:T(8,128)} %get-tuple-element.97) | data formatting | bytes 524288 | tf_op jit(solution)/shard_map/reshape | solution.py:52
  63.5 1.8 %convolution_bitcast_fusion.3 = f32[2,256,64]{1,2,0:T(8,128)S(1)} fusion(f32[2,8,64,64]{3,2,1,0:T(8,128)S(1)} %reshape.256, bf16[256,2,8,64]{0,3,2,1:T(8,128)(2,1)S(1)} %bitcast.197, f32[256,2,8]{0,2,1:T(8,128)} %copy-done.13), kind=kOutput, calls=%fused_computation.48 | convolution fusion | flops 201850880 | bytes 933888 | tf_op jit(solution)/shard_map/transpose(jvp(tgn,ghpn->tghp))/dot_general | solution.py:126
  65.3 1.6 %fusion.70 = (f32[256,2,8]{0,2,1:T(8,128)S(1)}, f32[256,2,8,64]{0,3,2,1:T(8,128)}) fusion(bf16[256,2,512]{0,2,1:T(8,128)(2,1)S(1)} %copy.107, f32[2,8,64,64]{3,2,1,0:T(8,128)S(1)} %reshape.256, bf16[256,2,64]{0,2,1:T(8,128)(2,1)S(1)} %get-tuple-element.133), kind=kOutput, calls=%fused_computation.67 | convolution fusion | flops 202108928 | bytes 1916928 | tf_op jit(solution)/shard_map/jvp(tgn,ghpn->tghp)/dot_general | solution.py:126
  67.8 1.6 %fusion.69 = (f32[256,2,8]{0,2,1:T(8,128)S(1)}, f32[256,2,8,64]{0,3,2,1:T(8,128)}) fusion(bf16[256,2,512]{0,2,1:T(8,128)(2,1)S(1)} %copy.104, f32[2,8,64,64]{3,2,1,0:T(8,128)S(1)} %reshape.257, bf16[256,2,64]{0,2,1:T(8,128)(2,1)S(1)} %get-tuple-element.98), kind=kOutput, calls=%fused_computation.66 | convolution fusion | flops 202633216 | bytes 1916928 | tf_op jit(solution)/shard_map/transpose(jvp(sghp,sgn->ghpn))/dot_general | solution.py:121
  69.5 0.7 reduce_sum.90
  70.1 1.2 %fusion.118 = (f32[2,8]{1,0:T(2,128)}, f32[2,8,256]{2,1,0:T(8,128)S(1)}, f32[256,2,8]{0,2,1:T(8,128)}) fusion(f32[256,2,8]{0,2,1:T(8,128)S(1)} %get-tuple-element.129, f32[2,8]{1,0:T(2,128)S(1)} %copy-done.37, f32[256,16]{0,1:S(1)} %copy-done.11, f32[256,2,8]{0,2,1:T(8,128)S(1)} %copy-done.24, f32[2,8]{1,0:T(2,128)S(1)} %copy-done.57, ...), kind=kLoop, calls=%fused_computation.161 | loop fusion | flops 49136 | bytes 98496 | tf_op jit(solution)/shard_map/transpose(jvp())/reduce_sum | solution.py:119
  71.4 6.0 %fusion.18 = (f32[2,8,256]{2,1,0:T(8,128)}, f32[2,8,256]{2,1,0:T(8,128)}, f32[2,8,256]{2,1,0:T(8,128)}, f32[2,256,256]{2,1,0:T(8,128)S(1)}) fusion(f32[2,8,256]{2,1,0:T(8,128)} %bitcast.213, f32[2,8,256]{2,1,0:T(8,128)S(1)} %get-tuple-element.111, f32[2,256,256]{2,1,0:T(8,128)} %fusion.140, pred[256,256]{1,0:T(8,128)(4,1)} %iota_compare_fusion, ...), kind=kOutput, calls=%fused_computation.27 | convolution fusion | flops 156094464 | bytes 2244608 | tf_op jit(solution)/shard_map/transpose(jvp(ghts,sghp->tghp))/dot_general | solution.py:109
  77.5 2.3 %fusion.48 = bf16[256,2,8,64]{0,3,2,1:T(8,128)(2,1)} fusion(bf16[2,8,64,256]{3,2,1,0:T(8,128)(2,1)S(1)} %bitcast.200, f32[2,8,256]{2,1,0:T(8,128)S(1)} %get-tuple-element.111, f32[2,8,256]{2,1,0:T(8,128)S(1)} %bitcast.214, f32[2,256,256]{2,1,0:T(8,128)S(1)} %copy-done.5, pred[256,256]{1,0:T(8,128)(4,1)S(1)} %copy-done.21, ...), kind=kOutput, calls=%fused_computation.41 | convolution fusion | flops 142606336 | bytes 3260480 | tf_op jit(solution)/shard_map/transpose(jvp(ghts,sghp->tghp))/dot_general | solution.py:109
  79.9 1.9 %fusion.30 = bf16[256,2,8,64]{0,3,2,1:T(8,128)(2,1)S(1)} fusion(bf16[256,2,8,64]{0,3,2,1:T(8,128)(2,1)S(1)} %bitcast.204, f32[2,8,256]{2,1,0:T(8,128)S(1)} %get-tuple-element.111, f32[2,8,256]{2,1,0:T(8,128)S(1)} %bitcast.215, f32[2,256,256]{2,1,0:T(8,128)S(1)} %copy-done.5, pred[256,256]{1,0:T(8,128)(4,1)S(1)} %copy-done.21, ...), kind=kOutput, calls=%fused_computation.35 | convolution fusion | flops 142082048 | bytes 2736192 | tf_op jit(solution)/shard_map/jvp(ghts,sghp->tghp)/dot_general | solution.py:109
  81.8 0.7 copy.117
  84.1 1.1 %bitcast_convert_fusion = f32[256,2,512]{0,2,1:T(8,128)} fusion(bf16[256,2,8,64]{0,3,2,1:T(8,128)(2,1)S(1)} %copy-done.4), kind=kLoop, calls=%fused_computation.72 | loop fusion | flops 262144 | bytes 1572864 | tf_op jit(solution)/shard_map/convert_element_type | solution.py:70
  85.2 1.5 %copy.109 = f32[256,2,512]{2,1,0:T(2,128)S(1)} copy(f32[256,2,512]{0,2,1:T(8,128)} %bitcast_convert_fusion) | data formatting | bytes 2097152 | tf_op jit(solution)/shard_map/convert_element_type | solution.py:70
  86.8 1.5 %multiply_multiply_fusion = f32[256,2,512]{2,1,0:T(2,128)S(1)} fusion(f32[256,2,512]{2,1,0:T(2,128)S(1)} %copy.109, f32[256,2,512]{2,1,0:T(2,128)S(1)} %get-tuple-element.103), kind=kLoop, calls=%fused_computation.68 | loop fusion | flops 2097152 | bytes 3145728 | tf_op jit(solution)/shard_map/mul | solution.py:70
  88.5 1.3 %multiply_add_fusion = f32[259,2,512]{2,1,0:T(2,128)S(1)} fusion(f32[256,2,512]{2,1,0:T(2,128)S(1)} %multiply_multiply_fusion, f32[2,512]{1,0:T(2,128)S(1)} %copy-done.31, f32[2,512]{1,0:T(2,128)S(1)} %copy-done.33, f32[2,512]{1,0:T(2,128)S(1)} %copy-done.29, f32[2,512]{1,0:T(2,128)S(1)} %copy-done.27), kind=kLoop, calls=%fused_computation.64 | loop fusion | flops 1856512 | bytes 2125824 | tf_op jit(solution)/shard_map/add | solution.py:78
  89.8 1.3 %collective-permute-start.4 = (f32[3,1280]{1,0:T(4,128)S(1)}, f32[3,1280]{1,0:T(4,128)S(1)}, u32[]{:S(2)}, u32[]{:S(2)}) collective-permute-start(f32[3,1280]{1,0:T(4,128)S(1)} %pad_maximum_fusion.5), channel_id=1, source_target_pairs={{2,0},{4,2},{6,4},{8,6},{10,8},{12,10},{14,12},{3,1},{5,3},{7,5},{... | collective-permute-start | bytes 46088 | tf_op jit(solution)/shard_map/ppermute | solution.py:12
  91.7 0.9 fusion.64
  93.1 1.2 %copy.118 = bf16[256,2,512]{2,1,0:T(2,128)(2,1)} copy(bf16[256,2,512]{0,2,1:T(8,128)(2,1)S(1)} %bitcast.205) | data formatting | bytes 1048576
  94.3 1.2 %collective-permute-done.4 = f32[3,1280]{1,0:T(4,128)S(1)} collective-permute-done((f32[3,1280]{1,0:T(4,128)S(1)}, f32[3,1280]{1,0:T(4,128)S(1)}, u32[]{:S(2)}, u32[]{:S(2)}) %collective-permute-start.4) | collective-permute-done | bytes 15392 | tf_op jit(solution)/shard_map/ppermute | solution.py:12
  97.5 0.8 copy-done.6
  (200 shorter events, 11.1 us)
Async XLA Ops:
  0.6 15.9 %copy-start.18 = (bf16[256,2,64]{0,2,1:T(8,128)(2,1)S(1)}, bf16[256,2,64]{0,2,1:T(8,128)(2,1)}, u32[]{:S(2)}) copy-start(bf16[256,2,64]{0,2,1:T(8,128)(2,1)} %param.21) | copy-start | bytes 196612
  0.6 15.9 %copy-start.17 = (bf16[256,2,64]{0,2,1:T(8,128)(2,1)S(1)}, bf16[256,2,64]{0,2,1:T(8,128)(2,1)}, u32[]{:S(2)}) copy-start(bf16[256,2,64]{0,2,1:T(8,128)(2,1)} %param.22) | copy-start | bytes 196612
  3.3 12.9 %collective-permute-start = (bf16[3,1280]{1,0:T(4,128)(2,1)S(1)}, bf16[3,1280]{1,0:T(4,128)(2,1)S(1)}, u32[]{:S(2)}, u32[]{:S(2)}) collective-permute-start(bf16[3,1280]{1,0:T(4,128)(2,1)S(1)} %pad_maximum_fusion.6), channel_id=1, source_target_pairs={{0,2},{2,4},{4,6},{6,8},{8,10},{10,12},{12,14},{1,3},{3,5},{5,7},{... | collective-permute-start | bytes 23048 | tf_op jit(solution)/shard_map/ppermute | solution.py:12
  9.6 8.7 %copy-start.39 = (f32[2,64]{1,0:T(2,128)}, f32[2,64]{1,0:T(2,128)S(1)}, u32[]{:S(2)}) copy-start(f32[2,64]{1,0:T(2,128)S(1)} %get-tuple-element.121) | copy-start | bytes 1540
  9.6 8.7 %copy-start.41 = (f32[2,64]{1,0:T(2,128)}, f32[2,64]{1,0:T(2,128)S(1)}, u32[]{:S(2)}) copy-start(f32[2,64]{1,0:T(2,128)S(1)} %get-tuple-element.122) | copy-start | bytes 1540
  9.6 8.7 %copy-start.43 = (f32[2,64]{1,0:T(2,128)}, f32[2,64]{1,0:T(2,128)S(1)}, u32[]{:S(2)}) copy-start(f32[2,64]{1,0:T(2,128)S(1)} %get-tuple-element.123) | copy-start | bytes 1540
  9.6 8.7 %copy-start.45 = (f32[2,64]{1,0:T(2,128)}, f32[2,64]{1,0:T(2,128)S(1)}, u32[]{:S(2)}) copy-start(f32[2,64]{1,0:T(2,128)S(1)} %get-tuple-element.124) | copy-start | bytes 1540
  10.6 3.8 %copy-start.10 = (f32[256,16]{0,1}, f32[256,16]{0,1:S(1)}, u32[]{:S(2)}) copy-start(f32[256,16]{0,1:S(1)} %fusion.82) | copy-start | bytes 49156
  10.8 5.7 %copy-start.36 = (f32[2,8]{1,0:T(2,128)}, f32[2,8]{1,0:T(2,128)S(1)}, u32[]{:S(2)}) copy-start(f32[2,8]{1,0:T(2,128)S(1)} %get-tuple-element.93) | copy-start | bytes 196
  12.1 7.5 %copy-start.26 = (f32[2,512]{1,0:T(2,128)}, f32[2,512]{1,0:T(2,128)S(1)}, u32[]{:S(2)}) copy-start(f32[2,512]{1,0:T(2,128)S(1)} %get-tuple-element.115) | copy-start | bytes 12292
  12.1 7.5 %copy-start.28 = (f32[2,512]{1,0:T(2,128)}, f32[2,512]{1,0:T(2,128)S(1)}, u32[]{:S(2)}) copy-start(f32[2,512]{1,0:T(2,128)S(1)} %get-tuple-element.116) | copy-start | bytes 12292
  13.5 4.8 %copy-start.13 = (f32[256,2,8]{0,2,1:T(8,128)}, f32[256,2,8]{0,2,1:T(8,128)S(1)}, u32[]{:S(2)}) copy-start(f32[256,2,8]{0,2,1:T(8,128)S(1)} %get-tuple-element.114) | copy-start | bytes 49156
  14.3 4.1 %copy-start.47 = (f32[2,64]{1,0:T(2,128)}, f32[2,64]{1,0:T(2,128)S(1)}, u32[]{:S(2)}) copy-start(f32[2,64]{1,0:T(2,128)S(1)} %get-tuple-element.125) | copy-start | bytes 1540
  14.3 4.1 %copy-start.49 = (f32[2,64]{1,0:T(2,128)}, f32[2,64]{1,0:T(2,128)S(1)}, u32[]{:S(2)}) copy-start(f32[2,64]{1,0:T(2,128)S(1)} %get-tuple-element.126) | copy-start | bytes 1540
  14.3 4.1 %copy-start.51 = (f32[2,64]{1,0:T(2,128)}, f32[2,64]{1,0:T(2,128)S(1)}, u32[]{:S(2)}) copy-start(f32[2,64]{1,0:T(2,128)S(1)} %get-tuple-element.127) | copy-start | bytes 1540
  14.3 4.1 %copy-start.53 = (f32[2,64]{1,0:T(2,128)}, f32[2,64]{1,0:T(2,128)S(1)}, u32[]{:S(2)}) copy-start(f32[2,64]{1,0:T(2,128)S(1)} %get-tuple-element.128) | copy-start | bytes 1540
  23.9 10.3 %copy-start = (f32[16,4096]{1,0:T(8,128)}, f32[16,4096]{1,0:T(8,128)S(1)}, u32[]{:S(2)}) copy-start(f32[16,4096]{1,0:T(8,128)S(1)} %reshape.252) | copy-start | bytes 786436
  23.9 10.1 %copy-start.61 = (f32[16]{0:T(128)S(1)}, f32[16]{0:T(128)}, u32[]{:S(2)}) copy-start(f32[16]{0:T(128)} %copy-done.60) | copy-start | bytes 196
  24.1 7.9 %collective-permute-start.1 = (bf16[16,8320]{1,0:T(8,128)(2,1)S(1)}, bf16[16,8320]{1,0:T(8,128)(2,1)S(1)}, u32[]{:S(2)}, u32[]{:S(2)}) collective-permute-start(bf16[16,8320]{1,0:T(8,128)(2,1)S(1)} %pad_maximum_fusion), channel_id=1, source_target_pairs={{0,2},{2,0},{4,6},{6,4},{8,10},{10,8},{12,14},{14,12},{1,3},{3,1},... | collective-permute-start | bytes 798728 | tf_op jit(solution)/shard_map/ppermute | solution.py:43
  34.3 7.1 %collective-permute-start.2 = (bf16[16,8320]{1,0:T(8,128)(2,1)S(1)}, bf16[16,8320]{1,0:T(8,128)(2,1)}, u32[]{:S(2)}, u32[]{:S(2)}) collective-permute-start(bf16[16,8320]{1,0:T(8,128)(2,1)S(1)} %pad_maximum_fusion.1), channel_id=1, source_target_pairs={{0,4},{2,6},{4,0},{6,2},{8,12},{10,14},{12,8},{14,10},{1,5},{3,7},... | collective-permute-start | bytes 798728 | tf_op jit(solution)/shard_map/ppermute | solution.py:43
  46.1 12.9 %collective-permute-start.3 = (bf16[16,8320]{1,0:T(8,128)(2,1)}, bf16[16,8320]{1,0:T(8,128)(2,1)}, u32[]{:S(2)}, u32[]{:S(2)}) collective-permute-start(bf16[16,8320]{1,0:T(8,128)(2,1)} %pad_maximum_fusion.2), channel_id=1, source_target_pairs={{0,8},{2,10},{4,12},{6,14},{8,0},{10,2},{12,4},{14,6},{1,9},{3,11}... | collective-permute-start | bytes 798728 | tf_op jit(solution)/shard_map/ppermute | solution.py:43
  67.8 2.3 %copy-start.11 = (f32[256,16]{0,1:S(1)}, f32[256,16]{0,1}, u32[]{:S(2)}) copy-start(f32[256,16]{0,1} %copy-done.10) | copy-start | bytes 49156
  67.8 2.3 %copy-start.24 = (f32[256,2,8]{0,2,1:T(8,128)S(1)}, f32[256,2,8]{0,2,1:T(8,128)}, u32[]{:S(2)}) copy-start(f32[256,2,8]{0,2,1:T(8,128)} %param.23) | copy-start | bytes 49156
  71.4 6.1 %copy-start.3 = (f32[256,2,8,64]{0,3,2,1:T(8,128)S(1)}, f32[256,2,8,64]{0,3,2,1:T(8,128)}, u32[]{:S(2)}) copy-start(f32[256,2,8,64]{0,3,2,1:T(8,128)} %get-tuple-element.130) | copy-start | bytes 3145732
  71.4 6.1 %copy-start.5 = (f32[2,256,256]{2,1,0:T(8,128)S(1)}, f32[2,256,256]{2,1,0:T(8,128)}, u32[]{:S(2)}) copy-start(f32[2,256,256]{2,1,0:T(8,128)} %fusion.140) | copy-start | bytes 1572868
  71.4 6.1 %copy-start.12 = (f32[256,16]{0,1:S(1)}, f32[256,16]{0,1}, u32[]{:S(2)}) copy-start(f32[256,16]{0,1} %copy-done.10) | copy-start | bytes 49156
  71.4 6.1 %copy-start.16 = (f32[256,2,8]{0,2,1:T(8,128)S(1)}, f32[256,2,8]{0,2,1:T(8,128)}, u32[]{:S(2)}) copy-start(f32[256,2,8]{0,2,1:T(8,128)} %get-tuple-element.113) | copy-start | bytes 49156
  71.4 6.1 %copy-start.21 = (pred[256,256]{1,0:T(8,128)(4,1)S(1)}, pred[256,256]{1,0:T(8,128)(4,1)}, u32[]{:S(2)}) copy-start(pred[256,256]{1,0:T(8,128)(4,1)} %iota_compare_fusion) | copy-start | bytes 196612
  71.4 6.1 %copy-start.67 = (f32[2,8]{1,0:T(2,128)S(1)}, f32[2,8]{1,0:T(2,128)}, u32[]{:S(2)}) copy-start(f32[2,8]{1,0:T(2,128)} %param.26) | copy-start | bytes 196
  77.5 2.4 %copy-start.2 = (f32[256,2,8,64]{0,3,2,1:T(8,128)S(1)}, f32[256,2,8,64]{0,3,2,1:T(8,128)}, u32[]{:S(2)}) copy-start(f32[256,2,8,64]{0,3,2,1:T(8,128)} %get-tuple-element.132) | copy-start | bytes 3145732
  77.5 2.4 %copy-start.14 = (f32[256,2,8]{0,2,1:T(8,128)S(1)}, f32[256,2,8]{0,2,1:T(8,128)}, u32[]{:S(2)}) copy-start(f32[256,2,8]{0,2,1:T(8,128)} %copy-done.13) | copy-start | bytes 49156
  79.9 2.7 %copy-start.8 = (f32[256,2,64]{0,2,1:T(8,128)S(1)}, f32[256,2,64]{0,2,1:T(8,128)}, u32[]{:S(2)}) copy-start(f32[256,2,64]{0,2,1:T(8,128)} %get-tuple-element.99) | copy-start | bytes 393220
  79.9 3.0 %copy-start.40 = (f32[2,64]{1,0:T(2,128)S(1)}, f32[2,64]{1,0:T(2,128)}, u32[]{:S(2)}) copy-start(f32[2,64]{1,0:T(2,128)} %copy-done.39) | copy-start | bytes 1540
  79.9 3.0 %copy-start.42 = (f32[2,64]{1,0:T(2,128)S(1)}, f32[2,64]{1,0:T(2,128)}, u32[]{:S(2)}) copy-start(f32[2,64]{1,0:T(2,128)} %copy-done.41) | copy-start | bytes 1540
  79.9 3.0 %copy-start.44 = (f32[2,64]{1,0:T(2,128)S(1)}, f32[2,64]{1,0:T(2,128)}, u32[]{:S(2)}) copy-start(f32[2,64]{1,0:T(2,128)} %copy-done.43) | copy-start | bytes 1540
  79.9 3.0 %copy-start.46 = (f32[2,64]{1,0:T(2,128)S(1)}, f32[2,64]{1,0:T(2,128)}, u32[]{:S(2)}) copy-start(f32[2,64]{1,0:T(2,128)} %copy-done.45) | copy-start | bytes 1540
  88.4 2.8 %copy-start.34 = (f32[256,2,8]{0,2,1:T(8,128)S(1)}, f32[256,2,8]{0,2,1:T(8,128)}, u32[]{:S(2)}) copy-start(f32[256,2,8]{0,2,1:T(8,128)} %get-tuple-element.112) | copy-start | bytes 49156
  88.4 2.7 %copy-start.35 = (f32[1,2,8]{0,2,1:T(8,128)S(1)}, f32[1,2,8]{0,2,1:T(8,128)}, u32[]{:S(2)}) copy-start(f32[1,2,8]{0,2,1:T(8,128)} %reduce_sum.90) | copy-start | bytes 196
  88.4 3.0 %copy-start.65 = (f32[2,8]{1,0:T(2,128)S(1)}, f32[2,8]{1,0:T(2,128)}, u32[]{:S(2)}) copy-start(f32[2,8]{1,0:T(2,128)} %copy-done.64) | copy-start | bytes 196
  88.4 3.0 %copy-start.68 = (f32[2,8,256]{2,1,0:T(8,128)S(1)}, f32[2,8,256]{2,1,0:T(8,128)}, u32[]{:S(2)}) copy-start(f32[2,8,256]{2,1,0:T(8,128)} %get-tuple-element.82) | copy-start | bytes 49156
  88.4 3.0 %copy-start.69 = (f32[2,8,256]{2,1,0:T(8,128)S(1)}, f32[2,8,256]{2,1,0:T(8,128)}, u32[]{:S(2)}) copy-start(f32[2,8,256]{2,1,0:T(8,128)} %get-tuple-element.83) | copy-start | bytes 49156
  88.4 3.0 %copy-start.70 = (f32[2,8,256]{2,1,0:T(8,128)S(1)}, f32[2,8,256]{2,1,0:T(8,128)}, u32[]{:S(2)}) copy-start(f32[2,8,256]{2,1,0:T(8,128)} %get-tuple-element.84) | copy-start | bytes 49156
  88.4 3.2 %copy-start.20 = (f32[256,2,8]{0,2,1:T(8,128)S(1)}, f32[256,2,8]{0,2,1:T(8,128)}, u32[]{:S(2)}) copy-start(f32[256,2,8]{0,2,1:T(8,128)} %copy-done.19) | copy-start | bytes 49156
  88.5 3.2 %copy-start.25 = (f32[256,2,8]{0,2,1:T(8,128)S(1)}, f32[256,2,8]{0,2,1:T(8,128)}, u32[]{:S(2)}) copy-start(f32[256,2,8]{0,2,1:T(8,128)} %param.23) | copy-start | bytes 49156
  88.5 3.2 %copy-start.38 = (f32[2,8]{1,0:T(2,128)S(1)}, f32[2,8]{1,0:T(2,128)}, u32[]{:S(2)}) copy-start(f32[2,8]{1,0:T(2,128)} %copy-done.36) | copy-start | bytes 196
  88.5 3.2 %copy-start.55 = (f32[1,2,8]{0,2,1:T(8,128)S(1)}, f32[1,2,8]{0,2,1:T(8,128)}, u32[]{:S(2)}) copy-start(f32[1,2,8]{0,2,1:T(8,128)} %copy.117) | copy-start | bytes 196
  88.5 3.2 %copy-start.58 = (f32[2,8]{1,0:T(2,128)S(1)}, f32[2,8]{1,0:T(2,128)}, u32[]{:S(2)}) copy-start(f32[2,8]{1,0:T(2,128)} %param.25) | copy-start | bytes 196
  89.8 5.7 %collective-permute-start.4 = (f32[3,1280]{1,0:T(4,128)S(1)}, f32[3,1280]{1,0:T(4,128)S(1)}, u32[]{:S(2)}, u32[]{:S(2)}) collective-permute-start(f32[3,1280]{1,0:T(4,128)S(1)} %pad_maximum_fusion.5), channel_id=1, source_target_pairs={{2,0},{4,2},{6,4},{8,6},{10,8},{12,10},{14,12},{3,1},{5,3},{7,5},{... | collective-permute-start | bytes 46088 | tf_op jit(solution)/shard_map/ppermute | solution.py:12
  (28 other events, 38.8 us)

commit v10 on v5

--- a/solution.py
+++ b/solution.py
@@ -66,12 +66,10 @@
 def conv_forward(extended, weight):
     kernel_width = weight.shape[0]
     length = extended.shape[0] - kernel_width + 1
-    running = weight[0] * extended[0:length].astype(jnp.float32)
-    for tap_index in range(1, kernel_width):
-        running = running + weight[tap_index] * extended[tap_index : tap_index + length].astype(
-            jnp.float32
-        )
-    return running
+    windows = jnp.stack(
+        [extended[tap_index : tap_index + length] for tap_index in range(kernel_width)], 0
+    )
+    return jnp.sum(weight[:, None] * windows.astype(jnp.float32), axis=0)
 
 
 def conv_backward(grad_out, running, weight):
@@ -81,11 +79,14 @@
     ext_len = inner_grad.shape[0] + kernel_width - 1
     padding = [(kernel_width - 1, kernel_width - 1)] + [(0, 0)] * (inner_grad.ndim - 1)
     padded = jnp.pad(inner_grad, padding)
-    result = weight[0] * padded[kernel_width - 1 : kernel_width - 1 + ext_len]
-    for tap_index in range(1, kernel_width):
-        offset = kernel_width - 1 - tap_index
-        result = result + weight[tap_index] * padded[offset : offset + ext_len]
-    return result
+    windows = jnp.stack(
+        [
+            padded[kernel_width - 1 - tap_index : kernel_width - 1 - tap_index + ext_len]
+            for tap_index in range(kernel_width)
+        ],
+        0,
+    )
+    return jnp.sum(weight[:, None] * windows, axis=0)
 
 
 def ssd_cum(dt_raw, rate, dt_bias):
@@ -146,21 +147,12 @@
     x_span = groups * channels
     b_span = groups * state_size
     outgoing = jnp.concatenate(
-        [
-            x_in[length - halo_rows :].reshape(halo_rows, x_span),
-            b_in[length - halo_rows :].reshape(halo_rows, b_span),
-            c_in[length - halo_rows :].reshape(halo_rows, b_span),
-        ],
-        1,
+        [x_in[length - halo_rows :], b_in[length - halo_rows :], c_in[length - halo_rows :]], 2
     )
     incoming = from_behind(outgoing, "ctx", 1)
-    x_ext = jnp.concatenate([incoming[:, :x_span].reshape(halo_rows, groups, channels), x_in], 0)
-    b_ext = jnp.concatenate(
-        [incoming[:, x_span : x_span + b_span].reshape(halo_rows, groups, state_size), b_in], 0
-    )
-    c_ext = jnp.concatenate(
-        [incoming[:, x_span + b_span :].reshape(halo_rows, groups, state_size), c_in], 0
-    )
+    x_ext = jnp.concatenate([incoming[:, :, :channels], x_in], 0)
+    b_ext = jnp.concatenate([incoming[:, :, channels : channels + state_size], b_in], 0)
+    c_ext = jnp.concatenate([incoming[:, :, channels + state_size :], c_in], 0)
     x_running = conv_forward(x_ext, conv_x)
     b_running = conv_forward(b_ext, conv_b)
     c_running = conv_forward(c_ext, conv_c)
@@ -202,17 +194,12 @@
     grad_c_ext = conv_backward(grad_c_part.astype(jnp.bfloat16), c_running, conv_c)
     grad_x_ext = conv_backward(grad_x_conv.astype(jnp.bfloat16), x_running, conv_x)
     leaving = jnp.concatenate(
-        [
-            grad_x_ext[:halo_rows].reshape(halo_rows, x_span),
-            grad_b_ext[:halo_rows].reshape(halo_rows, b_span),
-            grad_c_ext[:halo_rows].reshape(halo_rows, b_span),
-        ],
-        1,
+        [grad_x_ext[:halo_rows], grad_b_ext[:halo_rows], grad_c_ext[:halo_rows]], 2
     )
     returned = from_behind(leaving, "ctx", -1)
-    back_x = returned[:, :x_span].reshape(halo_rows, groups, channels)
-    back_b = returned[:, x_span : x_span + b_span].reshape(halo_rows, groups, state_size)
-    back_c = returned[:, x_span + b_span :].reshape(halo_rows, groups, state_size)
+    back_x = returned[:, :, :channels]
+    back_b = returned[:, :, channels : channels + state_size]
+    back_c = returned[:, :, channels + state_size :]
     grad_x = grad_x_ext[halo_rows:].at[length - halo_rows :].add(back_x).astype(jnp.bfloat16)
     grad_b = grad_b_ext[halo_rows:].at[length - halo_rows :].add(back_b).astype(jnp.bfloat16)
     grad_c = grad_c_ext[halo_rows:].at[length - halo_rows :].add(back_c).astype(jnp.bfloat16)

time: 96.4 us -> 99.9 us (1.036)
  other arithmetic: 13.4 us -> 16.6 us
  matrix products: 20.4 us -> 22 us
    reduce_sum x0 -> x6, other arithmetic: none -> 5.14 us  [the longest x3 4.27 us: conv_forward(): return jnp.sum(weight[:, None] * windows.astype(jnp.float32), axis=0)]
    another operation x8 -> x11, other arithmetic: 0.57 us -> 3.6 us  [the longest x3 2.37 us: conv_forward(): jnp.stack([extended[tap_index:tap_index + length] for tap_index in range(...]
    mul x3 -> x0, local copies, waits for them, and re-layouts: 2.21 us -> none  [conv_forward(): running = weight[0] * extended[0:length].astype(jnp.float32)]
    convert_element_type x1, other arithmetic: 2.42 us -> 0.28 us  [on_device(): x_float = jax.nn.silu(x_running).astype(jnp.bfloat16).astype(jnp.float32)]
    add x3 -> x0, other arithmetic: 1.86 us -> none  [conv_backward(): result = result + weight[tap_index] * padded[offset:offset + ext_len]]
    unnamed x129 -> x97, local copies, waits for them, and re-layouts: 5.13 us -> 6.37 us
    convert_element_type x1, local copies, waits for them, and re-layouts: 1.54 us -> 0.33 us  [conv_backward(): grad_out.astype(jnp.float32)]
    mul x1, other arithmetic: 1.51 us -> 0.4 us  [conv_backward(): grad_out.astype(jnp.float32)]
  transfers between devices with their start and end apart: 8 -> 8, of which waited for: 7 -> 7; matrix products, arithmetic and copies ran while one was open for 12% -> 11% of each run, Pallas kernels for 0% -> 0%
where the time goes in v10:
time: 99.9 us; the launch traced here: 98.9 us
  starting transfers between devices  22.6 us (23%)
  matrix products  22 us (22%)
  waiting for transfers between devices  19.9 us (20%)
  other arithmetic  16.6 us (17%)
  local copies, waits for them, and re-layouts  16.5 us (17%)
  between operations  1.46 us (1%)
    ppermute x6, waiting for transfers between devices, shift(): return lax.ppermute(packed, axis, pairs)  18.9 us
    ppermute x6, starting transfers between devices, shift(): return lax.ppermute(packed, axis, pairs)  16.3 us
    dot_general x3, matrix products, ssd_mix(): jnp.einsum('ghts,sghp->tghp', mixing, x_half, preferred_element_type=jnp....  10.5 us
    unnamed x97, local copies, waits for them, and re-layouts  6.37 us
    ppermute x2, starting transfers between devices, from_behind(): return lax.ppermute(array, axis, pairs)  6.25 us
    reduce_sum x3, other arithmetic, conv_forward(): return jnp.sum(weight[:, None] * windows.astype(jnp.float32), axis=0)  4.27 us
    dot_general x2, matrix products, carry_in(): carried = jnp.einsum('tgn,ghpn->tghp', c_float, state_in, precision=HIGH)  3.26 us
    dot_general x3, matrix products, ssd_state(): jnp.einsum('sghp,sgn->ghpn', weighted.astype(jnp.float32), b_float, preci...  3.16 us
  transfers between devices with their start and end apart: 8, of which 7 were waited for; matrix products, arithmetic and copies ran while one was open for 11% of the time, Pallas kernels for 0%

profile of v10, /device:TPU:0, one launch (start us, length us, event | category | flops | bytes accessed | tf_op | source)
XLA Modules:
  0.0 98.9 jit_solution(7792507592728643264)
XLA Ops:
  0.7 0.8 slice.245
  1.4 0.8 slice.246
  2.4 0.8 slice.247
  3.4 4.8 %collective-permute-start = (bf16[3,2,640]{2,1,0:T(2,128)(2,1)S(1)}, bf16[3,2,640]{2,1,0:T(2,128)(2,1)S(1)}, u32[]{:S(2)}, u32[]{:S(2)}) collective-permute-start(bf16[3,2,640]{2,1,0:T(2,128)(2,1)S(1)} %pad_maximum_fusion.10), channel_id=1, source_target_pairs={{0,2},{2,4},{4,6},{6,8},{8,10},{10,12},{12,14},{1,3},{3,5},{5,7},{... | collective-permute-start | bytes 23048 | tf_op jit(solution)/shard_map/ppermute | solution.py:12
  8.2 0.7 neg.33
  8.9 0.9 fusion.84
  10.1 1.4 %fusion.121 = (f32[256,2,8]{0,2,1:T(8,128)}, f32[256,2,8]{0,2,1:T(8,128)S(1)}) fusion(f32[2,8]{1,0:T(2,128)S(1)} %slice_reduce_fusion, f32[256,16]{0,1:S(1)} %fusion.84, f32[256,2,8]{0,2,1:T(8,128)} %param.23, f32[2,8]{1,0:T(2,128)} %param.25), kind=kLoop, calls=%fused_computation.175 | loop fusion | flops 36864 | bytes 65664 | tf_op jit(solution)/shard_map/jvp()/mul | solution.py:129
  11.5 0.6 fusion.139
  12.1 1.3 %copy.164 = bf16[256,2,512]{0,2,1:T(8,128)(2,1)S(1)} copy(bf16[256,2,512]{2,1,0:T(2,128)(2,1)} %param.30) | data formatting | bytes 1048576 | tf_op args[10]
  15.0 0.6 fusion.53
  15.8 0.7 convert.54
  16.5 2.1 %fusion.79 = (bf16[1,256,2,512]{3,2,1,0:T(2,128)(2,1)S(1)}, bf16[1,256,2,512]{3,2,1,0:T(2,128)(2,1)S(1)}, bf16[1,256,2,512]{3,2,1,0:T(2,128)(2,1)S(1)}) fusion(bf16[3,2,512]{2,1,0:T(2,128)(2,1)S(1)} %slice.298, bf16[256,2,512]{2,1,0:T(2,128)(2,1)S(1)} %copy-done), kind=kLoop, calls=%fused_computation.91 | loop fusion | flops 786432 | bytes 2103296 | tf_op jit(solution)/shard_map/stack | solution.py:69
  18.6 4.0 %multiply_reduce_fusion = f32[256,2,512]{2,1,0:T(2,128)S(1)} fusion(bf16[1,256,2,512]{3,2,1,0:T(2,128)(2,1)S(1)} %bitcast.213, bf16[1,256,2,512]{3,2,1,0:T(2,128)(2,1)S(1)} %get-tuple-element.109, bf16[1,256,2,512]{3,2,1,0:T(2,128)(2,1)S(1)} %get-tuple-element.110, bf16[1,256,2,512]{3,2,1,0:T(2,128)(2,1)S(1)} %get-tuple-element.108, ...), kind=kLoop, calls=%fused_computation.19 | loop fusion | flops 6029312 | bytes 3162112 | tf_op jit(solution)/shard_map/reduce_sum | solution.py:72
  22.6 0.6 copy.160
  24.5 0.7 broadcast_in_dim.33
  25.3 3.5 %collective-permute-start.1 = (bf16[2,8,4224]{2,1,0:T(8,128)(2,1)S(1)}, bf16[2,8,4224]{2,1,0:T(8,128)(2,1)S(1)}, u32[]{:S(2)}, u32[]{:S(2)}) collective-permute-start(bf16[2,8,4224]{2,1,0:T(8,128)(2,1)S(1)} %get-tuple-element.134), channel_id=1, source_target_pairs={{0,2},{2,4},{4,6},{6,8},{8,10},{10,12},{12,14},{1,3},{3,5},{5,7},{... | collective-permute-start | bytes 405512 | tf_op jit(solution)/shard_map/ppermute | solution.py:27
  28.7 1.3 %collective-permute-start.4 = (bf16[2,8,4224]{2,1,0:T(8,128)(2,1)S(1)}, bf16[2,8,4224]{2,1,0:T(8,128)(2,1)S(1)}, u32[]{:S(2)}, u32[]{:S(2)}) collective-permute-start(bf16[2,8,4224]{2,1,0:T(8,128)(2,1)S(1)} %get-tuple-element.135), channel_id=1, source_target_pairs={{2,0},{4,2},{6,4},{8,6},{10,8},{12,10},{14,12},{3,1},{5,3},{7,5},{... | collective-permute-start | bytes 405512 | tf_op jit(solution)/shard_map/ppermute | solution.py:27
  30.0 1.2 %collective-permute-done.1 = bf16[2,8,4224]{2,1,0:T(8,128)(2,1)S(1)} collective-permute-done((bf16[2,8,4224]{2,1,0:T(8,128)(2,1)S(1)}, bf16[2,8,4224]{2,1,0:T(8,128)(2,1)S(1)}, u32[]{:S(2)}, u32[]{:S(2)}) %collective-permute-start.1) | collective-permute-done | bytes 135200 | tf_op jit(solution)/shard_map/ppermute | solution.py:27
  31.4 4.2 %collective-permute-done.4 = bf16[2,8,4224]{2,1,0:T(8,128)(2,1)S(1)} collective-permute-done((bf16[2,8,4224]{2,1,0:T(8,128)(2,1)S(1)}, bf16[2,8,4224]{2,1,0:T(8,128)(2,1)S(1)}, u32[]{:S(2)}, u32[]{:S(2)}) %collective-permute-start.4) | collective-permute-done | bytes 135200 | tf_op jit(solution)/shard_map/ppermute | solution.py:27
  35.9 3.9 %collective-permute-start.2 = (bf16[2,8,4224]{2,1,0:T(8,128)(2,1)S(1)}, bf16[2,8,4224]{2,1,0:T(8,128)(2,1)S(1)}, u32[]{:S(2)}, u32[]{:S(2)}) collective-permute-start(bf16[2,8,4224]{2,1,0:T(8,128)(2,1)S(1)} %pad_maximum_fusion.3), channel_id=1, source_target_pairs={{0,4},{2,6},{4,8},{6,10},{8,12},{10,14},{1,5},{3,7},{5,9},{7,11},{... | collective-permute-start | bytes 405512 | tf_op jit(solution)/shard_map/ppermute | solution.py:27
  39.8 0.7 iota_compare_fusion
  40.5 1.9 %collective-permute-done.2 = bf16[2,8,4224]{2,1,0:T(8,128)(2,1)S(1)} collective-permute-done((bf16[2,8,4224]{2,1,0:T(8,128)(2,1)S(1)}, bf16[2,8,4224]{2,1,0:T(8,128)(2,1)S(1)}, u32[]{:S(2)}, u32[]{:S(2)}) %collective-permute-start.2) | collective-permute-done | bytes 135200 | tf_op jit(solution)/shard_map/ppermute | solution.py:27
  42.6 1.3 %collective-permute-start.5 = (bf16[2,8,4224]{2,1,0:T(8,128)(2,1)S(1)}, bf16[2,8,4224]{2,1,0:T(8,128)(2,1)S(1)}, u32[]{:S(2)}, u32[]{:S(2)}) collective-permute-start(bf16[2,8,4224]{2,1,0:T(8,128)(2,1)S(1)} %pad_maximum_fusion.5), channel_id=1, source_target_pairs={{4,0},{6,2},{8,4},{10,6},{12,8},{14,10},{5,1},{7,3},{9,5},{11,7},{... | collective-permute-start | bytes 405512 | tf_op jit(solution)/shard_map/ppermute | solution.py:27
  43.9 1.1 %fusion.140 = f32[2,256,256]{2,1,0:T(8,128)} fusion(bf16[256,2,64]{0,2,1:T(8,128)(2,1)S(1)} %get-tuple-element.145, bf16[256,2,64]{0,2,1:T(8,128)(2,1)S(1)} %get-tuple-element.144), kind=kOutput, calls=%fused_computation.209 | convolution fusion | flops 16777216 | bytes 655360 | tf_op jit(solution)/shard_map/jvp(tgn,sgn->gts)/dot_general | solution.py:117
  45.0 5.0 %collective-permute-done.5 = bf16[2,8,4224]{2,1,0:T(8,128)(2,1)S(1)} collective-permute-done((bf16[2,8,4224]{2,1,0:T(8,128)(2,1)S(1)}, bf16[2,8,4224]{2,1,0:T(8,128)(2,1)S(1)}, u32[]{:S(2)}, u32[]{:S(2)}) %collective-permute-start.5) | collective-permute-done | bytes 135200 | tf_op jit(solution)/shard_map/ppermute | solution.py:27
  50.4 4.9 %collective-permute-start.3 = (bf16[2,8,4224]{2,1,0:T(8,128)(2,1)S(1)}, bf16[2,8,4224]{2,1,0:T(8,128)(2,1)S(1)}, u32[]{:S(2)}, u32[]{:S(2)}) collective-permute-start(bf16[2,8,4224]{2,1,0:T(8,128)(2,1)S(1)} %pad_maximum_fusion.4), channel_id=1, source_target_pairs={{0,8},{2,10},{4,12},{6,14},{1,9},{3,11},{5,13},{7,15},{16,24},{18,... | collective-permute-start | bytes 405512 | tf_op jit(solution)/shard_map/ppermute | solution.py:27
  55.4 1.5 %collective-permute-start.6 = (bf16[2,8,4224]{2,1,0:T(8,128)(2,1)S(1)}, bf16[2,8,4224]{2,1,0:T(8,128)(2,1)S(1)}, u32[]{:S(2)}, u32[]{:S(2)}) collective-permute-start(bf16[2,8,4224]{2,1,0:T(8,128)(2,1)S(1)} %pad_maximum_fusion.6), channel_id=1, source_target_pairs={{8,0},{10,2},{12,4},{14,6},{9,1},{11,3},{13,5},{15,7},{24,16},{26,... | collective-permute-start | bytes 405512 | tf_op jit(solution)/shard_map/ppermute | solution.py:27
  57.1 0.8 collective-permute-done.3
  57.8 5.8 %collective-permute-done.6 = bf16[2,8,4224]{2,1,0:T(8,128)(2,1)S(1)} collective-permute-done((bf16[2,8,4224]{2,1,0:T(8,128)(2,1)S(1)}, bf16[2,8,4224]{2,1,0:T(8,128)(2,1)S(1)}, u32[]{:S(2)}, u32[]{:S(2)}) %collective-permute-start.6) | collective-permute-done | bytes 135200 | tf_op jit(solution)/shard_map/ppermute | solution.py:27
  63.7 0.8 multiply_reduce_fusion.3
  64.7 1.1 %convolution_bitcast_fusion.3 = f32[2,256,64]{1,2,0:T(8,128)S(1)} fusion(f32[2,8,64,64]{3,2,1,0:T(8,128)S(1)} %reshape.209, bf16[256,2,8,64]{0,3,2,1:T(8,128)(2,1)S(1)} %bitcast.208, f32[256,2,8]{0,2,1:T(8,128)S(1)} %copy-done.17), kind=kOutput, calls=%fused_computation.51 | convolution fusion | flops 201850880 | bytes 933888 | tf_op jit(solution)/shard_map/transpose(jvp(tgn,ghpn->tghp))/dot_general | solution.py:136
  65.8 2.2 %fusion.71 = (f32[256,2,8]{0,2,1:T(8,128)}, f32[256,2,8,64]{0,3,2,1:T(8,128)}) fusion(bf16[256,2,512]{0,2,1:T(8,128)(2,1)S(1)} %copy.164, f32[2,8,64,64]{3,2,1,0:T(8,128)S(1)} %reshape.209, bf16[256,2,64]{0,2,1:T(8,128)(2,1)S(1)} %get-tuple-element.145), kind=kOutput, calls=%fused_computation.73 | convolution fusion | flops 202108928 | bytes 1916928 | tf_op jit(solution)/shard_map/jvp(tgn,ghpn->tghp)/dot_general | solution.py:136
  68.2 0.6 convolution_bitcast_fusion.1
  68.8 2.3 %fusion.70 = (f32[256,2,8]{0,2,1:T(8,128)}, f32[256,2,8,64]{0,3,2,1:T(8,128)}) fusion(bf16[256,2,8,64]{0,3,2,1:T(8,128)(2,1)S(1)} %multiply_convert_fusion, f32[2,8,64,64]{3,2,1,0:T(8,128)S(1)} %reshape.213, bf16[256,2,64]{0,2,1:T(8,128)(2,1)S(1)} %get-tuple-element.144), kind=kOutput, calls=%fused_computation.72 | convolution fusion | flops 202633216 | bytes 1916928 | tf_op jit(solution)/shard_map/transpose(jvp(sghp,sgn->ghpn))/dot_general | solution.py:131
  71.1 1.3 %copy.178 = f32[1,2,8]{0,2,1:T(8,128)} copy(f32[1,2,8]{2,1,0:T(2,128)} %bitcast.225) | data formatting | bytes 128 | tf_op jit(solution)/shard_map/reduce_sum | solution.py:186
  72.4 2.0 %fusion.122 = (f32[2,8]{1,0:T(2,128)}, f32[2,8,256]{2,1,0:T(8,128)S(1)}, f32[256,2,8]{0,2,1:T(8,128)}) fusion(f32[256,2,8]{0,2,1:T(8,128)} %get-tuple-element.140, f32[2,8]{1,0:T(2,128)} %copy-done.36, f32[256,16]{0,1:S(1)} %fusion.84, f32[256,2,8]{0,2,1:T(8,128)} %param.23, f32[2,8]{1,0:T(2,128)} %param.25, f32[256,2,8]{0,2,1:T(8,128)} %get-tuple-element.142), kind=kLoop, calls=%fused_computation.176 | loop fusion | flops 49136 | bytes 98496 | tf_op jit(solution)/shard_map/transpose(jvp())/reduce_sum | solution.py:129
  74.5 5.8 %fusion.19 = (f32[2,8,256]{2,1,0:T(8,128)}, f32[2,8,256]{2,1,0:T(8,128)}, f32[2,8,256]{2,1,0:T(8,128)}, f32[2,256,256]{2,1,0:T(8,128)S(1)}) fusion(f32[2,8,256]{2,1,0:T(8,128)S(1)} %bitcast.220, f32[2,8,256]{2,1,0:T(8,128)S(1)} %get-tuple-element.128, f32[2,256,256]{2,1,0:T(8,128)S(1)} %copy-done.9, pred[256,256]{1,0:T(8,128)(4,1)} %iota_compare_fusion, ...), kind=kOutput, calls=%fused_computation.30 | convolution fusion | flops 156094464 | bytes 2244608 | tf_op jit(solution)/shard_map/transpose(jvp(ghts,sghp->tghp))/dot_general | solution.py:119
  80.3 2.3 %fusion.49 = bf16[256,2,8,64]{0,3,2,1:T(8,128)(2,1)} fusion(bf16[2,8,64,256]{3,2,1,0:T(8,128)(2,1)S(1)} %bitcast.211, f32[2,8,256]{2,1,0:T(8,128)S(1)} %get-tuple-element.128, f32[2,8,256]{2,1,0:T(8,128)S(1)} %bitcast.221, f32[2,256,256]{2,1,0:T(8,128)S(1)} %copy-done.10, pred[256,256]{1,0:T(8,128)(4,1)S(1)} %copy-done.25, ...), kind=kOutput, calls=%fused_computation.44 | convolution fusion | flops 142606336 | bytes 3260480 | tf_op jit(solution)/shard_map/transpose(jvp(ghts,sghp->tghp))/dot_general | solution.py:119
  82.6 2.4 %fusion.31 = bf16[256,2,8,64]{0,3,2,1:T(8,128)(2,1)} fusion(bf16[256,2,8,64]{0,3,2,1:T(8,128)(2,1)S(1)} %multiply_convert_fusion, f32[2,8,256]{2,1,0:T(8,128)S(1)} %get-tuple-element.128, f32[2,8,256]{2,1,0:T(8,128)S(1)} %bitcast.222, f32[2,256,256]{2,1,0:T(8,128)S(1)} %copy-done.10, pred[256,256]{1,0:T(8,128)(4,1)S(1)} %copy-done.25, ...), kind=kOutput, calls=%fused_computation.38 | convolution fusion | flops 142082048 | bytes 2736192 | tf_op jit(solution)/shard_map/jvp(ghts,sghp->tghp)/dot_general | solution.py:119
  85.0 1.0 %fusion.61 = f32[256,2,64]{0,2,1:T(8,128)} fusion(f32[2,256,64]{1,2,0:T(8,128)S(1)} %convolution_bitcast_fusion.3, f32[2,256,256]{2,1,0:T(8,128)S(1)} %get-tuple-element.90, bf16[256,2,64]{0,2,1:T(8,128)(2,1)S(1)} %get-tuple-element.144, f32[256,2,64]{0,2,1:T(8,128)S(1)} %copy-done.2), kind=kOutput, calls=%fused_computation.58 | convolution fusion | flops 101023744 | bytes 983040 | tf_op jit(solution)/shard_map/transpose(jvp(tgn,sgn->gts))/dot_general | solution.py:117
  89.5 0.6 fusion
  90.3 1.4 %collective-permute-start.7 = (f32[3,2,640]{2,0,1:T(4,128)S(1)}, f32[3,2,640]{2,0,1:T(4,128)S(1)}, u32[]{:S(2)}, u32[]{:S(2)}) collective-permute-start(f32[3,2,640]{2,0,1:T(4,128)S(1)} %pad_maximum_fusion.9), channel_id=1, source_target_pairs={{2,0},{4,2},{6,4},{8,6},{10,8},{12,10},{14,12},{3,1},{5,3},{7,5},{... | collective-permute-start | bytes 46088 | tf_op jit(solution)/shard_map/ppermute | solution.py:12
  92.2 0.9 fusion.65
  93.4 1.2 %copy.180 = bf16[256,2,512]{2,1,0:T(2,128)(2,1)} copy(bf16[256,2,512]{0,2,1:T(8,128)(2,1)S(1)} %bitcast.214) | data formatting | bytes 1048576
  94.6 0.5 copy.190
  95.1 0.9 collective-permute-done.7
  97.6 0.6 copy-done.26
  98.1 0.8 copy-done.12
  (164 shorter events, 10.8 us)
Async XLA Ops:
  0.6 13.2 %copy-start.15 = (bf16[256,2,64]{0,2,1:T(8,128)(2,1)S(1)}, bf16[256,2,64]{0,2,1:T(8,128)(2,1)}, u32[]{:S(2)}) copy-start(bf16[256,2,64]{0,2,1:T(8,128)(2,1)} %param.21) | copy-start | bytes 196612
  0.6 13.1 %copy-start.14 = (bf16[256,2,64]{0,2,1:T(8,128)(2,1)S(1)}, bf16[256,2,64]{0,2,1:T(8,128)(2,1)}, u32[]{:S(2)}) copy-start(bf16[256,2,64]{0,2,1:T(8,128)(2,1)} %param.22) | copy-start | bytes 196612
  1.4 12.6 %copy-start.33 = (f32[4,2,64]{2,1,0:T(2,128)S(1)}, f32[4,2,64]{2,1,0:T(2,128)}, u32[]{:S(2)}) copy-start(f32[4,2,64]{2,1,0:T(2,128)} %param.29) | copy-start | bytes 6148
  3.4 10.0 %collective-permute-start = (bf16[3,2,640]{2,1,0:T(2,128)(2,1)S(1)}, bf16[3,2,640]{2,1,0:T(2,128)(2,1)S(1)}, u32[]{:S(2)}, u32[]{:S(2)}) collective-permute-start(bf16[3,2,640]{2,1,0:T(2,128)(2,1)S(1)} %pad_maximum_fusion.10), channel_id=1, source_target_pairs={{0,2},{2,4},{4,6},{6,8},{8,10},{10,12},{12,14},{1,3},{3,5},{5,7},{... | collective-permute-start | bytes 23048 | tf_op jit(solution)/shard_map/ppermute | solution.py:12
  8.9 4.5 %copy-start.40 = (f32[2,8]{1,0:T(2,128)}, f32[2,8]{1,0:T(2,128)S(1)}, u32[]{:S(2)}) copy-start(f32[2,8]{1,0:T(2,128)S(1)} %neg.33) | copy-start | bytes 196
  10.1 3.4 %copy-start.36 = (f32[2,8]{1,0:T(2,128)}, f32[2,8]{1,0:T(2,128)S(1)}, u32[]{:S(2)}) copy-start(f32[2,8]{1,0:T(2,128)S(1)} %slice_reduce_fusion) | copy-start | bytes 196
  11.5 3.5 %copy-start.16 = (f32[256,2,8]{0,2,1:T(8,128)}, f32[256,2,8]{0,2,1:T(8,128)S(1)}, u32[]{:S(2)}) copy-start(f32[256,2,8]{0,2,1:T(8,128)S(1)} %get-tuple-element.131) | copy-start | bytes 49156
  11.5 2.7 %copy-start.31 = (f32[4,2,64]{2,1,0:T(2,128)S(1)}, f32[4,2,64]{2,1,0:T(2,128)}, u32[]{:S(2)}) copy-start(f32[4,2,64]{2,1,0:T(2,128)} %param.28) | copy-start | bytes 6148
  15.0 1.5 %copy-start = (bf16[256,2,512]{2,1,0:T(2,128)(2,1)S(1)}, bf16[256,2,512]{2,1,0:T(2,128)(2,1)}, u32[]{:S(2)}) copy-start(bf16[256,2,512]{2,1,0:T(2,128)(2,1)} %param.20) | copy-start | bytes 1572868
  16.5 2.1 %copy-start.22 = (f32[4,2,512]{2,1,0:T(2,128)S(1)}, f32[4,2,512]{2,1,0:T(2,128)}, u32[]{:S(2)}) copy-start(f32[4,2,512]{2,1,0:T(2,128)} %param.27) | copy-start | bytes 49156
  24.0 1.2 %copy-start.13 = (bf16[2,8,4096]{2,1,0:T(8,128)(2,1)S(1)}, bf16[2,8,4096]{2,1,0:T(8,128)(2,1)}, u32[]{:S(2)}) copy-start(bf16[2,8,4096]{2,1,0:T(8,128)(2,1)} %convert.54) | copy-start | bytes 393220
  24.5 6.8 %copy-start.35 = (f32[2,8]{1,0:T(2,128)S(1)}, f32[2,8]{1,0:T(2,128)}, u32[]{:S(2)}) copy-start(f32[2,8]{1,0:T(2,128)} %get-tuple-element.138) | copy-start | bytes 196
  25.3 6.0 %collective-permute-start.1 = (bf16[2,8,4224]{2,1,0:T(8,128)(2,1)S(1)}, bf16[2,8,4224]{2,1,0:T(8,128)(2,1)S(1)}, u32[]{:S(2)}, u32[]{:S(2)}) collective-permute-start(bf16[2,8,4224]{2,1,0:T(8,128)(2,1)S(1)} %get-tuple-element.134), channel_id=1, source_target_pairs={{0,2},{2,4},{4,6},{6,8},{8,10},{10,12},{12,14},{1,3},{3,5},{5,7},{... | collective-permute-start | bytes 405512 | tf_op jit(solution)/shard_map/ppermute | solution.py:27
  28.7 6.9 %collective-permute-start.4 = (bf16[2,8,4224]{2,1,0:T(8,128)(2,1)S(1)}, bf16[2,8,4224]{2,1,0:T(8,128)(2,1)S(1)}, u32[]{:S(2)}, u32[]{:S(2)}) collective-permute-start(bf16[2,8,4224]{2,1,0:T(8,128)(2,1)S(1)} %get-tuple-element.135), channel_id=1, source_target_pairs={{2,0},{4,2},{6,4},{8,6},{10,8},{12,10},{14,12},{3,1},{5,3},{7,5},{... | collective-permute-start | bytes 405512 | tf_op jit(solution)/shard_map/ppermute | solution.py:27
  35.9 6.4 %collective-permute-start.2 = (bf16[2,8,4224]{2,1,0:T(8,128)(2,1)S(1)}, bf16[2,8,4224]{2,1,0:T(8,128)(2,1)S(1)}, u32[]{:S(2)}, u32[]{:S(2)}) collective-permute-start(bf16[2,8,4224]{2,1,0:T(8,128)(2,1)S(1)} %pad_maximum_fusion.3), channel_id=1, source_target_pairs={{0,4},{2,6},{4,8},{6,10},{8,12},{10,14},{1,5},{3,7},{5,9},{7,11},{... | collective-permute-start | bytes 405512 | tf_op jit(solution)/shard_map/ppermute | solution.py:27
  42.6 7.3 %collective-permute-start.5 = (bf16[2,8,4224]{2,1,0:T(8,128)(2,1)S(1)}, bf16[2,8,4224]{2,1,0:T(8,128)(2,1)S(1)}, u32[]{:S(2)}, u32[]{:S(2)}) collective-permute-start(bf16[2,8,4224]{2,1,0:T(8,128)(2,1)S(1)} %pad_maximum_fusion.5), channel_id=1, source_target_pairs={{4,0},{6,2},{8,4},{10,6},{12,8},{14,10},{5,1},{7,3},{9,5},{11,7},{... | collective-permute-start | bytes 405512 | tf_op jit(solution)/shard_map/ppermute | solution.py:27
  50.4 7.5 %collective-permute-start.3 = (bf16[2,8,4224]{2,1,0:T(8,128)(2,1)S(1)}, bf16[2,8,4224]{2,1,0:T(8,128)(2,1)S(1)}, u32[]{:S(2)}, u32[]{:S(2)}) collective-permute-start(bf16[2,8,4224]{2,1,0:T(8,128)(2,1)S(1)} %pad_maximum_fusion.4), channel_id=1, source_target_pairs={{0,8},{2,10},{4,12},{6,14},{1,9},{3,11},{5,13},{7,15},{16,24},{18,... | collective-permute-start | bytes 405512 | tf_op jit(solution)/shard_map/ppermute | solution.py:27
  55.4 8.3 %collective-permute-start.6 = (bf16[2,8,4224]{2,1,0:T(8,128)(2,1)S(1)}, bf16[2,8,4224]{2,1,0:T(8,128)(2,1)S(1)}, u32[]{:S(2)}, u32[]{:S(2)}) collective-permute-start(bf16[2,8,4224]{2,1,0:T(8,128)(2,1)S(1)} %pad_maximum_fusion.6), channel_id=1, source_target_pairs={{8,0},{10,2},{12,4},{14,6},{9,1},{11,3},{13,5},{15,7},{24,16},{26,... | collective-permute-start | bytes 405512 | tf_op jit(solution)/shard_map/ppermute | solution.py:27
  63.7 1.0 %copy-start.17 = (f32[256,2,8]{0,2,1:T(8,128)S(1)}, f32[256,2,8]{0,2,1:T(8,128)}, u32[]{:S(2)}) copy-start(f32[256,2,8]{0,2,1:T(8,128)} %copy-done.16) | copy-start | bytes 49156
  65.8 2.4 %copy-start.20 = (f32[256,2,8]{0,2,1:T(8,128)S(1)}, f32[256,2,8]{0,2,1:T(8,128)}, u32[]{:S(2)}) copy-start(f32[256,2,8]{0,2,1:T(8,128)} %get-tuple-element.130) | copy-start | bytes 49156
  68.8 5.6 %copy-start.9 = (f32[2,256,256]{2,1,0:T(8,128)S(1)}, f32[2,256,256]{2,1,0:T(8,128)}, u32[]{:S(2)}) copy-start(f32[2,256,256]{2,1,0:T(8,128)} %fusion.140) | copy-start | bytes 1572868
  74.4 5.8 %copy-start.6 = (f32[256,2,8,64]{0,3,2,1:T(8,128)S(1)}, f32[256,2,8,64]{0,3,2,1:T(8,128)}, u32[]{:S(2)}) copy-start(f32[256,2,8,64]{0,3,2,1:T(8,128)} %get-tuple-element.141) | copy-start | bytes 3145732
  74.4 5.8 %copy-start.10 = (f32[2,256,256]{2,1,0:T(8,128)S(1)}, f32[2,256,256]{2,1,0:T(8,128)}, u32[]{:S(2)}) copy-start(f32[2,256,256]{2,1,0:T(8,128)} %fusion.140) | copy-start | bytes 1572868
  74.4 5.8 %copy-start.21 = (f32[256,2,8]{0,2,1:T(8,128)S(1)}, f32[256,2,8]{0,2,1:T(8,128)}, u32[]{:S(2)}) copy-start(f32[256,2,8]{0,2,1:T(8,128)} %get-tuple-element.130) | copy-start | bytes 49156
  74.4 5.8 %copy-start.25 = (pred[256,256]{1,0:T(8,128)(4,1)S(1)}, pred[256,256]{1,0:T(8,128)(4,1)}, u32[]{:S(2)}) copy-start(pred[256,256]{1,0:T(8,128)(4,1)} %iota_compare_fusion) | copy-start | bytes 196612
  74.4 5.8 %copy-start.42 = (f32[2,8]{1,0:T(2,128)S(1)}, f32[2,8]{1,0:T(2,128)}, u32[]{:S(2)}) copy-start(f32[2,8]{1,0:T(2,128)} %param.26) | copy-start | bytes 196
  80.2 2.4 %copy-start.5 = (f32[256,2,8,64]{0,3,2,1:T(8,128)S(1)}, f32[256,2,8,64]{0,3,2,1:T(8,128)}, u32[]{:S(2)}) copy-start(f32[256,2,8,64]{0,3,2,1:T(8,128)} %get-tuple-element.143) | copy-start | bytes 3145732
  80.2 2.4 %copy-start.18 = (f32[256,2,8]{0,2,1:T(8,128)S(1)}, f32[256,2,8]{0,2,1:T(8,128)}, u32[]{:S(2)}) copy-start(f32[256,2,8]{0,2,1:T(8,128)} %copy-done.16) | copy-start | bytes 49156
  82.6 2.4 %copy-start.2 = (f32[256,2,64]{0,2,1:T(8,128)S(1)}, f32[256,2,64]{0,2,1:T(8,128)}, u32[]{:S(2)}) copy-start(f32[256,2,64]{0,2,1:T(8,128)} %copy-done.1) | copy-start | bytes 393220
  82.6 3.5 %copy-start.4 = (f32[256,2,64]{0,2,1:T(8,128)S(1)}, f32[256,2,64]{0,2,1:T(8,128)}, u32[]{:S(2)}) copy-start(f32[256,2,64]{0,2,1:T(8,128)} %copy-done.3) | copy-start | bytes 393220
  85.0 1.4 %copy-start.39 = (f32[2,8]{1,0:T(2,128)S(1)}, f32[2,8]{1,0:T(2,128)}, u32[]{:S(2)}) copy-start(f32[2,8]{1,0:T(2,128)} %get-tuple-element.127) | copy-start | bytes 196
  85.0 1.5 %copy-start.7 = (bf16[256,2,8,64]{0,3,2,1:T(8,128)(2,1)S(1)}, bf16[256,2,8,64]{0,3,2,1:T(8,128)(2,1)}, u32[]{:S(2)}) copy-start(bf16[256,2,8,64]{0,3,2,1:T(8,128)(2,1)} %fusion.49) | copy-start | bytes 1572868
  87.4 0.9 copy-start.8
  87.6 0.9 copy-start.34
  88.7 0.7 copy-start.23
  89.5 2.2 %copy-start.29 = (f32[256,2,8]{0,2,1:T(8,128)S(1)}, f32[256,2,8]{0,2,1:T(8,128)}, u32[]{:S(2)}) copy-start(f32[256,2,8]{0,2,1:T(8,128)} %get-tuple-element.129) | copy-start | bytes 49156
  89.5 2.2 %copy-start.30 = (f32[1,2,8]{0,2,1:T(8,128)S(1)}, f32[1,2,8]{0,2,1:T(8,128)}, u32[]{:S(2)}) copy-start(f32[1,2,8]{0,2,1:T(8,128)} %copy.178) | copy-start | bytes 196
  89.5 2.5 %copy-start.41 = (f32[2,8]{1,0:T(2,128)S(1)}, f32[2,8]{1,0:T(2,128)}, u32[]{:S(2)}) copy-start(f32[2,8]{1,0:T(2,128)} %copy-done.40) | copy-start | bytes 196
  89.5 2.5 %copy-start.43 = (f32[2,8,256]{2,1,0:T(8,128)S(1)}, f32[2,8,256]{2,1,0:T(8,128)}, u32[]{:S(2)}) copy-start(f32[2,8,256]{2,1,0:T(8,128)} %get-tuple-element.87) | copy-start | bytes 49156
  89.5 2.5 %copy-start.44 = (f32[2,8,256]{2,1,0:T(8,128)S(1)}, f32[2,8,256]{2,1,0:T(8,128)}, u32[]{:S(2)}) copy-start(f32[2,8,256]{2,1,0:T(8,128)} %get-tuple-element.88) | copy-start | bytes 49156
  89.5 2.5 %copy-start.45 = (f32[2,8,256]{2,1,0:T(8,128)S(1)}, f32[2,8,256]{2,1,0:T(8,128)}, u32[]{:S(2)}) copy-start(f32[2,8,256]{2,1,0:T(8,128)} %get-tuple-element.89) | copy-start | bytes 49156
  89.5 2.7 %copy-start.24 = (f32[256,2,8]{0,2,1:T(8,128)S(1)}, f32[256,2,8]{0,2,1:T(8,128)}, u32[]{:S(2)}) copy-start(f32[256,2,8]{0,2,1:T(8,128)} %get-tuple-element.140) | copy-start | bytes 49156
  89.5 2.7 %copy-start.28 = (f32[256,2,8]{0,2,1:T(8,128)S(1)}, f32[256,2,8]{0,2,1:T(8,128)}, u32[]{:S(2)}) copy-start(f32[256,2,8]{0,2,1:T(8,128)} %param.23) | copy-start | bytes 49156
  89.5 2.7 %copy-start.37 = (f32[2,8]{1,0:T(2,128)S(1)}, f32[2,8]{1,0:T(2,128)}, u32[]{:S(2)}) copy-start(f32[2,8]{1,0:T(2,128)} %copy-done.36) | copy-start | bytes 196
  89.5 2.7 %copy-start.38 = (f32[2,8]{1,0:T(2,128)S(1)}, f32[2,8]{1,0:T(2,128)}, u32[]{:S(2)}) copy-start(f32[2,8]{1,0:T(2,128)} %param.25) | copy-start | bytes 196
  90.1 3.2 %copy-start.11 = (bf16[256,2,8,64]{0,3,2,1:T(8,128)(2,1)S(1)}, bf16[256,2,8,64]{0,3,2,1:T(8,128)(2,1)}, u32[]{:S(2)}) copy-start(bf16[256,2,8,64]{0,3,2,1:T(8,128)(2,1)} %fusion.31) | copy-start | bytes 1572868
  90.3 5.8 %collective-permute-start.7 = (f32[3,2,640]{2,0,1:T(4,128)S(1)}, f32[3,2,640]{2,0,1:T(4,128)S(1)}, u32[]{:S(2)}, u32[]{:S(2)}) collective-permute-start(f32[3,2,640]{2,0,1:T(4,128)S(1)} %pad_maximum_fusion.9), channel_id=1, source_target_pairs={{2,0},{4,2},{6,4},{8,6},{10,8},{12,10},{14,12},{3,1},{5,3},{7,5},{... | collective-permute-start | bytes 46088 | tf_op jit(solution)/shard_map/ppermute | solution.py:12
  98.1 0.8 copy-start.12
  (6 other events, 4.0 us)

commit v11 on v10

--- a/solution.py
+++ b/solution.py
@@ -66,10 +66,12 @@
 def conv_forward(extended, weight):
     kernel_width = weight.shape[0]
     length = extended.shape[0] - kernel_width + 1
-    windows = jnp.stack(
-        [extended[tap_index : tap_index + length] for tap_index in range(kernel_width)], 0
-    )
-    return jnp.sum(weight[:, None] * windows.astype(jnp.float32), axis=0)
+    running = weight[0] * extended[0:length].astype(jnp.float32)
+    for tap_index in range(1, kernel_width):
+        running = running + weight[tap_index] * extended[tap_index : tap_index + length].astype(
+            jnp.float32
+        )
+    return running
 
 
 def conv_backward(grad_out, running, weight):
@@ -79,14 +81,11 @@
     ext_len = inner_grad.shape[0] + kernel_width - 1
     padding = [(kernel_width - 1, kernel_width - 1)] + [(0, 0)] * (inner_grad.ndim - 1)
     padded = jnp.pad(inner_grad, padding)
-    windows = jnp.stack(
-        [
-            padded[kernel_width - 1 - tap_index : kernel_width - 1 - tap_index + ext_len]
-            for tap_index in range(kernel_width)
-        ],
-        0,
-    )
-    return jnp.sum(weight[:, None] * windows, axis=0)
+    result = weight[0] * padded[kernel_width - 1 : kernel_width - 1 + ext_len]
+    for tap_index in range(1, kernel_width):
+        offset = kernel_width - 1 - tap_index
+        result = result + weight[tap_index] * padded[offset : offset + ext_len]
+    return result
 
 
 def ssd_cum(dt_raw, rate, dt_bias):

time: 99.9 us -> 93.4 us (0.935)
  other arithmetic: 16.6 us -> 9.75 us
  matrix products: 22 us -> 20.4 us
  waiting for transfers between devices: 19.9 us -> 21 us
    reduce_sum x6 -> x0, other arithmetic: 5.14 us -> none  [the longest x3 4.27 us: conv_forward(): return jnp.sum(weight[:, None] * windows.astype(jnp.float32), axis=0)]
    another operation x11 -> x8, other arithmetic: 3.6 us -> 0.57 us  [the longest x3 2.37 us: conv_forward(): jnp.stack([extended[tap_index:tap_index + length] for tap_index in range(...]
    mul x0 -> x3, local copies, waits for them, and re-layouts: none -> 2.21 us  [conv_forward(): running = weight[0] * extended[0:length].astype(jnp.float32)]
    convert_element_type x1, local copies, waits for them, and re-layouts: 0.33 us -> 1.55 us  [conv_backward(): grad_out.astype(jnp.float32)]
    add x0 -> x4, other arithmetic: none -> 1.05 us  [the longest x3 1.04 us: conv_backward(): result = result + weight[tap_index] * padded[offset:offset + ext_len]]
    unnamed x97 -> x128, local copies, waits for them, and re-layouts: 6.37 us -> 5.99 us
  transfers between devices with their start and end apart: 8 -> 8, of which waited for: 7 -> 7; matrix products, arithmetic and copies ran while one was open for 11% -> 12% of each run, Pallas kernels for 0% -> 0%
where the time goes in v11:
time: 93.4 us; the launch traced here: 92.6 us
  starting transfers between devices  22.4 us (24%)
  waiting for transfers between devices  21 us (22%)
  matrix products  20.4 us (22%)
  local copies, waits for them, and re-layouts  17.4 us (19%)
  other arithmetic  9.75 us (10%)
  between operations  1.66 us (2%)
    ppermute x6, waiting for transfers between devices, shift(): return lax.ppermute(packed, axis, pairs)  19.5 us
    ppermute x6, starting transfers between devices, shift(): return lax.ppermute(packed, axis, pairs)  16.3 us
    dot_general x3, matrix products, ssd_mix(): jnp.einsum('ghts,sghp->tghp', mixing, x_half, preferred_element_type=jnp....  10.8 us
    ppermute x2, starting transfers between devices, from_behind(): return lax.ppermute(array, axis, pairs)  6.12 us
    unnamed x128, local copies, waits for them, and re-layouts  5.99 us
    dot_general x2, matrix products, carry_in(): carried = jnp.einsum('tgn,ghpn->tghp', c_float, state_in, precision=HIGH)  2.67 us
    dot_general x3, matrix products, ssd_state(): jnp.einsum('sghp,sgn->ghpn', weighted.astype(jnp.float32), b_float, preci...  2.5 us
    mul x3, local copies, waits for them, and re-layouts, conv_forward(): running = weight[0] * extended[0:length].astype(jnp.float32)  2.21 us
  transfers between devices with their start and end apart: 8, of which 7 were waited for; matrix products, arithmetic and copies ran while one was open for 12% of the time, Pallas kernels for 0%

profile of v11, /device:TPU:0, one launch (start us, length us, event | category | flops | bytes accessed | tf_op | source)
XLA Modules:
  0.0 92.6 jit_solution(3543635181016283215)
XLA Ops:
  0.6 0.8 slice.294
  1.4 0.8 slice.295
  2.3 0.8 slice.296
  3.4 4.8 %collective-permute-start = (bf16[3,2,640]{2,0,1:T(4,128)(2,1)S(1)}, bf16[3,2,640]{2,0,1:T(4,128)(2,1)S(1)}, u32[]{:S(2)}, u32[]{:S(2)}) collective-permute-start(bf16[3,2,640]{2,0,1:T(4,128)(2,1)S(1)} %copy.120), channel_id=1, source_target_pairs={{0,2},{2,4},{4,6},{6,8},{8,10},{10,12},{12,14},{1,3},{3,5},{5,7},{... | collective-permute-start | bytes 23048 | tf_op jit(solution)/shard_map/ppermute | solution.py:12
  8.2 0.7 neg.30
  8.9 0.7 slice_bitcast_fusion.7
  9.7 0.7 slice_bitcast_fusion.11
  10.4 0.9 %fusion.78 = f32[256,16]{0,1:S(1)} fusion(f32[2,8]{1,0:T(2,128)S(1)} %neg.30, f32[256,2,8]{0,2,1:T(8,128)} %param.23, f32[2,8]{1,0:T(2,128)} %param.25), kind=kOutput, calls=%fused_computation.97 | convolution fusion | flops 12681216 | bytes 32896
  11.6 0.7 slice_bitcast_fusion.3
  12.3 0.8 fusion.115
  13.2 0.6 fusion.131
  13.8 1.1 %copy.121 = bf16[256,2,512]{2,0,1:T(8,128)(2,1)S(1)} copy(bf16[256,2,512]{2,1,0:T(2,128)(2,1)} %param.20) | data formatting | bytes 1048576 | tf_op args[0]
  14.9 0.5 copy.127
  15.9 1.1 %multiply_convert_fusion.1 = (bf16[256,2,64]{0,2,1:T(8,128)(2,1)S(1)}, f32[256,2,64]{0,2,1:T(8,128)}, bf16[256,2,64]{0,2,1:T(8,128)(2,1)S(1)}, f32[256,2,64]{0,2,1:T(8,128)}) fusion(bf16[256,2,64]{0,2,1:T(8,128)(2,1)S(1)} %copy-done.10, f32[2,64]{1,0:T(2,128)S(1)} %get-tuple-element.120, bf16[3,2,64]{0,2,1:T(8,128)(2,1)S(1)} %copy.125, ...), kind=kLoop, calls=%fused_computation.118 | loop fusion | flops 1638400 | bytes 529920 | tf_op jit(solution)/shard_map/convert_element_type | solution.py:159
  16.9 0.6 fusion.52
  17.9 0.7 multiply_convert_fusion
  19.5 3.5 %collective-permute-start.1 = (bf16[2,8,4224]{2,1,0:T(8,128)(2,1)S(1)}, bf16[2,8,4224]{2,1,0:T(8,128)(2,1)S(1)}, u32[]{:S(2)}, u32[]{:S(2)}) collective-permute-start(bf16[2,8,4224]{2,1,0:T(8,128)(2,1)S(1)} %get-tuple-element.116), channel_id=1, source_target_pairs={{0,2},{2,4},{4,6},{6,8},{8,10},{10,12},{12,14},{1,3},{3,5},{5,7},{... | collective-permute-start | bytes 405512 | tf_op jit(solution)/shard_map/ppermute | solution.py:27
  23.0 1.3 %collective-permute-start.4 = (bf16[2,8,4224]{2,1,0:T(8,128)(2,1)S(1)}, bf16[2,8,4224]{2,1,0:T(8,128)(2,1)S(1)}, u32[]{:S(2)}, u32[]{:S(2)}) collective-permute-start(bf16[2,8,4224]{2,1,0:T(8,128)(2,1)S(1)} %get-tuple-element.117), channel_id=1, source_target_pairs={{2,0},{4,2},{6,4},{8,6},{10,8},{12,10},{14,12},{3,1},{5,3},{7,5},{... | collective-permute-start | bytes 405512 | tf_op jit(solution)/shard_map/ppermute | solution.py:27
  24.3 1.2 %collective-permute-done.1 = bf16[2,8,4224]{2,1,0:T(8,128)(2,1)S(1)} collective-permute-done((bf16[2,8,4224]{2,1,0:T(8,128)(2,1)S(1)}, bf16[2,8,4224]{2,1,0:T(8,128)(2,1)S(1)}, u32[]{:S(2)}, u32[]{:S(2)}) %collective-permute-start.1) | collective-permute-done | bytes 135200 | tf_op jit(solution)/shard_map/ppermute | solution.py:27
  25.7 4.2 %collective-permute-done.4 = bf16[2,8,4224]{2,1,0:T(8,128)(2,1)S(1)} collective-permute-done((bf16[2,8,4224]{2,1,0:T(8,128)(2,1)S(1)}, bf16[2,8,4224]{2,1,0:T(8,128)(2,1)S(1)}, u32[]{:S(2)}, u32[]{:S(2)}) %collective-permute-start.4) | collective-permute-done | bytes 135200 | tf_op jit(solution)/shard_map/ppermute | solution.py:27
  30.2 3.8 %collective-permute-start.2 = (bf16[2,8,4224]{2,1,0:T(8,128)(2,1)S(1)}, bf16[2,8,4224]{2,1,0:T(8,128)(2,1)S(1)}, u32[]{:S(2)}, u32[]{:S(2)}) collective-permute-start(bf16[2,8,4224]{2,1,0:T(8,128)(2,1)S(1)} %pad_maximum_fusion.3), channel_id=1, source_target_pairs={{0,4},{2,6},{4,8},{6,10},{8,12},{10,14},{1,5},{3,7},{5,9},{7,11},{... | collective-permute-start | bytes 405512 | tf_op jit(solution)/shard_map/ppermute | solution.py:27
  34.1 2.5 %collective-permute-done.2 = bf16[2,8,4224]{2,1,0:T(8,128)(2,1)S(1)} collective-permute-done((bf16[2,8,4224]{2,1,0:T(8,128)(2,1)S(1)}, bf16[2,8,4224]{2,1,0:T(8,128)(2,1)S(1)}, u32[]{:S(2)}, u32[]{:S(2)}) %collective-permute-start.2) | collective-permute-done | bytes 135200 | tf_op jit(solution)/shard_map/ppermute | solution.py:27
  36.8 1.3 %collective-permute-start.5 = (bf16[2,8,4224]{2,1,0:T(8,128)(2,1)S(1)}, bf16[2,8,4224]{2,1,0:T(8,128)(2,1)S(1)}, u32[]{:S(2)}, u32[]{:S(2)}) collective-permute-start(bf16[2,8,4224]{2,1,0:T(8,128)(2,1)S(1)} %pad_maximum_fusion.5), channel_id=1, source_target_pairs={{4,0},{6,2},{8,4},{10,6},{12,8},{14,10},{5,1},{7,3},{9,5},{11,7},{... | collective-permute-start | bytes 405512 | tf_op jit(solution)/shard_map/ppermute | solution.py:27
  38.1 1.1 %fusion.132 = f32[2,256,256]{2,1,0:T(8,128)} fusion(bf16[256,2,64]{0,2,1:T(8,128)(2,1)S(1)} %get-tuple-element.134, bf16[256,2,64]{0,2,1:T(8,128)(2,1)S(1)} %get-tuple-element.97), kind=kOutput, calls=%fused_computation.208 | convolution fusion | flops 16777216 | bytes 655360 | tf_op jit(solution)/shard_map/jvp(tgn,sgn->gts)/dot_general | solution.py:116
  39.2 5.0 %collective-permute-done.5 = bf16[2,8,4224]{2,1,0:T(8,128)(2,1)S(1)} collective-permute-done((bf16[2,8,4224]{2,1,0:T(8,128)(2,1)S(1)}, bf16[2,8,4224]{2,1,0:T(8,128)(2,1)S(1)}, u32[]{:S(2)}, u32[]{:S(2)}) %collective-permute-start.5) | collective-permute-done | bytes 135200 | tf_op jit(solution)/shard_map/ppermute | solution.py:27
  44.6 4.9 %collective-permute-start.3 = (bf16[2,8,4224]{2,1,0:T(8,128)(2,1)S(1)}, bf16[2,8,4224]{2,1,0:T(8,128)(2,1)S(1)}, u32[]{:S(2)}, u32[]{:S(2)}) collective-permute-start(bf16[2,8,4224]{2,1,0:T(8,128)(2,1)S(1)} %pad_maximum_fusion.4), channel_id=1, source_target_pairs={{0,8},{2,10},{4,12},{6,14},{1,9},{3,11},{5,13},{7,15},{16,24},{18,... | collective-permute-start | bytes 405512 | tf_op jit(solution)/shard_map/ppermute | solution.py:27
  49.7 1.5 %collective-permute-start.6 = (bf16[2,8,4224]{2,1,0:T(8,128)(2,1)S(1)}, bf16[2,8,4224]{2,1,0:T(8,128)(2,1)S(1)}, u32[]{:S(2)}, u32[]{:S(2)}) collective-permute-start(bf16[2,8,4224]{2,1,0:T(8,128)(2,1)S(1)} %pad_maximum_fusion.6), channel_id=1, source_target_pairs={{8,0},{10,2},{12,4},{14,6},{9,1},{11,3},{13,5},{15,7},{24,16},{26,... | collective-permute-start | bytes 405512 | tf_op jit(solution)/shard_map/ppermute | solution.py:27
  51.3 0.8 collective-permute-done.3
  52.1 5.8 %collective-permute-done.6 = bf16[2,8,4224]{2,1,0:T(8,128)(2,1)S(1)} collective-permute-done((bf16[2,8,4224]{2,1,0:T(8,128)(2,1)S(1)}, bf16[2,8,4224]{2,1,0:T(8,128)(2,1)S(1)}, u32[]{:S(2)}, u32[]{:S(2)}) %collective-permute-start.6) | collective-permute-done | bytes 135200 | tf_op jit(solution)/shard_map/ppermute | solution.py:27
  57.9 0.8 multiply_reduce_fusion
  59.0 1.1 %convolution_bitcast_fusion.3 = f32[2,256,64]{1,2,0:T(8,128)S(1)} fusion(f32[2,8,64,64]{3,2,1,0:T(8,128)S(1)} %reshape.212, bf16[256,2,8,64]{0,3,2,1:T(8,128)(2,1)S(1)} %bitcast.188, f32[256,2,8]{0,2,1:T(8,128)S(1)} %get-tuple-element.107), kind=kOutput, calls=%fused_computation.48 | convolution fusion | flops 201850880 | bytes 933888 | tf_op jit(solution)/shard_map/transpose(jvp(tgn,ghpn->tghp))/dot_general | solution.py:135
  60.0 1.6 %fusion.70 = (f32[256,2,8]{0,2,1:T(8,128)S(1)}, f32[256,2,8,64]{0,3,2,1:T(8,128)}) fusion(bf16[256,2,512]{0,2,1:T(8,128)(2,1)S(1)} %copy.127, f32[2,8,64,64]{3,2,1,0:T(8,128)S(1)} %reshape.212, bf16[256,2,64]{0,2,1:T(8,128)(2,1)S(1)} %get-tuple-element.134), kind=kOutput, calls=%fused_computation.67 | convolution fusion | flops 202108928 | bytes 1916928 | tf_op jit(solution)/shard_map/jvp(tgn,ghpn->tghp)/dot_general | solution.py:135
  61.9 0.6 convolution_bitcast_fusion.1
  62.5 1.6 %fusion.69 = (f32[256,2,8]{0,2,1:T(8,128)S(1)}, f32[256,2,8,64]{0,3,2,1:T(8,128)}) fusion(bf16[256,2,512]{0,2,1:T(8,128)(2,1)S(1)} %copy.123, f32[2,8,64,64]{3,2,1,0:T(8,128)S(1)} %reshape.216, bf16[256,2,64]{0,2,1:T(8,128)(2,1)S(1)} %get-tuple-element.97), kind=kOutput, calls=%fused_computation.66 | convolution fusion | flops 202633216 | bytes 1916928 | tf_op jit(solution)/shard_map/transpose(jvp(sghp,sgn->ghpn))/dot_general | solution.py:130
  64.1 0.7 copy.138
  64.8 1.2 %fusion.116 = (f32[2,8]{1,0:T(2,128)}, f32[2,8,256]{2,1,0:T(8,128)S(1)}, f32[256,2,8]{0,2,1:T(8,128)}) fusion(f32[256,2,8]{0,2,1:T(8,128)S(1)} %get-tuple-element.130, f32[2,8]{1,0:T(2,128)S(1)} %copy-done.30, f32[256,16]{0,1:S(1)} %fusion.78, f32[256,2,8]{0,2,1:T(8,128)S(1)} %copy-done.16, f32[2,8]{1,0:T(2,128)S(1)} %copy-done.49, ...), kind=kLoop, calls=%fused_computation.166 | loop fusion | flops 49136 | bytes 98496 | tf_op jit(solution)/shard_map/transpose(jvp())/reduce_sum | solution.py:128
  66.1 5.9 %fusion.18 = (f32[2,8,256]{2,1,0:T(8,128)}, f32[2,8,256]{2,1,0:T(8,128)}, f32[2,8,256]{2,1,0:T(8,128)}, f32[2,256,256]{2,1,0:T(8,128)S(1)}) fusion(f32[2,8,256]{2,1,0:T(8,128)S(1)} %bitcast.200, f32[2,8,256]{2,1,0:T(8,128)S(1)} %get-tuple-element.104, f32[2,256,256]{2,1,0:T(8,128)} %fusion.132, pred[256,256]{1,0:T(8,128)(4,1)S(1)} %iota_compare_fusion, ...), kind=kOutput, calls=%fused_computation.27 | convolution fusion | flops 156094464 | bytes 2244608 | tf_op jit(solution)/shard_map/transpose(jvp(ghts,sghp->tghp))/dot_general | solution.py:118
  72.0 2.3 %fusion.48 = bf16[256,2,8,64]{0,3,2,1:T(8,128)(2,1)} fusion(bf16[2,8,64,256]{3,2,1,0:T(8,128)(2,1)S(1)} %bitcast.191, f32[2,8,256]{2,1,0:T(8,128)S(1)} %get-tuple-element.104, f32[2,8,256]{2,1,0:T(8,128)S(1)} %bitcast.201, f32[2,256,256]{2,1,0:T(8,128)S(1)} %copy-done.3, pred[256,256]{1,0:T(8,128)(4,1)S(1)} %iota_compare_fusion, ...), kind=kOutput, calls=%fused_computation.41 | convolution fusion | flops 142606336 | bytes 3260480 | tf_op jit(solution)/shard_map/transpose(jvp(ghts,sghp->tghp))/dot_general | solution.py:118
  74.4 2.6 %fusion.30 = bf16[256,2,8,64]{0,3,2,1:T(8,128)(2,1)S(1)} fusion(bf16[256,2,8,64]{0,3,2,1:T(8,128)(2,1)S(1)} %bitcast.195, f32[2,8,256]{2,1,0:T(8,128)S(1)} %get-tuple-element.104, f32[2,8,256]{2,1,0:T(8,128)S(1)} %bitcast.202, f32[2,256,256]{2,1,0:T(8,128)S(1)} %copy-done.3, pred[256,256]{1,0:T(8,128)(4,1)} %copy-done.13, ...), kind=kOutput, calls=%fused_computation.35 | convolution fusion | flops 142082048 | bytes 2736192 | tf_op jit(solution)/shard_map/jvp(ghts,sghp->tghp)/dot_general | solution.py:118
  77.0 0.7 copy.139
  79.3 1.1 %bitcast_convert_fusion = f32[256,2,512]{0,2,1:T(8,128)} fusion(bf16[256,2,8,64]{0,3,2,1:T(8,128)(2,1)S(1)} %copy-done.2), kind=kLoop, calls=%fused_computation.77 | loop fusion | flops 262144 | bytes 1572864 | tf_op jit(solution)/shard_map/convert_element_type | solution.py:79
  80.4 1.6 %copy.129 = f32[256,2,512]{2,0,1:T(8,128)S(1)} copy(f32[256,2,512]{0,2,1:T(8,128)} %bitcast_convert_fusion) | data formatting | bytes 2097152 | tf_op jit(solution)/shard_map/convert_element_type | solution.py:79
  83.3 1.3 %collective-permute-start.7 = (f32[3,2,640]{2,1,0:T(2,128)S(1)}, f32[3,2,640]{2,1,0:T(2,128)S(1)}, u32[]{:S(2)}, u32[]{:S(2)}) collective-permute-start(f32[3,2,640]{2,1,0:T(2,128)S(1)} %pad_maximum_fusion.9), channel_id=1, source_target_pairs={{2,0},{4,2},{6,4},{8,6},{10,8},{12,10},{14,12},{3,1},{5,3},{7,5},{... | collective-permute-start | bytes 46088 | tf_op jit(solution)/shard_map/ppermute | solution.py:12
  85.2 0.9 fusion.64
  86.3 1.2 %copy.140 = bf16[256,2,512]{2,1,0:T(2,128)(2,1)} copy(bf16[256,2,512]{0,2,1:T(8,128)(2,1)S(1)} %bitcast.196) | data formatting | bytes 1048576
  87.5 1.4 %collective-permute-done.7 = f32[3,2,640]{2,1,0:T(2,128)S(1)} collective-permute-done((f32[3,2,640]{2,1,0:T(2,128)S(1)}, f32[3,2,640]{2,1,0:T(2,128)S(1)}, u32[]{:S(2)}, u32[]{:S(2)}) %collective-permute-start.7) | collective-permute-done | bytes 15392 | tf_op jit(solution)/shard_map/ppermute | solution.py:12
  89.1 1.3 %copy.141 = bf16[256,2,512]{2,1,0:T(2,128)(2,1)} copy(bf16[256,2,512]{2,0,1:T(8,128)(2,1)S(1)} %scatter-add.14) | data formatting | bytes 1048576
  92.0 0.6 copy-done.14
  (190 shorter events, 9.0 us)
Async XLA Ops:
  0.6 14.3 %copy-start.4 = (bf16[256,2,512]{2,1,0:T(2,128)(2,1)S(1)}, bf16[256,2,512]{2,1,0:T(2,128)(2,1)}, u32[]{:S(2)}) copy-start(bf16[256,2,512]{2,1,0:T(2,128)(2,1)} %param.30) | copy-start | bytes 1572868
  3.4 12.1 %collective-permute-start = (bf16[3,2,640]{2,0,1:T(4,128)(2,1)S(1)}, bf16[3,2,640]{2,0,1:T(4,128)(2,1)S(1)}, u32[]{:S(2)}, u32[]{:S(2)}) collective-permute-start(bf16[3,2,640]{2,0,1:T(4,128)(2,1)S(1)} %copy.120), channel_id=1, source_target_pairs={{0,2},{2,4},{4,6},{6,8},{8,10},{10,12},{12,14},{1,3},{3,5},{5,7},{... | collective-permute-start | bytes 23048 | tf_op jit(solution)/shard_map/ppermute | solution.py:12
  8.9 6.5 %copy-start.54 = (f32[2,8]{1,0:T(2,128)}, f32[2,8]{1,0:T(2,128)S(1)}, u32[]{:S(2)}) copy-start(f32[2,8]{1,0:T(2,128)S(1)} %neg.30) | copy-start | bytes 196
  9.7 6.2 %copy-start.40 = (f32[2,64]{1,0:T(2,128)}, f32[2,64]{1,0:T(2,128)S(1)}, u32[]{:S(2)}) copy-start(f32[2,64]{1,0:T(2,128)S(1)} %get-tuple-element.118) | copy-start | bytes 1540
  9.7 6.2 %copy-start.42 = (f32[2,64]{1,0:T(2,128)}, f32[2,64]{1,0:T(2,128)S(1)}, u32[]{:S(2)}) copy-start(f32[2,64]{1,0:T(2,128)S(1)} %get-tuple-element.119) | copy-start | bytes 1540
  9.7 6.2 %copy-start.44 = (f32[2,64]{1,0:T(2,128)}, f32[2,64]{1,0:T(2,128)S(1)}, u32[]{:S(2)}) copy-start(f32[2,64]{1,0:T(2,128)S(1)} %get-tuple-element.120) | copy-start | bytes 1540
  9.7 6.2 %copy-start.46 = (f32[2,64]{1,0:T(2,128)}, f32[2,64]{1,0:T(2,128)S(1)}, u32[]{:S(2)}) copy-start(f32[2,64]{1,0:T(2,128)S(1)} %get-tuple-element.121) | copy-start | bytes 1540
  10.4 5.4 %copy-start.32 = (f32[2,64]{1,0:T(2,128)}, f32[2,64]{1,0:T(2,128)S(1)}, u32[]{:S(2)}) copy-start(f32[2,64]{1,0:T(2,128)S(1)} %get-tuple-element.122) | copy-start | bytes 1540
  10.4 5.4 %copy-start.34 = (f32[2,64]{1,0:T(2,128)}, f32[2,64]{1,0:T(2,128)S(1)}, u32[]{:S(2)}) copy-start(f32[2,64]{1,0:T(2,128)S(1)} %get-tuple-element.123) | copy-start | bytes 1540
  10.4 5.4 %copy-start.36 = (f32[2,64]{1,0:T(2,128)}, f32[2,64]{1,0:T(2,128)S(1)}, u32[]{:S(2)}) copy-start(f32[2,64]{1,0:T(2,128)S(1)} %get-tuple-element.124) | copy-start | bytes 1540
  10.4 5.5 %copy-start.38 = (f32[2,64]{1,0:T(2,128)}, f32[2,64]{1,0:T(2,128)S(1)}, u32[]{:S(2)}) copy-start(f32[2,64]{1,0:T(2,128)S(1)} %get-tuple-element.125) | copy-start | bytes 1540
  12.3 5.5 %copy-start.18 = (f32[2,512]{1,0:T(2,128)}, f32[2,512]{1,0:T(2,128)S(1)}, u32[]{:S(2)}) copy-start(f32[2,512]{1,0:T(2,128)S(1)} %get-tuple-element.108) | copy-start | bytes 12292
  12.3 5.5 %copy-start.20 = (f32[2,512]{1,0:T(2,128)}, f32[2,512]{1,0:T(2,128)S(1)}, u32[]{:S(2)}) copy-start(f32[2,512]{1,0:T(2,128)S(1)} %get-tuple-element.109) | copy-start | bytes 12292
  12.3 5.5 %copy-start.22 = (f32[2,512]{1,0:T(2,128)}, f32[2,512]{1,0:T(2,128)S(1)}, u32[]{:S(2)}) copy-start(f32[2,512]{1,0:T(2,128)S(1)} %get-tuple-element.110) | copy-start | bytes 12292
  12.3 5.5 %copy-start.24 = (f32[2,512]{1,0:T(2,128)}, f32[2,512]{1,0:T(2,128)S(1)}, u32[]{:S(2)}) copy-start(f32[2,512]{1,0:T(2,128)S(1)} %get-tuple-element.111) | copy-start | bytes 12292
  13.2 45.8 %copy-start.7 = (f32[256,2,8]{0,2,1:T(8,128)}, f32[256,2,8]{0,2,1:T(8,128)S(1)}, u32[]{:S(2)}) copy-start(f32[256,2,8]{0,2,1:T(8,128)S(1)} %get-tuple-element.107) | copy-start | bytes 49156
  19.1 6.5 %copy-start.28 = (f32[2,8]{1,0:T(2,128)S(1)}, f32[2,8]{1,0:T(2,128)}, u32[]{:S(2)}) copy-start(f32[2,8]{1,0:T(2,128)} %get-tuple-element.128) | copy-start | bytes 196
  19.5 6.0 %collective-permute-start.1 = (bf16[2,8,4224]{2,1,0:T(8,128)(2,1)S(1)}, bf16[2,8,4224]{2,1,0:T(8,128)(2,1)S(1)}, u32[]{:S(2)}, u32[]{:S(2)}) collective-permute-start(bf16[2,8,4224]{2,1,0:T(8,128)(2,1)S(1)} %get-tuple-element.116), channel_id=1, source_target_pairs={{0,2},{2,4},{4,6},{6,8},{8,10},{10,12},{12,14},{1,3},{3,5},{5,7},{... | collective-permute-start | bytes 405512 | tf_op jit(solution)/shard_map/ppermute | solution.py:27
  23.0 6.9 %collective-permute-start.4 = (bf16[2,8,4224]{2,1,0:T(8,128)(2,1)S(1)}, bf16[2,8,4224]{2,1,0:T(8,128)(2,1)S(1)}, u32[]{:S(2)}, u32[]{:S(2)}) collective-permute-start(bf16[2,8,4224]{2,1,0:T(8,128)(2,1)S(1)} %get-tuple-element.117), channel_id=1, source_target_pairs={{2,0},{4,2},{6,4},{8,6},{10,8},{12,10},{14,12},{3,1},{5,3},{7,5},{... | collective-permute-start | bytes 405512 | tf_op jit(solution)/shard_map/ppermute | solution.py:27
  30.2 6.4 %collective-permute-start.2 = (bf16[2,8,4224]{2,1,0:T(8,128)(2,1)S(1)}, bf16[2,8,4224]{2,1,0:T(8,128)(2,1)S(1)}, u32[]{:S(2)}, u32[]{:S(2)}) collective-permute-start(bf16[2,8,4224]{2,1,0:T(8,128)(2,1)S(1)} %pad_maximum_fusion.3), channel_id=1, source_target_pairs={{0,4},{2,6},{4,8},{6,10},{8,12},{10,14},{1,5},{3,7},{5,9},{7,11},{... | collective-permute-start | bytes 405512 | tf_op jit(solution)/shard_map/ppermute | solution.py:27
  34.1 37.9 %copy-start.13 = (pred[256,256]{1,0:T(8,128)(4,1)}, pred[256,256]{1,0:T(8,128)(4,1)S(1)}, u32[]{:S(2)}) copy-start(pred[256,256]{1,0:T(8,128)(4,1)S(1)} %iota_compare_fusion) | copy-start | bytes 196612
  36.8 7.3 %collective-permute-start.5 = (bf16[2,8,4224]{2,1,0:T(8,128)(2,1)S(1)}, bf16[2,8,4224]{2,1,0:T(8,128)(2,1)S(1)}, u32[]{:S(2)}, u32[]{:S(2)}) collective-permute-start(bf16[2,8,4224]{2,1,0:T(8,128)(2,1)S(1)} %pad_maximum_fusion.5), channel_id=1, source_target_pairs={{4,0},{6,2},{8,4},{10,6},{12,8},{14,10},{5,1},{7,3},{9,5},{11,7},{... | collective-permute-start | bytes 405512 | tf_op jit(solution)/shard_map/ppermute | solution.py:27
  44.6 7.5 %collective-permute-start.3 = (bf16[2,8,4224]{2,1,0:T(8,128)(2,1)S(1)}, bf16[2,8,4224]{2,1,0:T(8,128)(2,1)S(1)}, u32[]{:S(2)}, u32[]{:S(2)}) collective-permute-start(bf16[2,8,4224]{2,1,0:T(8,128)(2,1)S(1)} %pad_maximum_fusion.4), channel_id=1, source_target_pairs={{0,8},{2,10},{4,12},{6,14},{1,9},{3,11},{5,13},{7,15},{16,24},{18,... | collective-permute-start | bytes 405512 | tf_op jit(solution)/shard_map/ppermute | solution.py:27
  49.7 8.3 %collective-permute-start.6 = (bf16[2,8,4224]{2,1,0:T(8,128)(2,1)S(1)}, bf16[2,8,4224]{2,1,0:T(8,128)(2,1)S(1)}, u32[]{:S(2)}, u32[]{:S(2)}) collective-permute-start(bf16[2,8,4224]{2,1,0:T(8,128)(2,1)S(1)} %pad_maximum_fusion.6), channel_id=1, source_target_pairs={{8,0},{10,2},{12,4},{14,6},{9,1},{11,3},{13,5},{15,7},{24,16},{26,... | collective-permute-start | bytes 405512 | tf_op jit(solution)/shard_map/ppermute | solution.py:27
  62.5 2.3 %copy-start.16 = (f32[256,2,8]{0,2,1:T(8,128)S(1)}, f32[256,2,8]{0,2,1:T(8,128)}, u32[]{:S(2)}) copy-start(f32[256,2,8]{0,2,1:T(8,128)} %param.23) | copy-start | bytes 49156
  62.5 2.3 %copy-start.30 = (f32[2,8]{1,0:T(2,128)S(1)}, f32[2,8]{1,0:T(2,128)}, u32[]{:S(2)}) copy-start(f32[2,8]{1,0:T(2,128)} %copy-done.29) | copy-start | bytes 196
  62.5 2.3 %copy-start.49 = (f32[2,8]{1,0:T(2,128)S(1)}, f32[2,8]{1,0:T(2,128)}, u32[]{:S(2)}) copy-start(f32[2,8]{1,0:T(2,128)} %param.25) | copy-start | bytes 196
  64.1 7.8 %copy-start.11 = (f32[256,2,8]{0,2,1:T(8,128)}, f32[256,2,8]{0,2,1:T(8,128)S(1)}, u32[]{:S(2)}) copy-start(f32[256,2,8]{0,2,1:T(8,128)S(1)} %get-tuple-element.130) | copy-start | bytes 49156
  66.0 5.9 %copy-start.1 = (f32[256,2,8,64]{0,3,2,1:T(8,128)S(1)}, f32[256,2,8,64]{0,3,2,1:T(8,128)}, u32[]{:S(2)}) copy-start(f32[256,2,8,64]{0,3,2,1:T(8,128)} %get-tuple-element.131) | copy-start | bytes 3145732
  66.0 5.9 %copy-start.3 = (f32[2,256,256]{2,1,0:T(8,128)S(1)}, f32[2,256,256]{2,1,0:T(8,128)}, u32[]{:S(2)}) copy-start(f32[2,256,256]{2,1,0:T(8,128)} %fusion.132) | copy-start | bytes 1572868
  66.0 5.9 %copy-start.56 = (f32[2,8]{1,0:T(2,128)S(1)}, f32[2,8]{1,0:T(2,128)}, u32[]{:S(2)}) copy-start(f32[2,8]{1,0:T(2,128)} %param.26) | copy-start | bytes 196
  72.0 2.4 %copy-start = (f32[256,2,8,64]{0,3,2,1:T(8,128)S(1)}, f32[256,2,8,64]{0,3,2,1:T(8,128)}, u32[]{:S(2)}) copy-start(f32[256,2,8,64]{0,3,2,1:T(8,128)} %get-tuple-element.133) | copy-start | bytes 3145732
  72.0 2.4 %copy-start.8 = (f32[256,2,8]{0,2,1:T(8,128)S(1)}, f32[256,2,8]{0,2,1:T(8,128)}, u32[]{:S(2)}) copy-start(f32[256,2,8]{0,2,1:T(8,128)} %copy-done.7) | copy-start | bytes 49156
  74.3 2.6 %copy-start.52 = (f32[2,8]{1,0:T(2,128)S(1)}, f32[2,8]{1,0:T(2,128)}, u32[]{:S(2)}) copy-start(f32[2,8]{1,0:T(2,128)} %get-tuple-element.103) | copy-start | bytes 196
  74.3 3.3 %copy-start.6 = (f32[256,2,64]{0,2,1:T(8,128)S(1)}, f32[256,2,64]{0,2,1:T(8,128)}, u32[]{:S(2)}) copy-start(f32[256,2,64]{0,2,1:T(8,128)} %get-tuple-element.98) | copy-start | bytes 393220
  74.3 3.7 %copy-start.41 = (f32[2,64]{1,0:T(2,128)S(1)}, f32[2,64]{1,0:T(2,128)}, u32[]{:S(2)}) copy-start(f32[2,64]{1,0:T(2,128)} %copy-done.40) | copy-start | bytes 1540
  74.4 3.7 %copy-start.43 = (f32[2,64]{1,0:T(2,128)S(1)}, f32[2,64]{1,0:T(2,128)}, u32[]{:S(2)}) copy-start(f32[2,64]{1,0:T(2,128)} %copy-done.42) | copy-start | bytes 1540
  74.4 3.7 %copy-start.45 = (f32[2,64]{1,0:T(2,128)S(1)}, f32[2,64]{1,0:T(2,128)}, u32[]{:S(2)}) copy-start(f32[2,64]{1,0:T(2,128)} %copy-done.44) | copy-start | bytes 1540
  74.4 3.7 %copy-start.47 = (f32[2,64]{1,0:T(2,128)S(1)}, f32[2,64]{1,0:T(2,128)}, u32[]{:S(2)}) copy-start(f32[2,64]{1,0:T(2,128)} %copy-done.46) | copy-start | bytes 1540
  82.7 2.2 %copy-start.57 = (f32[2,8,256]{2,1,0:T(8,128)S(1)}, f32[2,8,256]{2,1,0:T(8,128)}, u32[]{:S(2)}) copy-start(f32[2,8,256]{2,1,0:T(8,128)} %get-tuple-element.82) | copy-start | bytes 49156
  82.7 2.2 %copy-start.58 = (f32[2,8,256]{2,1,0:T(8,128)S(1)}, f32[2,8,256]{2,1,0:T(8,128)}, u32[]{:S(2)}) copy-start(f32[2,8,256]{2,1,0:T(8,128)} %get-tuple-element.83) | copy-start | bytes 49156
  82.7 2.2 %copy-start.59 = (f32[2,8,256]{2,1,0:T(8,128)S(1)}, f32[2,8,256]{2,1,0:T(8,128)}, u32[]{:S(2)}) copy-start(f32[2,8,256]{2,1,0:T(8,128)} %get-tuple-element.84) | copy-start | bytes 49156
  82.7 2.4 %copy-start.12 = (f32[256,2,8]{0,2,1:T(8,128)S(1)}, f32[256,2,8]{0,2,1:T(8,128)}, u32[]{:S(2)}) copy-start(f32[256,2,8]{0,2,1:T(8,128)} %copy-done.11) | copy-start | bytes 49156
  82.7 2.4 %copy-start.17 = (f32[256,2,8]{0,2,1:T(8,128)S(1)}, f32[256,2,8]{0,2,1:T(8,128)}, u32[]{:S(2)}) copy-start(f32[256,2,8]{0,2,1:T(8,128)} %param.23) | copy-start | bytes 49156
  82.7 2.4 %copy-start.31 = (f32[2,8]{1,0:T(2,128)S(1)}, f32[2,8]{1,0:T(2,128)}, u32[]{:S(2)}) copy-start(f32[2,8]{1,0:T(2,128)} %copy-done.29) | copy-start | bytes 196
  82.7 2.4 %copy-start.48 = (f32[1,2,8]{0,2,1:T(8,128)S(1)}, f32[1,2,8]{0,2,1:T(8,128)}, u32[]{:S(2)}) copy-start(f32[1,2,8]{0,2,1:T(8,128)} %copy.139) | copy-start | bytes 196
  82.7 2.4 %copy-start.50 = (f32[2,8]{1,0:T(2,128)S(1)}, f32[2,8]{1,0:T(2,128)}, u32[]{:S(2)}) copy-start(f32[2,8]{1,0:T(2,128)} %param.25) | copy-start | bytes 196
  83.3 5.6 %collective-permute-start.7 = (f32[3,2,640]{2,1,0:T(2,128)S(1)}, f32[3,2,640]{2,1,0:T(2,128)S(1)}, u32[]{:S(2)}, u32[]{:S(2)}) collective-permute-start(f32[3,2,640]{2,1,0:T(2,128)S(1)} %pad_maximum_fusion.9), channel_id=1, source_target_pairs={{2,0},{4,2},{6,4},{8,6},{10,8},{12,10},{14,12},{3,1},{5,3},{7,5},{... | collective-permute-start | bytes 46088 | tf_op jit(solution)/shard_map/ppermute | solution.py:12
  (20 other events, 25.4 us)

commit v12 on v11

--- a/solution.py
+++ b/solution.py
@@ -12,14 +12,14 @@
     return lax.ppermute(array, axis, pairs)
 
 
-def scanned_pair(decay, forward_state, backward_state, axis, riders):
+def scanned_pair(decay, forward_state, backward_state, axis):
     count = lax.axis_size(axis)
-    groups, heads, rows, cols = forward_state.shape
-    lanes = 128
+    groups, rows, lanes = forward_state.shape
+    pad_rows = 8
 
     def pack(decay_part, state_part):
         return jnp.concatenate(
-            [state_part, jnp.broadcast_to(decay_part[:, :, None], (groups, heads, lanes))], 2
+            [state_part, jnp.broadcast_to(decay_part[:, None, :], (groups, pad_rows, lanes))], 1
         ).astype(jnp.bfloat16)
 
     def shift(packed, by, sign):
@@ -28,39 +28,28 @@
 
     def unpack(got):
         got = got.astype(jnp.float32)
-        return got[:, :, rows * cols], got[:, :, : rows * cols]
+        return got[:, rows, :], got[:, :rows, :]
 
     def fold(window, got_decay, got_state):
         before_decay, before_state, upto_decay, upto_state = window
         return (
             before_decay * got_decay,
-            before_decay[:, :, None] * got_state + before_state,
+            before_decay[:, None, :] * got_state + before_state,
             upto_decay * got_decay,
-            upto_decay[:, :, None] * got_state + upto_state,
+            upto_decay[:, None, :] * got_state + upto_state,
         )
 
-    flats = [s.reshape(groups, heads, rows * cols) for s in (forward_state, backward_state)]
     windows = [
-        (jnp.ones_like(decay), jnp.zeros_like(flat), decay, flat) for flat in flats
+        (jnp.ones_like(decay), jnp.zeros_like(state), decay, state)
+        for state in (forward_state, backward_state)
     ]
-    tied = []
     by = 1
-    step = 0
     while by < count:
         sent = [pack(w[2], w[3]) for w in windows]
-        if step < len(riders):
-            work, arguments = riders[step]
-            sent, arguments = lax.optimization_barrier((sent, arguments))
         got = [shift(s, by, sign) for s, sign in zip(sent, (1, -1))]
-        if step < len(riders):
-            done = work(*arguments)
-            got, done = lax.optimization_barrier((got, done))
-            tied.append(done)
         windows = [fold(w, *unpack(g)) for w, g in zip(windows, got)]
         by *= 2
-        step += 1
-    state_in, adjoint = [w[1].reshape(groups, heads, rows, cols) for w in windows]
-    return state_in, adjoint, tied
+    return windows[0][1], windows[1][1]
 
 
 def conv_forward(extended, weight):
@@ -127,13 +116,19 @@
     x_heads = x_float.reshape(length, groups, head_count, head_size)
     tail_weight = jnp.exp(cum_log[-1][None] - cum_log) * step_size
     weighted = (x_heads * tail_weight[..., None]).astype(jnp.bfloat16)
-    state_end = jnp.einsum("sghp,sgn->ghpn", weighted.astype(jnp.float32), b_float, precision=HIGH)
+    state_end = jnp.einsum(
+        "sgn,sgk->gnk",
+        b_float,
+        weighted.reshape(length, groups, channels).astype(jnp.float32),
+        precision=HIGH,
+    )
     return (cum_log, state_end)
 
 
 def carry_in(c_float, cum_log, state_in):
-    carried = jnp.einsum("tgn,ghpn->tghp", c_float, state_in, precision=HIGH)
-    return carried * jnp.exp(cum_log)[..., None]
+    length, groups, heads = cum_log.shape
+    carried = jnp.einsum("tgn,gnk->tgk", c_float, state_in, precision=HIGH)
+    return carried.reshape(length, groups, heads, -1) * jnp.exp(cum_log)[..., None]
 
 
 def on_device(x_in, b_in, c_in, dt_in, rate, dt_bias, skip, conv_x, conv_b, conv_c, grad_y):
@@ -169,12 +164,15 @@
     decay_total = jnp.exp(cum_log[-1])
     grad_heads = grad_y.astype(jnp.float32).reshape(length, groups, head_count, head_size)
     seed_state = jnp.einsum(
-        "tghp,tgn->ghpn", jnp.exp(cum_log)[..., None] * grad_heads, c_float, precision=HIGH
-    )
-
+        "tgn,tgk->gnk",
+        c_float,
+        (jnp.exp(cum_log)[..., None] * grad_heads).reshape(length, groups, channels),
+        precision=HIGH,
+    )
     y_local, mix_pull = jax.vjp(mix_map, x_float, b_float, c_float, dt_in)
     mix_x, mix_b, mix_c, mix_dt = mix_pull(grad_heads)
-    state_in, adjoint, _ = scanned_pair(decay_total, state_end, seed_state, "ctx", [])
+    decay_lanes = jnp.repeat(decay_total, head_size, axis=1)
+    state_in, adjoint = scanned_pair(decay_lanes, state_end, seed_state, "ctx")
 
     def carry_map(c_arg, cum_arg):
         return carry_in(c_arg, cum_arg, state_in)
@@ -182,7 +180,9 @@
     y_carry, carry_pull = jax.vjp(carry_map, c_float, cum_log)
     y_out = (y_local + y_carry).reshape(length, groups, channels).astype(jnp.bfloat16)
     grad_c_carry, grad_cum_carry = carry_pull(grad_heads)
-    end_term = jnp.sum(adjoint * state_in, axis=(2, 3)) * decay_total
+    end_term = (adjoint * state_in).reshape(groups, state_size, head_count, head_size).sum(
+        axis=(1, 3)
+    ) * decay_total
     grad_cum = grad_cum_carry.at[length - 1].add(end_term)
     state_x, state_b, state_dt = state_pull((grad_cum, adjoint))
     grad_x_conv = mix_x + state_x

time: 93.4 us -> 94.4 us (1.011)
  the two profiles are of different devices: /device:TPU:0 before, /device:TPU:26 now
where the time goes in v12:
time: 94.4 us; the launch traced here: 93.4 us
  local copies, waits for them, and re-layouts  20.8 us (22%)
  waiting for transfers between devices  19 us (20%)
  other arithmetic  18.3 us (19%)
  matrix products  17.1 us (18%)
  starting transfers between devices  16.4 us (17%)
  between operations  1.85 us (2%)
    ppermute x6, waiting for transfers between devices, shift(): return lax.ppermute(packed, axis, pairs)  15.5 us
    ppermute x6, starting transfers between devices, shift(): return lax.ppermute(packed, axis, pairs)  12.3 us
    dot_general x3, matrix products, ssd_mix(): jnp.einsum('ghts,sghp->tghp', mixing, x_half, preferred_element_type=jnp....  8.75 us
    unnamed x168, local copies, waits for them, and re-layouts  7.99 us
    ppermute x2, starting transfers between devices, from_behind(): return lax.ppermute(array, axis, pairs)  4.04 us
    ppermute x2, waiting for transfers between devices, from_behind(): return lax.ppermute(array, axis, pairs)  3.5 us
    add x3, other arithmetic, conv_backward(): result = result + weight[tap_index] * padded[offset:offset + ext_len]  2.59 us
    convert_element_type x1, other arithmetic, ssd_state(): weighted = (x_heads * tail_weight[..., None]).astype(jnp.bfloat16)  2.4 us
  transfers between devices with their start and end apart: 8, of which 5 were waited for; matrix products, arithmetic and copies ran while one was open for 16% of the time, Pallas kernels for 0%

profile of v12, /device:TPU:26, one launch (start us, length us, event | category | flops | bytes accessed | tf_op | source)
XLA Modules:
  0.0 93.4 jit_solution(10700569837217144299)
XLA Ops:
  0.6 0.8 slice.296
  1.6 0.8 slice.295
  2.5 0.7 slice.294
  3.3 0.9 %copy.68 = bf16[3,2,640]{0,2,1:T(8,128)(2,1)} copy(bf16[3,2,640]{2,1,0:T(2,128)(2,1)S(1)} %pad_maximum_fusion.10) | data formatting | bytes 15360 | tf_op jit(solution)/shard_map/concatenate | solution.py:143
  4.2 1.3 %collective-permute-start = (bf16[3,2,640]{0,2,1:T(8,128)(2,1)}, bf16[3,2,640]{0,2,1:T(8,128)(2,1)S(1)}, u32[]{:S(2)}, u32[]{:S(2)}) collective-permute-start(bf16[3,2,640]{0,2,1:T(8,128)(2,1)} %copy.68), channel_id=1, source_target_pairs={{0,2},{2,4},{4,6},{6,8},{8,10},{10,12},{12,14},{1,3},{3,5},{5,7},{... | collective-permute-start | bytes 23048 | tf_op jit(solution)/shard_map/ppermute | solution.py:12
  5.5 0.7 neg.30
  6.2 0.9 fusion.76
  7.4 0.8 fusion.109
  8.2 0.7 slice_bitcast_fusion.3
  9.0 0.7 slice_bitcast_fusion.7
  12.3 3.5 %collective-permute-done = bf16[3,2,640]{0,2,1:T(8,128)(2,1)S(1)} collective-permute-done((bf16[3,2,640]{0,2,1:T(8,128)(2,1)}, bf16[3,2,640]{0,2,1:T(8,128)(2,1)S(1)}, u32[]{:S(2)}, u32[]{:S(2)}) %collective-permute-start) | collective-permute-done | bytes 7712 | tf_op jit(solution)/shard_map/ppermute | solution.py:12
  15.9 2.4 %fusion.65 = (bf16[256,2,512]{0,2,1:T(8,128)(2,1)S(1)}, f32[256,2,512]{0,2,1:T(8,128)}, f32[256,2,512]{0,2,1:T(8,128)}) fusion(f32[256,2,8]{0,2,1:T(8,128)S(1)} %get-tuple-element.106, bf16[256,2,512]{0,2,1:T(8,128)(2,1)S(1)} %copy.69, f32[2,512]{1,0:T(2,128)S(1)} %get-tuple-element.104, bf16[3,2,512]{0,2,1:T(8,128)(2,1)S(1)} %slice.358, ...), kind=kLoop, calls=%fused_computation.64 | loop fusion | flops 7340032 | bytes 3184640 | tf_op jit(solution)/shard_map/jvp()/convert_element_type | solution.py:118
  18.4 1.1 %multiply_convert_fusion.1 = (bf16[256,2,64]{0,2,1:T(8,128)(2,1)S(1)}, f32[256,2,64]{0,2,1:T(8,128)}, bf16[256,2,64]{0,2,1:T(8,128)(2,1)S(1)}, f32[256,2,64]{0,2,1:T(8,128)}) fusion(bf16[256,2,64]{0,2,1:T(8,128)(2,1)S(1)} %copy-done.20, f32[2,64]{1,0:T(2,128)S(1)} %get-tuple-element.118, bf16[3,2,64]{0,2,1:T(8,128)(2,1)S(1)} %get-tuple-element.91, ...), kind=kLoop, calls=%fused_computation.125 | loop fusion | flops 1638400 | bytes 529920 | tf_op jit(solution)/shard_map/convert_element_type | solution.py:154
  20.3 0.7 pad_maximum_fusion.2
  21.1 3.3 %collective-permute-start.4 = (bf16[2,72,512]{2,1,0:T(8,128)(2,1)S(1)}, bf16[2,72,512]{2,1,0:T(8,128)(2,1)S(1)}, u32[]{:S(2)}, u32[]{:S(2)}) collective-permute-start(bf16[2,72,512]{2,1,0:T(8,128)(2,1)S(1)} %get-tuple-element.101), channel_id=1, source_target_pairs={{2,0},{4,2},{6,4},{8,6},{10,8},{12,10},{14,12},{3,1},{5,3},{7,5},{... | collective-permute-start | bytes 442376 | tf_op jit(solution)/shard_map/ppermute | solution.py:27
  24.4 1.3 %collective-permute-start.1 = (bf16[2,72,512]{2,1,0:T(8,128)(2,1)}, bf16[2,72,512]{2,1,0:T(8,128)(2,1)S(1)}, u32[]{:S(2)}, u32[]{:S(2)}) collective-permute-start(bf16[2,72,512]{2,1,0:T(8,128)(2,1)} %get-tuple-element.100), channel_id=1, source_target_pairs={{0,2},{2,4},{4,6},{6,8},{8,10},{10,12},{12,14},{1,3},{3,5},{5,7},{... | collective-permute-start | bytes 442376 | tf_op jit(solution)/shard_map/ppermute | solution.py:27
  25.8 2.9 %collective-permute-done.4 = bf16[2,72,512]{2,1,0:T(8,128)(2,1)S(1)} collective-permute-done((bf16[2,72,512]{2,1,0:T(8,128)(2,1)S(1)}, bf16[2,72,512]{2,1,0:T(8,128)(2,1)S(1)}, u32[]{:S(2)}, u32[]{:S(2)}) %collective-permute-start.4) | collective-permute-done | bytes 147488 | tf_op jit(solution)/shard_map/ppermute | solution.py:27
  29.3 2.3 %collective-permute-done.1 = bf16[2,72,512]{2,1,0:T(8,128)(2,1)S(1)} collective-permute-done((bf16[2,72,512]{2,1,0:T(8,128)(2,1)}, bf16[2,72,512]{2,1,0:T(8,128)(2,1)S(1)}, u32[]{:S(2)}, u32[]{:S(2)}) %collective-permute-start.1) | collective-permute-done | bytes 147488 | tf_op jit(solution)/shard_map/ppermute | solution.py:27
  32.3 0.8 fusion.91
  33.8 3.5 %collective-permute-start.5 = (bf16[2,72,512]{2,1,0:T(8,128)(2,1)}, bf16[2,72,512]{2,1,0:T(8,128)(2,1)}, u32[]{:S(2)}, u32[]{:S(2)}) collective-permute-start(bf16[2,72,512]{2,1,0:T(8,128)(2,1)} %pad_maximum_fusion.5), channel_id=1, source_target_pairs={{4,0},{6,2},{8,4},{10,6},{12,8},{14,10},{5,1},{7,3},{9,5},{11,7},{... | collective-permute-start | bytes 442376 | tf_op jit(solution)/shard_map/ppermute | solution.py:27
  38.5 1.2 %copy.73 = bf16[256,2,512]{0,2,1:T(8,128)(2,1)} copy(bf16[256,2,512]{2,1,0:T(2,128)(2,1)S(1)} %copy-done) | data formatting | bytes 1048576 | tf_op args[10]
  39.7 0.9 pad_maximum_fusion.3
  40.7 1.3 %collective-permute-start.2 = (bf16[2,72,512]{2,1,0:T(8,128)(2,1)S(1)}, bf16[2,72,512]{2,1,0:T(8,128)(2,1)S(1)}, u32[]{:S(2)}, u32[]{:S(2)}) collective-permute-start(bf16[2,72,512]{2,1,0:T(8,128)(2,1)S(1)} %pad_maximum_fusion.3), channel_id=1, source_target_pairs={{0,4},{2,6},{4,8},{6,10},{8,12},{10,14},{1,5},{3,7},{5,9},{7,11},{... | collective-permute-start | bytes 442376 | tf_op jit(solution)/shard_map/ppermute | solution.py:27
  42.0 0.9 convert_element_type.193
  43.0 4.7 %collective-permute-done.2 = bf16[2,72,512]{2,1,0:T(8,128)(2,1)S(1)} collective-permute-done((bf16[2,72,512]{2,1,0:T(8,128)(2,1)S(1)}, bf16[2,72,512]{2,1,0:T(8,128)(2,1)S(1)}, u32[]{:S(2)}, u32[]{:S(2)}) %collective-permute-start.2) | collective-permute-done | bytes 147488 | tf_op jit(solution)/shard_map/ppermute | solution.py:27
  47.7 0.8 slice_multiply_fusion.1
  48.5 1.3 %add_convert_fusion.1 = (bf16[2,64,512]{2,1,0:T(8,128)(2,1)S(1)}, bf16[2,64,512]{2,1,0:T(8,128)(2,1)S(1)}) fusion(f32[2,72,512]{2,1,0:T(8,128)S(1)} %convert_element_type.185, f32[2,512]{1,0:T(2,128)S(1)} %bitcast.216, f32[2,64,512]{2,1,0:T(8,128)} %copy-done.5, f32[2,72,512]{2,1,0:T(8,128)} %copy-done.3, f32[2,512]{1,0:T(2,128)S(1)} %copy-done.27, ...), kind=kLoop, calls=%fused_computation.91 | loop fusion | flops 655360 | bytes 1847296 | tf_op jit(solution)/shard_map/convert.14
  49.9 1.4 %collective-permute-start.6 = (bf16[2,72,512]{2,1,0:T(8,128)(2,1)S(1)}, bf16[2,72,512]{2,1,0:T(8,128)(2,1)S(1)}, u32[]{:S(2)}, u32[]{:S(2)}) collective-permute-start(bf16[2,72,512]{2,1,0:T(8,128)(2,1)S(1)} %pad_maximum_fusion.6), channel_id=1, source_target_pairs={{8,0},{10,2},{12,4},{14,6},{9,1},{11,3},{13,5},{15,7},{24,16},{26,... | collective-permute-start | bytes 442376 | tf_op jit(solution)/shard_map/ppermute | solution.py:27
  51.4 1.5 %collective-permute-start.3 = (bf16[2,72,512]{2,1,0:T(8,128)(2,1)S(1)}, bf16[2,72,512]{2,1,0:T(8,128)(2,1)S(1)}, u32[]{:S(2)}, u32[]{:S(2)}) collective-permute-start(bf16[2,72,512]{2,1,0:T(8,128)(2,1)S(1)} %pad_maximum_fusion.4), channel_id=1, source_target_pairs={{0,8},{2,10},{4,12},{6,14},{1,9},{3,11},{5,13},{7,15},{16,24},{18,... | collective-permute-start | bytes 442376 | tf_op jit(solution)/shard_map/ppermute | solution.py:27
  53.2 0.7 slice.379
  53.9 0.7 slice.374
  54.6 5.5 %collective-permute-done.3 = bf16[2,72,512]{2,1,0:T(8,128)(2,1)S(1)} collective-permute-done((bf16[2,72,512]{2,1,0:T(8,128)(2,1)S(1)}, bf16[2,72,512]{2,1,0:T(8,128)(2,1)S(1)}, u32[]{:S(2)}, u32[]{:S(2)}) %collective-permute-start.3) | collective-permute-done | bytes 147488 | tf_op jit(solution)/shard_map/ppermute | solution.py:27
  60.2 0.7 multiply_reduce_fusion.2
  60.9 0.7 multiply_reduce_fusion.1
  62.4 1.3 %fusion.110 = (f32[2,8]{1,0:T(2,128)}, f32[2,8,256]{2,1,0:T(8,128)S(1)}, f32[256,2,8]{0,2,1:T(8,128)}) fusion(f32[256,2,8]{0,2,1:T(8,128)S(1)} %get-tuple-element.128, f32[2,8]{1,0:T(2,128)S(1)} %copy-done.46, f32[256,16]{0,1:S(1)} %copy-done.22, f32[256,2,8]{0,2,1:T(8,128)S(1)} %copy-done.33, f32[2,8]{1,0:T(2,128)S(1)} %copy-done.65, ...), kind=kLoop, calls=%fused_computation.168 | loop fusion | flops 49136 | bytes 98496 | tf_op jit(solution)/shard_map/transpose(jvp())/reduce_sum | solution.py:117
  63.7 4.9 %fusion.25 = (f32[2,8,256]{2,1,0:T(8,128)}, f32[2,8,256]{2,1,0:T(8,128)}, f32[2,8,256]{2,1,0:T(8,128)}, f32[2,256,256]{2,1,0:T(8,128)S(1)}) fusion(f32[2,8,256]{2,1,0:T(8,128)S(1)} %bitcast.212, f32[2,8,256]{2,1,0:T(8,128)S(1)} %get-tuple-element.98, f32[2,256,256]{2,1,0:T(8,128)S(1)} %fusion.126, pred[256,256]{1,0:T(8,128)(4,1)S(1)} %copy-done.30, ...), kind=kOutput, calls=%fused_computation.34 | convolution fusion | flops 156356608 | bytes 2768896 | tf_op jit(solution)/shard_map/transpose(jvp(ghts,sghp->tghp))/dot_general | solution.py:107
  69.0 1.0 %convolution_bitcast_fusion.1 = f32[256,2,64]{0,2,1:T(8,128)} fusion(f32[2,256,256]{2,1,0:T(8,128)S(1)} %get-tuple-element.80, bf16[256,2,64]{0,2,1:T(8,128)(2,1)S(1)} %get-tuple-element.132), kind=kOutput, calls=%fused_computation.47 | convolution fusion | flops 100663296 | bytes 720896 | tf_op jit(solution)/shard_map/transpose(jvp(tgn,sgn->gts))/dot_general | solution.py:105
  70.0 2.4 %fusion.35 = bf16[256,2,8,64]{0,3,2,1:T(8,128)(2,1)} fusion(f32[2,8,256]{2,1,0:T(8,128)S(1)} %get-tuple-element.98, f32[2,8,256]{2,1,0:T(8,128)S(1)} %bitcast.213, f32[2,256,256]{2,1,0:T(8,128)S(1)} %fusion.126, pred[256,256]{1,0:T(8,128)(4,1)S(1)} %copy-done.30, f32[256,2,8,64]{0,3,2,1:T(8,128)S(1)} %bitcast.207, f32[256,2,8,64]{0,3,2,1:T(8,128)S(1)} %bitcast.204, ...), kind=kOutput, calls=%fused_computation.38 | convolution fusion | flops 142082048 | bytes 3260480 | tf_op jit(solution)/shard_map/jvp(ghts,sghp->tghp)/dot_general | solution.py:107
  72.4 1.4 %fusion.47 = f32[256,2,8,64]{0,3,2,1:T(8,128)S(1)} fusion(bf16[2,8,64,256]{3,2,1,0:T(8,128)(2,1)S(1)} %bitcast.209, f32[2,8,256]{2,1,0:T(8,128)S(1)} %get-tuple-element.98, f32[2,8,256]{2,1,0:T(8,128)S(1)} %bitcast.214, f32[2,256,256]{2,1,0:T(8,128)S(1)} %fusion.126, pred[256,256]{1,0:T(8,128)(4,1)S(1)} %copy-done.30, f32[256,2,8,64]{0,3,2,1:T(8,128)S(1)} %bitcast.202, ...), kind=kOutput, calls=%fused_computation.42 | convolution fusion | flops 141557760 | bytes 3244096 | tf_op jit(solution)/shard_map/transpose(jvp(ghts,sghp->tghp))/dot_general | solution.py:107
  74.6 2.0 %fusion.20 = f32[259,2,512]{0,2,1:T(8,128)S(1)} fusion(f32[256,2,512]{0,2,1:T(8,128)S(1)} %multiply_multiply_fusion, f32[2,512]{1,0:T(2,128)S(1)} %copy-done.40, f32[2,512]{1,0:T(2,128)S(1)} %copy-done.42, f32[2,512]{1,0:T(2,128)S(1)} %copy-done.38, f32[2,512]{1,0:T(2,128)S(1)} %copy-done.36), kind=kLoop, calls=%fused_computation.27 | loop fusion | flops 1856512 | bytes 2125824 | tf_op jit(solution)/shard_map/add | solution.py:76
  76.6 1.2 %fusion.55 = f32[256,2,64]{0,2,1:T(8,128)S(1)} fusion(f32[2,256,64]{1,2,0:T(8,128)S(1)} %fusion.127, f32[2,64,512]{2,1,0:T(8,128)S(1)} %get-tuple-element.83, f32[2,512,256]{1,0,2:T(2,128)S(1)} %bitcast.200, f32[256,2,64]{0,2,1:T(8,128)S(1)} %copy-done.16), kind=kOutput, calls=%fused_computation.52 | convolution fusion | flops 201687040 | bytes 1703936 | tf_op jit(solution)/shard_map/transpose(jvp(tgn,gnk->tgk))/dot_general | solution.py:130
  78.9 1.3 %fusion.58 = f32[256,2,64]{0,2,1:T(8,128)S(1)} fusion(f32[256,2,64]{0,2,1:T(8,128)} %convolution_bitcast_fusion.1, f32[2,64,512]{2,1,0:T(8,128)S(1)} %copy-done.8, bf16[256,2,512]{0,2,1:T(8,128)(2,1)S(1)} %get-tuple-element.84, f32[256,2,64]{0,2,1:T(8,128)S(1)} %copy-done.15), kind=kOutput, calls=%fused_computation.55 | convolution fusion | flops 201687040 | bytes 1179648 | tf_op jit(solution)/shard_map/transpose(jvp(sgn,sgk->gnk))/dot_general | solution.py:119
  81.1 2.8 %collective-permute-start.7 = (f32[3,2,640]{2,1,0:T(2,128)S(1)}, f32[3,2,640]{2,1,0:T(2,128)S(1)}, u32[]{:S(2)}, u32[]{:S(2)}) collective-permute-start(f32[3,2,640]{2,1,0:T(2,128)S(1)} %pad_maximum_fusion.9), channel_id=1, source_target_pairs={{2,0},{4,2},{6,4},{8,6},{10,8},{12,10},{14,12},{3,1},{5,3},{7,5},{... | collective-permute-start | bytes 46088 | tf_op jit(solution)/shard_map/ppermute | solution.py:12
  84.8 0.9 fusion.62
  86.0 1.2 %copy.86 = bf16[256,2,512]{2,1,0:T(2,128)(2,1)} copy(bf16[256,2,512]{0,2,1:T(8,128)(2,1)S(1)} %bitcast.210) | data formatting | bytes 1048576
  87.5 1.7 %scatter-add.14 = bf16[256,2,512]{0,2,1:T(8,128)(2,1)S(1)} dynamic-update-slice(bf16[256,2,512]{0,2,1:T(8,128)(2,1)S(1)} %slice.384, bf16[3,2,512]{0,2,1:T(8,128)(2,1)S(1)} %slice_add_fusion, s32[]{:T(128)} %constant.115.clone.1, s32[]{:T(128)} %constant.116.clone.1, s32[]{:T(128)} %constant.116.clone.1) | dynamic-update-slice | bytes 12292 | tf_op jit(solution)/shard_map/scatter-add | solution.py:202
  89.2 1.2 %copy.87 = bf16[256,2,512]{2,1,0:T(2,128)(2,1)} copy(bf16[256,2,512]{0,2,1:T(8,128)(2,1)S(1)} %scatter-add.14) | data formatting | bytes 1048576
  90.7 0.9 slice_add_fusion.1
  (228 shorter events, 14.6 us)
Async XLA Ops:
  4.2 11.5 %collective-permute-start = (bf16[3,2,640]{0,2,1:T(8,128)(2,1)}, bf16[3,2,640]{0,2,1:T(8,128)(2,1)S(1)}, u32[]{:S(2)}, u32[]{:S(2)}) collective-permute-start(bf16[3,2,640]{0,2,1:T(8,128)(2,1)} %copy.68), channel_id=1, source_target_pairs={{0,2},{2,4},{4,6},{6,8},{8,10},{10,12},{12,14},{1,3},{3,5},{5,7},{... | collective-permute-start | bytes 23048 | tf_op jit(solution)/shard_map/ppermute | solution.py:12
  6.2 3.5 %copy-start.69 = (f32[2,8]{1,0:T(2,128)}, f32[2,8]{1,0:T(2,128)S(1)}, u32[]{:S(2)}) copy-start(f32[2,8]{1,0:T(2,128)S(1)} %neg.30) | copy-start | bytes 196
  7.4 4.7 %copy-start.45 = (f32[2,8]{1,0:T(2,128)}, f32[2,8]{1,0:T(2,128)S(1)}, u32[]{:S(2)}) copy-start(f32[2,8]{1,0:T(2,128)S(1)} %slice_reduce_fusion) | copy-start | bytes 196
  8.9 6.9 %copy-start.35 = (f32[2,512]{1,0:T(2,128)}, f32[2,512]{1,0:T(2,128)S(1)}, u32[]{:S(2)}) copy-start(f32[2,512]{1,0:T(2,128)S(1)} %get-tuple-element.102) | copy-start | bytes 12292
  8.9 6.9 %copy-start.37 = (f32[2,512]{1,0:T(2,128)}, f32[2,512]{1,0:T(2,128)S(1)}, u32[]{:S(2)}) copy-start(f32[2,512]{1,0:T(2,128)S(1)} %get-tuple-element.103) | copy-start | bytes 12292
  8.9 6.9 %copy-start.39 = (f32[2,512]{1,0:T(2,128)}, f32[2,512]{1,0:T(2,128)S(1)}, u32[]{:S(2)}) copy-start(f32[2,512]{1,0:T(2,128)S(1)} %get-tuple-element.104) | copy-start | bytes 12292
  9.0 6.9 %copy-start.41 = (f32[2,512]{1,0:T(2,128)}, f32[2,512]{1,0:T(2,128)S(1)}, u32[]{:S(2)}) copy-start(f32[2,512]{1,0:T(2,128)S(1)} %get-tuple-element.105) | copy-start | bytes 12292
  9.7 8.6 %copy-start.49 = (f32[2,64]{1,0:T(2,128)}, f32[2,64]{1,0:T(2,128)S(1)}, u32[]{:S(2)}) copy-start(f32[2,64]{1,0:T(2,128)S(1)} %get-tuple-element.116) | copy-start | bytes 1540
  9.7 8.6 %copy-start.51 = (f32[2,64]{1,0:T(2,128)}, f32[2,64]{1,0:T(2,128)S(1)}, u32[]{:S(2)}) copy-start(f32[2,64]{1,0:T(2,128)S(1)} %get-tuple-element.117) | copy-start | bytes 1540
  9.7 8.6 %copy-start.53 = (f32[2,64]{1,0:T(2,128)}, f32[2,64]{1,0:T(2,128)S(1)}, u32[]{:S(2)}) copy-start(f32[2,64]{1,0:T(2,128)S(1)} %get-tuple-element.118) | copy-start | bytes 1540
  9.7 8.6 %copy-start.55 = (f32[2,64]{1,0:T(2,128)}, f32[2,64]{1,0:T(2,128)S(1)}, u32[]{:S(2)}) copy-start(f32[2,64]{1,0:T(2,128)S(1)} %get-tuple-element.119) | copy-start | bytes 1540
  11.5 6.8 %copy-start.57 = (f32[2,64]{1,0:T(2,128)}, f32[2,64]{1,0:T(2,128)S(1)}, u32[]{:S(2)}) copy-start(f32[2,64]{1,0:T(2,128)S(1)} %get-tuple-element.120) | copy-start | bytes 1540
  11.5 6.8 %copy-start.59 = (f32[2,64]{1,0:T(2,128)}, f32[2,64]{1,0:T(2,128)S(1)}, u32[]{:S(2)}) copy-start(f32[2,64]{1,0:T(2,128)S(1)} %get-tuple-element.121) | copy-start | bytes 1540
  11.5 6.8 %copy-start.61 = (f32[2,64]{1,0:T(2,128)}, f32[2,64]{1,0:T(2,128)S(1)}, u32[]{:S(2)}) copy-start(f32[2,64]{1,0:T(2,128)S(1)} %get-tuple-element.122) | copy-start | bytes 1540
  11.5 6.8 %copy-start.63 = (f32[2,64]{1,0:T(2,128)}, f32[2,64]{1,0:T(2,128)S(1)}, u32[]{:S(2)}) copy-start(f32[2,64]{1,0:T(2,128)S(1)} %get-tuple-element.123) | copy-start | bytes 1540
  12.3 20.1 %copy-start.26 = (f32[2,512]{1,0:T(2,128)}, f32[2,512]{1,0:T(2,128)S(1)}, u32[]{:S(2)}) copy-start(f32[2,512]{1,0:T(2,128)S(1)} %broadcast_in_dim.38) | copy-start | bytes 12292
  19.4 6.4 %copy-start.9 = (bf16[256,2,64]{0,2,1:T(8,128)(2,1)}, bf16[256,2,64]{0,2,1:T(8,128)(2,1)S(1)}, u32[]{:S(2)}) copy-start(bf16[256,2,64]{0,2,1:T(8,128)(2,1)S(1)} %get-tuple-element.87) | copy-start | bytes 196612
  19.7 13.4 %copy-start.5 = (f32[2,64,512]{2,1,0:T(8,128)}, f32[2,64,512]{2,1,0:T(8,128)S(1)}, u32[]{:S(2)}) copy-start(f32[2,64,512]{2,1,0:T(8,128)S(1)} %get-tuple-element.125) | copy-start | bytes 786436
  20.3 13.5 %copy-start.6 = (f32[2,64,512]{2,1,0:T(8,128)}, f32[2,64,512]{2,1,0:T(8,128)S(1)}, u32[]{:S(2)}) copy-start(f32[2,64,512]{2,1,0:T(8,128)S(1)} %get-tuple-element.127) | copy-start | bytes 786436
  21.1 7.6 %collective-permute-start.4 = (bf16[2,72,512]{2,1,0:T(8,128)(2,1)S(1)}, bf16[2,72,512]{2,1,0:T(8,128)(2,1)S(1)}, u32[]{:S(2)}, u32[]{:S(2)}) collective-permute-start(bf16[2,72,512]{2,1,0:T(8,128)(2,1)S(1)} %get-tuple-element.101), channel_id=1, source_target_pairs={{2,0},{4,2},{6,4},{8,6},{10,8},{12,10},{14,12},{3,1},{5,3},{7,5},{... | collective-permute-start | bytes 442376 | tf_op jit(solution)/shard_map/ppermute | solution.py:27
  24.4 7.2 %collective-permute-start.1 = (bf16[2,72,512]{2,1,0:T(8,128)(2,1)}, bf16[2,72,512]{2,1,0:T(8,128)(2,1)S(1)}, u32[]{:S(2)}, u32[]{:S(2)}) collective-permute-start(bf16[2,72,512]{2,1,0:T(8,128)(2,1)} %get-tuple-element.100), channel_id=1, source_target_pairs={{0,2},{2,4},{4,6},{6,8},{8,10},{10,12},{12,14},{1,3},{3,5},{5,7},{... | collective-permute-start | bytes 442376 | tf_op jit(solution)/shard_map/ppermute | solution.py:27
  31.7 5.6 %copy-start.3 = (f32[2,72,512]{2,1,0:T(8,128)}, f32[2,72,512]{2,1,0:T(8,128)S(1)}, u32[]{:S(2)}) copy-start(f32[2,72,512]{2,1,0:T(8,128)S(1)} %convert_element_type.184) | copy-start | bytes 884740
  33.8 8.2 %collective-permute-start.5 = (bf16[2,72,512]{2,1,0:T(8,128)(2,1)}, bf16[2,72,512]{2,1,0:T(8,128)(2,1)}, u32[]{:S(2)}, u32[]{:S(2)}) collective-permute-start(bf16[2,72,512]{2,1,0:T(8,128)(2,1)} %pad_maximum_fusion.5), channel_id=1, source_target_pairs={{4,0},{6,2},{8,4},{10,6},{12,8},{14,10},{5,1},{7,3},{9,5},{11,7},{... | collective-permute-start | bytes 442376 | tf_op jit(solution)/shard_map/ppermute | solution.py:27
  37.9 10.6 %copy-start.27 = (f32[2,512]{1,0:T(2,128)S(1)}, f32[2,512]{1,0:T(2,128)}, u32[]{:S(2)}) copy-start(f32[2,512]{1,0:T(2,128)} %copy-done.26) | copy-start | bytes 12292
  40.7 7.0 %collective-permute-start.2 = (bf16[2,72,512]{2,1,0:T(8,128)(2,1)S(1)}, bf16[2,72,512]{2,1,0:T(8,128)(2,1)S(1)}, u32[]{:S(2)}, u32[]{:S(2)}) collective-permute-start(bf16[2,72,512]{2,1,0:T(8,128)(2,1)S(1)} %pad_maximum_fusion.3), channel_id=1, source_target_pairs={{0,4},{2,6},{4,8},{6,10},{8,12},{10,14},{1,5},{3,7},{5,9},{7,11},{... | collective-permute-start | bytes 442376 | tf_op jit(solution)/shard_map/ppermute | solution.py:27
  42.9 10.0 %copy-start.10 = (bf16[256,2,64]{0,2,1:T(8,128)(2,1)S(1)}, bf16[256,2,64]{0,2,1:T(8,128)(2,1)}, u32[]{:S(2)}) copy-start(bf16[256,2,64]{0,2,1:T(8,128)(2,1)} %copy-done.9) | copy-start | bytes 196612
  48.5 11.7 %copy-start.4 = (f32[2,72,512]{2,1,0:T(8,128)S(1)}, f32[2,72,512]{2,1,0:T(8,128)}, u32[]{:S(2)}) copy-start(f32[2,72,512]{2,1,0:T(8,128)} %copy-done.3) | copy-start | bytes 884740
  49.9 11.0 %copy-start.1 = (f32[256,2,512]{0,2,1:T(8,128)S(1)}, f32[256,2,512]{0,2,1:T(8,128)}, u32[]{:S(2)}) copy-start(f32[256,2,512]{0,2,1:T(8,128)} %get-tuple-element.85) | copy-start | bytes 3145732
  49.9 4.7 %collective-permute-start.6 = (bf16[2,72,512]{2,1,0:T(8,128)(2,1)S(1)}, bf16[2,72,512]{2,1,0:T(8,128)(2,1)S(1)}, u32[]{:S(2)}, u32[]{:S(2)}) collective-permute-start(bf16[2,72,512]{2,1,0:T(8,128)(2,1)S(1)} %pad_maximum_fusion.6), channel_id=1, source_target_pairs={{8,0},{10,2},{12,4},{14,6},{9,1},{11,3},{13,5},{15,7},{24,16},{26,... | collective-permute-start | bytes 442376 | tf_op jit(solution)/shard_map/ppermute | solution.py:27
  51.4 8.8 %collective-permute-start.3 = (bf16[2,72,512]{2,1,0:T(8,128)(2,1)S(1)}, bf16[2,72,512]{2,1,0:T(8,128)(2,1)S(1)}, u32[]{:S(2)}, u32[]{:S(2)}) collective-permute-start(bf16[2,72,512]{2,1,0:T(8,128)(2,1)S(1)} %pad_maximum_fusion.4), channel_id=1, source_target_pairs={{0,8},{2,10},{4,12},{6,14},{1,9},{3,11},{5,13},{7,15},{16,24},{18,... | collective-permute-start | bytes 442376 | tf_op jit(solution)/shard_map/ppermute | solution.py:27
  63.7 6.3 %copy-start.29 = (f32[256,2,8]{0,2,1:T(8,128)S(1)}, f32[256,2,8]{0,2,1:T(8,128)}, u32[]{:S(2)}) copy-start(f32[256,2,8]{0,2,1:T(8,128)} %copy-done.28) | copy-start | bytes 49156
  63.7 6.3 %copy-start.71 = (f32[2,8]{1,0:T(2,128)S(1)}, f32[2,8]{1,0:T(2,128)}, u32[]{:S(2)}) copy-start(f32[2,8]{1,0:T(2,128)} %param.26) | copy-start | bytes 196
  74.6 3.3 %copy-start.64 = (f32[2,64]{1,0:T(2,128)S(1)}, f32[2,64]{1,0:T(2,128)}, u32[]{:S(2)}) copy-start(f32[2,64]{1,0:T(2,128)} %copy-done.63) | copy-start | bytes 1540
  78.2 7.7 %copy-start.11 = (f32[259,2,64]{0,2,1:T(8,128)}, f32[259,2,64]{0,2,1:T(8,128)S(1)}, u32[]{:S(2)}) copy-start(f32[259,2,64]{0,2,1:T(8,128)S(1)} %fusion.87) | copy-start | bytes 397828
  78.9 5.3 %copy-start.23 = (f32[256,16]{0,1:S(1)}, f32[256,16]{0,1}, u32[]{:S(2)}) copy-start(f32[256,16]{0,1} %copy-done.21) | copy-start | bytes 49156
  80.3 3.6 %copy-start.67 = (f32[2,8]{1,0:T(2,128)S(1)}, f32[2,8]{1,0:T(2,128)}, u32[]{:S(2)}) copy-start(f32[2,8]{1,0:T(2,128)} %get-tuple-element.97) | copy-start | bytes 196
  80.3 3.7 %copy-start.44 = (f32[2,512]{1,0:T(2,128)S(1)}, f32[2,512]{1,0:T(2,128)}, u32[]{:S(2)}) copy-start(f32[2,512]{1,0:T(2,128)} %get-tuple-element.81) | copy-start | bytes 12292
  80.3 3.9 %copy-start.43 = (f32[256,2,8]{0,2,1:T(8,128)S(1)}, f32[256,2,8]{0,2,1:T(8,128)}, u32[]{:S(2)}) copy-start(f32[256,2,8]{0,2,1:T(8,128)} %get-tuple-element.99) | copy-start | bytes 49156
  80.3 4.0 %copy-start.70 = (f32[2,8]{1,0:T(2,128)S(1)}, f32[2,8]{1,0:T(2,128)}, u32[]{:S(2)}) copy-start(f32[2,8]{1,0:T(2,128)} %copy-done.69) | copy-start | bytes 196
  80.3 4.0 %copy-start.72 = (f32[2,8,256]{2,1,0:T(8,128)S(1)}, f32[2,8,256]{2,1,0:T(8,128)}, u32[]{:S(2)}) copy-start(f32[2,8,256]{2,1,0:T(8,128)} %get-tuple-element.77) | copy-start | bytes 49156
  80.4 4.0 %copy-start.73 = (f32[2,8,256]{2,1,0:T(8,128)S(1)}, f32[2,8,256]{2,1,0:T(8,128)}, u32[]{:S(2)}) copy-start(f32[2,8,256]{2,1,0:T(8,128)} %get-tuple-element.78) | copy-start | bytes 49156
  80.4 4.0 %copy-start.74 = (f32[2,8,256]{2,1,0:T(8,128)S(1)}, f32[2,8,256]{2,1,0:T(8,128)}, u32[]{:S(2)}) copy-start(f32[2,8,256]{2,1,0:T(8,128)} %get-tuple-element.79) | copy-start | bytes 49156
  80.4 4.4 %copy-start.25 = (f32[256,2,8]{0,2,1:T(8,128)S(1)}, f32[256,2,8]{0,2,1:T(8,128)}, u32[]{:S(2)}) copy-start(f32[256,2,8]{0,2,1:T(8,128)} %copy-done.24) | copy-start | bytes 49156
  80.4 4.4 %copy-start.34 = (f32[256,2,8]{0,2,1:T(8,128)S(1)}, f32[256,2,8]{0,2,1:T(8,128)}, u32[]{:S(2)}) copy-start(f32[256,2,8]{0,2,1:T(8,128)} %param.23) | copy-start | bytes 49156
  80.4 4.4 %copy-start.47 = (f32[2,8]{1,0:T(2,128)S(1)}, f32[2,8]{1,0:T(2,128)}, u32[]{:S(2)}) copy-start(f32[2,8]{1,0:T(2,128)} %copy-done.45) | copy-start | bytes 196
  80.4 4.4 %copy-start.66 = (f32[2,8]{1,0:T(2,128)S(1)}, f32[2,8]{1,0:T(2,128)}, u32[]{:S(2)}) copy-start(f32[2,8]{1,0:T(2,128)} %param.25) | copy-start | bytes 196
  80.8 5.2 %copy-start.14 = (bf16[256,2,8,64]{0,3,2,1:T(8,128)(2,1)S(1)}, bf16[256,2,8,64]{0,3,2,1:T(8,128)(2,1)}, u32[]{:S(2)}) copy-start(bf16[256,2,8,64]{0,3,2,1:T(8,128)(2,1)} %fusion.35) | copy-start | bytes 1572868
  81.1 6.1 %collective-permute-start.7 = (f32[3,2,640]{2,1,0:T(2,128)S(1)}, f32[3,2,640]{2,1,0:T(2,128)S(1)}, u32[]{:S(2)}, u32[]{:S(2)}) collective-permute-start(f32[3,2,640]{2,1,0:T(2,128)S(1)} %pad_maximum_fusion.9), channel_id=1, source_target_pairs={{2,0},{4,2},{6,4},{8,6},{10,8},{12,10},{14,12},{3,1},{5,3},{7,5},{... | collective-permute-start | bytes 46088 | tf_op jit(solution)/shard_map/ppermute | solution.py:12
  (35 other events, 56.2 us)

commit v13 on v12

--- a/solution.py
+++ b/solution.py
@@ -199,9 +199,14 @@
     back_x = returned[:, :, :channels]
     back_b = returned[:, :, channels : channels + state_size]
     back_c = returned[:, :, channels + state_size :]
-    grad_x = grad_x_ext[halo_rows:].at[length - halo_rows :].add(back_x).astype(jnp.bfloat16)
-    grad_b = grad_b_ext[halo_rows:].at[length - halo_rows :].add(back_b).astype(jnp.bfloat16)
-    grad_c = grad_c_ext[halo_rows:].at[length - halo_rows :].add(back_c).astype(jnp.bfloat16)
+    def settle(grad_ext, back):
+        body = grad_ext[halo_rows:length]
+        edge = grad_ext[length : length + halo_rows] + back
+        return jnp.concatenate([body, edge], 0).astype(jnp.bfloat16)
+
+    grad_x = settle(grad_x_ext, back_x)
+    grad_b = settle(grad_b_ext, back_b)
+    grad_c = settle(grad_c_ext, back_c)
     return (y_out, grad_x, grad_b, grad_c, grad_dt)
 
 

time: 94.4 us -> 105 us (1.11)
  the two profiles are of different devices: /device:TPU:26 before, /device:TPU:16 now
where the time goes in v13:
time: 105 us; the launch traced here: 104 us
  local copies, waits for them, and re-layouts  26.9 us (26%)
  matrix products  23 us (22%)
  starting transfers between devices  22.9 us (22%)
  other arithmetic  22.4 us (21%)
  waiting for transfers between devices  7.48 us (7%)
  between operations  1.91 us (2%)
    ppermute x6, starting transfers between devices, shift(): return lax.ppermute(packed, axis, pairs)  15.2 us
    dot_general x3, matrix products, ssd_mix(): jnp.einsum('ghts,sghp->tghp', mixing, x_half, preferred_element_type=jnp....  11.6 us
    ppermute x2, starting transfers between devices, from_behind(): return lax.ppermute(array, axis, pairs)  7.71 us
    ppermute x6, waiting for transfers between devices, shift(): return lax.ppermute(packed, axis, pairs)  7.48 us
    unnamed x160, local copies, waits for them, and re-layouts  6.39 us
    convert_element_type x1, other arithmetic, ssd_state(): weighted = (x_heads * tail_weight[..., None]).astype(jnp.bfloat16)  4.02 us
    dot_general x3, matrix products, ssd_state(): jnp.einsum('sgn,sgk->gnk', b_float, weighted.reshape(length, groups, chan...  3.54 us
    concatenate x3, other arithmetic, settle(): return jnp.concatenate([body, edge], 0).astype(jnp.bfloat16)  2.9 us
  transfers between devices with their start and end apart: 8, of which 3 were waited for; matrix products, arithmetic and copies ran while one was open for 20% of the time, Pallas kernels for 0%

profile of v13, /device:TPU:16, one launch (start us, length us, event | category | flops | bytes accessed | tf_op | source)
XLA Modules:
  0.0 104.5 jit_solution(1429619839443557736)
XLA Ops:
  0.6 0.8 slice.233
  1.6 0.8 slice.232
  3.3 3.4 %collective-permute-start = (bf16[3,2,640]{2,1,0:T(2,128)(2,1)S(1)}, bf16[3,2,640]{2,1,0:T(2,128)(2,1)S(1)}, u32[]{:S(2)}, u32[]{:S(2)}) collective-permute-start(bf16[3,2,640]{2,1,0:T(2,128)(2,1)S(1)} %pad_maximum_fusion.13), channel_id=1, source_target_pairs={{0,2},{2,4},{4,6},{6,8},{8,10},{10,12},{12,14},{1,3},{3,5},{5,7},{... | collective-permute-start | bytes 23048 | tf_op jit(solution)/shard_map/ppermute | solution.py:12
  7.4 0.9 fusion.69
  8.5 0.7 slice_bitcast_fusion.7
  9.3 0.8 fusion.104
  10.1 0.7 slice_bitcast_fusion.3
  14.1 1.1 %mul.550 = f32[256,2,8,64]{0,3,2,1:T(8,128)} broadcast(f32[256,2,8]{0,2,1:T(8,128)S(1)} %get-tuple-element.78), dimensions={0,1,2} | broadcast | bytes 1064960 | tf_op jit(solution)/shard_map/jvp()/mul | solution.py:118
  15.2 1.6 %copy.116 = f32[256,2,512]{2,1,0:T(2,128)S(1)} copy(f32[256,2,512]{0,2,1:T(8,128)} %bitcast.187) | data formatting | bytes 2097152 | tf_op jit(solution)/shard_map/jvp()/mul | solution.py:118
  17.2 0.9 multiply_convert_fusion.2
  18.1 4.0 %multiply_convert_fusion = (bf16[256,2,512]{2,1,0:T(2,128)(2,1)S(1)}, f32[256,2,512]{2,1,0:T(2,128)}, f32[256,2,512]{2,1,0:T(2,128)}) fusion(f32[256,2,512]{2,1,0:T(2,128)S(1)} %copy.116, bf16[256,2,512]{2,1,0:T(2,128)(2,1)S(1)} %copy-done.7, f32[2,512]{1,0:T(2,128)S(1)} %get-tuple-element.76, bf16[3,2,512]{2,1,0:T(2,128)(2,1)S(1)} %slice.295, ...), kind=kLoop, calls=%fused_computation.59 | loop fusion | flops 5767168 | bytes 4216832 | tf_op jit(solution)/shard_map/jvp()/convert_element_type | solution.py:118
  22.4 0.9 multiply_convert_fusion.3
  23.9 0.7 pad_maximum_fusion.3
  24.7 3.3 %collective-permute-start.4 = (bf16[2,72,512]{2,1,0:T(8,128)(2,1)}, bf16[2,72,512]{2,1,0:T(8,128)(2,1)S(1)}, u32[]{:S(2)}, u32[]{:S(2)}) collective-permute-start(bf16[2,72,512]{2,1,0:T(8,128)(2,1)} %get-tuple-element.73), channel_id=1, source_target_pairs={{2,0},{4,2},{6,4},{8,6},{10,8},{12,10},{14,12},{3,1},{5,3},{7,5},{... | collective-permute-start | bytes 442376 | tf_op jit(solution)/shard_map/ppermute | solution.py:27
  28.0 2.5 %collective-permute-start.1 = (bf16[2,72,512]{2,1,0:T(8,128)(2,1)}, bf16[2,72,512]{2,1,0:T(8,128)(2,1)}, u32[]{:S(2)}, u32[]{:S(2)}) collective-permute-start(bf16[2,72,512]{2,1,0:T(8,128)(2,1)} %get-tuple-element.72), channel_id=1, source_target_pairs={{0,2},{2,4},{4,6},{6,8},{8,10},{10,12},{12,14},{1,3},{3,5},{5,7},{... | collective-permute-start | bytes 442376 | tf_op jit(solution)/shard_map/ppermute | solution.py:27
  30.5 0.8 reshape.111
  31.3 1.3 %copy.118 = f32[256,2,512]{0,2,1:T(8,128)} copy(bf16[256,2,512]{2,1,0:T(2,128)(2,1)S(1)} %copy-done) | data formatting | bytes 1572864 | tf_op jit(solution)/shard_map/convert_element_type | solution.py:165
  32.6 1.2 %copy.119 = bf16[256,2,512]{0,2,1:T(8,128)(2,1)} copy(bf16[256,2,512]{2,1,0:T(2,128)(2,1)S(1)} %copy-done) | data formatting | bytes 1048576 | tf_op args[10]
  34.5 2.3 %copy.113 = f32[256,2,512]{0,2,1:T(8,128)} copy(f32[256,2,512]{2,1,0:T(2,128)} %get-tuple-element.59) | data formatting | bytes 2097152 | tf_op jit(solution)/shard_map/convert_element_type | solution.py:153
  36.8 1.0 convert_element_type.178
  38.0 2.4 %collective-permute-start.5 = (bf16[2,72,512]{2,1,0:T(8,128)(2,1)S(1)}, bf16[2,72,512]{2,1,0:T(8,128)(2,1)S(1)}, u32[]{:S(2)}, u32[]{:S(2)}) collective-permute-start(bf16[2,72,512]{2,1,0:T(8,128)(2,1)S(1)} %pad_maximum_fusion.6), channel_id=1, source_target_pairs={{4,0},{6,2},{8,4},{10,6},{12,8},{14,10},{5,1},{7,3},{9,5},{11,7},{... | collective-permute-start | bytes 442376 | tf_op jit(solution)/shard_map/ppermute | solution.py:27
  40.4 3.5 %collective-permute-start.2 = (bf16[2,72,512]{2,1,0:T(8,128)(2,1)S(1)}, bf16[2,72,512]{2,1,0:T(8,128)(2,1)S(1)}, u32[]{:S(2)}, u32[]{:S(2)}) collective-permute-start(bf16[2,72,512]{2,1,0:T(8,128)(2,1)S(1)} %pad_maximum_fusion.4), channel_id=1, source_target_pairs={{0,4},{2,6},{4,8},{6,10},{8,12},{10,14},{1,5},{3,7},{5,9},{7,11},{... | collective-permute-start | bytes 442376 | tf_op jit(solution)/shard_map/ppermute | solution.py:27
  43.9 1.1 %collective-permute-done.5 = bf16[2,72,512]{2,1,0:T(8,128)(2,1)S(1)} collective-permute-done((bf16[2,72,512]{2,1,0:T(8,128)(2,1)S(1)}, bf16[2,72,512]{2,1,0:T(8,128)(2,1)S(1)}, u32[]{:S(2)}, u32[]{:S(2)}) %collective-permute-start.5) | collective-permute-done | bytes 147488 | tf_op jit(solution)/shard_map/ppermute | solution.py:27
  45.1 2.4 %collective-permute-done.2 = bf16[2,72,512]{2,1,0:T(8,128)(2,1)S(1)} collective-permute-done((bf16[2,72,512]{2,1,0:T(8,128)(2,1)S(1)}, bf16[2,72,512]{2,1,0:T(8,128)(2,1)S(1)}, u32[]{:S(2)}, u32[]{:S(2)}) %collective-permute-start.2) | collective-permute-done | bytes 147488 | tf_op jit(solution)/shard_map/ppermute | solution.py:27
  47.8 2.0 %collective-permute-start.6 = (bf16[2,72,512]{2,1,0:T(8,128)(2,1)S(1)}, bf16[2,72,512]{2,1,0:T(8,128)(2,1)S(1)}, u32[]{:S(2)}, u32[]{:S(2)}) collective-permute-start(bf16[2,72,512]{2,1,0:T(8,128)(2,1)S(1)} %pad_maximum_fusion.7), channel_id=1, source_target_pairs={{8,0},{10,2},{12,4},{14,6},{9,1},{11,3},{13,5},{15,7},{24,16},{26,... | collective-permute-start | bytes 442376 | tf_op jit(solution)/shard_map/ppermute | solution.py:27
  49.8 1.5 %collective-permute-start.3 = (bf16[2,72,512]{2,1,0:T(8,128)(2,1)S(1)}, bf16[2,72,512]{2,1,0:T(8,128)(2,1)S(1)}, u32[]{:S(2)}, u32[]{:S(2)}) collective-permute-start(bf16[2,72,512]{2,1,0:T(8,128)(2,1)S(1)} %pad_maximum_fusion.5), channel_id=1, source_target_pairs={{0,8},{2,10},{4,12},{6,14},{1,9},{3,11},{5,13},{7,15},{16,24},{18,... | collective-permute-start | bytes 442376 | tf_op jit(solution)/shard_map/ppermute | solution.py:27
  51.3 1.1 %fusion.122 = f32[2,256,256]{2,1,0:T(8,128)} fusion(bf16[256,2,64]{0,2,1:T(8,128)(2,1)S(1)} %get-tuple-element.63, bf16[256,2,64]{0,2,1:T(8,128)(2,1)S(1)} %get-tuple-element.61), kind=kOutput, calls=%fused_computation.210 | convolution fusion | flops 16777216 | bytes 655360 | tf_op jit(solution)/shard_map/jvp(tgn,sgn->gts)/dot_general | solution.py:105
  53.8 4.0 %collective-permute-done.3 = bf16[2,72,512]{2,1,0:T(8,128)(2,1)S(1)} collective-permute-done((bf16[2,72,512]{2,1,0:T(8,128)(2,1)S(1)}, bf16[2,72,512]{2,1,0:T(8,128)(2,1)S(1)}, u32[]{:S(2)}, u32[]{:S(2)}) %collective-permute-start.3) | collective-permute-done | bytes 147488 | tf_op jit(solution)/shard_map/ppermute | solution.py:27
  57.8 0.7 multiply_reduce_fusion.2
  59.3 1.6 %fusion.43 = f32[2,512,256]{2,1,0:T(8,128)} fusion(f32[2,64,512]{2,1,0:T(8,128)S(1)} %get-tuple-element.56, bf16[256,2,64]{0,2,1:T(8,128)(2,1)S(1)} %get-tuple-element.61), kind=kOutput, calls=%fused_computation.31 | convolution fusion | flops 201850880 | bytes 1376256 | tf_op jit(solution)/shard_map/transpose(jvp(sgn,sgk->gnk))/dot_general | solution.py:119
  60.9 1.5 %copy.147 = f32[2,512,256]{1,0,2:T(2,128)S(1)} copy(f32[2,512,256]{2,1,0:T(8,128)} %fusion.43) | data formatting | bytes 2097152
  62.4 1.4 %copy.131 = f32[256,2,512]{0,2,1:T(8,128)} copy(f32[256,2,512]{2,1,0:T(2,128)S(1)} %bitcast.179) | data formatting | bytes 2097152 | tf_op jit(solution)/shard_map/transpose(jvp())/convert_element_type | solution.py:118
  63.8 1.8 %multiply_reduce_fusion.1 = f32[256,2,8]{0,2,1:T(8,128)S(1)} fusion(f32[256,2,512]{0,2,1:T(8,128)} %copy.131, f32[256,2,512]{0,2,1:T(8,128)} %copy.113), kind=kLoop, calls=%fused_computation.56 | loop fusion | flops 520192 | bytes 2113536 | tf_op jit(solution)/shard_map/transpose(jvp())/reduce_sum | solution.py:118
  65.7 1.6 %multiply_reduce_fusion = (f32[256,2,8]{0,2,1:T(8,128)S(1)}, f32[2,512,256]{2,1,0:T(8,128)}) fusion(f32[256,2,512]{0,2,1:T(8,128)S(1)} %copy-done.2, f32[2,64,512]{2,1,0:T(8,128)S(1)} %get-tuple-element.57, bf16[256,2,64]{0,2,1:T(8,128)(2,1)S(1)} %get-tuple-element.63), kind=kOutput, calls=%fused_computation.55 | convolution fusion | flops 201846784 | bytes 2441216 | tf_op jit(solution)/shard_map/jvp(tgn,gnk->tgk)/dot_general | solution.py:130
  67.3 1.3 %fusion.105 = (f32[2,8]{1,0:T(2,128)}, f32[2,8,256]{2,1,0:T(8,128)S(1)}, f32[256,2,8]{0,2,1:T(8,128)}) fusion(f32[256,2,8]{0,2,1:T(8,128)S(1)} %multiply_reduce_fusion.1, f32[2,8]{1,0:T(2,128)S(1)} %copy-done.39, f32[256,16]{0,1:S(1)} %fusion.69, f32[256,2,8]{0,2,1:T(8,128)S(1)} %copy-done.26, f32[2,8]{1,0:T(2,128)S(1)} %copy-done.62, ...), kind=kLoop, calls=%fused_computation.163 | loop fusion | flops 49136 | bytes 98496 | tf_op jit(solution)/shard_map/transpose(jvp())/reduce_sum | solution.py:117
  68.7 4.9 %fusion.18 = (f32[2,8,256]{2,1,0:T(8,128)}, f32[2,8,256]{2,1,0:T(8,128)}, f32[2,8,256]{2,1,0:T(8,128)}, f32[2,256,256]{2,1,0:T(8,128)S(1)}) fusion(f32[2,8,256]{2,1,0:T(8,128)S(1)} %bitcast.195, f32[2,8,256]{2,1,0:T(8,128)S(1)} %get-tuple-element.70, f32[2,256,256]{2,1,0:T(8,128)S(1)} %copy-done.8, pred[256,256]{1,0:T(8,128)(4,1)S(1)} %copy-done.24, ...), kind=kOutput, calls=%fused_computation.21 | convolution fusion | flops 156356608 | bytes 2768896 | tf_op jit(solution)/shard_map/transpose(jvp(ghts,sghp->tghp))/dot_general | solution.py:107
  74.0 1.0 convolution_bitcast_fusion.1
  75.0 1.2 %fusion.48 = f32[256,2,64]{0,2,1:T(8,128)S(1)} fusion(f32[2,256,64]{1,2,0:T(8,128)S(1)} %fusion.123, f32[2,64,512]{2,1,0:T(8,128)S(1)} %get-tuple-element.57, f32[2,512,256]{1,0,2:T(2,128)S(1)} %bitcast.181, f32[256,2,64]{0,2,1:T(8,128)S(1)} %copy-done.13), kind=kOutput, calls=%fused_computation.39 | convolution fusion | flops 201687040 | bytes 1703936 | tf_op jit(solution)/shard_map/transpose(jvp(tgn,gnk->tgk))/dot_general | solution.py:130
  77.3 1.7 %fusion.51 = f32[256,2,64]{0,2,1:T(8,128)S(1)} fusion(f32[256,2,64]{0,2,1:T(8,128)} %convolution_bitcast_fusion.1, f32[2,64,512]{2,1,0:T(8,128)} %copy-done.6, bf16[256,2,512]{2,1,0:T(2,128)(2,1)} %copy-done.5, f32[256,2,64]{0,2,1:T(8,128)S(1)} %copy-done.17), kind=kOutput, calls=%fused_computation.42 | convolution fusion | flops 201687040 | bytes 1179648 | tf_op jit(solution)/shard_map/transpose(jvp(sgn,sgk->gnk))/dot_general | solution.py:119
  80.1 4.2 %fusion.28 = bf16[256,2,8,64]{0,3,2,1:T(8,128)(2,1)} fusion(f32[2,8,256]{2,1,0:T(8,128)} %copy-done.41, f32[2,8,256]{2,1,0:T(8,128)S(1)} %bitcast.196, f32[2,256,256]{2,1,0:T(8,128)} %fusion.122, pred[256,256]{1,0:T(8,128)(4,1)} %iota_compare_fusion, f32[256,2,8,64]{0,3,2,1:T(8,128)} %bitcast.189, f32[256,2,8,64]{0,3,2,1:T(8,128)} %bitcast.184, ...), kind=kOutput, calls=%fused_computation.25 | convolution fusion | flops 142082048 | bytes 3260480 | tf_op jit(solution)/shard_map/jvp(ghts,sghp->tghp)/dot_general | solution.py:107
  84.4 2.4 %fusion.40 = f32[256,2,8,64]{0,3,2,1:T(8,128)} fusion(bf16[2,8,64,256]{3,2,1,0:T(8,128)(2,1)S(1)} %bitcast.192, f32[2,8,256]{2,1,0:T(8,128)S(1)} %copy-done.42, f32[2,8,256]{2,1,0:T(8,128)S(1)} %bitcast.197, f32[2,256,256]{2,1,0:T(8,128)S(1)} %copy-done.9, pred[256,256]{1,0:T(8,128)(4,1)S(1)} %copy-done.25, f32[256,2,8,64]{0,3,2,1:T(8,128)S(1)} %bitcast.183, ...), kind=kOutput, calls=%fused_computation.29 | convolution fusion | flops 141557760 | bytes 3244096 | tf_op jit(solution)/shard_map/transpose(jvp(ghts,sghp->tghp))/dot_general | solution.py:107
  86.8 2.4 %copy.124 = f32[256,2,512]{2,1,0:T(2,128)} copy(f32[256,2,512]{0,2,1:T(8,128)} %bitcast.190) | data formatting | bytes 2097152 | tf_op jit(solution)/shard_map/transpose(jvp())/reshape | solution.py:95
  89.2 2.7 %multiply_multiply_fusion = f32[256,2,512]{2,1,0:T(2,128)S(1)} fusion(f32[256,2,512]{2,1,0:T(2,128)S(1)} %copy-done.1, f32[256,2,512]{2,1,0:T(2,128)} %copy.124, f32[256,2,512]{2,1,0:T(2,128)S(1)} %copy.116, f32[2,512,256]{1,0,2:T(2,128)S(1)} %copy.147), kind=kLoop, calls=%fused_computation.57 | loop fusion | flops 3145728 | bytes 5242880 | tf_op jit(solution)/shard_map/mul | solution.py:68
  92.0 1.3 %multiply_add_fusion = f32[259,2,512]{2,1,0:T(2,128)S(1)} fusion(f32[256,2,512]{2,1,0:T(2,128)S(1)} %multiply_multiply_fusion, f32[2,512]{1,0:T(2,128)S(1)} %copy-done.33, f32[2,512]{1,0:T(2,128)S(1)} %copy-done.35, f32[2,512]{1,0:T(2,128)S(1)} %copy-done.31, f32[2,512]{1,0:T(2,128)S(1)} %copy-done.29), kind=kLoop, calls=%fused_computation.51 | loop fusion | flops 1856512 | bytes 2125824 | tf_op jit(solution)/shard_map/add | solution.py:76
  93.4 4.3 %collective-permute-start.7 = (f32[3,2,640]{2,1,0:T(2,128)S(1)}, f32[3,2,640]{2,1,0:T(2,128)S(1)}, u32[]{:S(2)}, u32[]{:S(2)}) collective-permute-start(f32[3,2,640]{2,1,0:T(2,128)S(1)} %pad_maximum_fusion.12), channel_id=1, source_target_pairs={{2,0},{4,2},{6,4},{8,6},{10,8},{12,10},{14,12},{3,1},{5,3},{7,5},{... | collective-permute-start | bytes 46088 | tf_op jit(solution)/shard_map/ppermute | solution.py:12
  98.6 0.9 fusion.55
  100.0 1.2 %copy.134 = bf16[256,2,512]{2,1,0:T(2,128)(2,1)} copy(bf16[256,2,512]{0,2,1:T(8,128)(2,1)S(1)} %bitcast.193) | data formatting | bytes 1048576
  101.6 1.5 %pad_maximum_fusion.1 = bf16[256,2,512]{2,1,0:T(2,128)(2,1)} fusion(bf16[3,2,512]{2,1,0:T(2,128)(2,1)S(1)} %fusion.106, bf16[253,2,512]{2,1,0:T(2,128)(2,1)S(1)} %slice.486), kind=kLoop, calls=%fused_computation.70 | loop fusion | flops 262144 | bytes 1048576 | tf_op jit(solution)/shard_map/concatenate | solution.py:205
  (224 shorter events, 15.2 us)
Async XLA Ops:
  3.3 13.5 %collective-permute-start = (bf16[3,2,640]{2,1,0:T(2,128)(2,1)S(1)}, bf16[3,2,640]{2,1,0:T(2,128)(2,1)S(1)}, u32[]{:S(2)}, u32[]{:S(2)}) collective-permute-start(bf16[3,2,640]{2,1,0:T(2,128)(2,1)S(1)} %pad_maximum_fusion.13), channel_id=1, source_target_pairs={{0,2},{2,4},{4,6},{6,8},{8,10},{10,12},{12,14},{1,3},{3,5},{5,7},{... | collective-permute-start | bytes 23048 | tf_op jit(solution)/shard_map/ppermute | solution.py:12
  8.5 4.8 %copy-start.38 = (f32[2,8]{1,0:T(2,128)}, f32[2,8]{1,0:T(2,128)S(1)}, u32[]{:S(2)}) copy-start(f32[2,8]{1,0:T(2,128)S(1)} %slice_reduce_fusion) | copy-start | bytes 196
  9.3 7.8 %copy-start.45 = (f32[2,64]{1,0:T(2,128)}, f32[2,64]{1,0:T(2,128)S(1)}, u32[]{:S(2)}) copy-start(f32[2,64]{1,0:T(2,128)S(1)} %get-tuple-element.90) | copy-start | bytes 1540
  9.3 7.8 %copy-start.47 = (f32[2,64]{1,0:T(2,128)}, f32[2,64]{1,0:T(2,128)S(1)}, u32[]{:S(2)}) copy-start(f32[2,64]{1,0:T(2,128)S(1)} %get-tuple-element.91) | copy-start | bytes 1540
  9.3 7.9 %copy-start.49 = (f32[2,64]{1,0:T(2,128)}, f32[2,64]{1,0:T(2,128)S(1)}, u32[]{:S(2)}) copy-start(f32[2,64]{1,0:T(2,128)S(1)} %get-tuple-element.92) | copy-start | bytes 1540
  9.3 7.9 %copy-start.51 = (f32[2,64]{1,0:T(2,128)}, f32[2,64]{1,0:T(2,128)S(1)}, u32[]{:S(2)}) copy-start(f32[2,64]{1,0:T(2,128)S(1)} %get-tuple-element.93) | copy-start | bytes 1540
  10.9 7.2 %copy-start.28 = (f32[2,512]{1,0:T(2,128)}, f32[2,512]{1,0:T(2,128)S(1)}, u32[]{:S(2)}) copy-start(f32[2,512]{1,0:T(2,128)S(1)} %get-tuple-element.74) | copy-start | bytes 12292
  10.9 7.2 %copy-start.30 = (f32[2,512]{1,0:T(2,128)}, f32[2,512]{1,0:T(2,128)S(1)}, u32[]{:S(2)}) copy-start(f32[2,512]{1,0:T(2,128)S(1)} %get-tuple-element.75) | copy-start | bytes 12292
  10.9 7.2 %copy-start.32 = (f32[2,512]{1,0:T(2,128)}, f32[2,512]{1,0:T(2,128)S(1)}, u32[]{:S(2)}) copy-start(f32[2,512]{1,0:T(2,128)S(1)} %get-tuple-element.76) | copy-start | bytes 12292
  10.9 7.2 %copy-start.34 = (f32[2,512]{1,0:T(2,128)}, f32[2,512]{1,0:T(2,128)S(1)}, u32[]{:S(2)}) copy-start(f32[2,512]{1,0:T(2,128)S(1)} %get-tuple-element.77) | copy-start | bytes 12292
  15.2 2.9 %copy-start.7 = (bf16[256,2,512]{2,1,0:T(2,128)(2,1)S(1)}, bf16[256,2,512]{2,1,0:T(2,128)(2,1)}, u32[]{:S(2)}) copy-start(bf16[256,2,512]{2,1,0:T(2,128)(2,1)} %param.14) | copy-start | bytes 1572868
  18.1 4.3 %copy-start.16 = (bf16[256,2,64]{0,2,1:T(8,128)(2,1)S(1)}, bf16[256,2,64]{0,2,1:T(8,128)(2,1)}, u32[]{:S(2)}) copy-start(bf16[256,2,64]{0,2,1:T(8,128)(2,1)} %param.16) | copy-start | bytes 196612
  18.1 4.3 %copy-start.53 = (f32[2,64]{1,0:T(2,128)S(1)}, f32[2,64]{1,0:T(2,128)}, u32[]{:S(2)}) copy-start(f32[2,64]{1,0:T(2,128)} %get-tuple-element.94) | copy-start | bytes 1540
  18.1 4.3 %copy-start.55 = (f32[2,64]{1,0:T(2,128)S(1)}, f32[2,64]{1,0:T(2,128)}, u32[]{:S(2)}) copy-start(f32[2,64]{1,0:T(2,128)} %get-tuple-element.95) | copy-start | bytes 1540
  18.1 4.3 %copy-start.57 = (f32[2,64]{1,0:T(2,128)S(1)}, f32[2,64]{1,0:T(2,128)}, u32[]{:S(2)}) copy-start(f32[2,64]{1,0:T(2,128)} %get-tuple-element.96) | copy-start | bytes 1540
  18.1 4.3 %copy-start.59 = (f32[2,64]{1,0:T(2,128)S(1)}, f32[2,64]{1,0:T(2,128)}, u32[]{:S(2)}) copy-start(f32[2,64]{1,0:T(2,128)} %get-tuple-element.97) | copy-start | bytes 1540
  24.7 12.1 %collective-permute-start.4 = (bf16[2,72,512]{2,1,0:T(8,128)(2,1)}, bf16[2,72,512]{2,1,0:T(8,128)(2,1)S(1)}, u32[]{:S(2)}, u32[]{:S(2)}) collective-permute-start(bf16[2,72,512]{2,1,0:T(8,128)(2,1)} %get-tuple-element.73), channel_id=1, source_target_pairs={{2,0},{4,2},{6,4},{8,6},{10,8},{12,10},{14,12},{3,1},{5,3},{7,5},{... | collective-permute-start | bytes 442376 | tf_op jit(solution)/shard_map/ppermute | solution.py:27
  28.0 8.8 %collective-permute-start.1 = (bf16[2,72,512]{2,1,0:T(8,128)(2,1)}, bf16[2,72,512]{2,1,0:T(8,128)(2,1)}, u32[]{:S(2)}, u32[]{:S(2)}) collective-permute-start(bf16[2,72,512]{2,1,0:T(8,128)(2,1)} %get-tuple-element.72), channel_id=1, source_target_pairs={{0,2},{2,4},{4,6},{6,8},{8,10},{10,12},{12,14},{1,3},{3,5},{5,7},{... | collective-permute-start | bytes 442376 | tf_op jit(solution)/shard_map/ppermute | solution.py:27
  34.5 3.3 %copy-start.22 = (f32[2,512]{1,0:T(2,128)S(1)}, f32[2,512]{1,0:T(2,128)}, u32[]{:S(2)}) copy-start(f32[2,512]{1,0:T(2,128)} %copy-done.21) | copy-start | bytes 12292
  38.0 7.0 %collective-permute-start.5 = (bf16[2,72,512]{2,1,0:T(8,128)(2,1)S(1)}, bf16[2,72,512]{2,1,0:T(8,128)(2,1)S(1)}, u32[]{:S(2)}, u32[]{:S(2)}) collective-permute-start(bf16[2,72,512]{2,1,0:T(8,128)(2,1)S(1)} %pad_maximum_fusion.6), channel_id=1, source_target_pairs={{4,0},{6,2},{8,4},{10,6},{12,8},{14,10},{5,1},{7,3},{9,5},{11,7},{... | collective-permute-start | bytes 442376 | tf_op jit(solution)/shard_map/ppermute | solution.py:27
  40.4 7.0 %collective-permute-start.2 = (bf16[2,72,512]{2,1,0:T(8,128)(2,1)S(1)}, bf16[2,72,512]{2,1,0:T(8,128)(2,1)S(1)}, u32[]{:S(2)}, u32[]{:S(2)}) collective-permute-start(bf16[2,72,512]{2,1,0:T(8,128)(2,1)S(1)} %pad_maximum_fusion.4), channel_id=1, source_target_pairs={{0,4},{2,6},{4,8},{6,10},{8,12},{10,14},{1,5},{3,7},{5,9},{7,11},{... | collective-permute-start | bytes 442376 | tf_op jit(solution)/shard_map/ppermute | solution.py:27
  47.8 6.1 %collective-permute-start.6 = (bf16[2,72,512]{2,1,0:T(8,128)(2,1)S(1)}, bf16[2,72,512]{2,1,0:T(8,128)(2,1)S(1)}, u32[]{:S(2)}, u32[]{:S(2)}) collective-permute-start(bf16[2,72,512]{2,1,0:T(8,128)(2,1)S(1)} %pad_maximum_fusion.7), channel_id=1, source_target_pairs={{8,0},{10,2},{12,4},{14,6},{9,1},{11,3},{13,5},{15,7},{24,16},{26,... | collective-permute-start | bytes 442376 | tf_op jit(solution)/shard_map/ppermute | solution.py:27
  49.8 8.0 %collective-permute-start.3 = (bf16[2,72,512]{2,1,0:T(8,128)(2,1)S(1)}, bf16[2,72,512]{2,1,0:T(8,128)(2,1)S(1)}, u32[]{:S(2)}, u32[]{:S(2)}) collective-permute-start(bf16[2,72,512]{2,1,0:T(8,128)(2,1)S(1)} %pad_maximum_fusion.5), channel_id=1, source_target_pairs={{0,8},{2,10},{4,12},{6,14},{1,9},{3,11},{5,13},{7,15},{16,24},{18,... | collective-permute-start | bytes 442376 | tf_op jit(solution)/shard_map/ppermute | solution.py:27
  65.7 3.0 %copy-start.4 = (f32[256,2,512]{0,2,1:T(8,128)S(1)}, f32[256,2,512]{0,2,1:T(8,128)}, u32[]{:S(2)}) copy-start(f32[256,2,512]{0,2,1:T(8,128)} %copy.113) | copy-start | bytes 3145732
  65.7 3.0 %copy-start.8 = (f32[2,256,256]{2,1,0:T(8,128)S(1)}, f32[2,256,256]{2,1,0:T(8,128)}, u32[]{:S(2)}) copy-start(f32[2,256,256]{2,1,0:T(8,128)} %fusion.122) | copy-start | bytes 1572868
  65.7 3.0 %copy-start.10 = (bf16[256,2,512]{0,2,1:T(8,128)(2,1)S(1)}, bf16[256,2,512]{0,2,1:T(8,128)(2,1)}, u32[]{:S(2)}) copy-start(bf16[256,2,512]{0,2,1:T(8,128)(2,1)} %copy.119) | copy-start | bytes 1572868
  65.7 2.9 %copy-start.24 = (pred[256,256]{1,0:T(8,128)(4,1)S(1)}, pred[256,256]{1,0:T(8,128)(4,1)}, u32[]{:S(2)}) copy-start(pred[256,256]{1,0:T(8,128)(4,1)} %iota_compare_fusion) | copy-start | bytes 196612
  68.6 5.0 %copy-start.41 = (f32[2,8,256]{2,1,0:T(8,128)}, f32[2,8,256]{2,1,0:T(8,128)S(1)}, u32[]{:S(2)}) copy-start(f32[2,8,256]{2,1,0:T(8,128)S(1)} %get-tuple-element.70) | copy-start | bytes 49156
  76.3 2.8 %copy-start.46 = (f32[2,64]{1,0:T(2,128)S(1)}, f32[2,64]{1,0:T(2,128)}, u32[]{:S(2)}) copy-start(f32[2,64]{1,0:T(2,128)} %copy-done.45) | copy-start | bytes 1540
  80.0 4.3 %copy-start.3 = (f32[256,2,512]{0,2,1:T(8,128)S(1)}, f32[256,2,512]{0,2,1:T(8,128)}, u32[]{:S(2)}) copy-start(f32[256,2,512]{0,2,1:T(8,128)} %copy.118) | copy-start | bytes 3145732
  80.0 4.3 %copy-start.9 = (f32[2,256,256]{2,1,0:T(8,128)S(1)}, f32[2,256,256]{2,1,0:T(8,128)}, u32[]{:S(2)}) copy-start(f32[2,256,256]{2,1,0:T(8,128)} %fusion.122) | copy-start | bytes 1572868
  80.1 4.3 %copy-start.11 = (bf16[256,2,512]{0,2,1:T(8,128)(2,1)S(1)}, bf16[256,2,512]{0,2,1:T(8,128)(2,1)}, u32[]{:S(2)}) copy-start(bf16[256,2,512]{0,2,1:T(8,128)(2,1)} %copy.119) | copy-start | bytes 1572868
  80.1 4.3 %copy-start.25 = (pred[256,256]{1,0:T(8,128)(4,1)S(1)}, pred[256,256]{1,0:T(8,128)(4,1)}, u32[]{:S(2)}) copy-start(pred[256,256]{1,0:T(8,128)(4,1)} %iota_compare_fusion) | copy-start | bytes 196612
  80.1 4.3 %copy-start.42 = (f32[2,8,256]{2,1,0:T(8,128)S(1)}, f32[2,8,256]{2,1,0:T(8,128)}, u32[]{:S(2)}) copy-start(f32[2,8,256]{2,1,0:T(8,128)} %copy-done.41) | copy-start | bytes 49156
  80.1 4.3 %copy-start.68 = (f32[2,8]{1,0:T(2,128)S(1)}, f32[2,8]{1,0:T(2,128)}, u32[]{:S(2)}) copy-start(f32[2,8]{1,0:T(2,128)} %param.20) | copy-start | bytes 196
  91.9 5.9 %copy-start.64 = (f32[2,8]{1,0:T(2,128)S(1)}, f32[2,8]{1,0:T(2,128)}, u32[]{:S(2)}) copy-start(f32[2,8]{1,0:T(2,128)} %get-tuple-element.69) | copy-start | bytes 196
  91.9 6.0 %copy-start.37 = (f32[2,512]{1,0:T(2,128)S(1)}, f32[2,512]{1,0:T(2,128)}, u32[]{:S(2)}) copy-start(f32[2,512]{1,0:T(2,128)} %get-tuple-element.55) | copy-start | bytes 12292
  91.9 6.2 %copy-start.36 = (f32[256,2,8]{0,2,1:T(8,128)S(1)}, f32[256,2,8]{0,2,1:T(8,128)}, u32[]{:S(2)}) copy-start(f32[256,2,8]{0,2,1:T(8,128)} %get-tuple-element.71) | copy-start | bytes 49156
  91.9 6.3 %copy-start.67 = (f32[2,8]{1,0:T(2,128)S(1)}, f32[2,8]{1,0:T(2,128)}, u32[]{:S(2)}) copy-start(f32[2,8]{1,0:T(2,128)} %copy-done.66) | copy-start | bytes 196
  91.9 6.3 %copy-start.69 = (f32[2,8,256]{2,1,0:T(8,128)S(1)}, f32[2,8,256]{2,1,0:T(8,128)}, u32[]{:S(2)}) copy-start(f32[2,8,256]{2,1,0:T(8,128)} %get-tuple-element.51) | copy-start | bytes 49156
  92.0 6.3 %copy-start.70 = (f32[2,8,256]{2,1,0:T(8,128)S(1)}, f32[2,8,256]{2,1,0:T(8,128)}, u32[]{:S(2)}) copy-start(f32[2,8,256]{2,1,0:T(8,128)} %get-tuple-element.52) | copy-start | bytes 49156
  92.0 6.3 %copy-start.71 = (f32[2,8,256]{2,1,0:T(8,128)S(1)}, f32[2,8,256]{2,1,0:T(8,128)}, u32[]{:S(2)}) copy-start(f32[2,8,256]{2,1,0:T(8,128)} %get-tuple-element.53) | copy-start | bytes 49156
  92.0 6.6 %copy-start.20 = (f32[256,2,8]{0,2,1:T(8,128)S(1)}, f32[256,2,8]{0,2,1:T(8,128)}, u32[]{:S(2)}) copy-start(f32[256,2,8]{0,2,1:T(8,128)} %copy-done.19) | copy-start | bytes 49156
  92.0 6.6 %copy-start.27 = (f32[256,2,8]{0,2,1:T(8,128)S(1)}, f32[256,2,8]{0,2,1:T(8,128)}, u32[]{:S(2)}) copy-start(f32[256,2,8]{0,2,1:T(8,128)} %param.17) | copy-start | bytes 49156
  92.0 6.6 %copy-start.40 = (f32[2,8]{1,0:T(2,128)S(1)}, f32[2,8]{1,0:T(2,128)}, u32[]{:S(2)}) copy-start(f32[2,8]{1,0:T(2,128)} %copy-done.38) | copy-start | bytes 196
  92.0 6.6 %copy-start.63 = (f32[2,8]{1,0:T(2,128)S(1)}, f32[2,8]{1,0:T(2,128)}, u32[]{:S(2)}) copy-start(f32[2,8]{1,0:T(2,128)} %param.19) | copy-start | bytes 196
  93.3 6.7 %copy-start.12 = (bf16[256,2,8,64]{0,3,2,1:T(8,128)(2,1)S(1)}, bf16[256,2,8,64]{0,3,2,1:T(8,128)(2,1)}, u32[]{:S(2)}) copy-start(bf16[256,2,8,64]{0,3,2,1:T(8,128)(2,1)} %fusion.28) | copy-start | bytes 1572868
  93.4 7.8 %collective-permute-start.7 = (f32[3,2,640]{2,1,0:T(2,128)S(1)}, f32[3,2,640]{2,1,0:T(2,128)S(1)}, u32[]{:S(2)}, u32[]{:S(2)}) collective-permute-start(f32[3,2,640]{2,1,0:T(2,128)S(1)} %pad_maximum_fusion.12), channel_id=1, source_target_pairs={{2,0},{4,2},{6,4},{8,6},{10,8},{12,10},{14,12},{3,1},{5,3},{7,5},{... | collective-permute-start | bytes 46088 | tf_op jit(solution)/shard_map/ppermute | solution.py:12
  (32 other events, 59.6 us)

commit v14 on v12

--- a/solution.py
+++ b/solution.py
@@ -14,42 +14,39 @@
 
 def scanned_pair(decay, forward_state, backward_state, axis):
     count = lax.axis_size(axis)
+    place = lax.axis_index(axis)
     groups, rows, lanes = forward_state.shape
     pad_rows = 8
 
-    def pack(decay_part, state_part):
-        return jnp.concatenate(
-            [state_part, jnp.broadcast_to(decay_part[:, None, :], (groups, pad_rows, lanes))], 1
+    def join(earlier, later):
+        return (earlier[0] * later[0], later[0][:, None, :] * earlier[1] + later[1])
+
+    def pick(flag, when_true, when_false):
+        return jax.tree.map(lambda a, b: a * flag + b * (1.0 - flag), when_true, when_false)
+
+    ones = jnp.ones_like(decay)
+    zeros = jnp.zeros_like(forward_state)
+    front = (decay, forward_state)
+    back = (decay, backward_state)
+    before = (ones, zeros)
+    after = (ones, zeros)
+    bit = 1
+    while bit < count:
+        upper = ((place // bit) % 2).astype(jnp.float32)
+        packed = jnp.concatenate(
+            [front[1], back[1], jnp.broadcast_to(front[0][:, None, :], (groups, pad_rows, lanes))], 1
         ).astype(jnp.bfloat16)
-
-    def shift(packed, by, sign):
-        pairs = [(i, i + sign * by) for i in range(count) if 0 <= i + sign * by < count]
-        return lax.ppermute(packed, axis, pairs)
-
-    def unpack(got):
-        got = got.astype(jnp.float32)
-        return got[:, rows, :], got[:, :rows, :]
-
-    def fold(window, got_decay, got_state):
-        before_decay, before_state, upto_decay, upto_state = window
-        return (
-            before_decay * got_decay,
-            before_decay[:, None, :] * got_state + before_state,
-            upto_decay * got_decay,
-            upto_decay[:, None, :] * got_state + upto_state,
-        )
-
-    windows = [
-        (jnp.ones_like(decay), jnp.zeros_like(state), decay, state)
-        for state in (forward_state, backward_state)
-    ]
-    by = 1
-    while by < count:
-        sent = [pack(w[2], w[3]) for w in windows]
-        got = [shift(s, by, sign) for s, sign in zip(sent, (1, -1))]
-        windows = [fold(w, *unpack(g)) for w, g in zip(windows, got)]
-        by *= 2
-    return windows[0][1], windows[1][1]
+        pairs = [(i, i ^ bit) for i in range(count)]
+        other = lax.ppermute(packed, axis, pairs).astype(jnp.float32)
+        other_decay = other[:, 2 * rows, :]
+        other_front = (other_decay, other[:, :rows, :])
+        other_back = (other_decay, other[:, rows : 2 * rows, :])
+        before = pick(upper, join(other_front, before), before)
+        after = pick(upper, after, join(other_back, after))
+        front = pick(upper, join(other_front, front), join(front, other_front))
+        back = pick(upper, join(back, other_back), join(other_back, back))
+        bit *= 2
+    return before[1], after[1]
 
 
 def conv_forward(extended, weight):

time: 94.4 us -> 99.9 us (1.058)
  the two profiles are of different devices: /device:TPU:26 before, /device:TPU:0 now
where the time goes in v14:
time: 99.9 us; the launch traced here: 99 us
  local copies, waits for them, and re-layouts  24.1 us (24%)
  other arithmetic  20.8 us (21%)
  matrix products  20.3 us (20%)
  waiting for transfers between devices  19.5 us (20%)
  starting transfers between devices  12.5 us (13%)
  between operations  1.71 us (2%)
    ppermute x3, waiting for transfers between devices, scanned_pair(): other = lax.ppermute(packed, axis, pairs).astype(jnp.float32)  18.2 us
    dot_general x3, matrix products, ssd_mix(): jnp.einsum('ghts,sghp->tghp', mixing, x_half, preferred_element_type=jnp....  9.94 us
    unnamed x149, local copies, waits for them, and re-layouts  8.3 us
    ppermute x3, starting transfers between devices, scanned_pair(): other = lax.ppermute(packed, axis, pairs).astype(jnp.float32)  6.35 us
    ppermute x2, starting transfers between devices, from_behind(): return lax.ppermute(array, axis, pairs)  6.13 us
    add x3, other arithmetic, conv_backward(): result = result + weight[tap_index] * padded[offset:offset + ext_len]  4.14 us
    dot_general x3, matrix products, ssd_mix(): scores = jnp.einsum('tgn,sgn->gts', c_float, b_float, precision=HIGH)  3.98 us
    mul x3, local copies, waits for them, and re-layouts, conv_forward(): running = weight[0] * extended[0:length].astype(jnp.float32)  2.69 us
  transfers between devices with their start and end apart: 5, of which 4 were waited for; matrix products, arithmetic and copies ran while one was open for 14% of the time, Pallas kernels for 0%

profile of v14, /device:TPU:0, one launch (start us, length us, event | category | flops | bytes accessed | tf_op | source)
XLA Modules:
  0.0 99.0 jit_solution(9939589437892199417)
XLA Ops:
  0.6 0.7 slice.282
  1.3 0.8 slice.283
  2.3 0.8 slice.284
  3.3 0.9 copy.68
  4.2 4.8 %collective-permute-start = (bf16[3,2,640]{0,2,1:T(8,128)(2,1)}, bf16[3,2,640]{0,2,1:T(8,128)(2,1)S(1)}, u32[]{:S(2)}, u32[]{:S(2)}) collective-permute-start(bf16[3,2,640]{0,2,1:T(8,128)(2,1)} %copy.68), channel_id=1, source_target_pairs={{0,2},{2,4},{4,6},{6,8},{8,10},{10,12},{12,14},{1,3},{3,5},{5,7},{... | collective-permute-start | bytes 23048 | tf_op jit(solution)/shard_map/ppermute | solution.py:12
  9.1 0.7 neg.30
  9.8 1.3 %slice_bitcast_fusion.7 = (f32[2,64]{1,0:T(2,128)}, f32[2,64]{1,0:T(2,128)}, f32[2,64]{1,0:T(2,128)}, f32[2,64]{1,0:T(2,128)}) fusion(f32[4,2,64]{2,1,0:T(2,128)} %param.28), kind=kLoop, calls=%fused_computation.199 | loop fusion | bytes 4096 | tf_op jit(solution)/shard_map/mul | solution.py:55
  11.1 0.9 fusion.83
  12.3 1.4 %slice_bitcast_fusion.3 = (f32[2,512]{1,0:T(2,128)}, f32[2,512]{1,0:T(2,128)}, f32[2,512]{1,0:T(2,128)}, f32[2,512]{1,0:T(2,128)}) fusion(f32[4,2,512]{2,1,0:T(2,128)} %param.27), kind=kLoop, calls=%fused_computation.192 | loop fusion | bytes 32768 | tf_op jit(solution)/shard_map/mul | solution.py:55
  13.6 0.8 fusion.114
  17.8 2.2 %multiply_convert_fusion.1 = (bf16[256,2,64]{0,2,1:T(8,128)(2,1)S(1)}, f32[256,2,64]{0,2,1:T(8,128)}, bf16[256,2,64]{0,2,1:T(8,128)(2,1)S(1)}, f32[256,2,64]{0,2,1:T(8,128)}) fusion(bf16[256,2,64]{0,2,1:T(8,128)(2,1)} %param.21, f32[2,64]{1,0:T(2,128)} %get-tuple-element.117, bf16[3,2,64]{0,2,1:T(8,128)(2,1)S(1)} %get-tuple-element.102, ...), kind=kLoop, calls=%fused_computation.129 | loop fusion | flops 1638400 | bytes 529920 | tf_op jit(solution)/shard_map/convert_element_type | solution.py:151
  20.7 2.4 %fusion.65 = (bf16[256,2,512]{0,2,1:T(8,128)(2,1)S(1)}, f32[256,2,512]{0,2,1:T(8,128)}, f32[256,2,512]{0,2,1:T(8,128)}) fusion(f32[256,2,8]{0,2,1:T(8,128)S(1)} %get-tuple-element.111, bf16[256,2,512]{0,2,1:T(8,128)(2,1)S(1)} %copy.69, f32[2,512]{1,0:T(2,128)S(1)} %copy-done.37, bf16[3,2,512]{0,2,1:T(8,128)(2,1)S(1)} %slice.342, f32[2,512]{1,0:T(2,128)S(1)} %copy-done.39, ...), kind=kLoop, calls=%fused_computation.64 | loop fusion | flops 7340032 | bytes 3184640 | tf_op jit(solution)/shard_map/jvp()/convert_element_type | solution.py:115
  23.4 1.8 %collective-permute-start.1 = (bf16[2,136,512]{2,1,0:T(8,128)(2,1)S(1)}, bf16[2,136,512]{2,1,0:T(8,128)(2,1)S(1)}, u32[]{:S(2)}, u32[]{:S(2)}) collective-permute-start(bf16[2,136,512]{2,1,0:T(8,128)(2,1)S(1)} %pad_maximum_fusion.1), channel_id=1, source_target_pairs={{0,2},{2,0},{4,6},{6,4},{8,10},{10,8},{12,14},{14,12},{1,3},{3,1},... | collective-permute-start | bytes 835592 | tf_op jit(solution)/shard_map/ppermute | solution.py:40
  25.2 6.3 %collective-permute-done.1 = bf16[2,136,512]{2,1,0:T(8,128)(2,1)S(1)} collective-permute-done((bf16[2,136,512]{2,1,0:T(8,128)(2,1)S(1)}, bf16[2,136,512]{2,1,0:T(8,128)(2,1)S(1)}, u32[]{:S(2)}, u32[]{:S(2)}) %collective-permute-start.1) | collective-permute-done | bytes 278560 | tf_op jit(solution)/shard_map/ppermute | solution.py:40
  31.9 0.7 pad_maximum_fusion.2
  32.6 2.1 %collective-permute-start.2 = (bf16[2,136,512]{2,1,0:T(8,128)(2,1)}, bf16[2,136,512]{2,1,0:T(8,128)(2,1)S(1)}, u32[]{:S(2)}, u32[]{:S(2)}) collective-permute-start(bf16[2,136,512]{2,1,0:T(8,128)(2,1)} %pad_maximum_fusion.2), channel_id=1, source_target_pairs={{0,4},{2,6},{4,0},{6,2},{8,12},{10,14},{12,8},{14,10},{1,5},{3,7},... | collective-permute-start | bytes 835592 | tf_op jit(solution)/shard_map/ppermute | solution.py:40
  34.7 5.3 %collective-permute-done.2 = bf16[2,136,512]{2,1,0:T(8,128)(2,1)S(1)} collective-permute-done((bf16[2,136,512]{2,1,0:T(8,128)(2,1)}, bf16[2,136,512]{2,1,0:T(8,128)(2,1)S(1)}, u32[]{:S(2)}, u32[]{:S(2)}) %collective-permute-start.2) | collective-permute-done | bytes 278560 | tf_op jit(solution)/shard_map/ppermute | solution.py:40
  40.1 0.7 copy-done.16
  40.7 1.0 %convert_element_type.188 = f32[2,136,512]{2,1,0:T(8,128)S(1)} convert(bf16[2,136,512]{2,1,0:T(8,128)(2,1)} %copy-done.16) | non-fusion elementwise | flops 139264 | bytes 835584 | tf_op jit(solution)/shard_map/convert_element_type | solution.py:40
  41.8 1.3 %multiply_add_fusion.7 = (f32[2,1,512]{2,1,0:T(1,128)}, f32[2,1,512]{2,1,0:T(1,128)}, f32[2,1,512]{2,1,0:T(1,128)}, f32[2,1,512]{2,1,0:T(1,128)}, bf16[2,1,512]{2,1,0:T(2,128)(2,1)S(1)}) fusion(f32[]{:T(128)S(6)} %sub.71, f32[]{:T(128)S(6)} %convert_element_type.189, f32[2,136,512]{2,1,0:T(8,128)S(1)} %convert_element_type.188, f32[]{:T(128)S(6)} %sub.69, ...), kind=kLoop, calls=%fused_computation.186 | loop fusion | flops 15360 | bytes 30740 | tf_op jit(solution)/shard_map/add | solution.py:25
  43.1 1.2 %add_convert_fusion.1 = (bf16[2,64,512]{2,1,0:T(8,128)(2,1)S(1)}, bf16[2,64,512]{2,1,0:T(8,128)(2,1)S(1)}) fusion(f32[2,136,512]{2,1,0:T(8,128)S(1)} %convert_element_type.188, f32[]{:T(128)S(6)} %sub.71, f32[2,512]{1,0:T(2,128)S(1)} %bitcast.220, f32[]{:T(128)S(6)} %convert_element_type.189, f32[2,512]{1,0:T(2,128)S(1)} %bitcast.217, f32[]{:T(128)S(6)} %sub.69, ...), kind=kLoop, calls=%fused_computation.99 | loop fusion | flops 1966080 | bytes 1851408 | tf_op jit(solution)/shard_map/convert.6
  44.3 0.7 pad_maximum_fusion.3
  45.0 2.5 %collective-permute-start.3 = (bf16[2,136,512]{2,1,0:T(8,128)(2,1)}, bf16[2,136,512]{2,1,0:T(8,128)(2,1)}, u32[]{:S(2)}, u32[]{:S(2)}) collective-permute-start(bf16[2,136,512]{2,1,0:T(8,128)(2,1)} %pad_maximum_fusion.3), channel_id=1, source_target_pairs={{0,8},{2,10},{4,12},{6,14},{8,0},{10,2},{12,4},{14,6},{1,9},{3,11}... | collective-permute-start | bytes 835592 | tf_op jit(solution)/shard_map/ppermute | solution.py:40
  48.2 1.2 %copy.75 = bf16[256,2,512]{0,2,1:T(8,128)(2,1)} copy(bf16[256,2,512]{2,1,0:T(2,128)(2,1)S(1)} %copy-done) | data formatting | bytes 1048576 | tf_op args[10]
  49.4 1.3 %copy.74 = f32[256,2,512]{0,2,1:T(8,128)} copy(bf16[256,2,512]{2,1,0:T(2,128)(2,1)S(1)} %copy-done) | data formatting | bytes 1572864 | tf_op jit(solution)/shard_map/convert_element_type | solution.py:162
  50.8 1.1 %fusion.134 = f32[2,256,256]{2,1,0:T(8,128)} fusion(bf16[256,2,64]{0,2,1:T(8,128)(2,1)S(1)} %get-tuple-element.131, bf16[256,2,64]{0,2,1:T(8,128)(2,1)S(1)} %copy-done.6), kind=kOutput, calls=%fused_computation.216 | convolution fusion | flops 16777216 | bytes 655360 | tf_op jit(solution)/shard_map/jvp(tgn,sgn->gts)/dot_general | solution.py:102
  51.9 6.5 %collective-permute-done.3 = bf16[2,136,512]{2,1,0:T(8,128)(2,1)} collective-permute-done((bf16[2,136,512]{2,1,0:T(8,128)(2,1)}, bf16[2,136,512]{2,1,0:T(8,128)(2,1)}, u32[]{:S(2)}, u32[]{:S(2)}) %collective-permute-start.3) | collective-permute-done | bytes 278560 | tf_op jit(solution)/shard_map/ppermute | solution.py:40
  58.4 1.0 %convert_element_type.190 = f32[2,136,512]{2,1,0:T(8,128)S(1)} convert(bf16[2,136,512]{2,1,0:T(8,128)(2,1)} %collective-permute-done.3) | non-fusion elementwise | flops 139264 | bytes 835584 | tf_op jit(solution)/shard_map/convert_element_type | solution.py:40
  59.4 0.8 multiply_reduce_fusion.2
  60.3 0.8 reduce_sum.98
  61.2 0.7 copy.84
  61.9 1.9 %fusion.68 = f32[2,256,64]{1,2,0:T(8,128)} fusion(f32[2,64,512]{2,1,0:T(8,128)S(1)} %get-tuple-element.83, f32[2,512,256]{1,0,2:T(2,128)S(1)} %bitcast.197), kind=kOutput, calls=%fused_computation.67 | convolution fusion | flops 201326592 | bytes 1441792 | tf_op jit(solution)/shard_map/transpose(jvp(tgn,gnk->tgk))/dot_general | solution.py:127
  65.8 0.7 fusion.115
  66.5 5.1 %fusion.25 = (f32[2,8,256]{2,1,0:T(8,128)}, f32[2,8,256]{2,1,0:T(8,128)}, f32[2,8,256]{2,1,0:T(8,128)}, f32[2,256,256]{2,1,0:T(8,128)}) fusion(f32[2,8,256]{2,1,0:T(8,128)S(1)} %bitcast.209, f32[2,8,256]{2,1,0:T(8,128)S(1)} %get-tuple-element.105, f32[2,256,256]{2,1,0:T(8,128)S(1)} %copy-done.9, pred[256,256]{1,0:T(8,128)(4,1)S(1)} %copy-done.27, ...), kind=kOutput, calls=%fused_computation.34 | convolution fusion | flops 156356608 | bytes 2768896 | tf_op jit(solution)/shard_map/transpose(jvp(ghts,sghp->tghp))/dot_general | solution.py:104
  71.6 2.4 %fusion.35 = bf16[256,2,8,64]{0,3,2,1:T(8,128)(2,1)} fusion(f32[2,8,256]{2,1,0:T(8,128)S(1)} %get-tuple-element.105, f32[2,8,256]{2,1,0:T(8,128)S(1)} %bitcast.210, f32[2,256,256]{2,1,0:T(8,128)S(1)} %copy-done.9, pred[256,256]{1,0:T(8,128)(4,1)S(1)} %copy-done.27, f32[256,2,8,64]{0,3,2,1:T(8,128)S(1)} %bitcast.204, f32[256,2,8,64]{0,3,2,1:T(8,128)S(1)} %bitcast.201, ...), kind=kOutput, calls=%fused_computation.38 | convolution fusion | flops 142082048 | bytes 3260480 | tf_op jit(solution)/shard_map/jvp(ghts,sghp->tghp)/dot_general | solution.py:104
  74.0 2.4 %fusion.47 = f32[256,2,8,64]{0,3,2,1:T(8,128)} fusion(bf16[2,8,64,256]{3,2,1,0:T(8,128)(2,1)S(1)} %bitcast.207, f32[2,8,256]{2,1,0:T(8,128)S(1)} %get-tuple-element.105, f32[2,8,256]{2,1,0:T(8,128)S(1)} %bitcast.211, f32[2,256,256]{2,1,0:T(8,128)S(1)} %copy-done.9, pred[256,256]{1,0:T(8,128)(4,1)S(1)} %copy-done.27, f32[256,2,8,64]{0,3,2,1:T(8,128)S(1)} %bitcast.199, ...), kind=kOutput, calls=%fused_computation.42 | convolution fusion | flops 141557760 | bytes 3244096 | tf_op jit(solution)/shard_map/transpose(jvp(ghts,sghp->tghp))/dot_general | solution.py:104
  77.1 1.4 %convolution_bitcast_fusion.1 = f32[256,2,64]{0,2,1:T(8,128)S(1)} fusion(f32[2,256,256]{2,1,0:T(8,128)} %get-tuple-element.80, bf16[256,2,64]{0,2,1:T(8,128)(2,1)S(1)} %get-tuple-element.131), kind=kOutput, calls=%fused_computation.48 | convolution fusion | flops 100663296 | bytes 720896 | tf_op jit(solution)/shard_map/transpose(jvp(tgn,sgn->gts))/dot_general | solution.py:102
  78.5 1.5 %fusion.58 = f32[256,2,64]{0,2,1:T(8,128)S(1)} fusion(f32[2,256,64]{1,2,0:T(8,128)} %fusion.68, f32[2,256,256]{2,1,0:T(8,128)} %get-tuple-element.80, bf16[256,2,64]{0,2,1:T(8,128)(2,1)S(1)} %copy-done.7, f32[256,2,64]{0,2,1:T(8,128)S(1)} %copy-done.13), kind=kOutput, calls=%fused_computation.55 | convolution fusion | flops 101023744 | bytes 983040 | tf_op jit(solution)/shard_map/transpose(jvp(tgn,sgn->gts))/dot_general | solution.py:102
  80.1 1.0 fusion.94
  82.1 1.0 fusion.87
  83.8 1.6 %multiply_multiply_fusion = f32[256,2,512]{0,2,1:T(8,128)S(1)} fusion(f32[256,2,512]{0,2,1:T(8,128)S(1)} %copy-done.3, f32[2,512,256]{2,1,0:T(8,128)S(1)} %get-tuple-element.128, f32[256,2,8,64]{0,3,2,1:T(8,128)} %fusion.47, f32[256,2,8]{0,2,1:T(8,128)S(1)} %get-tuple-element.111), kind=kLoop, calls=%fused_computation.73 | loop fusion | flops 3145728 | bytes 4210688 | tf_op jit(solution)/shard_map/mul | solution.py:65
  85.6 2.2 %fusion.20 = f32[259,2,512]{0,2,1:T(8,128)S(1)} fusion(f32[256,2,512]{0,2,1:T(8,128)S(1)} %multiply_multiply_fusion, f32[2,512]{1,0:T(2,128)S(1)} %copy-done.38, f32[2,512]{1,0:T(2,128)S(1)} %copy-done.40, f32[2,512]{1,0:T(2,128)S(1)} %copy-done.36, f32[2,512]{1,0:T(2,128)S(1)} %copy-done.34), kind=kLoop, calls=%fused_computation.27 | loop fusion | flops 1856512 | bytes 2125824 | tf_op jit(solution)/shard_map/add | solution.py:73
  88.1 1.3 %collective-permute-start.4 = (f32[3,2,640]{2,1,0:T(2,128)S(1)}, f32[3,2,640]{2,1,0:T(2,128)S(1)}, u32[]{:S(2)}, u32[]{:S(2)}) collective-permute-start(f32[3,2,640]{2,1,0:T(2,128)S(1)} %pad_maximum_fusion.6), channel_id=1, source_target_pairs={{2,0},{4,2},{6,4},{8,6},{10,8},{12,10},{14,12},{3,1},{5,3},{7,5},{... | collective-permute-start | bytes 46088 | tf_op jit(solution)/shard_map/ppermute | solution.py:12
  90.0 0.9 fusion.62
  91.2 1.2 %copy.86 = bf16[256,2,512]{2,1,0:T(2,128)(2,1)} copy(bf16[256,2,512]{0,2,1:T(8,128)(2,1)S(1)} %bitcast.205) | data formatting | bytes 1048576
  92.4 1.3 %collective-permute-done.4 = f32[3,2,640]{2,1,0:T(2,128)S(1)} collective-permute-done((f32[3,2,640]{2,1,0:T(2,128)S(1)}, f32[3,2,640]{2,1,0:T(2,128)S(1)}, u32[]{:S(2)}, u32[]{:S(2)}) %collective-permute-start.4) | collective-permute-done | bytes 15392 | tf_op jit(solution)/shard_map/ppermute | solution.py:12
  94.4 1.7 %scatter-add.14 = bf16[256,2,512]{0,2,1:T(8,128)(2,1)S(1)} dynamic-update-slice(bf16[256,2,512]{0,2,1:T(8,128)(2,1)S(1)} %slice.366, bf16[3,2,512]{0,2,1:T(8,128)(2,1)S(1)} %slice_add_fusion, s32[]{:T(128)} %constant.174.clone.1, s32[]{:T(128)} %constant.169.clone.1, s32[]{:T(128)} %constant.169.clone.1) | dynamic-update-slice | bytes 12292 | tf_op jit(solution)/shard_map/scatter-add | solution.py:199
  96.1 1.2 %copy.87 = bf16[256,2,512]{2,1,0:T(2,128)(2,1)} copy(bf16[256,2,512]{0,2,1:T(8,128)(2,1)S(1)} %scatter-add.14) | data formatting | bytes 1048576
  (197 shorter events, 13.5 us)
Async XLA Ops:
  4.2 12.8 %collective-permute-start = (bf16[3,2,640]{0,2,1:T(8,128)(2,1)}, bf16[3,2,640]{0,2,1:T(8,128)(2,1)S(1)}, u32[]{:S(2)}, u32[]{:S(2)}) collective-permute-start(bf16[3,2,640]{0,2,1:T(8,128)(2,1)} %copy.68), channel_id=1, source_target_pairs={{0,2},{2,4},{4,6},{6,8},{8,10},{10,12},{12,14},{1,3},{3,5},{5,7},{... | collective-permute-start | bytes 23048 | tf_op jit(solution)/shard_map/ppermute | solution.py:12
  9.8 4.7 %copy-start.60 = (f32[2,8]{1,0:T(2,128)}, f32[2,8]{1,0:T(2,128)S(1)}, u32[]{:S(2)}) copy-start(f32[2,8]{1,0:T(2,128)S(1)} %neg.30) | copy-start | bytes 196
  12.0 3.1 %copy-start.17 = (f32[256,16]{0,1}, f32[256,16]{0,1:S(1)}, u32[]{:S(2)}) copy-start(f32[256,16]{0,1:S(1)} %fusion.83) | copy-start | bytes 49156
  12.3 3.6 %copy-start.43 = (f32[2,8]{1,0:T(2,128)}, f32[2,8]{1,0:T(2,128)S(1)}, u32[]{:S(2)}) copy-start(f32[2,8]{1,0:T(2,128)S(1)} %slice_reduce_fusion) | copy-start | bytes 196
  15.9 4.0 %copy-start.54 = (f32[2,64]{1,0:T(2,128)}, f32[2,64]{1,0:T(2,128)S(1)}, u32[]{:S(2)}) copy-start(f32[2,64]{1,0:T(2,128)S(1)} %get-tuple-element.121) | copy-start | bytes 1540
  15.9 4.0 %copy-start.55 = (f32[2,64]{1,0:T(2,128)}, f32[2,64]{1,0:T(2,128)S(1)}, u32[]{:S(2)}) copy-start(f32[2,64]{1,0:T(2,128)S(1)} %get-tuple-element.122) | copy-start | bytes 1540
  15.9 4.6 %copy-start.52 = (f32[2,64]{1,0:T(2,128)}, f32[2,64]{1,0:T(2,128)S(1)}, u32[]{:S(2)}) copy-start(f32[2,64]{1,0:T(2,128)S(1)} %get-tuple-element.119) | copy-start | bytes 1540
  15.9 4.6 %copy-start.53 = (f32[2,64]{1,0:T(2,128)}, f32[2,64]{1,0:T(2,128)S(1)}, u32[]{:S(2)}) copy-start(f32[2,64]{1,0:T(2,128)S(1)} %get-tuple-element.120) | copy-start | bytes 1540
  16.8 3.8 %copy-start.33 = (f32[2,512]{1,0:T(2,128)S(1)}, f32[2,512]{1,0:T(2,128)}, u32[]{:S(2)}) copy-start(f32[2,512]{1,0:T(2,128)} %get-tuple-element.107) | copy-start | bytes 12292
  16.8 3.8 %copy-start.35 = (f32[2,512]{1,0:T(2,128)S(1)}, f32[2,512]{1,0:T(2,128)}, u32[]{:S(2)}) copy-start(f32[2,512]{1,0:T(2,128)} %get-tuple-element.108) | copy-start | bytes 12292
  16.8 3.8 %copy-start.37 = (f32[2,512]{1,0:T(2,128)S(1)}, f32[2,512]{1,0:T(2,128)}, u32[]{:S(2)}) copy-start(f32[2,512]{1,0:T(2,128)} %get-tuple-element.109) | copy-start | bytes 12292
  16.8 3.8 %copy-start.39 = (f32[2,512]{1,0:T(2,128)S(1)}, f32[2,512]{1,0:T(2,128)}, u32[]{:S(2)}) copy-start(f32[2,512]{1,0:T(2,128)} %get-tuple-element.110) | copy-start | bytes 12292
  17.8 2.8 %copy-start.15 = (bf16[3,2,640]{0,2,1:T(8,128)(2,1)S(1)}, bf16[3,2,640]{0,2,1:T(8,128)(2,1)}, u32[]{:S(2)}) copy-start(bf16[3,2,640]{0,2,1:T(8,128)(2,1)} %copy-done.14) | copy-start | bytes 23044
  19.9 3.1 %copy-start.5 = (bf16[256,2,64]{0,2,1:T(8,128)(2,1)}, bf16[256,2,64]{0,2,1:T(8,128)(2,1)S(1)}, u32[]{:S(2)}) copy-start(bf16[256,2,64]{0,2,1:T(8,128)(2,1)S(1)} %get-tuple-element.91) | copy-start | bytes 196612
  23.1 8.6 %copy-start.23 = (f32[2,512]{1,0:T(2,128)S(1)}, f32[2,512]{1,0:T(2,128)}, u32[]{:S(2)}) copy-start(f32[2,512]{1,0:T(2,128)} %copy-done.22) | copy-start | bytes 12292
  23.4 9.3 %copy-start.4 = (f32[2,64,512]{2,1,0:T(8,128)}, f32[2,64,512]{2,1,0:T(8,128)S(1)}, u32[]{:S(2)}) copy-start(f32[2,64,512]{2,1,0:T(8,128)S(1)} %get-tuple-element.126) | copy-start | bytes 786436
  23.4 8.2 %collective-permute-start.1 = (bf16[2,136,512]{2,1,0:T(8,128)(2,1)S(1)}, bf16[2,136,512]{2,1,0:T(8,128)(2,1)S(1)}, u32[]{:S(2)}, u32[]{:S(2)}) collective-permute-start(bf16[2,136,512]{2,1,0:T(8,128)(2,1)S(1)} %pad_maximum_fusion.1), channel_id=1, source_target_pairs={{0,2},{2,0},{4,6},{6,4},{8,10},{10,8},{12,14},{14,12},{1,3},{3,1},... | collective-permute-start | bytes 835592 | tf_op jit(solution)/shard_map/ppermute | solution.py:40
  31.6 8.4 %copy-start.32 = (f32[2,1,512]{2,0,1:T(2,128)}, f32[2,1,512]{2,0,1:T(2,128)S(1)}, u32[]{:S(2)}) copy-start(f32[2,1,512]{2,0,1:T(2,128)S(1)} %copy.124) | copy-start | bytes 12292
  31.7 8.4 %copy-start.26 = (f32[2,1,512]{2,1,0:T(1,128)}, f32[2,1,512]{2,1,0:T(1,128)S(1)}, u32[]{:S(2)}) copy-start(f32[2,1,512]{2,1,0:T(1,128)S(1)} %multiply_multiply_fusion.3) | copy-start | bytes 12292
  32.6 7.4 %collective-permute-start.2 = (bf16[2,136,512]{2,1,0:T(8,128)(2,1)}, bf16[2,136,512]{2,1,0:T(8,128)(2,1)S(1)}, u32[]{:S(2)}, u32[]{:S(2)}) collective-permute-start(bf16[2,136,512]{2,1,0:T(8,128)(2,1)} %pad_maximum_fusion.2), channel_id=1, source_target_pairs={{0,4},{2,6},{4,0},{6,2},{8,12},{10,14},{12,8},{14,10},{1,5},{3,7},... | collective-permute-start | bytes 835592 | tf_op jit(solution)/shard_map/ppermute | solution.py:40
  44.3 6.5 %copy-start.6 = (bf16[256,2,64]{0,2,1:T(8,128)(2,1)S(1)}, bf16[256,2,64]{0,2,1:T(8,128)(2,1)}, u32[]{:S(2)}) copy-start(bf16[256,2,64]{0,2,1:T(8,128)(2,1)} %copy-done.5) | copy-start | bytes 196612
  45.0 13.4 %collective-permute-start.3 = (bf16[2,136,512]{2,1,0:T(8,128)(2,1)}, bf16[2,136,512]{2,1,0:T(8,128)(2,1)}, u32[]{:S(2)}, u32[]{:S(2)}) collective-permute-start(bf16[2,136,512]{2,1,0:T(8,128)(2,1)} %pad_maximum_fusion.3), channel_id=1, source_target_pairs={{0,8},{2,10},{4,12},{6,14},{8,0},{10,2},{12,4},{14,6},{1,9},{3,11}... | collective-permute-start | bytes 835592 | tf_op jit(solution)/shard_map/ppermute | solution.py:40
  48.2 3.6 %copy-start.49 = (f32[2,1,512]{2,1,0:T(1,128)S(1)}, f32[2,1,512]{2,1,0:T(1,128)}, u32[]{:S(2)}) copy-start(f32[2,1,512]{2,1,0:T(1,128)} %get-tuple-element.86) | copy-start | bytes 12292
  48.2 3.6 %copy-start.48 = (f32[2,1,512]{2,1,0:T(1,128)S(1)}, f32[2,1,512]{2,1,0:T(1,128)}, u32[]{:S(2)}) copy-start(f32[2,1,512]{2,1,0:T(1,128)} %get-tuple-element.87) | copy-start | bytes 12292
  48.2 3.7 %copy-start.47 = (f32[2,1,512]{2,1,0:T(1,128)S(1)}, f32[2,1,512]{2,1,0:T(1,128)}, u32[]{:S(2)}) copy-start(f32[2,1,512]{2,1,0:T(1,128)} %get-tuple-element.97) | copy-start | bytes 12292
  48.2 3.7 %copy-start.46 = (f32[2,1,512]{2,1,0:T(1,128)S(1)}, f32[2,1,512]{2,1,0:T(1,128)}, u32[]{:S(2)}) copy-start(f32[2,1,512]{2,1,0:T(1,128)} %get-tuple-element.98) | copy-start | bytes 12292
  60.3 3.5 %copy-start.1 = (f32[256,2,512]{0,2,1:T(8,128)S(1)}, f32[256,2,512]{0,2,1:T(8,128)}, u32[]{:S(2)}) copy-start(f32[256,2,512]{0,2,1:T(8,128)} %copy.74) | copy-start | bytes 3145732
  65.7 5.9 %copy-start.20 = (f32[256,2,8]{0,2,1:T(8,128)}, f32[256,2,8]{0,2,1:T(8,128)S(1)}, u32[]{:S(2)}) copy-start(f32[256,2,8]{0,2,1:T(8,128)S(1)} %get-tuple-element.127) | copy-start | bytes 49156
  66.5 5.1 %copy-start.25 = (f32[256,2,8]{0,2,1:T(8,128)S(1)}, f32[256,2,8]{0,2,1:T(8,128)}, u32[]{:S(2)}) copy-start(f32[256,2,8]{0,2,1:T(8,128)} %copy-done.24) | copy-start | bytes 49156
  66.5 5.1 %copy-start.62 = (f32[2,8]{1,0:T(2,128)S(1)}, f32[2,8]{1,0:T(2,128)}, u32[]{:S(2)}) copy-start(f32[2,8]{1,0:T(2,128)} %param.26) | copy-start | bytes 196
  74.0 4.5 %copy-start.13 = (f32[256,2,64]{0,2,1:T(8,128)S(1)}, f32[256,2,64]{0,2,1:T(8,128)}, u32[]{:S(2)}) copy-start(f32[256,2,64]{0,2,1:T(8,128)} %get-tuple-element.132) | copy-start | bytes 393220
  76.4 5.3 %copy-start.12 = (f32[256,2,64]{0,2,1:T(8,128)S(1)}, f32[256,2,64]{0,2,1:T(8,128)}, u32[]{:S(2)}) copy-start(f32[256,2,64]{0,2,1:T(8,128)} %get-tuple-element.92) | copy-start | bytes 393220
  78.5 5.3 %copy-start.3 = (f32[256,2,512]{0,2,1:T(8,128)S(1)}, f32[256,2,512]{0,2,1:T(8,128)}, u32[]{:S(2)}) copy-start(f32[256,2,512]{0,2,1:T(8,128)} %get-tuple-element.90) | copy-start | bytes 3145732
  85.4 2.6 %copy-start.50 = (f32[3,2,64]{2,1,0:T(2,128)S(1)}, f32[3,2,64]{2,1,0:T(2,128)}, u32[]{:S(2)}) copy-start(f32[3,2,64]{2,1,0:T(2,128)} %copy.80) | copy-start | bytes 4612
  85.5 4.0 %copy-start.19 = (f32[256,16]{0,1:S(1)}, f32[256,16]{0,1}, u32[]{:S(2)}) copy-start(f32[256,16]{0,1} %copy-done.17) | copy-start | bytes 49156
  85.5 4.0 %copy-start.41 = (f32[256,2,8]{0,2,1:T(8,128)S(1)}, f32[256,2,8]{0,2,1:T(8,128)}, u32[]{:S(2)}) copy-start(f32[256,2,8]{0,2,1:T(8,128)} %get-tuple-element.106) | copy-start | bytes 49156
  85.5 4.0 %copy-start.42 = (f32[1,2,8]{0,2,1:T(8,128)S(1)}, f32[1,2,8]{0,2,1:T(8,128)}, u32[]{:S(2)}) copy-start(f32[1,2,8]{0,2,1:T(8,128)} %copy.84) | copy-start | bytes 196
  85.5 4.2 %copy-start.61 = (f32[2,8]{1,0:T(2,128)S(1)}, f32[2,8]{1,0:T(2,128)}, u32[]{:S(2)}) copy-start(f32[2,8]{1,0:T(2,128)} %copy-done.60) | copy-start | bytes 196
  85.5 4.2 %copy-start.63 = (f32[2,8,256]{2,1,0:T(8,128)S(1)}, f32[2,8,256]{2,1,0:T(8,128)}, u32[]{:S(2)}) copy-start(f32[2,8,256]{2,1,0:T(8,128)} %get-tuple-element.77) | copy-start | bytes 49156
  85.5 4.2 %copy-start.64 = (f32[2,8,256]{2,1,0:T(8,128)S(1)}, f32[2,8,256]{2,1,0:T(8,128)}, u32[]{:S(2)}) copy-start(f32[2,8,256]{2,1,0:T(8,128)} %get-tuple-element.78) | copy-start | bytes 49156
  85.5 4.2 %copy-start.65 = (f32[2,8,256]{2,1,0:T(8,128)S(1)}, f32[2,8,256]{2,1,0:T(8,128)}, u32[]{:S(2)}) copy-start(f32[2,8,256]{2,1,0:T(8,128)} %get-tuple-element.79) | copy-start | bytes 49156
  85.5 4.4 %copy-start.21 = (f32[256,2,8]{0,2,1:T(8,128)S(1)}, f32[256,2,8]{0,2,1:T(8,128)}, u32[]{:S(2)}) copy-start(f32[256,2,8]{0,2,1:T(8,128)} %copy-done.20) | copy-start | bytes 49156
  85.5 4.4 %copy-start.31 = (f32[256,2,8]{0,2,1:T(8,128)S(1)}, f32[256,2,8]{0,2,1:T(8,128)}, u32[]{:S(2)}) copy-start(f32[256,2,8]{0,2,1:T(8,128)} %param.23) | copy-start | bytes 49156
  85.6 4.4 %copy-start.45 = (f32[2,8]{1,0:T(2,128)S(1)}, f32[2,8]{1,0:T(2,128)}, u32[]{:S(2)}) copy-start(f32[2,8]{1,0:T(2,128)} %copy-done.43) | copy-start | bytes 196
  85.6 4.4 %copy-start.56 = (f32[1,2,8]{0,2,1:T(8,128)S(1)}, f32[1,2,8]{0,2,1:T(8,128)}, u32[]{:S(2)}) copy-start(f32[1,2,8]{0,2,1:T(8,128)} %copy.85) | copy-start | bytes 196
  85.6 4.4 %copy-start.58 = (f32[2,8]{1,0:T(2,128)S(1)}, f32[2,8]{1,0:T(2,128)}, u32[]{:S(2)}) copy-start(f32[2,8]{1,0:T(2,128)} %param.25) | copy-start | bytes 196
  87.8 3.4 %copy-start.10 = (bf16[256,2,8,64]{0,3,2,1:T(8,128)(2,1)S(1)}, bf16[256,2,8,64]{0,3,2,1:T(8,128)(2,1)}, u32[]{:S(2)}) copy-start(bf16[256,2,8,64]{0,3,2,1:T(8,128)(2,1)} %fusion.35) | copy-start | bytes 1572868
  88.1 5.6 %collective-permute-start.4 = (f32[3,2,640]{2,1,0:T(2,128)S(1)}, f32[3,2,640]{2,1,0:T(2,128)S(1)}, u32[]{:S(2)}, u32[]{:S(2)}) collective-permute-start(f32[3,2,640]{2,1,0:T(2,128)S(1)} %pad_maximum_fusion.6), channel_id=1, source_target_pairs={{2,0},{4,2},{6,4},{8,6},{10,8},{12,10},{14,12},{3,1},{5,3},{7,5},{... | collective-permute-start | bytes 46088 | tf_op jit(solution)/shard_map/ppermute | solution.py:12
  (23 other events, 29.4 us)

commit v15 on v11

--- a/solution.py
+++ b/solution.py
@@ -159,21 +159,16 @@
     b_float = jax.nn.silu(b_running).astype(jnp.bfloat16).astype(jnp.float32)
     c_float = jax.nn.silu(c_running).astype(jnp.bfloat16).astype(jnp.float32)
 
-    def mix_map(x_arg, b_arg, c_arg, dt_arg):
-        return ssd_mix(x_arg, b_arg, c_arg, dt_arg, rate, dt_bias, skip)
-
-    def state_map(x_arg, b_arg, dt_arg):
-        return ssd_state(x_arg, b_arg, dt_arg, rate, dt_bias)
-
-    (cum_log, state_end), state_pull = jax.vjp(state_map, x_float, b_float, dt_in)
+    def local_map(x_arg, b_arg, c_arg, dt_arg):
+        y_arg = ssd_mix(x_arg, b_arg, c_arg, dt_arg, rate, dt_bias, skip)
+        return (y_arg,) + ssd_state(x_arg, b_arg, dt_arg, rate, dt_bias)
+
+    (y_local, cum_log, state_end), local_pull = jax.vjp(local_map, x_float, b_float, c_float, dt_in)
     decay_total = jnp.exp(cum_log[-1])
     grad_heads = grad_y.astype(jnp.float32).reshape(length, groups, head_count, head_size)
     seed_state = jnp.einsum(
         "tghp,tgn->ghpn", jnp.exp(cum_log)[..., None] * grad_heads, c_float, precision=HIGH
     )
-
-    y_local, mix_pull = jax.vjp(mix_map, x_float, b_float, c_float, dt_in)
-    mix_x, mix_b, mix_c, mix_dt = mix_pull(grad_heads)
     state_in, adjoint, _ = scanned_pair(decay_total, state_end, seed_state, "ctx", [])
 
     def carry_map(c_arg, cum_arg):
@@ -184,11 +179,8 @@
     grad_c_carry, grad_cum_carry = carry_pull(grad_heads)
     end_term = jnp.sum(adjoint * state_in, axis=(2, 3)) * decay_total
     grad_cum = grad_cum_carry.at[length - 1].add(end_term)
-    state_x, state_b, state_dt = state_pull((grad_cum, adjoint))
-    grad_x_conv = mix_x + state_x
-    grad_b_part = mix_b + state_b
-    grad_dt = mix_dt + state_dt
-    grad_c_part = mix_c + grad_c_carry
+    grad_x_conv, grad_b_part, grad_c_local, grad_dt = local_pull((grad_heads, grad_cum, adjoint))
+    grad_c_part = grad_c_local + grad_c_carry
     grad_b_ext = conv_backward(grad_b_part.astype(jnp.bfloat16), b_running, conv_b)
     grad_c_ext = conv_backward(grad_c_part.astype(jnp.bfloat16), c_running, conv_c)
     grad_x_ext = conv_backward(grad_x_conv.astype(jnp.bfloat16), x_running, conv_x)

time: 93.4 us -> 93.4 us (level)
  no operation moved by 1% of the time
where the time goes in v15:
time: 93.4 us; the launch traced here: 92.6 us
  starting transfers between devices  22.4 us (24%)
  waiting for transfers between devices  21 us (22%)
  matrix products  20.4 us (22%)
  local copies, waits for them, and re-layouts  17.4 us (19%)
  other arithmetic  9.75 us (10%)
  between operations  1.65 us (2%)
    ppermute x6, waiting for transfers between devices, shift(): return lax.ppermute(packed, axis, pairs)  19.5 us
    ppermute x6, starting transfers between devices, shift(): return lax.ppermute(packed, axis, pairs)  16.3 us
    dot_general x3, matrix products, ssd_mix(): jnp.einsum('ghts,sghp->tghp', mixing, x_half, preferred_element_type=jnp....  10.8 us
    ppermute x2, starting transfers between devices, from_behind(): return lax.ppermute(array, axis, pairs)  6.12 us
    unnamed x128, local copies, waits for them, and re-layouts  5.99 us
    dot_general x2, matrix products, carry_in(): carried = jnp.einsum('tgn,ghpn->tghp', c_float, state_in, precision=HIGH)  2.67 us
    dot_general x3, matrix products, ssd_state(): jnp.einsum('sghp,sgn->ghpn', weighted.astype(jnp.float32), b_float, preci...  2.5 us
    mul x3, local copies, waits for them, and re-layouts, conv_forward(): running = weight[0] * extended[0:length].astype(jnp.float32)  2.21 us
  transfers between devices with their start and end apart: 8, of which 7 were waited for; matrix products, arithmetic and copies ran while one was open for 12% of the time, Pallas kernels for 0%

profile of v15, /device:TPU:0, one launch (start us, length us, event | category | flops | bytes accessed | tf_op | source)
XLA Modules:
  0.0 92.6 jit_solution(16117381631447138821)
XLA Ops:
  0.6 0.8 slice.294
  1.4 0.8 slice.295
  2.3 0.8 slice.296
  3.4 4.8 %collective-permute-start = (bf16[3,2,640]{2,0,1:T(4,128)(2,1)S(1)}, bf16[3,2,640]{2,0,1:T(4,128)(2,1)S(1)}, u32[]{:S(2)}, u32[]{:S(2)}) collective-permute-start(bf16[3,2,640]{2,0,1:T(4,128)(2,1)S(1)} %copy.120), channel_id=1, source_target_pairs={{0,2},{2,4},{4,6},{6,8},{8,10},{10,12},{12,14},{1,3},{3,5},{5,7},{... | collective-permute-start | bytes 23048 | tf_op jit(solution)/shard_map/ppermute | solution.py:12
  8.2 0.7 neg.30
  8.9 0.7 slice_bitcast_fusion.7
  9.7 0.7 slice_bitcast_fusion.11
  10.4 0.9 %fusion.78 = f32[256,16]{0,1:S(1)} fusion(f32[2,8]{1,0:T(2,128)S(1)} %neg.30, f32[256,2,8]{0,2,1:T(8,128)} %param.23, f32[2,8]{1,0:T(2,128)} %param.25), kind=kOutput, calls=%fused_computation.97 | convolution fusion | flops 12681216 | bytes 32896
  11.6 0.7 slice_bitcast_fusion.3
  12.3 0.8 fusion.115
  13.2 0.6 fusion.131
  13.8 1.1 %copy.121 = bf16[256,2,512]{2,0,1:T(8,128)(2,1)S(1)} copy(bf16[256,2,512]{2,1,0:T(2,128)(2,1)} %param.20) | data formatting | bytes 1048576 | tf_op args[0]
  14.9 0.5 copy.127
  15.9 1.1 %multiply_convert_fusion.1 = (bf16[256,2,64]{0,2,1:T(8,128)(2,1)S(1)}, f32[256,2,64]{0,2,1:T(8,128)}, bf16[256,2,64]{0,2,1:T(8,128)(2,1)S(1)}, f32[256,2,64]{0,2,1:T(8,128)}) fusion(bf16[256,2,64]{0,2,1:T(8,128)(2,1)S(1)} %copy-done.10, f32[2,64]{1,0:T(2,128)S(1)} %get-tuple-element.120, bf16[3,2,64]{0,2,1:T(8,128)(2,1)S(1)} %copy.125, ...), kind=kLoop, calls=%fused_computation.118 | loop fusion | flops 1638400 | bytes 529920 | tf_op jit(solution)/shard_map/convert_element_type | solution.py:159
  16.9 0.6 fusion.52
  17.9 0.7 multiply_convert_fusion
  19.5 3.5 %collective-permute-start.1 = (bf16[2,8,4224]{2,1,0:T(8,128)(2,1)S(1)}, bf16[2,8,4224]{2,1,0:T(8,128)(2,1)S(1)}, u32[]{:S(2)}, u32[]{:S(2)}) collective-permute-start(bf16[2,8,4224]{2,1,0:T(8,128)(2,1)S(1)} %get-tuple-element.116), channel_id=1, source_target_pairs={{0,2},{2,4},{4,6},{6,8},{8,10},{10,12},{12,14},{1,3},{3,5},{5,7},{... | collective-permute-start | bytes 405512 | tf_op jit(solution)/shard_map/ppermute | solution.py:27
  23.0 1.3 %collective-permute-start.4 = (bf16[2,8,4224]{2,1,0:T(8,128)(2,1)S(1)}, bf16[2,8,4224]{2,1,0:T(8,128)(2,1)S(1)}, u32[]{:S(2)}, u32[]{:S(2)}) collective-permute-start(bf16[2,8,4224]{2,1,0:T(8,128)(2,1)S(1)} %get-tuple-element.117), channel_id=1, source_target_pairs={{2,0},{4,2},{6,4},{8,6},{10,8},{12,10},{14,12},{3,1},{5,3},{7,5},{... | collective-permute-start | bytes 405512 | tf_op jit(solution)/shard_map/ppermute | solution.py:27
  24.3 1.2 %collective-permute-done.1 = bf16[2,8,4224]{2,1,0:T(8,128)(2,1)S(1)} collective-permute-done((bf16[2,8,4224]{2,1,0:T(8,128)(2,1)S(1)}, bf16[2,8,4224]{2,1,0:T(8,128)(2,1)S(1)}, u32[]{:S(2)}, u32[]{:S(2)}) %collective-permute-start.1) | collective-permute-done | bytes 135200 | tf_op jit(solution)/shard_map/ppermute | solution.py:27
  25.7 4.2 %collective-permute-done.4 = bf16[2,8,4224]{2,1,0:T(8,128)(2,1)S(1)} collective-permute-done((bf16[2,8,4224]{2,1,0:T(8,128)(2,1)S(1)}, bf16[2,8,4224]{2,1,0:T(8,128)(2,1)S(1)}, u32[]{:S(2)}, u32[]{:S(2)}) %collective-permute-start.4) | collective-permute-done | bytes 135200 | tf_op jit(solution)/shard_map/ppermute | solution.py:27
  30.2 3.8 %collective-permute-start.2 = (bf16[2,8,4224]{2,1,0:T(8,128)(2,1)S(1)}, bf16[2,8,4224]{2,1,0:T(8,128)(2,1)S(1)}, u32[]{:S(2)}, u32[]{:S(2)}) collective-permute-start(bf16[2,8,4224]{2,1,0:T(8,128)(2,1)S(1)} %pad_maximum_fusion.3), channel_id=1, source_target_pairs={{0,4},{2,6},{4,8},{6,10},{8,12},{10,14},{1,5},{3,7},{5,9},{7,11},{... | collective-permute-start | bytes 405512 | tf_op jit(solution)/shard_map/ppermute | solution.py:27
  34.1 2.5 %collective-permute-done.2 = bf16[2,8,4224]{2,1,0:T(8,128)(2,1)S(1)} collective-permute-done((bf16[2,8,4224]{2,1,0:T(8,128)(2,1)S(1)}, bf16[2,8,4224]{2,1,0:T(8,128)(2,1)S(1)}, u32[]{:S(2)}, u32[]{:S(2)}) %collective-permute-start.2) | collective-permute-done | bytes 135200 | tf_op jit(solution)/shard_map/ppermute | solution.py:27
  36.8 1.3 %collective-permute-start.5 = (bf16[2,8,4224]{2,1,0:T(8,128)(2,1)S(1)}, bf16[2,8,4224]{2,1,0:T(8,128)(2,1)S(1)}, u32[]{:S(2)}, u32[]{:S(2)}) collective-permute-start(bf16[2,8,4224]{2,1,0:T(8,128)(2,1)S(1)} %pad_maximum_fusion.5), channel_id=1, source_target_pairs={{4,0},{6,2},{8,4},{10,6},{12,8},{14,10},{5,1},{7,3},{9,5},{11,7},{... | collective-permute-start | bytes 405512 | tf_op jit(solution)/shard_map/ppermute | solution.py:27
  38.1 1.1 %fusion.132 = f32[2,256,256]{2,1,0:T(8,128)} fusion(bf16[256,2,64]{0,2,1:T(8,128)(2,1)S(1)} %get-tuple-element.134, bf16[256,2,64]{0,2,1:T(8,128)(2,1)S(1)} %get-tuple-element.97), kind=kOutput, calls=%fused_computation.208 | convolution fusion | flops 16777216 | bytes 655360 | tf_op jit(solution)/shard_map/jvp(tgn,sgn->gts)/dot_general | solution.py:116
  39.2 5.0 %collective-permute-done.5 = bf16[2,8,4224]{2,1,0:T(8,128)(2,1)S(1)} collective-permute-done((bf16[2,8,4224]{2,1,0:T(8,128)(2,1)S(1)}, bf16[2,8,4224]{2,1,0:T(8,128)(2,1)S(1)}, u32[]{:S(2)}, u32[]{:S(2)}) %collective-permute-start.5) | collective-permute-done | bytes 135200 | tf_op jit(solution)/shard_map/ppermute | solution.py:27
  44.6 4.9 %collective-permute-start.3 = (bf16[2,8,4224]{2,1,0:T(8,128)(2,1)S(1)}, bf16[2,8,4224]{2,1,0:T(8,128)(2,1)S(1)}, u32[]{:S(2)}, u32[]{:S(2)}) collective-permute-start(bf16[2,8,4224]{2,1,0:T(8,128)(2,1)S(1)} %pad_maximum_fusion.4), channel_id=1, source_target_pairs={{0,8},{2,10},{4,12},{6,14},{1,9},{3,11},{5,13},{7,15},{16,24},{18,... | collective-permute-start | bytes 405512 | tf_op jit(solution)/shard_map/ppermute | solution.py:27
  49.7 1.5 %collective-permute-start.6 = (bf16[2,8,4224]{2,1,0:T(8,128)(2,1)S(1)}, bf16[2,8,4224]{2,1,0:T(8,128)(2,1)S(1)}, u32[]{:S(2)}, u32[]{:S(2)}) collective-permute-start(bf16[2,8,4224]{2,1,0:T(8,128)(2,1)S(1)} %pad_maximum_fusion.6), channel_id=1, source_target_pairs={{8,0},{10,2},{12,4},{14,6},{9,1},{11,3},{13,5},{15,7},{24,16},{26,... | collective-permute-start | bytes 405512 | tf_op jit(solution)/shard_map/ppermute | solution.py:27
  51.3 0.8 collective-permute-done.3
  52.1 5.8 %collective-permute-done.6 = bf16[2,8,4224]{2,1,0:T(8,128)(2,1)S(1)} collective-permute-done((bf16[2,8,4224]{2,1,0:T(8,128)(2,1)S(1)}, bf16[2,8,4224]{2,1,0:T(8,128)(2,1)S(1)}, u32[]{:S(2)}, u32[]{:S(2)}) %collective-permute-start.6) | collective-permute-done | bytes 135200 | tf_op jit(solution)/shard_map/ppermute | solution.py:27
  57.9 0.8 multiply_reduce_fusion
  59.0 1.1 %convolution_bitcast_fusion.3 = f32[2,256,64]{1,2,0:T(8,128)S(1)} fusion(f32[2,8,64,64]{3,2,1,0:T(8,128)S(1)} %reshape.212, bf16[256,2,8,64]{0,3,2,1:T(8,128)(2,1)S(1)} %bitcast.188, f32[256,2,8]{0,2,1:T(8,128)S(1)} %get-tuple-element.107), kind=kOutput, calls=%fused_computation.48 | convolution fusion | flops 201850880 | bytes 933888 | tf_op jit(solution)/shard_map/transpose(jvp(tgn,ghpn->tghp))/dot_general | solution.py:135
  60.0 1.6 %fusion.70 = (f32[256,2,8]{0,2,1:T(8,128)S(1)}, f32[256,2,8,64]{0,3,2,1:T(8,128)}) fusion(bf16[256,2,512]{0,2,1:T(8,128)(2,1)S(1)} %copy.127, f32[2,8,64,64]{3,2,1,0:T(8,128)S(1)} %reshape.212, bf16[256,2,64]{0,2,1:T(8,128)(2,1)S(1)} %get-tuple-element.134), kind=kOutput, calls=%fused_computation.67 | convolution fusion | flops 202108928 | bytes 1916928 | tf_op jit(solution)/shard_map/jvp(tgn,ghpn->tghp)/dot_general | solution.py:135
  61.9 0.6 convolution_bitcast_fusion.2
  62.5 1.6 %fusion.69 = (f32[256,2,8]{0,2,1:T(8,128)S(1)}, f32[256,2,8,64]{0,3,2,1:T(8,128)}) fusion(bf16[256,2,512]{0,2,1:T(8,128)(2,1)S(1)} %copy.123, f32[2,8,64,64]{3,2,1,0:T(8,128)S(1)} %reshape.216, bf16[256,2,64]{0,2,1:T(8,128)(2,1)S(1)} %get-tuple-element.97), kind=kOutput, calls=%fused_computation.66 | convolution fusion | flops 202633216 | bytes 1916928 | tf_op jit(solution)/shard_map/transpose(jvp(sghp,sgn->ghpn))/dot_general | solution.py:130
  64.1 0.7 copy.138
  64.8 1.2 %fusion.116 = (f32[2,8]{1,0:T(2,128)}, f32[2,8,256]{2,1,0:T(8,128)S(1)}, f32[256,2,8]{0,2,1:T(8,128)}) fusion(f32[256,2,8]{0,2,1:T(8,128)S(1)} %get-tuple-element.130, f32[2,8]{1,0:T(2,128)S(1)} %copy-done.30, f32[256,16]{0,1:S(1)} %fusion.78, f32[256,2,8]{0,2,1:T(8,128)S(1)} %copy-done.16, f32[2,8]{1,0:T(2,128)S(1)} %copy-done.49, ...), kind=kLoop, calls=%fused_computation.166 | loop fusion | flops 49136 | bytes 98496 | tf_op jit(solution)/shard_map/transpose(jvp())/reduce_sum | solution.py:128
  66.1 5.9 %fusion.18 = (f32[2,8,256]{2,1,0:T(8,128)}, f32[2,8,256]{2,1,0:T(8,128)}, f32[2,8,256]{2,1,0:T(8,128)}, f32[2,256,256]{2,1,0:T(8,128)S(1)}) fusion(f32[2,8,256]{2,1,0:T(8,128)S(1)} %bitcast.200, f32[2,8,256]{2,1,0:T(8,128)S(1)} %get-tuple-element.104, f32[2,256,256]{2,1,0:T(8,128)} %fusion.132, pred[256,256]{1,0:T(8,128)(4,1)S(1)} %iota_compare_fusion, ...), kind=kOutput, calls=%fused_computation.27 | convolution fusion | flops 156094464 | bytes 2244608 | tf_op jit(solution)/shard_map/transpose(jvp(ghts,sghp->tghp))/dot_general | solution.py:118
  72.0 2.3 %fusion.48 = bf16[256,2,8,64]{0,3,2,1:T(8,128)(2,1)} fusion(bf16[2,8,64,256]{3,2,1,0:T(8,128)(2,1)S(1)} %bitcast.191, f32[2,8,256]{2,1,0:T(8,128)S(1)} %get-tuple-element.104, f32[2,8,256]{2,1,0:T(8,128)S(1)} %bitcast.201, f32[2,256,256]{2,1,0:T(8,128)S(1)} %copy-done.3, pred[256,256]{1,0:T(8,128)(4,1)S(1)} %iota_compare_fusion, ...), kind=kOutput, calls=%fused_computation.41 | convolution fusion | flops 142606336 | bytes 3260480 | tf_op jit(solution)/shard_map/transpose(jvp(ghts,sghp->tghp))/dot_general | solution.py:118
  74.4 2.6 %fusion.30 = bf16[256,2,8,64]{0,3,2,1:T(8,128)(2,1)S(1)} fusion(bf16[256,2,8,64]{0,3,2,1:T(8,128)(2,1)S(1)} %bitcast.195, f32[2,8,256]{2,1,0:T(8,128)S(1)} %get-tuple-element.104, f32[2,8,256]{2,1,0:T(8,128)S(1)} %bitcast.202, f32[2,256,256]{2,1,0:T(8,128)S(1)} %copy-done.3, pred[256,256]{1,0:T(8,128)(4,1)} %copy-done.13, ...), kind=kOutput, calls=%fused_computation.35 | convolution fusion | flops 142082048 | bytes 2736192 | tf_op jit(solution)/shard_map/jvp(ghts,sghp->tghp)/dot_general | solution.py:118
  77.0 0.7 copy.139
  79.3 1.1 %bitcast_convert_fusion = f32[256,2,512]{0,2,1:T(8,128)} fusion(bf16[256,2,8,64]{0,3,2,1:T(8,128)(2,1)S(1)} %copy-done.2), kind=kLoop, calls=%fused_computation.77 | loop fusion | flops 262144 | bytes 1572864 | tf_op jit(solution)/shard_map/convert_element_type | solution.py:79
  80.4 1.6 %copy.129 = f32[256,2,512]{2,0,1:T(8,128)S(1)} copy(f32[256,2,512]{0,2,1:T(8,128)} %bitcast_convert_fusion) | data formatting | bytes 2097152 | tf_op jit(solution)/shard_map/convert_element_type | solution.py:79
  83.3 1.3 %collective-permute-start.7 = (f32[3,2,640]{2,1,0:T(2,128)S(1)}, f32[3,2,640]{2,1,0:T(2,128)S(1)}, u32[]{:S(2)}, u32[]{:S(2)}) collective-permute-start(f32[3,2,640]{2,1,0:T(2,128)S(1)} %pad_maximum_fusion.9), channel_id=1, source_target_pairs={{2,0},{4,2},{6,4},{8,6},{10,8},{12,10},{14,12},{3,1},{5,3},{7,5},{... | collective-permute-start | bytes 46088 | tf_op jit(solution)/shard_map/ppermute | solution.py:12
  85.2 0.8 fusion.64
  86.4 1.2 %copy.140 = bf16[256,2,512]{2,1,0:T(2,128)(2,1)} copy(bf16[256,2,512]{0,2,1:T(8,128)(2,1)S(1)} %bitcast.196) | data formatting | bytes 1048576
  87.5 1.4 %collective-permute-done.7 = f32[3,2,640]{2,1,0:T(2,128)S(1)} collective-permute-done((f32[3,2,640]{2,1,0:T(2,128)S(1)}, f32[3,2,640]{2,1,0:T(2,128)S(1)}, u32[]{:S(2)}, u32[]{:S(2)}) %collective-permute-start.7) | collective-permute-done | bytes 15392 | tf_op jit(solution)/shard_map/ppermute | solution.py:12
  89.1 1.3 %copy.141 = bf16[256,2,512]{2,1,0:T(2,128)(2,1)} copy(bf16[256,2,512]{2,0,1:T(8,128)(2,1)S(1)} %scatter-add.14) | data formatting | bytes 1048576
  92.0 0.6 copy-done.14
  (190 shorter events, 9.1 us)
Async XLA Ops:
  0.6 14.3 %copy-start.4 = (bf16[256,2,512]{2,1,0:T(2,128)(2,1)S(1)}, bf16[256,2,512]{2,1,0:T(2,128)(2,1)}, u32[]{:S(2)}) copy-start(bf16[256,2,512]{2,1,0:T(2,128)(2,1)} %param.30) | copy-start | bytes 1572868
  3.4 12.1 %collective-permute-start = (bf16[3,2,640]{2,0,1:T(4,128)(2,1)S(1)}, bf16[3,2,640]{2,0,1:T(4,128)(2,1)S(1)}, u32[]{:S(2)}, u32[]{:S(2)}) collective-permute-start(bf16[3,2,640]{2,0,1:T(4,128)(2,1)S(1)} %copy.120), channel_id=1, source_target_pairs={{0,2},{2,4},{4,6},{6,8},{8,10},{10,12},{12,14},{1,3},{3,5},{5,7},{... | collective-permute-start | bytes 23048 | tf_op jit(solution)/shard_map/ppermute | solution.py:12
  8.9 6.5 %copy-start.54 = (f32[2,8]{1,0:T(2,128)}, f32[2,8]{1,0:T(2,128)S(1)}, u32[]{:S(2)}) copy-start(f32[2,8]{1,0:T(2,128)S(1)} %neg.30) | copy-start | bytes 196
  9.7 6.2 %copy-start.40 = (f32[2,64]{1,0:T(2,128)}, f32[2,64]{1,0:T(2,128)S(1)}, u32[]{:S(2)}) copy-start(f32[2,64]{1,0:T(2,128)S(1)} %get-tuple-element.118) | copy-start | bytes 1540
  9.7 6.2 %copy-start.42 = (f32[2,64]{1,0:T(2,128)}, f32[2,64]{1,0:T(2,128)S(1)}, u32[]{:S(2)}) copy-start(f32[2,64]{1,0:T(2,128)S(1)} %get-tuple-element.119) | copy-start | bytes 1540
  9.7 6.2 %copy-start.44 = (f32[2,64]{1,0:T(2,128)}, f32[2,64]{1,0:T(2,128)S(1)}, u32[]{:S(2)}) copy-start(f32[2,64]{1,0:T(2,128)S(1)} %get-tuple-element.120) | copy-start | bytes 1540
  9.7 6.2 %copy-start.46 = (f32[2,64]{1,0:T(2,128)}, f32[2,64]{1,0:T(2,128)S(1)}, u32[]{:S(2)}) copy-start(f32[2,64]{1,0:T(2,128)S(1)} %get-tuple-element.121) | copy-start | bytes 1540
  10.4 5.4 %copy-start.32 = (f32[2,64]{1,0:T(2,128)}, f32[2,64]{1,0:T(2,128)S(1)}, u32[]{:S(2)}) copy-start(f32[2,64]{1,0:T(2,128)S(1)} %get-tuple-element.122) | copy-start | bytes 1540
  10.4 5.4 %copy-start.34 = (f32[2,64]{1,0:T(2,128)}, f32[2,64]{1,0:T(2,128)S(1)}, u32[]{:S(2)}) copy-start(f32[2,64]{1,0:T(2,128)S(1)} %get-tuple-element.123) | copy-start | bytes 1540
  10.4 5.4 %copy-start.36 = (f32[2,64]{1,0:T(2,128)}, f32[2,64]{1,0:T(2,128)S(1)}, u32[]{:S(2)}) copy-start(f32[2,64]{1,0:T(2,128)S(1)} %get-tuple-element.124) | copy-start | bytes 1540
  10.4 5.5 %copy-start.38 = (f32[2,64]{1,0:T(2,128)}, f32[2,64]{1,0:T(2,128)S(1)}, u32[]{:S(2)}) copy-start(f32[2,64]{1,0:T(2,128)S(1)} %get-tuple-element.125) | copy-start | bytes 1540
  12.3 5.5 %copy-start.18 = (f32[2,512]{1,0:T(2,128)}, f32[2,512]{1,0:T(2,128)S(1)}, u32[]{:S(2)}) copy-start(f32[2,512]{1,0:T(2,128)S(1)} %get-tuple-element.108) | copy-start | bytes 12292
  12.3 5.5 %copy-start.20 = (f32[2,512]{1,0:T(2,128)}, f32[2,512]{1,0:T(2,128)S(1)}, u32[]{:S(2)}) copy-start(f32[2,512]{1,0:T(2,128)S(1)} %get-tuple-element.109) | copy-start | bytes 12292
  12.3 5.5 %copy-start.22 = (f32[2,512]{1,0:T(2,128)}, f32[2,512]{1,0:T(2,128)S(1)}, u32[]{:S(2)}) copy-start(f32[2,512]{1,0:T(2,128)S(1)} %get-tuple-element.110) | copy-start | bytes 12292
  12.3 5.5 %copy-start.24 = (f32[2,512]{1,0:T(2,128)}, f32[2,512]{1,0:T(2,128)S(1)}, u32[]{:S(2)}) copy-start(f32[2,512]{1,0:T(2,128)S(1)} %get-tuple-element.111) | copy-start | bytes 12292
  13.2 45.8 %copy-start.7 = (f32[256,2,8]{0,2,1:T(8,128)}, f32[256,2,8]{0,2,1:T(8,128)S(1)}, u32[]{:S(2)}) copy-start(f32[256,2,8]{0,2,1:T(8,128)S(1)} %get-tuple-element.107) | copy-start | bytes 49156
  19.1 6.5 %copy-start.28 = (f32[2,8]{1,0:T(2,128)S(1)}, f32[2,8]{1,0:T(2,128)}, u32[]{:S(2)}) copy-start(f32[2,8]{1,0:T(2,128)} %get-tuple-element.128) | copy-start | bytes 196
  19.5 6.0 %collective-permute-start.1 = (bf16[2,8,4224]{2,1,0:T(8,128)(2,1)S(1)}, bf16[2,8,4224]{2,1,0:T(8,128)(2,1)S(1)}, u32[]{:S(2)}, u32[]{:S(2)}) collective-permute-start(bf16[2,8,4224]{2,1,0:T(8,128)(2,1)S(1)} %get-tuple-element.116), channel_id=1, source_target_pairs={{0,2},{2,4},{4,6},{6,8},{8,10},{10,12},{12,14},{1,3},{3,5},{5,7},{... | collective-permute-start | bytes 405512 | tf_op jit(solution)/shard_map/ppermute | solution.py:27
  23.0 6.9 %collective-permute-start.4 = (bf16[2,8,4224]{2,1,0:T(8,128)(2,1)S(1)}, bf16[2,8,4224]{2,1,0:T(8,128)(2,1)S(1)}, u32[]{:S(2)}, u32[]{:S(2)}) collective-permute-start(bf16[2,8,4224]{2,1,0:T(8,128)(2,1)S(1)} %get-tuple-element.117), channel_id=1, source_target_pairs={{2,0},{4,2},{6,4},{8,6},{10,8},{12,10},{14,12},{3,1},{5,3},{7,5},{... | collective-permute-start | bytes 405512 | tf_op jit(solution)/shard_map/ppermute | solution.py:27
  30.2 6.4 %collective-permute-start.2 = (bf16[2,8,4224]{2,1,0:T(8,128)(2,1)S(1)}, bf16[2,8,4224]{2,1,0:T(8,128)(2,1)S(1)}, u32[]{:S(2)}, u32[]{:S(2)}) collective-permute-start(bf16[2,8,4224]{2,1,0:T(8,128)(2,1)S(1)} %pad_maximum_fusion.3), channel_id=1, source_target_pairs={{0,4},{2,6},{4,8},{6,10},{8,12},{10,14},{1,5},{3,7},{5,9},{7,11},{... | collective-permute-start | bytes 405512 | tf_op jit(solution)/shard_map/ppermute | solution.py:27
  34.1 37.9 %copy-start.13 = (pred[256,256]{1,0:T(8,128)(4,1)}, pred[256,256]{1,0:T(8,128)(4,1)S(1)}, u32[]{:S(2)}) copy-start(pred[256,256]{1,0:T(8,128)(4,1)S(1)} %iota_compare_fusion) | copy-start | bytes 196612
  36.8 7.3 %collective-permute-start.5 = (bf16[2,8,4224]{2,1,0:T(8,128)(2,1)S(1)}, bf16[2,8,4224]{2,1,0:T(8,128)(2,1)S(1)}, u32[]{:S(2)}, u32[]{:S(2)}) collective-permute-start(bf16[2,8,4224]{2,1,0:T(8,128)(2,1)S(1)} %pad_maximum_fusion.5), channel_id=1, source_target_pairs={{4,0},{6,2},{8,4},{10,6},{12,8},{14,10},{5,1},{7,3},{9,5},{11,7},{... | collective-permute-start | bytes 405512 | tf_op jit(solution)/shard_map/ppermute | solution.py:27
  44.6 7.5 %collective-permute-start.3 = (bf16[2,8,4224]{2,1,0:T(8,128)(2,1)S(1)}, bf16[2,8,4224]{2,1,0:T(8,128)(2,1)S(1)}, u32[]{:S(2)}, u32[]{:S(2)}) collective-permute-start(bf16[2,8,4224]{2,1,0:T(8,128)(2,1)S(1)} %pad_maximum_fusion.4), channel_id=1, source_target_pairs={{0,8},{2,10},{4,12},{6,14},{1,9},{3,11},{5,13},{7,15},{16,24},{18,... | collective-permute-start | bytes 405512 | tf_op jit(solution)/shard_map/ppermute | solution.py:27
  49.7 8.3 %collective-permute-start.6 = (bf16[2,8,4224]{2,1,0:T(8,128)(2,1)S(1)}, bf16[2,8,4224]{2,1,0:T(8,128)(2,1)S(1)}, u32[]{:S(2)}, u32[]{:S(2)}) collective-permute-start(bf16[2,8,4224]{2,1,0:T(8,128)(2,1)S(1)} %pad_maximum_fusion.6), channel_id=1, source_target_pairs={{8,0},{10,2},{12,4},{14,6},{9,1},{11,3},{13,5},{15,7},{24,16},{26,... | collective-permute-start | bytes 405512 | tf_op jit(solution)/shard_map/ppermute | solution.py:27
  62.5 2.3 %copy-start.16 = (f32[256,2,8]{0,2,1:T(8,128)S(1)}, f32[256,2,8]{0,2,1:T(8,128)}, u32[]{:S(2)}) copy-start(f32[256,2,8]{0,2,1:T(8,128)} %param.23) | copy-start | bytes 49156
  62.5 2.3 %copy-start.30 = (f32[2,8]{1,0:T(2,128)S(1)}, f32[2,8]{1,0:T(2,128)}, u32[]{:S(2)}) copy-start(f32[2,8]{1,0:T(2,128)} %copy-done.29) | copy-start | bytes 196
  62.5 2.3 %copy-start.49 = (f32[2,8]{1,0:T(2,128)S(1)}, f32[2,8]{1,0:T(2,128)}, u32[]{:S(2)}) copy-start(f32[2,8]{1,0:T(2,128)} %param.25) | copy-start | bytes 196
  64.1 7.8 %copy-start.11 = (f32[256,2,8]{0,2,1:T(8,128)}, f32[256,2,8]{0,2,1:T(8,128)S(1)}, u32[]{:S(2)}) copy-start(f32[256,2,8]{0,2,1:T(8,128)S(1)} %get-tuple-element.130) | copy-start | bytes 49156
  66.0 5.9 %copy-start.1 = (f32[256,2,8,64]{0,3,2,1:T(8,128)S(1)}, f32[256,2,8,64]{0,3,2,1:T(8,128)}, u32[]{:S(2)}) copy-start(f32[256,2,8,64]{0,3,2,1:T(8,128)} %get-tuple-element.131) | copy-start | bytes 3145732
  66.0 5.9 %copy-start.3 = (f32[2,256,256]{2,1,0:T(8,128)S(1)}, f32[2,256,256]{2,1,0:T(8,128)}, u32[]{:S(2)}) copy-start(f32[2,256,256]{2,1,0:T(8,128)} %fusion.132) | copy-start | bytes 1572868
  66.0 5.9 %copy-start.56 = (f32[2,8]{1,0:T(2,128)S(1)}, f32[2,8]{1,0:T(2,128)}, u32[]{:S(2)}) copy-start(f32[2,8]{1,0:T(2,128)} %param.26) | copy-start | bytes 196
  72.0 2.4 %copy-start = (f32[256,2,8,64]{0,3,2,1:T(8,128)S(1)}, f32[256,2,8,64]{0,3,2,1:T(8,128)}, u32[]{:S(2)}) copy-start(f32[256,2,8,64]{0,3,2,1:T(8,128)} %get-tuple-element.133) | copy-start | bytes 3145732
  72.0 2.4 %copy-start.8 = (f32[256,2,8]{0,2,1:T(8,128)S(1)}, f32[256,2,8]{0,2,1:T(8,128)}, u32[]{:S(2)}) copy-start(f32[256,2,8]{0,2,1:T(8,128)} %copy-done.7) | copy-start | bytes 49156
  74.3 2.6 %copy-start.52 = (f32[2,8]{1,0:T(2,128)S(1)}, f32[2,8]{1,0:T(2,128)}, u32[]{:S(2)}) copy-start(f32[2,8]{1,0:T(2,128)} %get-tuple-element.103) | copy-start | bytes 196
  74.3 3.3 %copy-start.6 = (f32[256,2,64]{0,2,1:T(8,128)S(1)}, f32[256,2,64]{0,2,1:T(8,128)}, u32[]{:S(2)}) copy-start(f32[256,2,64]{0,2,1:T(8,128)} %get-tuple-element.98) | copy-start | bytes 393220
  74.3 3.7 %copy-start.41 = (f32[2,64]{1,0:T(2,128)S(1)}, f32[2,64]{1,0:T(2,128)}, u32[]{:S(2)}) copy-start(f32[2,64]{1,0:T(2,128)} %copy-done.40) | copy-start | bytes 1540
  74.4 3.7 %copy-start.43 = (f32[2,64]{1,0:T(2,128)S(1)}, f32[2,64]{1,0:T(2,128)}, u32[]{:S(2)}) copy-start(f32[2,64]{1,0:T(2,128)} %copy-done.42) | copy-start | bytes 1540
  74.4 3.7 %copy-start.45 = (f32[2,64]{1,0:T(2,128)S(1)}, f32[2,64]{1,0:T(2,128)}, u32[]{:S(2)}) copy-start(f32[2,64]{1,0:T(2,128)} %copy-done.44) | copy-start | bytes 1540
  74.4 3.7 %copy-start.47 = (f32[2,64]{1,0:T(2,128)S(1)}, f32[2,64]{1,0:T(2,128)}, u32[]{:S(2)}) copy-start(f32[2,64]{1,0:T(2,128)} %copy-done.46) | copy-start | bytes 1540
  82.7 2.2 %copy-start.17 = (f32[256,2,8]{0,2,1:T(8,128)S(1)}, f32[256,2,8]{0,2,1:T(8,128)}, u32[]{:S(2)}) copy-start(f32[256,2,8]{0,2,1:T(8,128)} %param.23) | copy-start | bytes 49156
  82.7 2.2 %copy-start.31 = (f32[2,8]{1,0:T(2,128)S(1)}, f32[2,8]{1,0:T(2,128)}, u32[]{:S(2)}) copy-start(f32[2,8]{1,0:T(2,128)} %copy-done.29) | copy-start | bytes 196
  82.7 2.2 %copy-start.48 = (f32[1,2,8]{0,2,1:T(8,128)S(1)}, f32[1,2,8]{0,2,1:T(8,128)}, u32[]{:S(2)}) copy-start(f32[1,2,8]{0,2,1:T(8,128)} %copy.139) | copy-start | bytes 196
  82.7 2.2 %copy-start.50 = (f32[2,8]{1,0:T(2,128)S(1)}, f32[2,8]{1,0:T(2,128)}, u32[]{:S(2)}) copy-start(f32[2,8]{1,0:T(2,128)} %param.25) | copy-start | bytes 196
  82.7 2.2 %copy-start.55 = (f32[2,8]{1,0:T(2,128)S(1)}, f32[2,8]{1,0:T(2,128)}, u32[]{:S(2)}) copy-start(f32[2,8]{1,0:T(2,128)} %copy-done.54) | copy-start | bytes 196
  82.7 2.5 %copy-start.57 = (f32[2,8,256]{2,1,0:T(8,128)S(1)}, f32[2,8,256]{2,1,0:T(8,128)}, u32[]{:S(2)}) copy-start(f32[2,8,256]{2,1,0:T(8,128)} %get-tuple-element.82) | copy-start | bytes 49156
  82.7 2.5 %copy-start.58 = (f32[2,8,256]{2,1,0:T(8,128)S(1)}, f32[2,8,256]{2,1,0:T(8,128)}, u32[]{:S(2)}) copy-start(f32[2,8,256]{2,1,0:T(8,128)} %get-tuple-element.83) | copy-start | bytes 49156
  82.8 2.5 %copy-start.59 = (f32[2,8,256]{2,1,0:T(8,128)S(1)}, f32[2,8,256]{2,1,0:T(8,128)}, u32[]{:S(2)}) copy-start(f32[2,8,256]{2,1,0:T(8,128)} %get-tuple-element.84) | copy-start | bytes 49156
  83.3 5.6 %collective-permute-start.7 = (f32[3,2,640]{2,1,0:T(2,128)S(1)}, f32[3,2,640]{2,1,0:T(2,128)S(1)}, u32[]{:S(2)}, u32[]{:S(2)}) collective-permute-start(f32[3,2,640]{2,1,0:T(2,128)S(1)} %pad_maximum_fusion.9), channel_id=1, source_target_pairs={{2,0},{4,2},{6,4},{8,6},{10,8},{12,10},{14,12},{3,1},{5,3},{7,5},{... | collective-permute-start | bytes 46088 | tf_op jit(solution)/shard_map/ppermute | solution.py:12
  (20 other events, 25.4 us)

commit v16 on v15

--- a/solution.py
+++ b/solution.py
@@ -191,9 +191,14 @@
     back_x = returned[:, :, :channels]
     back_b = returned[:, :, channels : channels + state_size]
     back_c = returned[:, :, channels + state_size :]
-    grad_x = grad_x_ext[halo_rows:].at[length - halo_rows :].add(back_x).astype(jnp.bfloat16)
-    grad_b = grad_b_ext[halo_rows:].at[length - halo_rows :].add(back_b).astype(jnp.bfloat16)
-    grad_c = grad_c_ext[halo_rows:].at[length - halo_rows :].add(back_c).astype(jnp.bfloat16)
+    def settle(grad_ext, back):
+        edge = grad_ext[length : length + halo_rows] + back
+        whole = lax.dynamic_update_slice_in_dim(grad_ext, edge, length, 0)
+        return whole[halo_rows:].astype(jnp.bfloat16)
+
+    grad_x = settle(grad_x_ext, back_x)
+    grad_b = settle(grad_b_ext, back_b)
+    grad_c = settle(grad_c_ext, back_c)
     return (y_out, grad_x, grad_b, grad_c, grad_dt)
 
 

time: 93.4 us -> 93.1 us (level)
    slice x3, local copies, waits for them, and re-layouts: 0.3 us -> 1.57 us  [settle(): return whole[halo_rows:].astype(jnp.bfloat16)]
    scatter-add x3 -> x0, local copies, waits for them, and re-layouts: 1.21 us -> none  [the longest x1 0.53 us: on_device(): grad_c_ext[halo_rows:].at[length - halo_rows:].add(back_c)]
    unnamed x128 -> x124, local copies, waits for them, and re-layouts: 5.99 us -> 5.27 us
where the time goes in v16:
time: 93.1 us; the launch traced here: 92.3 us
  starting transfers between devices  22.4 us (24%)
  waiting for transfers between devices  21.3 us (23%)
  matrix products  20.4 us (22%)
  local copies, waits for them, and re-layouts  16.7 us (18%)
  other arithmetic  9.82 us (11%)
  between operations  1.61 us (2%)
    ppermute x6, waiting for transfers between devices, shift(): return lax.ppermute(packed, axis, pairs)  19.5 us
    ppermute x6, starting transfers between devices, shift(): return lax.ppermute(packed, axis, pairs)  16.3 us
    dot_general x3, matrix products, ssd_mix(): jnp.einsum('ghts,sghp->tghp', mixing, x_half, preferred_element_type=jnp....  10.8 us
    ppermute x2, starting transfers between devices, from_behind(): return lax.ppermute(array, axis, pairs)  6.12 us
    unnamed x124, local copies, waits for them, and re-layouts  5.27 us
    dot_general x2, matrix products, carry_in(): carried = jnp.einsum('tgn,ghpn->tghp', c_float, state_in, precision=HIGH)  2.68 us
    dot_general x3, matrix products, ssd_state(): jnp.einsum('sghp,sgn->ghpn', weighted.astype(jnp.float32), b_float, preci...  2.5 us
    mul x3, local copies, waits for them, and re-layouts, conv_forward(): running = weight[0] * extended[0:length].astype(jnp.float32)  2.21 us
  transfers between devices with their start and end apart: 8, of which 7 were waited for; matrix products, arithmetic and copies ran while one was open for 12% of the time, Pallas kernels for 0%

profile of v16, /device:TPU:0, one launch (start us, length us, event | category | flops | bytes accessed | tf_op | source)
XLA Modules:
  0.0 92.3 jit_solution(13569731367478404849)
XLA Ops:
  0.6 0.8 slice.231
  1.4 0.8 slice.232
  2.3 0.8 slice.233
  3.4 4.8 %collective-permute-start = (bf16[3,2,640]{2,0,1:T(4,128)(2,1)S(1)}, bf16[3,2,640]{2,0,1:T(4,128)(2,1)S(1)}, u32[]{:S(2)}, u32[]{:S(2)}) collective-permute-start(bf16[3,2,640]{2,0,1:T(4,128)(2,1)S(1)} %copy.120), channel_id=1, source_target_pairs={{0,2},{2,4},{4,6},{6,8},{8,10},{10,12},{12,14},{1,3},{3,5},{5,7},{... | collective-permute-start | bytes 23048 | tf_op jit(solution)/shard_map/ppermute | solution.py:12
  8.2 0.7 neg.30
  8.9 0.7 slice_bitcast_fusion.7
  9.7 0.7 slice_bitcast_fusion.11
  10.4 0.9 %fusion.78 = f32[256,16]{0,1:S(1)} fusion(f32[2,8]{1,0:T(2,128)S(1)} %neg.30, f32[256,2,8]{0,2,1:T(8,128)} %param.17, f32[2,8]{1,0:T(2,128)} %param.19), kind=kOutput, calls=%fused_computation.98 | convolution fusion | flops 12681216 | bytes 32896
  11.6 0.7 slice_bitcast_fusion.3
  12.3 0.8 fusion.118
  13.2 0.6 fusion.134
  13.8 1.1 %copy.121 = bf16[256,2,512]{2,0,1:T(8,128)(2,1)S(1)} copy(bf16[256,2,512]{2,1,0:T(2,128)(2,1)} %param.14) | data formatting | bytes 1048576 | tf_op args[0]
  15.9 1.0 %multiply_convert_fusion.1 = (bf16[256,2,64]{0,2,1:T(8,128)(2,1)S(1)}, f32[256,2,64]{0,2,1:T(8,128)}, bf16[256,2,64]{0,2,1:T(8,128)(2,1)S(1)}, f32[256,2,64]{0,2,1:T(8,128)}) fusion(bf16[256,2,64]{0,2,1:T(8,128)(2,1)S(1)} %copy-done.10, f32[2,64]{1,0:T(2,128)S(1)} %get-tuple-element.84, bf16[3,2,64]{0,2,1:T(8,128)(2,1)S(1)} %copy.125, ...), kind=kLoop, calls=%fused_computation.121 | loop fusion | flops 1638400 | bytes 529920 | tf_op jit(solution)/shard_map/convert_element_type | solution.py:159
  16.9 0.6 fusion.52
  17.9 0.7 multiply_convert_fusion
  19.5 3.5 %collective-permute-start.1 = (bf16[2,8,4224]{2,1,0:T(8,128)(2,1)S(1)}, bf16[2,8,4224]{2,1,0:T(8,128)(2,1)S(1)}, u32[]{:S(2)}, u32[]{:S(2)}) collective-permute-start(bf16[2,8,4224]{2,1,0:T(8,128)(2,1)S(1)} %get-tuple-element.80), channel_id=1, source_target_pairs={{0,2},{2,4},{4,6},{6,8},{8,10},{10,12},{12,14},{1,3},{3,5},{5,7},{... | collective-permute-start | bytes 405512 | tf_op jit(solution)/shard_map/ppermute | solution.py:27
  23.0 1.3 %collective-permute-start.4 = (bf16[2,8,4224]{2,1,0:T(8,128)(2,1)S(1)}, bf16[2,8,4224]{2,1,0:T(8,128)(2,1)S(1)}, u32[]{:S(2)}, u32[]{:S(2)}) collective-permute-start(bf16[2,8,4224]{2,1,0:T(8,128)(2,1)S(1)} %get-tuple-element.81), channel_id=1, source_target_pairs={{2,0},{4,2},{6,4},{8,6},{10,8},{12,10},{14,12},{3,1},{5,3},{7,5},{... | collective-permute-start | bytes 405512 | tf_op jit(solution)/shard_map/ppermute | solution.py:27
  24.3 1.2 %collective-permute-done.1 = bf16[2,8,4224]{2,1,0:T(8,128)(2,1)S(1)} collective-permute-done((bf16[2,8,4224]{2,1,0:T(8,128)(2,1)S(1)}, bf16[2,8,4224]{2,1,0:T(8,128)(2,1)S(1)}, u32[]{:S(2)}, u32[]{:S(2)}) %collective-permute-start.1) | collective-permute-done | bytes 135200 | tf_op jit(solution)/shard_map/ppermute | solution.py:27
  25.7 4.2 %collective-permute-done.4 = bf16[2,8,4224]{2,1,0:T(8,128)(2,1)S(1)} collective-permute-done((bf16[2,8,4224]{2,1,0:T(8,128)(2,1)S(1)}, bf16[2,8,4224]{2,1,0:T(8,128)(2,1)S(1)}, u32[]{:S(2)}, u32[]{:S(2)}) %collective-permute-start.4) | collective-permute-done | bytes 135200 | tf_op jit(solution)/shard_map/ppermute | solution.py:27
  30.2 3.8 %collective-permute-start.2 = (bf16[2,8,4224]{2,1,0:T(8,128)(2,1)S(1)}, bf16[2,8,4224]{2,1,0:T(8,128)(2,1)S(1)}, u32[]{:S(2)}, u32[]{:S(2)}) collective-permute-start(bf16[2,8,4224]{2,1,0:T(8,128)(2,1)S(1)} %pad_maximum_fusion.3), channel_id=1, source_target_pairs={{0,4},{2,6},{4,8},{6,10},{8,12},{10,14},{1,5},{3,7},{5,9},{7,11},{... | collective-permute-start | bytes 405512 | tf_op jit(solution)/shard_map/ppermute | solution.py:27
  34.1 2.5 %collective-permute-done.2 = bf16[2,8,4224]{2,1,0:T(8,128)(2,1)S(1)} collective-permute-done((bf16[2,8,4224]{2,1,0:T(8,128)(2,1)S(1)}, bf16[2,8,4224]{2,1,0:T(8,128)(2,1)S(1)}, u32[]{:S(2)}, u32[]{:S(2)}) %collective-permute-start.2) | collective-permute-done | bytes 135200 | tf_op jit(solution)/shard_map/ppermute | solution.py:27
  36.8 1.3 %collective-permute-start.5 = (bf16[2,8,4224]{2,1,0:T(8,128)(2,1)S(1)}, bf16[2,8,4224]{2,1,0:T(8,128)(2,1)S(1)}, u32[]{:S(2)}, u32[]{:S(2)}) collective-permute-start(bf16[2,8,4224]{2,1,0:T(8,128)(2,1)S(1)} %pad_maximum_fusion.5), channel_id=1, source_target_pairs={{4,0},{6,2},{8,4},{10,6},{12,8},{14,10},{5,1},{7,3},{9,5},{11,7},{... | collective-permute-start | bytes 405512 | tf_op jit(solution)/shard_map/ppermute | solution.py:27
  38.1 1.1 %fusion.135 = f32[2,256,256]{2,1,0:T(8,128)} fusion(bf16[256,2,64]{0,2,1:T(8,128)(2,1)S(1)} %get-tuple-element.98, bf16[256,2,64]{0,2,1:T(8,128)(2,1)S(1)} %get-tuple-element.61), kind=kOutput, calls=%fused_computation.214 | convolution fusion | flops 16777216 | bytes 655360 | tf_op jit(solution)/shard_map/jvp(tgn,sgn->gts)/dot_general | solution.py:116
  39.2 5.0 %collective-permute-done.5 = bf16[2,8,4224]{2,1,0:T(8,128)(2,1)S(1)} collective-permute-done((bf16[2,8,4224]{2,1,0:T(8,128)(2,1)S(1)}, bf16[2,8,4224]{2,1,0:T(8,128)(2,1)S(1)}, u32[]{:S(2)}, u32[]{:S(2)}) %collective-permute-start.5) | collective-permute-done | bytes 135200 | tf_op jit(solution)/shard_map/ppermute | solution.py:27
  44.6 4.9 %collective-permute-start.3 = (bf16[2,8,4224]{2,1,0:T(8,128)(2,1)S(1)}, bf16[2,8,4224]{2,1,0:T(8,128)(2,1)S(1)}, u32[]{:S(2)}, u32[]{:S(2)}) collective-permute-start(bf16[2,8,4224]{2,1,0:T(8,128)(2,1)S(1)} %pad_maximum_fusion.4), channel_id=1, source_target_pairs={{0,8},{2,10},{4,12},{6,14},{1,9},{3,11},{5,13},{7,15},{16,24},{18,... | collective-permute-start | bytes 405512 | tf_op jit(solution)/shard_map/ppermute | solution.py:27
  49.6 1.5 %collective-permute-start.6 = (bf16[2,8,4224]{2,1,0:T(8,128)(2,1)S(1)}, bf16[2,8,4224]{2,1,0:T(8,128)(2,1)S(1)}, u32[]{:S(2)}, u32[]{:S(2)}) collective-permute-start(bf16[2,8,4224]{2,1,0:T(8,128)(2,1)S(1)} %pad_maximum_fusion.6), channel_id=1, source_target_pairs={{8,0},{10,2},{12,4},{14,6},{9,1},{11,3},{13,5},{15,7},{24,16},{26,... | collective-permute-start | bytes 405512 | tf_op jit(solution)/shard_map/ppermute | solution.py:27
  51.3 0.8 collective-permute-done.3
  52.1 5.8 %collective-permute-done.6 = bf16[2,8,4224]{2,1,0:T(8,128)(2,1)S(1)} collective-permute-done((bf16[2,8,4224]{2,1,0:T(8,128)(2,1)S(1)}, bf16[2,8,4224]{2,1,0:T(8,128)(2,1)S(1)}, u32[]{:S(2)}, u32[]{:S(2)}) %collective-permute-start.6) | collective-permute-done | bytes 135200 | tf_op jit(solution)/shard_map/ppermute | solution.py:27
  57.9 0.8 multiply_reduce_fusion
  59.0 1.1 %convolution_bitcast_fusion.3 = f32[2,256,64]{1,2,0:T(8,128)S(1)} fusion(f32[2,8,64,64]{3,2,1,0:T(8,128)S(1)} %reshape.127, bf16[256,2,8,64]{0,3,2,1:T(8,128)(2,1)S(1)} %bitcast.188, f32[256,2,8]{0,2,1:T(8,128)S(1)} %get-tuple-element.71), kind=kOutput, calls=%fused_computation.48 | convolution fusion | flops 201850880 | bytes 933888 | tf_op jit(solution)/shard_map/transpose(jvp(tgn,ghpn->tghp))/dot_general | solution.py:135
  60.0 1.6 %fusion.70 = (f32[256,2,8]{0,2,1:T(8,128)S(1)}, f32[256,2,8,64]{0,3,2,1:T(8,128)}) fusion(bf16[256,2,512]{0,2,1:T(8,128)(2,1)S(1)} %copy.127, f32[2,8,64,64]{3,2,1,0:T(8,128)S(1)} %reshape.127, bf16[256,2,64]{0,2,1:T(8,128)(2,1)S(1)} %get-tuple-element.98), kind=kOutput, calls=%fused_computation.67 | convolution fusion | flops 202108928 | bytes 1916928 | tf_op jit(solution)/shard_map/jvp(tgn,ghpn->tghp)/dot_general | solution.py:135
  61.9 0.6 convolution_bitcast_fusion.2
  62.5 1.6 %fusion.69 = (f32[256,2,8]{0,2,1:T(8,128)S(1)}, f32[256,2,8,64]{0,3,2,1:T(8,128)}) fusion(bf16[256,2,512]{0,2,1:T(8,128)(2,1)S(1)} %copy.123, f32[2,8,64,64]{3,2,1,0:T(8,128)S(1)} %reshape.131, bf16[256,2,64]{0,2,1:T(8,128)(2,1)S(1)} %get-tuple-element.61), kind=kOutput, calls=%fused_computation.66 | convolution fusion | flops 202633216 | bytes 1916928 | tf_op jit(solution)/shard_map/transpose(jvp(sghp,sgn->ghpn))/dot_general | solution.py:130
  64.1 0.7 copy.138
  64.8 1.3 %fusion.119 = (f32[2,8]{1,0:T(2,128)}, f32[2,8,256]{2,1,0:T(8,128)S(1)}, f32[256,2,8]{0,2,1:T(8,128)}) fusion(f32[256,2,8]{0,2,1:T(8,128)S(1)} %get-tuple-element.94, f32[2,8]{1,0:T(2,128)S(1)} %copy-done.28, f32[256,16]{0,1:S(1)} %fusion.78, f32[256,2,8]{0,2,1:T(8,128)S(1)} %copy-done.14, f32[2,8]{1,0:T(2,128)S(1)} %copy-done.47, ...), kind=kLoop, calls=%fused_computation.172 | loop fusion | flops 49136 | bytes 98496 | tf_op jit(solution)/shard_map/transpose(jvp())/reduce_sum | solution.py:128
  66.1 5.9 %fusion.18 = (f32[2,8,256]{2,1,0:T(8,128)}, f32[2,8,256]{2,1,0:T(8,128)}, f32[2,8,256]{2,1,0:T(8,128)}, f32[2,256,256]{2,1,0:T(8,128)S(1)}) fusion(f32[2,8,256]{2,1,0:T(8,128)S(1)} %bitcast.200, f32[2,8,256]{2,1,0:T(8,128)S(1)} %get-tuple-element.68, f32[2,256,256]{2,1,0:T(8,128)} %fusion.135, pred[256,256]{1,0:T(8,128)(4,1)S(1)} %iota_compare_fusion, ...), kind=kOutput, calls=%fused_computation.27 | convolution fusion | flops 156094464 | bytes 2244608 | tf_op jit(solution)/shard_map/transpose(jvp(ghts,sghp->tghp))/dot_general | solution.py:118
  72.1 2.3 %fusion.48 = bf16[256,2,8,64]{0,3,2,1:T(8,128)(2,1)} fusion(bf16[2,8,64,256]{3,2,1,0:T(8,128)(2,1)S(1)} %bitcast.191, f32[2,8,256]{2,1,0:T(8,128)S(1)} %get-tuple-element.68, f32[2,8,256]{2,1,0:T(8,128)S(1)} %bitcast.201, f32[2,256,256]{2,1,0:T(8,128)S(1)} %copy-done.3, pred[256,256]{1,0:T(8,128)(4,1)S(1)} %iota_compare_fusion, ...), kind=kOutput, calls=%fused_computation.41 | convolution fusion | flops 142606336 | bytes 3260480 | tf_op jit(solution)/shard_map/transpose(jvp(ghts,sghp->tghp))/dot_general | solution.py:118
  74.5 2.6 %fusion.30 = bf16[256,2,8,64]{0,3,2,1:T(8,128)(2,1)S(1)} fusion(bf16[256,2,8,64]{0,3,2,1:T(8,128)(2,1)S(1)} %bitcast.195, f32[2,8,256]{2,1,0:T(8,128)S(1)} %get-tuple-element.68, f32[2,8,256]{2,1,0:T(8,128)S(1)} %bitcast.202, f32[2,256,256]{2,1,0:T(8,128)S(1)} %copy-done.3, pred[256,256]{1,0:T(8,128)(4,1)} %copy-done.13, f32[256,2,8,64]{0,3,2,1:T(8,128)S(1)} %copy-done, ...), kind=kOutput, calls=%fused_computation.35 | convolution fusion | flops 142082048 | bytes 2736192 | tf_op jit(solution)/shard_map/jvp(ghts,sghp->tghp)/dot_general | solution.py:118
  77.0 0.7 copy.139
  79.4 1.1 %bitcast_convert_fusion = f32[256,2,512]{0,2,1:T(8,128)} fusion(bf16[256,2,8,64]{0,3,2,1:T(8,128)(2,1)S(1)} %copy-done.2), kind=kLoop, calls=%fused_computation.78 | loop fusion | flops 262144 | bytes 1572864 | tf_op jit(solution)/shard_map/convert_element_type | solution.py:79
  80.5 1.6 %copy.129 = f32[256,2,512]{2,0,1:T(8,128)S(1)} copy(f32[256,2,512]{0,2,1:T(8,128)} %bitcast_convert_fusion) | data formatting | bytes 2097152 | tf_op jit(solution)/shard_map/convert_element_type | solution.py:79
  83.4 1.3 %collective-permute-start.7 = (f32[3,2,640]{2,1,0:T(2,128)S(1)}, f32[3,2,640]{2,1,0:T(2,128)S(1)}, u32[]{:S(2)}, u32[]{:S(2)}) collective-permute-start(f32[3,2,640]{2,1,0:T(2,128)S(1)} %pad_maximum_fusion.9), channel_id=1, source_target_pairs={{2,0},{4,2},{6,4},{8,6},{10,8},{12,10},{14,12},{3,1},{5,3},{7,5},{... | collective-permute-start | bytes 46088 | tf_op jit(solution)/shard_map/ppermute | solution.py:12
  85.3 0.8 fusion.64
  86.1 1.2 %copy.140 = bf16[256,2,512]{2,1,0:T(2,128)(2,1)} copy(bf16[256,2,512]{0,2,1:T(8,128)(2,1)S(1)} %bitcast.196) | data formatting | bytes 1048576
  87.3 1.8 %collective-permute-done.7 = f32[3,2,640]{2,1,0:T(2,128)S(1)} collective-permute-done((f32[3,2,640]{2,1,0:T(2,128)S(1)}, f32[3,2,640]{2,1,0:T(2,128)S(1)}, u32[]{:S(2)}, u32[]{:S(2)}) %collective-permute-start.7) | collective-permute-done | bytes 15392 | tf_op jit(solution)/shard_map/ppermute | solution.py:12
  89.2 1.3 %copy.141 = bf16[256,2,512]{2,1,0:T(2,128)(2,1)} copy(bf16[256,2,512]{2,0,1:T(8,128)(2,1)S(1)} %slice.513) | data formatting | bytes 1048576
  90.7 0.7 slice.514
  91.6 0.7 slice.515
  (183 shorter events, 8.1 us)
Async XLA Ops:
  0.6 14.3 %copy-start.4 = (bf16[256,2,512]{2,1,0:T(2,128)(2,1)S(1)}, bf16[256,2,512]{2,1,0:T(2,128)(2,1)}, u32[]{:S(2)}) copy-start(bf16[256,2,512]{2,1,0:T(2,128)(2,1)} %param.24) | copy-start | bytes 1572868
  3.4 12.1 %collective-permute-start = (bf16[3,2,640]{2,0,1:T(4,128)(2,1)S(1)}, bf16[3,2,640]{2,0,1:T(4,128)(2,1)S(1)}, u32[]{:S(2)}, u32[]{:S(2)}) collective-permute-start(bf16[3,2,640]{2,0,1:T(4,128)(2,1)S(1)} %copy.120), channel_id=1, source_target_pairs={{0,2},{2,4},{4,6},{6,8},{8,10},{10,12},{12,14},{1,3},{3,5},{5,7},{... | collective-permute-start | bytes 23048 | tf_op jit(solution)/shard_map/ppermute | solution.py:12
  8.9 6.5 %copy-start.52 = (f32[2,8]{1,0:T(2,128)}, f32[2,8]{1,0:T(2,128)S(1)}, u32[]{:S(2)}) copy-start(f32[2,8]{1,0:T(2,128)S(1)} %neg.30) | copy-start | bytes 196
  9.7 6.2 %copy-start.38 = (f32[2,64]{1,0:T(2,128)}, f32[2,64]{1,0:T(2,128)S(1)}, u32[]{:S(2)}) copy-start(f32[2,64]{1,0:T(2,128)S(1)} %get-tuple-element.82) | copy-start | bytes 1540
  9.7 6.2 %copy-start.40 = (f32[2,64]{1,0:T(2,128)}, f32[2,64]{1,0:T(2,128)S(1)}, u32[]{:S(2)}) copy-start(f32[2,64]{1,0:T(2,128)S(1)} %get-tuple-element.83) | copy-start | bytes 1540
  9.7 6.2 %copy-start.42 = (f32[2,64]{1,0:T(2,128)}, f32[2,64]{1,0:T(2,128)S(1)}, u32[]{:S(2)}) copy-start(f32[2,64]{1,0:T(2,128)S(1)} %get-tuple-element.84) | copy-start | bytes 1540
  9.7 6.2 %copy-start.44 = (f32[2,64]{1,0:T(2,128)}, f32[2,64]{1,0:T(2,128)S(1)}, u32[]{:S(2)}) copy-start(f32[2,64]{1,0:T(2,128)S(1)} %get-tuple-element.85) | copy-start | bytes 1540
  10.4 5.4 %copy-start.30 = (f32[2,64]{1,0:T(2,128)}, f32[2,64]{1,0:T(2,128)S(1)}, u32[]{:S(2)}) copy-start(f32[2,64]{1,0:T(2,128)S(1)} %get-tuple-element.86) | copy-start | bytes 1540
  10.4 5.4 %copy-start.32 = (f32[2,64]{1,0:T(2,128)}, f32[2,64]{1,0:T(2,128)S(1)}, u32[]{:S(2)}) copy-start(f32[2,64]{1,0:T(2,128)S(1)} %get-tuple-element.87) | copy-start | bytes 1540
  10.4 5.4 %copy-start.34 = (f32[2,64]{1,0:T(2,128)}, f32[2,64]{1,0:T(2,128)S(1)}, u32[]{:S(2)}) copy-start(f32[2,64]{1,0:T(2,128)S(1)} %get-tuple-element.88) | copy-start | bytes 1540
  10.4 5.5 %copy-start.36 = (f32[2,64]{1,0:T(2,128)}, f32[2,64]{1,0:T(2,128)S(1)}, u32[]{:S(2)}) copy-start(f32[2,64]{1,0:T(2,128)S(1)} %get-tuple-element.89) | copy-start | bytes 1540
  12.3 5.5 %copy-start.16 = (f32[2,512]{1,0:T(2,128)}, f32[2,512]{1,0:T(2,128)S(1)}, u32[]{:S(2)}) copy-start(f32[2,512]{1,0:T(2,128)S(1)} %get-tuple-element.72) | copy-start | bytes 12292
  12.3 5.5 %copy-start.18 = (f32[2,512]{1,0:T(2,128)}, f32[2,512]{1,0:T(2,128)S(1)}, u32[]{:S(2)}) copy-start(f32[2,512]{1,0:T(2,128)S(1)} %get-tuple-element.73) | copy-start | bytes 12292
  12.3 5.5 %copy-start.20 = (f32[2,512]{1,0:T(2,128)}, f32[2,512]{1,0:T(2,128)S(1)}, u32[]{:S(2)}) copy-start(f32[2,512]{1,0:T(2,128)S(1)} %get-tuple-element.74) | copy-start | bytes 12292
  12.3 5.5 %copy-start.22 = (f32[2,512]{1,0:T(2,128)}, f32[2,512]{1,0:T(2,128)S(1)}, u32[]{:S(2)}) copy-start(f32[2,512]{1,0:T(2,128)S(1)} %get-tuple-element.75) | copy-start | bytes 12292
  13.2 45.8 %copy-start.7 = (f32[256,2,8]{0,2,1:T(8,128)}, f32[256,2,8]{0,2,1:T(8,128)S(1)}, u32[]{:S(2)}) copy-start(f32[256,2,8]{0,2,1:T(8,128)S(1)} %get-tuple-element.71) | copy-start | bytes 49156
  19.1 6.5 %copy-start.26 = (f32[2,8]{1,0:T(2,128)S(1)}, f32[2,8]{1,0:T(2,128)}, u32[]{:S(2)}) copy-start(f32[2,8]{1,0:T(2,128)} %get-tuple-element.92) | copy-start | bytes 196
  19.5 6.0 %collective-permute-start.1 = (bf16[2,8,4224]{2,1,0:T(8,128)(2,1)S(1)}, bf16[2,8,4224]{2,1,0:T(8,128)(2,1)S(1)}, u32[]{:S(2)}, u32[]{:S(2)}) collective-permute-start(bf16[2,8,4224]{2,1,0:T(8,128)(2,1)S(1)} %get-tuple-element.80), channel_id=1, source_target_pairs={{0,2},{2,4},{4,6},{6,8},{8,10},{10,12},{12,14},{1,3},{3,5},{5,7},{... | collective-permute-start | bytes 405512 | tf_op jit(solution)/shard_map/ppermute | solution.py:27
  23.0 6.9 %collective-permute-start.4 = (bf16[2,8,4224]{2,1,0:T(8,128)(2,1)S(1)}, bf16[2,8,4224]{2,1,0:T(8,128)(2,1)S(1)}, u32[]{:S(2)}, u32[]{:S(2)}) collective-permute-start(bf16[2,8,4224]{2,1,0:T(8,128)(2,1)S(1)} %get-tuple-element.81), channel_id=1, source_target_pairs={{2,0},{4,2},{6,4},{8,6},{10,8},{12,10},{14,12},{3,1},{5,3},{7,5},{... | collective-permute-start | bytes 405512 | tf_op jit(solution)/shard_map/ppermute | solution.py:27
  30.2 6.4 %collective-permute-start.2 = (bf16[2,8,4224]{2,1,0:T(8,128)(2,1)S(1)}, bf16[2,8,4224]{2,1,0:T(8,128)(2,1)S(1)}, u32[]{:S(2)}, u32[]{:S(2)}) collective-permute-start(bf16[2,8,4224]{2,1,0:T(8,128)(2,1)S(1)} %pad_maximum_fusion.3), channel_id=1, source_target_pairs={{0,4},{2,6},{4,8},{6,10},{8,12},{10,14},{1,5},{3,7},{5,9},{7,11},{... | collective-permute-start | bytes 405512 | tf_op jit(solution)/shard_map/ppermute | solution.py:27
  34.1 37.9 %copy-start.13 = (pred[256,256]{1,0:T(8,128)(4,1)}, pred[256,256]{1,0:T(8,128)(4,1)S(1)}, u32[]{:S(2)}) copy-start(pred[256,256]{1,0:T(8,128)(4,1)S(1)} %iota_compare_fusion) | copy-start | bytes 196612
  36.8 7.3 %collective-permute-start.5 = (bf16[2,8,4224]{2,1,0:T(8,128)(2,1)S(1)}, bf16[2,8,4224]{2,1,0:T(8,128)(2,1)S(1)}, u32[]{:S(2)}, u32[]{:S(2)}) collective-permute-start(bf16[2,8,4224]{2,1,0:T(8,128)(2,1)S(1)} %pad_maximum_fusion.5), channel_id=1, source_target_pairs={{4,0},{6,2},{8,4},{10,6},{12,8},{14,10},{5,1},{7,3},{9,5},{11,7},{... | collective-permute-start | bytes 405512 | tf_op jit(solution)/shard_map/ppermute | solution.py:27
  44.6 7.5 %collective-permute-start.3 = (bf16[2,8,4224]{2,1,0:T(8,128)(2,1)S(1)}, bf16[2,8,4224]{2,1,0:T(8,128)(2,1)S(1)}, u32[]{:S(2)}, u32[]{:S(2)}) collective-permute-start(bf16[2,8,4224]{2,1,0:T(8,128)(2,1)S(1)} %pad_maximum_fusion.4), channel_id=1, source_target_pairs={{0,8},{2,10},{4,12},{6,14},{1,9},{3,11},{5,13},{7,15},{16,24},{18,... | collective-permute-start | bytes 405512 | tf_op jit(solution)/shard_map/ppermute | solution.py:27
  49.6 8.3 %collective-permute-start.6 = (bf16[2,8,4224]{2,1,0:T(8,128)(2,1)S(1)}, bf16[2,8,4224]{2,1,0:T(8,128)(2,1)S(1)}, u32[]{:S(2)}, u32[]{:S(2)}) collective-permute-start(bf16[2,8,4224]{2,1,0:T(8,128)(2,1)S(1)} %pad_maximum_fusion.6), channel_id=1, source_target_pairs={{8,0},{10,2},{12,4},{14,6},{9,1},{11,3},{13,5},{15,7},{24,16},{26,... | collective-permute-start | bytes 405512 | tf_op jit(solution)/shard_map/ppermute | solution.py:27
  62.5 2.3 %copy-start.14 = (f32[256,2,8]{0,2,1:T(8,128)S(1)}, f32[256,2,8]{0,2,1:T(8,128)}, u32[]{:S(2)}) copy-start(f32[256,2,8]{0,2,1:T(8,128)} %param.17) | copy-start | bytes 49156
  62.5 2.3 %copy-start.28 = (f32[2,8]{1,0:T(2,128)S(1)}, f32[2,8]{1,0:T(2,128)}, u32[]{:S(2)}) copy-start(f32[2,8]{1,0:T(2,128)} %copy-done.27) | copy-start | bytes 196
  62.5 2.3 %copy-start.47 = (f32[2,8]{1,0:T(2,128)S(1)}, f32[2,8]{1,0:T(2,128)}, u32[]{:S(2)}) copy-start(f32[2,8]{1,0:T(2,128)} %param.19) | copy-start | bytes 196
  64.1 7.9 %copy-start.11 = (f32[256,2,8]{0,2,1:T(8,128)}, f32[256,2,8]{0,2,1:T(8,128)S(1)}, u32[]{:S(2)}) copy-start(f32[256,2,8]{0,2,1:T(8,128)S(1)} %get-tuple-element.94) | copy-start | bytes 49156
  66.1 5.9 %copy-start.1 = (f32[256,2,8,64]{0,3,2,1:T(8,128)S(1)}, f32[256,2,8,64]{0,3,2,1:T(8,128)}, u32[]{:S(2)}) copy-start(f32[256,2,8,64]{0,3,2,1:T(8,128)} %get-tuple-element.95) | copy-start | bytes 3145732
  66.1 5.9 %copy-start.3 = (f32[2,256,256]{2,1,0:T(8,128)S(1)}, f32[2,256,256]{2,1,0:T(8,128)}, u32[]{:S(2)}) copy-start(f32[2,256,256]{2,1,0:T(8,128)} %fusion.135) | copy-start | bytes 1572868
  66.1 5.9 %copy-start.54 = (f32[2,8]{1,0:T(2,128)S(1)}, f32[2,8]{1,0:T(2,128)}, u32[]{:S(2)}) copy-start(f32[2,8]{1,0:T(2,128)} %param.20) | copy-start | bytes 196
  72.0 2.4 %copy-start = (f32[256,2,8,64]{0,3,2,1:T(8,128)S(1)}, f32[256,2,8,64]{0,3,2,1:T(8,128)}, u32[]{:S(2)}) copy-start(f32[256,2,8,64]{0,3,2,1:T(8,128)} %get-tuple-element.97) | copy-start | bytes 3145732
  72.0 2.4 %copy-start.8 = (f32[256,2,8]{0,2,1:T(8,128)S(1)}, f32[256,2,8]{0,2,1:T(8,128)}, u32[]{:S(2)}) copy-start(f32[256,2,8]{0,2,1:T(8,128)} %copy-done.7) | copy-start | bytes 49156
  74.4 2.6 %copy-start.50 = (f32[2,8]{1,0:T(2,128)S(1)}, f32[2,8]{1,0:T(2,128)}, u32[]{:S(2)}) copy-start(f32[2,8]{1,0:T(2,128)} %get-tuple-element.67) | copy-start | bytes 196
  74.4 3.3 %copy-start.6 = (f32[256,2,64]{0,2,1:T(8,128)S(1)}, f32[256,2,64]{0,2,1:T(8,128)}, u32[]{:S(2)}) copy-start(f32[256,2,64]{0,2,1:T(8,128)} %get-tuple-element.62) | copy-start | bytes 393220
  74.4 3.7 %copy-start.39 = (f32[2,64]{1,0:T(2,128)S(1)}, f32[2,64]{1,0:T(2,128)}, u32[]{:S(2)}) copy-start(f32[2,64]{1,0:T(2,128)} %copy-done.38) | copy-start | bytes 1540
  74.4 3.7 %copy-start.41 = (f32[2,64]{1,0:T(2,128)S(1)}, f32[2,64]{1,0:T(2,128)}, u32[]{:S(2)}) copy-start(f32[2,64]{1,0:T(2,128)} %copy-done.40) | copy-start | bytes 1540
  74.4 3.7 %copy-start.43 = (f32[2,64]{1,0:T(2,128)S(1)}, f32[2,64]{1,0:T(2,128)}, u32[]{:S(2)}) copy-start(f32[2,64]{1,0:T(2,128)} %copy-done.42) | copy-start | bytes 1540
  74.4 3.7 %copy-start.45 = (f32[2,64]{1,0:T(2,128)S(1)}, f32[2,64]{1,0:T(2,128)}, u32[]{:S(2)}) copy-start(f32[2,64]{1,0:T(2,128)} %copy-done.44) | copy-start | bytes 1540
  82.8 2.2 %copy-start.12 = (f32[256,2,8]{0,2,1:T(8,128)S(1)}, f32[256,2,8]{0,2,1:T(8,128)}, u32[]{:S(2)}) copy-start(f32[256,2,8]{0,2,1:T(8,128)} %copy-done.11) | copy-start | bytes 49156
  82.8 2.2 %copy-start.15 = (f32[256,2,8]{0,2,1:T(8,128)S(1)}, f32[256,2,8]{0,2,1:T(8,128)}, u32[]{:S(2)}) copy-start(f32[256,2,8]{0,2,1:T(8,128)} %param.17) | copy-start | bytes 49156
  82.8 2.2 %copy-start.29 = (f32[2,8]{1,0:T(2,128)S(1)}, f32[2,8]{1,0:T(2,128)}, u32[]{:S(2)}) copy-start(f32[2,8]{1,0:T(2,128)} %copy-done.27) | copy-start | bytes 196
  82.8 2.2 %copy-start.46 = (f32[1,2,8]{0,2,1:T(8,128)S(1)}, f32[1,2,8]{0,2,1:T(8,128)}, u32[]{:S(2)}) copy-start(f32[1,2,8]{0,2,1:T(8,128)} %copy.139) | copy-start | bytes 196
  82.8 2.2 %copy-start.48 = (f32[2,8]{1,0:T(2,128)S(1)}, f32[2,8]{1,0:T(2,128)}, u32[]{:S(2)}) copy-start(f32[2,8]{1,0:T(2,128)} %param.19) | copy-start | bytes 196
  82.8 2.5 %copy-start.55 = (f32[2,8,256]{2,1,0:T(8,128)S(1)}, f32[2,8,256]{2,1,0:T(8,128)}, u32[]{:S(2)}) copy-start(f32[2,8,256]{2,1,0:T(8,128)} %get-tuple-element.46) | copy-start | bytes 49156
  82.8 2.5 %copy-start.56 = (f32[2,8,256]{2,1,0:T(8,128)S(1)}, f32[2,8,256]{2,1,0:T(8,128)}, u32[]{:S(2)}) copy-start(f32[2,8,256]{2,1,0:T(8,128)} %get-tuple-element.47) | copy-start | bytes 49156
  82.8 2.5 %copy-start.57 = (f32[2,8,256]{2,1,0:T(8,128)S(1)}, f32[2,8,256]{2,1,0:T(8,128)}, u32[]{:S(2)}) copy-start(f32[2,8,256]{2,1,0:T(8,128)} %get-tuple-element.48) | copy-start | bytes 49156
  83.4 5.6 %collective-permute-start.7 = (f32[3,2,640]{2,1,0:T(2,128)S(1)}, f32[3,2,640]{2,1,0:T(2,128)S(1)}, u32[]{:S(2)}, u32[]{:S(2)}) collective-permute-start(f32[3,2,640]{2,1,0:T(2,128)S(1)} %pad_maximum_fusion.9), channel_id=1, source_target_pairs={{2,0},{4,2},{6,4},{8,6},{10,8},{12,10},{14,12},{3,1},{5,3},{7,5},{... | collective-permute-start | bytes 46088 | tf_op jit(solution)/shard_map/ppermute | solution.py:12
  (18 other events, 24.2 us)

commit v17 on v16

--- a/solution.py
+++ b/solution.py
@@ -98,6 +98,30 @@
     return step_size, cum_log
 
 
+@jax.custom_vjp
+def exact_scores(c_float, b_float):
+    return jnp.einsum(
+        "tgn,sgn->gts",
+        c_float.astype(jnp.bfloat16),
+        b_float.astype(jnp.bfloat16),
+        preferred_element_type=jnp.float32,
+    )
+
+
+def exact_scores_fwd(c_float, b_float):
+    return exact_scores(c_float, b_float), (c_float, b_float)
+
+
+def exact_scores_bwd(saved, grad_scores):
+    c_float, b_float = saved
+    grad_c = jnp.einsum("gts,sgn->tgn", grad_scores, b_float, precision=HIGH)
+    grad_b = jnp.einsum("gts,tgn->sgn", grad_scores, c_float, precision=HIGH)
+    return grad_c, grad_b
+
+
+exact_scores.defvjp(exact_scores_fwd, exact_scores_bwd)
+
+
 def ssd_mix(x_float, b_float, c_float, dt_raw, rate, dt_bias, skip):
     length, groups, channels = x_float.shape
     head_count = dt_raw.shape[2]
@@ -113,7 +137,7 @@
     decay_all = jnp.where(
         causal, jnp.exp(jnp.minimum(cum_heads[:, :, :, None] - cum_heads[:, :, None, :], 0.0)), 0.0
     )
-    scores = jnp.einsum("tgn,sgn->gts", c_float, b_float, precision=HIGH)
+    scores = exact_scores(c_float, b_float)
     mixing = (scores[:, None] * decay_all * step_heads[:, :, None, :]).astype(jnp.bfloat16)
     y_local = jnp.einsum("ghts,sghp->tghp", mixing, x_half, preferred_element_type=jnp.float32)
     return y_local + skip[None, :, :, None] * x_heads

time: 93.1 us -> 93.1 us (level)
  no operation moved by 1% of the time
where the time goes in v17:
time: 93.1 us; the launch traced here: 92.3 us
  starting transfers between devices  22.4 us (24%)
  waiting for transfers between devices  21.3 us (23%)
  matrix products  20.4 us (22%)
  local copies, waits for them, and re-layouts  16.7 us (18%)
  other arithmetic  9.82 us (11%)
  between operations  1.61 us (2%)
    ppermute x6, waiting for transfers between devices, shift(): return lax.ppermute(packed, axis, pairs)  19.5 us
    ppermute x6, starting transfers between devices, shift(): return lax.ppermute(packed, axis, pairs)  16.3 us
    dot_general x3, matrix products, ssd_mix(): jnp.einsum('ghts,sghp->tghp', mixing, x_half, preferred_element_type=jnp....  10.8 us
    ppermute x2, starting transfers between devices, from_behind(): return lax.ppermute(array, axis, pairs)  6.12 us
    unnamed x124, local copies, waits for them, and re-layouts  5.27 us
    dot_general x2, matrix products, carry_in(): carried = jnp.einsum('tgn,ghpn->tghp', c_float, state_in, precision=HIGH)  2.68 us
    dot_general x3, matrix products, ssd_state(): jnp.einsum('sghp,sgn->ghpn', weighted.astype(jnp.float32), b_float, preci...  2.5 us
    mul x3, local copies, waits for them, and re-layouts, conv_forward(): running = weight[0] * extended[0:length].astype(jnp.float32)  2.21 us
  transfers between devices with their start and end apart: 8, of which 7 were waited for; matrix products, arithmetic and copies ran while one was open for 12% of the time, Pallas kernels for 0%

profile of v17, /device:TPU:0, one launch (start us, length us, event | category | flops | bytes accessed | tf_op | source)
XLA Modules:
  0.0 92.3 jit_solution(8150190946427630764)
XLA Ops:
  0.6 0.8 slice.231
  1.4 0.8 slice.232
  2.3 0.8 slice.233
  3.4 4.8 %collective-permute-start = (bf16[3,2,640]{2,0,1:T(4,128)(2,1)S(1)}, bf16[3,2,640]{2,0,1:T(4,128)(2,1)S(1)}, u32[]{:S(2)}, u32[]{:S(2)}) collective-permute-start(bf16[3,2,640]{2,0,1:T(4,128)(2,1)S(1)} %copy.120), channel_id=1, source_target_pairs={{0,2},{2,4},{4,6},{6,8},{8,10},{10,12},{12,14},{1,3},{3,5},{5,7},{... | collective-permute-start | bytes 23048 | tf_op jit(solution)/shard_map/ppermute | solution.py:12
  8.2 0.7 neg.30
  8.9 0.7 slice_bitcast_fusion.7
  9.7 0.7 slice_bitcast_fusion.11
  10.4 0.9 %fusion.78 = f32[256,16]{0,1:S(1)} fusion(f32[2,8]{1,0:T(2,128)S(1)} %neg.30, f32[256,2,8]{0,2,1:T(8,128)} %param.17, f32[2,8]{1,0:T(2,128)} %param.19), kind=kOutput, calls=%fused_computation.98 | convolution fusion | flops 12681216 | bytes 32896
  11.6 0.7 slice_bitcast_fusion.3
  12.3 0.8 fusion.118
  13.2 0.6 fusion.134
  13.8 1.1 %copy.121 = bf16[256,2,512]{2,0,1:T(8,128)(2,1)S(1)} copy(bf16[256,2,512]{2,1,0:T(2,128)(2,1)} %param.14) | data formatting | bytes 1048576 | tf_op args[0]
  15.9 1.0 %multiply_convert_fusion.1 = (bf16[256,2,64]{0,2,1:T(8,128)(2,1)S(1)}, f32[256,2,64]{0,2,1:T(8,128)}, bf16[256,2,64]{0,2,1:T(8,128)(2,1)S(1)}, f32[256,2,64]{0,2,1:T(8,128)}) fusion(bf16[256,2,64]{0,2,1:T(8,128)(2,1)S(1)} %copy-done.10, f32[2,64]{1,0:T(2,128)S(1)} %get-tuple-element.84, bf16[3,2,64]{0,2,1:T(8,128)(2,1)S(1)} %copy.125, ...), kind=kLoop, calls=%fused_computation.121 | loop fusion | flops 1638400 | bytes 529920 | tf_op jit(solution)/shard_map/convert_element_type | solution.py:183
  16.9 0.6 fusion.52
  17.9 0.7 multiply_convert_fusion
  19.5 3.5 %collective-permute-start.1 = (bf16[2,8,4224]{2,1,0:T(8,128)(2,1)S(1)}, bf16[2,8,4224]{2,1,0:T(8,128)(2,1)S(1)}, u32[]{:S(2)}, u32[]{:S(2)}) collective-permute-start(bf16[2,8,4224]{2,1,0:T(8,128)(2,1)S(1)} %get-tuple-element.80), channel_id=1, source_target_pairs={{0,2},{2,4},{4,6},{6,8},{8,10},{10,12},{12,14},{1,3},{3,5},{5,7},{... | collective-permute-start | bytes 405512 | tf_op jit(solution)/shard_map/ppermute | solution.py:27
  23.0 1.3 %collective-permute-start.4 = (bf16[2,8,4224]{2,1,0:T(8,128)(2,1)S(1)}, bf16[2,8,4224]{2,1,0:T(8,128)(2,1)S(1)}, u32[]{:S(2)}, u32[]{:S(2)}) collective-permute-start(bf16[2,8,4224]{2,1,0:T(8,128)(2,1)S(1)} %get-tuple-element.81), channel_id=1, source_target_pairs={{2,0},{4,2},{6,4},{8,6},{10,8},{12,10},{14,12},{3,1},{5,3},{7,5},{... | collective-permute-start | bytes 405512 | tf_op jit(solution)/shard_map/ppermute | solution.py:27
  24.3 1.2 %collective-permute-done.1 = bf16[2,8,4224]{2,1,0:T(8,128)(2,1)S(1)} collective-permute-done((bf16[2,8,4224]{2,1,0:T(8,128)(2,1)S(1)}, bf16[2,8,4224]{2,1,0:T(8,128)(2,1)S(1)}, u32[]{:S(2)}, u32[]{:S(2)}) %collective-permute-start.1) | collective-permute-done | bytes 135200 | tf_op jit(solution)/shard_map/ppermute | solution.py:27
  25.7 4.2 %collective-permute-done.4 = bf16[2,8,4224]{2,1,0:T(8,128)(2,1)S(1)} collective-permute-done((bf16[2,8,4224]{2,1,0:T(8,128)(2,1)S(1)}, bf16[2,8,4224]{2,1,0:T(8,128)(2,1)S(1)}, u32[]{:S(2)}, u32[]{:S(2)}) %collective-permute-start.4) | collective-permute-done | bytes 135200 | tf_op jit(solution)/shard_map/ppermute | solution.py:27
  30.2 3.8 %collective-permute-start.2 = (bf16[2,8,4224]{2,1,0:T(8,128)(2,1)S(1)}, bf16[2,8,4224]{2,1,0:T(8,128)(2,1)S(1)}, u32[]{:S(2)}, u32[]{:S(2)}) collective-permute-start(bf16[2,8,4224]{2,1,0:T(8,128)(2,1)S(1)} %pad_maximum_fusion.3), channel_id=1, source_target_pairs={{0,4},{2,6},{4,8},{6,10},{8,12},{10,14},{1,5},{3,7},{5,9},{7,11},{... | collective-permute-start | bytes 405512 | tf_op jit(solution)/shard_map/ppermute | solution.py:27
  34.1 2.5 %collective-permute-done.2 = bf16[2,8,4224]{2,1,0:T(8,128)(2,1)S(1)} collective-permute-done((bf16[2,8,4224]{2,1,0:T(8,128)(2,1)S(1)}, bf16[2,8,4224]{2,1,0:T(8,128)(2,1)S(1)}, u32[]{:S(2)}, u32[]{:S(2)}) %collective-permute-start.2) | collective-permute-done | bytes 135200 | tf_op jit(solution)/shard_map/ppermute | solution.py:27
  36.8 1.3 %collective-permute-start.5 = (bf16[2,8,4224]{2,1,0:T(8,128)(2,1)S(1)}, bf16[2,8,4224]{2,1,0:T(8,128)(2,1)S(1)}, u32[]{:S(2)}, u32[]{:S(2)}) collective-permute-start(bf16[2,8,4224]{2,1,0:T(8,128)(2,1)S(1)} %pad_maximum_fusion.5), channel_id=1, source_target_pairs={{4,0},{6,2},{8,4},{10,6},{12,8},{14,10},{5,1},{7,3},{9,5},{11,7},{... | collective-permute-start | bytes 405512 | tf_op jit(solution)/shard_map/ppermute | solution.py:27
  38.1 1.1 %fusion.135 = f32[2,256,256]{2,1,0:T(8,128)} fusion(bf16[256,2,64]{0,2,1:T(8,128)(2,1)S(1)} %get-tuple-element.98, bf16[256,2,64]{0,2,1:T(8,128)(2,1)S(1)} %get-tuple-element.61), kind=kOutput, calls=%fused_computation.214 | convolution fusion | flops 16777216 | bytes 655360 | tf_op jit(solution)/shard_map/jvp(tgn,sgn->gts)/dot_general | solution.py:103
  39.2 5.0 %collective-permute-done.5 = bf16[2,8,4224]{2,1,0:T(8,128)(2,1)S(1)} collective-permute-done((bf16[2,8,4224]{2,1,0:T(8,128)(2,1)S(1)}, bf16[2,8,4224]{2,1,0:T(8,128)(2,1)S(1)}, u32[]{:S(2)}, u32[]{:S(2)}) %collective-permute-start.5) | collective-permute-done | bytes 135200 | tf_op jit(solution)/shard_map/ppermute | solution.py:27
  44.6 4.9 %collective-permute-start.3 = (bf16[2,8,4224]{2,1,0:T(8,128)(2,1)S(1)}, bf16[2,8,4224]{2,1,0:T(8,128)(2,1)S(1)}, u32[]{:S(2)}, u32[]{:S(2)}) collective-permute-start(bf16[2,8,4224]{2,1,0:T(8,128)(2,1)S(1)} %pad_maximum_fusion.4), channel_id=1, source_target_pairs={{0,8},{2,10},{4,12},{6,14},{1,9},{3,11},{5,13},{7,15},{16,24},{18,... | collective-permute-start | bytes 405512 | tf_op jit(solution)/shard_map/ppermute | solution.py:27
  49.6 1.5 %collective-permute-start.6 = (bf16[2,8,4224]{2,1,0:T(8,128)(2,1)S(1)}, bf16[2,8,4224]{2,1,0:T(8,128)(2,1)S(1)}, u32[]{:S(2)}, u32[]{:S(2)}) collective-permute-start(bf16[2,8,4224]{2,1,0:T(8,128)(2,1)S(1)} %pad_maximum_fusion.6), channel_id=1, source_target_pairs={{8,0},{10,2},{12,4},{14,6},{9,1},{11,3},{13,5},{15,7},{24,16},{26,... | collective-permute-start | bytes 405512 | tf_op jit(solution)/shard_map/ppermute | solution.py:27
  51.3 0.8 collective-permute-done.3
  52.1 5.8 %collective-permute-done.6 = bf16[2,8,4224]{2,1,0:T(8,128)(2,1)S(1)} collective-permute-done((bf16[2,8,4224]{2,1,0:T(8,128)(2,1)S(1)}, bf16[2,8,4224]{2,1,0:T(8,128)(2,1)S(1)}, u32[]{:S(2)}, u32[]{:S(2)}) %collective-permute-start.6) | collective-permute-done | bytes 135200 | tf_op jit(solution)/shard_map/ppermute | solution.py:27
  57.9 0.8 multiply_reduce_fusion
  59.0 1.1 %convolution_bitcast_fusion.3 = f32[256,2,64]{0,2,1:T(8,128)S(1)} fusion(f32[2,8,64,64]{3,2,1,0:T(8,128)S(1)} %reshape.127, bf16[256,2,8,64]{0,3,2,1:T(8,128)(2,1)S(1)} %bitcast.188, f32[256,2,8]{0,2,1:T(8,128)S(1)} %get-tuple-element.71), kind=kOutput, calls=%fused_computation.48 | convolution fusion | flops 201850880 | bytes 933888 | tf_op jit(solution)/shard_map/transpose(jvp(tgn,ghpn->tghp))/dot_general | solution.py:159
  60.0 1.6 %fusion.70 = (f32[256,2,8]{0,2,1:T(8,128)S(1)}, f32[256,2,8,64]{0,3,2,1:T(8,128)}) fusion(bf16[256,2,512]{0,2,1:T(8,128)(2,1)S(1)} %copy.127, f32[2,8,64,64]{3,2,1,0:T(8,128)S(1)} %reshape.127, bf16[256,2,64]{0,2,1:T(8,128)(2,1)S(1)} %get-tuple-element.98), kind=kOutput, calls=%fused_computation.67 | convolution fusion | flops 202108928 | bytes 1916928 | tf_op jit(solution)/shard_map/jvp(tgn,ghpn->tghp)/dot_general | solution.py:159
  61.9 0.6 convolution_bitcast_fusion.2
  62.5 1.6 %fusion.69 = (f32[256,2,8]{0,2,1:T(8,128)S(1)}, f32[256,2,8,64]{0,3,2,1:T(8,128)}) fusion(bf16[256,2,512]{0,2,1:T(8,128)(2,1)S(1)} %copy.123, f32[2,8,64,64]{3,2,1,0:T(8,128)S(1)} %reshape.131, bf16[256,2,64]{0,2,1:T(8,128)(2,1)S(1)} %get-tuple-element.61), kind=kOutput, calls=%fused_computation.66 | convolution fusion | flops 202633216 | bytes 1916928 | tf_op jit(solution)/shard_map/transpose(jvp(sghp,sgn->ghpn))/dot_general | solution.py:154
  64.1 0.7 copy.138
  64.8 1.3 %fusion.119 = (f32[2,8]{1,0:T(2,128)}, f32[2,8,256]{2,1,0:T(8,128)S(1)}, f32[256,2,8]{0,2,1:T(8,128)}) fusion(f32[256,2,8]{0,2,1:T(8,128)S(1)} %get-tuple-element.94, f32[2,8]{1,0:T(2,128)S(1)} %copy-done.28, f32[256,16]{0,1:S(1)} %fusion.78, f32[256,2,8]{0,2,1:T(8,128)S(1)} %copy-done.14, f32[2,8]{1,0:T(2,128)S(1)} %copy-done.47, ...), kind=kLoop, calls=%fused_computation.172 | loop fusion | flops 49136 | bytes 98496 | tf_op jit(solution)/shard_map/transpose(jvp())/reduce_sum | solution.py:152
  66.1 5.9 %fusion.18 = (f32[2,8,256]{2,1,0:T(8,128)}, f32[2,8,256]{2,1,0:T(8,128)}, f32[2,8,256]{2,1,0:T(8,128)}, f32[2,256,256]{2,1,0:T(8,128)S(1)}) fusion(f32[2,8,256]{2,1,0:T(8,128)S(1)} %bitcast.200, f32[2,8,256]{2,1,0:T(8,128)S(1)} %get-tuple-element.68, f32[2,256,256]{2,1,0:T(8,128)} %fusion.135, pred[256,256]{1,0:T(8,128)(4,1)S(1)} %iota_compare_fusion, ...), kind=kOutput, calls=%fused_computation.27 | convolution fusion | flops 156094464 | bytes 2244608 | tf_op jit(solution)/shard_map/transpose(jvp(ghts,sghp->tghp))/dot_general | solution.py:142
  72.1 2.3 %fusion.48 = bf16[256,2,8,64]{0,3,2,1:T(8,128)(2,1)} fusion(bf16[2,8,64,256]{3,2,1,0:T(8,128)(2,1)S(1)} %bitcast.191, f32[2,8,256]{2,1,0:T(8,128)S(1)} %get-tuple-element.68, f32[2,8,256]{2,1,0:T(8,128)S(1)} %bitcast.201, f32[2,256,256]{2,1,0:T(8,128)S(1)} %copy-done.3, pred[256,256]{1,0:T(8,128)(4,1)S(1)} %iota_compare_fusion, ...), kind=kOutput, calls=%fused_computation.41 | convolution fusion | flops 142606336 | bytes 3260480 | tf_op jit(solution)/shard_map/transpose(jvp(ghts,sghp->tghp))/dot_general | solution.py:142
  74.5 2.6 %fusion.30 = bf16[256,2,8,64]{0,3,2,1:T(8,128)(2,1)S(1)} fusion(bf16[256,2,8,64]{0,3,2,1:T(8,128)(2,1)S(1)} %bitcast.195, f32[2,8,256]{2,1,0:T(8,128)S(1)} %get-tuple-element.68, f32[2,8,256]{2,1,0:T(8,128)S(1)} %bitcast.202, f32[2,256,256]{2,1,0:T(8,128)S(1)} %copy-done.3, pred[256,256]{1,0:T(8,128)(4,1)} %copy-done.13, f32[256,2,8,64]{0,3,2,1:T(8,128)S(1)} %copy-done, ...), kind=kOutput, calls=%fused_computation.35 | convolution fusion | flops 142082048 | bytes 2736192 | tf_op jit(solution)/shard_map/jvp(ghts,sghp->tghp)/dot_general | solution.py:142
  77.0 0.7 copy.139
  79.4 1.1 %bitcast_convert_fusion = f32[256,2,512]{0,2,1:T(8,128)} fusion(bf16[256,2,8,64]{0,3,2,1:T(8,128)(2,1)S(1)} %copy-done.2), kind=kLoop, calls=%fused_computation.78 | loop fusion | flops 262144 | bytes 1572864 | tf_op jit(solution)/shard_map/convert_element_type | solution.py:79
  80.5 1.6 %copy.129 = f32[256,2,512]{2,0,1:T(8,128)S(1)} copy(f32[256,2,512]{0,2,1:T(8,128)} %bitcast_convert_fusion) | data formatting | bytes 2097152 | tf_op jit(solution)/shard_map/convert_element_type | solution.py:79
  83.4 1.3 %collective-permute-start.7 = (f32[3,2,640]{2,1,0:T(2,128)S(1)}, f32[3,2,640]{2,1,0:T(2,128)S(1)}, u32[]{:S(2)}, u32[]{:S(2)}) collective-permute-start(f32[3,2,640]{2,1,0:T(2,128)S(1)} %pad_maximum_fusion.9), channel_id=1, source_target_pairs={{2,0},{4,2},{6,4},{8,6},{10,8},{12,10},{14,12},{3,1},{5,3},{7,5},{... | collective-permute-start | bytes 46088 | tf_op jit(solution)/shard_map/ppermute | solution.py:12
  85.3 0.8 fusion.64
  86.1 1.2 %copy.140 = bf16[256,2,512]{2,1,0:T(2,128)(2,1)} copy(bf16[256,2,512]{0,2,1:T(8,128)(2,1)S(1)} %bitcast.196) | data formatting | bytes 1048576
  87.3 1.8 %collective-permute-done.7 = f32[3,2,640]{2,1,0:T(2,128)S(1)} collective-permute-done((f32[3,2,640]{2,1,0:T(2,128)S(1)}, f32[3,2,640]{2,1,0:T(2,128)S(1)}, u32[]{:S(2)}, u32[]{:S(2)}) %collective-permute-start.7) | collective-permute-done | bytes 15392 | tf_op jit(solution)/shard_map/ppermute | solution.py:12
  89.2 1.3 %copy.141 = bf16[256,2,512]{2,1,0:T(2,128)(2,1)} copy(bf16[256,2,512]{2,0,1:T(8,128)(2,1)S(1)} %slice.513) | data formatting | bytes 1048576
  90.7 0.7 slice.514
  91.6 0.7 slice.515
  (183 shorter events, 8.2 us)
Async XLA Ops:
  0.6 14.3 %copy-start.4 = (bf16[256,2,512]{2,1,0:T(2,128)(2,1)S(1)}, bf16[256,2,512]{2,1,0:T(2,128)(2,1)}, u32[]{:S(2)}) copy-start(bf16[256,2,512]{2,1,0:T(2,128)(2,1)} %param.24) | copy-start | bytes 1572868
  3.4 12.1 %collective-permute-start = (bf16[3,2,640]{2,0,1:T(4,128)(2,1)S(1)}, bf16[3,2,640]{2,0,1:T(4,128)(2,1)S(1)}, u32[]{:S(2)}, u32[]{:S(2)}) collective-permute-start(bf16[3,2,640]{2,0,1:T(4,128)(2,1)S(1)} %copy.120), channel_id=1, source_target_pairs={{0,2},{2,4},{4,6},{6,8},{8,10},{10,12},{12,14},{1,3},{3,5},{5,7},{... | collective-permute-start | bytes 23048 | tf_op jit(solution)/shard_map/ppermute | solution.py:12
  8.9 6.5 %copy-start.52 = (f32[2,8]{1,0:T(2,128)}, f32[2,8]{1,0:T(2,128)S(1)}, u32[]{:S(2)}) copy-start(f32[2,8]{1,0:T(2,128)S(1)} %neg.30) | copy-start | bytes 196
  9.7 6.2 %copy-start.38 = (f32[2,64]{1,0:T(2,128)}, f32[2,64]{1,0:T(2,128)S(1)}, u32[]{:S(2)}) copy-start(f32[2,64]{1,0:T(2,128)S(1)} %get-tuple-element.82) | copy-start | bytes 1540
  9.7 6.2 %copy-start.40 = (f32[2,64]{1,0:T(2,128)}, f32[2,64]{1,0:T(2,128)S(1)}, u32[]{:S(2)}) copy-start(f32[2,64]{1,0:T(2,128)S(1)} %get-tuple-element.83) | copy-start | bytes 1540
  9.7 6.2 %copy-start.42 = (f32[2,64]{1,0:T(2,128)}, f32[2,64]{1,0:T(2,128)S(1)}, u32[]{:S(2)}) copy-start(f32[2,64]{1,0:T(2,128)S(1)} %get-tuple-element.84) | copy-start | bytes 1540
  9.7 6.2 %copy-start.44 = (f32[2,64]{1,0:T(2,128)}, f32[2,64]{1,0:T(2,128)S(1)}, u32[]{:S(2)}) copy-start(f32[2,64]{1,0:T(2,128)S(1)} %get-tuple-element.85) | copy-start | bytes 1540
  10.4 5.4 %copy-start.30 = (f32[2,64]{1,0:T(2,128)}, f32[2,64]{1,0:T(2,128)S(1)}, u32[]{:S(2)}) copy-start(f32[2,64]{1,0:T(2,128)S(1)} %get-tuple-element.86) | copy-start | bytes 1540
  10.4 5.4 %copy-start.32 = (f32[2,64]{1,0:T(2,128)}, f32[2,64]{1,0:T(2,128)S(1)}, u32[]{:S(2)}) copy-start(f32[2,64]{1,0:T(2,128)S(1)} %get-tuple-element.87) | copy-start | bytes 1540
  10.4 5.4 %copy-start.34 = (f32[2,64]{1,0:T(2,128)}, f32[2,64]{1,0:T(2,128)S(1)}, u32[]{:S(2)}) copy-start(f32[2,64]{1,0:T(2,128)S(1)} %get-tuple-element.88) | copy-start | bytes 1540
  10.4 5.5 %copy-start.36 = (f32[2,64]{1,0:T(2,128)}, f32[2,64]{1,0:T(2,128)S(1)}, u32[]{:S(2)}) copy-start(f32[2,64]{1,0:T(2,128)S(1)} %get-tuple-element.89) | copy-start | bytes 1540
  12.3 5.5 %copy-start.16 = (f32[2,512]{1,0:T(2,128)}, f32[2,512]{1,0:T(2,128)S(1)}, u32[]{:S(2)}) copy-start(f32[2,512]{1,0:T(2,128)S(1)} %get-tuple-element.72) | copy-start | bytes 12292
  12.3 5.5 %copy-start.18 = (f32[2,512]{1,0:T(2,128)}, f32[2,512]{1,0:T(2,128)S(1)}, u32[]{:S(2)}) copy-start(f32[2,512]{1,0:T(2,128)S(1)} %get-tuple-element.73) | copy-start | bytes 12292
  12.3 5.5 %copy-start.20 = (f32[2,512]{1,0:T(2,128)}, f32[2,512]{1,0:T(2,128)S(1)}, u32[]{:S(2)}) copy-start(f32[2,512]{1,0:T(2,128)S(1)} %get-tuple-element.74) | copy-start | bytes 12292
  12.3 5.5 %copy-start.22 = (f32[2,512]{1,0:T(2,128)}, f32[2,512]{1,0:T(2,128)S(1)}, u32[]{:S(2)}) copy-start(f32[2,512]{1,0:T(2,128)S(1)} %get-tuple-element.75) | copy-start | bytes 12292
  13.2 45.8 %copy-start.7 = (f32[256,2,8]{0,2,1:T(8,128)}, f32[256,2,8]{0,2,1:T(8,128)S(1)}, u32[]{:S(2)}) copy-start(f32[256,2,8]{0,2,1:T(8,128)S(1)} %get-tuple-element.71) | copy-start | bytes 49156
  19.1 6.5 %copy-start.26 = (f32[2,8]{1,0:T(2,128)S(1)}, f32[2,8]{1,0:T(2,128)}, u32[]{:S(2)}) copy-start(f32[2,8]{1,0:T(2,128)} %get-tuple-element.92) | copy-start | bytes 196
  19.5 6.0 %collective-permute-start.1 = (bf16[2,8,4224]{2,1,0:T(8,128)(2,1)S(1)}, bf16[2,8,4224]{2,1,0:T(8,128)(2,1)S(1)}, u32[]{:S(2)}, u32[]{:S(2)}) collective-permute-start(bf16[2,8,4224]{2,1,0:T(8,128)(2,1)S(1)} %get-tuple-element.80), channel_id=1, source_target_pairs={{0,2},{2,4},{4,6},{6,8},{8,10},{10,12},{12,14},{1,3},{3,5},{5,7},{... | collective-permute-start | bytes 405512 | tf_op jit(solution)/shard_map/ppermute | solution.py:27
  23.0 6.9 %collective-permute-start.4 = (bf16[2,8,4224]{2,1,0:T(8,128)(2,1)S(1)}, bf16[2,8,4224]{2,1,0:T(8,128)(2,1)S(1)}, u32[]{:S(2)}, u32[]{:S(2)}) collective-permute-start(bf16[2,8,4224]{2,1,0:T(8,128)(2,1)S(1)} %get-tuple-element.81), channel_id=1, source_target_pairs={{2,0},{4,2},{6,4},{8,6},{10,8},{12,10},{14,12},{3,1},{5,3},{7,5},{... | collective-permute-start | bytes 405512 | tf_op jit(solution)/shard_map/ppermute | solution.py:27
  30.2 6.4 %collective-permute-start.2 = (bf16[2,8,4224]{2,1,0:T(8,128)(2,1)S(1)}, bf16[2,8,4224]{2,1,0:T(8,128)(2,1)S(1)}, u32[]{:S(2)}, u32[]{:S(2)}) collective-permute-start(bf16[2,8,4224]{2,1,0:T(8,128)(2,1)S(1)} %pad_maximum_fusion.3), channel_id=1, source_target_pairs={{0,4},{2,6},{4,8},{6,10},{8,12},{10,14},{1,5},{3,7},{5,9},{7,11},{... | collective-permute-start | bytes 405512 | tf_op jit(solution)/shard_map/ppermute | solution.py:27
  34.1 37.9 %copy-start.13 = (pred[256,256]{1,0:T(8,128)(4,1)}, pred[256,256]{1,0:T(8,128)(4,1)S(1)}, u32[]{:S(2)}) copy-start(pred[256,256]{1,0:T(8,128)(4,1)S(1)} %iota_compare_fusion) | copy-start | bytes 196612
  36.8 7.3 %collective-permute-start.5 = (bf16[2,8,4224]{2,1,0:T(8,128)(2,1)S(1)}, bf16[2,8,4224]{2,1,0:T(8,128)(2,1)S(1)}, u32[]{:S(2)}, u32[]{:S(2)}) collective-permute-start(bf16[2,8,4224]{2,1,0:T(8,128)(2,1)S(1)} %pad_maximum_fusion.5), channel_id=1, source_target_pairs={{4,0},{6,2},{8,4},{10,6},{12,8},{14,10},{5,1},{7,3},{9,5},{11,7},{... | collective-permute-start | bytes 405512 | tf_op jit(solution)/shard_map/ppermute | solution.py:27
  44.6 7.5 %collective-permute-start.3 = (bf16[2,8,4224]{2,1,0:T(8,128)(2,1)S(1)}, bf16[2,8,4224]{2,1,0:T(8,128)(2,1)S(1)}, u32[]{:S(2)}, u32[]{:S(2)}) collective-permute-start(bf16[2,8,4224]{2,1,0:T(8,128)(2,1)S(1)} %pad_maximum_fusion.4), channel_id=1, source_target_pairs={{0,8},{2,10},{4,12},{6,14},{1,9},{3,11},{5,13},{7,15},{16,24},{18,... | collective-permute-start | bytes 405512 | tf_op jit(solution)/shard_map/ppermute | solution.py:27
  49.6 8.3 %collective-permute-start.6 = (bf16[2,8,4224]{2,1,0:T(8,128)(2,1)S(1)}, bf16[2,8,4224]{2,1,0:T(8,128)(2,1)S(1)}, u32[]{:S(2)}, u32[]{:S(2)}) collective-permute-start(bf16[2,8,4224]{2,1,0:T(8,128)(2,1)S(1)} %pad_maximum_fusion.6), channel_id=1, source_target_pairs={{8,0},{10,2},{12,4},{14,6},{9,1},{11,3},{13,5},{15,7},{24,16},{26,... | collective-permute-start | bytes 405512 | tf_op jit(solution)/shard_map/ppermute | solution.py:27
  62.5 2.3 %copy-start.14 = (f32[256,2,8]{0,2,1:T(8,128)S(1)}, f32[256,2,8]{0,2,1:T(8,128)}, u32[]{:S(2)}) copy-start(f32[256,2,8]{0,2,1:T(8,128)} %param.17) | copy-start | bytes 49156
  62.5 2.3 %copy-start.28 = (f32[2,8]{1,0:T(2,128)S(1)}, f32[2,8]{1,0:T(2,128)}, u32[]{:S(2)}) copy-start(f32[2,8]{1,0:T(2,128)} %copy-done.27) | copy-start | bytes 196
  62.5 2.3 %copy-start.47 = (f32[2,8]{1,0:T(2,128)S(1)}, f32[2,8]{1,0:T(2,128)}, u32[]{:S(2)}) copy-start(f32[2,8]{1,0:T(2,128)} %param.19) | copy-start | bytes 196
  64.1 7.9 %copy-start.11 = (f32[256,2,8]{0,2,1:T(8,128)}, f32[256,2,8]{0,2,1:T(8,128)S(1)}, u32[]{:S(2)}) copy-start(f32[256,2,8]{0,2,1:T(8,128)S(1)} %get-tuple-element.94) | copy-start | bytes 49156
  66.1 5.9 %copy-start.1 = (f32[256,2,8,64]{0,3,2,1:T(8,128)S(1)}, f32[256,2,8,64]{0,3,2,1:T(8,128)}, u32[]{:S(2)}) copy-start(f32[256,2,8,64]{0,3,2,1:T(8,128)} %get-tuple-element.95) | copy-start | bytes 3145732
  66.1 5.9 %copy-start.3 = (f32[2,256,256]{2,1,0:T(8,128)S(1)}, f32[2,256,256]{2,1,0:T(8,128)}, u32[]{:S(2)}) copy-start(f32[2,256,256]{2,1,0:T(8,128)} %fusion.135) | copy-start | bytes 1572868
  66.1 5.9 %copy-start.54 = (f32[2,8]{1,0:T(2,128)S(1)}, f32[2,8]{1,0:T(2,128)}, u32[]{:S(2)}) copy-start(f32[2,8]{1,0:T(2,128)} %param.20) | copy-start | bytes 196
  72.0 2.4 %copy-start = (f32[256,2,8,64]{0,3,2,1:T(8,128)S(1)}, f32[256,2,8,64]{0,3,2,1:T(8,128)}, u32[]{:S(2)}) copy-start(f32[256,2,8,64]{0,3,2,1:T(8,128)} %get-tuple-element.97) | copy-start | bytes 3145732
  72.0 2.4 %copy-start.8 = (f32[256,2,8]{0,2,1:T(8,128)S(1)}, f32[256,2,8]{0,2,1:T(8,128)}, u32[]{:S(2)}) copy-start(f32[256,2,8]{0,2,1:T(8,128)} %copy-done.7) | copy-start | bytes 49156
  74.4 2.6 %copy-start.50 = (f32[2,8]{1,0:T(2,128)S(1)}, f32[2,8]{1,0:T(2,128)}, u32[]{:S(2)}) copy-start(f32[2,8]{1,0:T(2,128)} %get-tuple-element.67) | copy-start | bytes 196
  74.4 3.3 %copy-start.6 = (f32[256,2,64]{0,2,1:T(8,128)S(1)}, f32[256,2,64]{0,2,1:T(8,128)}, u32[]{:S(2)}) copy-start(f32[256,2,64]{0,2,1:T(8,128)} %get-tuple-element.62) | copy-start | bytes 393220
  74.4 3.7 %copy-start.39 = (f32[2,64]{1,0:T(2,128)S(1)}, f32[2,64]{1,0:T(2,128)}, u32[]{:S(2)}) copy-start(f32[2,64]{1,0:T(2,128)} %copy-done.38) | copy-start | bytes 1540
  74.4 3.7 %copy-start.41 = (f32[2,64]{1,0:T(2,128)S(1)}, f32[2,64]{1,0:T(2,128)}, u32[]{:S(2)}) copy-start(f32[2,64]{1,0:T(2,128)} %copy-done.40) | copy-start | bytes 1540
  74.4 3.7 %copy-start.43 = (f32[2,64]{1,0:T(2,128)S(1)}, f32[2,64]{1,0:T(2,128)}, u32[]{:S(2)}) copy-start(f32[2,64]{1,0:T(2,128)} %copy-done.42) | copy-start | bytes 1540
  74.4 3.7 %copy-start.45 = (f32[2,64]{1,0:T(2,128)S(1)}, f32[2,64]{1,0:T(2,128)}, u32[]{:S(2)}) copy-start(f32[2,64]{1,0:T(2,128)} %copy-done.44) | copy-start | bytes 1540
  82.8 2.2 %copy-start.12 = (f32[256,2,8]{0,2,1:T(8,128)S(1)}, f32[256,2,8]{0,2,1:T(8,128)}, u32[]{:S(2)}) copy-start(f32[256,2,8]{0,2,1:T(8,128)} %copy-done.11) | copy-start | bytes 49156
  82.8 2.2 %copy-start.15 = (f32[256,2,8]{0,2,1:T(8,128)S(1)}, f32[256,2,8]{0,2,1:T(8,128)}, u32[]{:S(2)}) copy-start(f32[256,2,8]{0,2,1:T(8,128)} %param.17) | copy-start | bytes 49156
  82.8 2.2 %copy-start.29 = (f32[2,8]{1,0:T(2,128)S(1)}, f32[2,8]{1,0:T(2,128)}, u32[]{:S(2)}) copy-start(f32[2,8]{1,0:T(2,128)} %copy-done.27) | copy-start | bytes 196
  82.8 2.2 %copy-start.46 = (f32[1,2,8]{0,2,1:T(8,128)S(1)}, f32[1,2,8]{0,2,1:T(8,128)}, u32[]{:S(2)}) copy-start(f32[1,2,8]{0,2,1:T(8,128)} %copy.139) | copy-start | bytes 196
  82.8 2.2 %copy-start.48 = (f32[2,8]{1,0:T(2,128)S(1)}, f32[2,8]{1,0:T(2,128)}, u32[]{:S(2)}) copy-start(f32[2,8]{1,0:T(2,128)} %param.19) | copy-start | bytes 196
  82.8 2.5 %copy-start.55 = (f32[2,8,256]{2,1,0:T(8,128)S(1)}, f32[2,8,256]{2,1,0:T(8,128)}, u32[]{:S(2)}) copy-start(f32[2,8,256]{2,1,0:T(8,128)} %get-tuple-element.46) | copy-start | bytes 49156
  82.8 2.5 %copy-start.56 = (f32[2,8,256]{2,1,0:T(8,128)S(1)}, f32[2,8,256]{2,1,0:T(8,128)}, u32[]{:S(2)}) copy-start(f32[2,8,256]{2,1,0:T(8,128)} %get-tuple-element.47) | copy-start | bytes 49156
  82.8 2.5 %copy-start.57 = (f32[2,8,256]{2,1,0:T(8,128)S(1)}, f32[2,8,256]{2,1,0:T(8,128)}, u32[]{:S(2)}) copy-start(f32[2,8,256]{2,1,0:T(8,128)} %get-tuple-element.48) | copy-start | bytes 49156
  83.4 5.6 %collective-permute-start.7 = (f32[3,2,640]{2,1,0:T(2,128)S(1)}, f32[3,2,640]{2,1,0:T(2,128)S(1)}, u32[]{:S(2)}, u32[]{:S(2)}) collective-permute-start(f32[3,2,640]{2,1,0:T(2,128)S(1)} %pad_maximum_fusion.9), channel_id=1, source_target_pairs={{2,0},{4,2},{6,4},{8,6},{10,8},{12,10},{14,12},{3,1},{5,3},{7,5},{... | collective-permute-start | bytes 46088 | tf_op jit(solution)/shard_map/ppermute | solution.py:12
  (18 other events, 24.2 us)
